TPU v7x, 32 devices: a whole 2x2x4 slice. The times are simulated.
32 devices in a mesh: dp: 2 (over y), row: 4 (over x, core), col: 4 (over z).
Axes of the slice: x: 2, y: 2, z: 4, core: 2. Of those that a mesh axis runs over, the one named last changes fastest.
Arguments:
- patches: bfloat16 [2, 512, 1456], P('dp', 'col', 'row'), may hold values from -6 to 6
- queries: bfloat16 [2, 512, 6144], P('dp', 'col', 'row'), may hold values from -6 to 6
- attn_keys: bfloat16 [2, 512, 6144], P('dp', 'col', 'row'), may hold values from -6 to 6
- attn_values: bfloat16 [2, 512, 6144], P('dp', 'col', 'row'), may hold values from -6 to 6
- out_weight: bfloat16 [6144, 12288], P('row', 'col'), may hold values from -0.15625 to 0.15625
- output_grad: bfloat16 [2, 512, 12288], P('dp', 'row', 'col'), may hold values from -4 to 4
Outputs:
- query_grad: float32 [2, 512, 6144], P('dp', 'col', 'row')
- key_grad: float32 [2, 512, 6144], P('dp', 'col', 'row')
- value_grad: float32 [2, 512, 6144], P('dp', 'col', 'row')
- out_weight_grad: float32 [6144, 12288], P('row', 'col')
- embed_weight_grad: float32 [1456, 12288], P('row', 'col')
All inputs are finite; a program needn't handle non-finite values.
Results may differ from a plain program's by a relative error of at most 0.025.
Values may be sent and summed in bfloat16 or wider, within the bound.
No kernel may reach another device: no remote copies, remote signals or barrier semaphores. Data moves between devices by JAX's collectives and lax.ppermute only.
A program may use at most 128 MiB of HBM per device.

v0:
```python
import jax
import jax.numpy as jnp
from jax import lax
from jax.sharding import PartitionSpec as P

DH = 128


def contract_rows(left, right):
    return lax.dot_general(
        left, right, (((0,), (0,)), ((), ())), preferred_element_type=jnp.float32
    )


def body(patches, queries, attn_keys, attn_values, out_weight, output_grad):
    factor = DH ** (-0.5)
    local_rows = queries.shape[1]
    feature_width = queries.shape[2]
    head_count = feature_width // DH
    every_key, every_value, every_patch = (
        lax.all_gather(attn_keys, "col", axis=1, tiled=True),
        lax.all_gather(attn_values, "col", axis=1, tiled=True),
        lax.all_gather(patches, "col", axis=1, tiled=True),
    )
    local_query = queries[0].reshape(local_rows, head_count, DH)
    all_keys = every_key[0].reshape(-1, head_count, DH)
    all_values = every_value[0].reshape(-1, head_count, DH)
    scores = (
        jnp.einsum("qhd,khd->hqk", local_query, all_keys, preferred_element_type=jnp.float32)
        * factor
    )
    row_max = jnp.max(scores, axis=2, keepdims=True)
    log_total = row_max + jnp.log(jnp.sum(jnp.exp(scores - row_max), axis=2, keepdims=True))
    attn_probs = jnp.exp(scores - log_total).astype(jnp.bfloat16)
    attn_out = jnp.einsum(
        "hqk,khd->qhd", attn_probs, all_values, preferred_element_type=jnp.float32
    ).astype(jnp.bfloat16)
    out_local = attn_out.reshape(1, local_rows, feature_width)
    dense_grad = lax.all_gather(output_grad, "row", axis=1, tiled=True)[0]
    attn_grad = lax.psum_scatter(
        lax.dot_general(
            dense_grad, out_weight, (((1,), (1,)), ((), ())), preferred_element_type=jnp.float32
        ),
        "col",
        scatter_dimension=0,
        tiled=True,
    ).astype(jnp.bfloat16)
    grad_heads = attn_grad.reshape(local_rows, head_count, DH)
    prob_grad = jnp.einsum(
        "qhd,khd->hqk", grad_heads, all_values, preferred_element_type=jnp.float32
    )
    row_dot = jnp.transpose(
        jnp.sum(grad_heads.astype(jnp.float32) * attn_out.astype(jnp.float32), axis=2)
    )[:, :, None]
    score_grad = (attn_probs.astype(jnp.float32) * (prob_grad - row_dot)).astype(jnp.bfloat16)
    query_grad = (
        jnp.einsum("hqk,khd->qhd", score_grad, all_keys, preferred_element_type=jnp.float32)
        * factor
    )
    every_out = lax.all_gather(out_local, "col", axis=1, tiled=True)
    key_term = (
        jnp.einsum("hqk,qhd->khd", score_grad, local_query, preferred_element_type=jnp.float32)
        * factor
    )
    value_term = jnp.einsum(
        "hqk,qhd->khd", attn_probs, grad_heads, preferred_element_type=jnp.float32
    )
    key_sum, value_sum = (
        lax.psum_scatter(
            key_term.reshape(-1, feature_width).astype(jnp.bfloat16),
            "col",
            scatter_dimension=0,
            tiled=True,
        ).astype(jnp.float32),
        lax.psum_scatter(
            value_term.reshape(-1, feature_width).astype(jnp.bfloat16),
            "col",
            scatter_dimension=0,
            tiled=True,
        ).astype(jnp.float32),
    )
    out_part = contract_rows(every_out[0], dense_grad)
    embed_part = contract_rows(every_patch[0], dense_grad)
    out_weight_grad, embed_weight_grad = (
        lax.psum(out_part.astype(jnp.bfloat16), "dp").astype(jnp.float32),
        lax.psum(embed_part.astype(jnp.bfloat16), "dp").astype(jnp.float32),
    )
    return (
        query_grad.reshape(1, local_rows, feature_width),
        key_sum.reshape(1, local_rows, feature_width),
        value_sum.reshape(1, local_rows, feature_width),
        out_weight_grad,
        embed_weight_grad,
    )


def solution(mesh):
    placed = (
        P("dp", "col", "row"),
        P("dp", "col", "row"),
        P("dp", "col", "row"),
        P("dp", "col", "row"),
        P("row", "col"),
        P("dp", "row", "col"),
    )
    return jax.shard_map(
        body,
        mesh=mesh,
        in_specs=placed,
        out_specs=(
            P("dp", "col", "row"),
            P("dp", "col", "row"),
            P("dp", "col", "row"),
            P("row", "col"),
            P("row", "col"),
        ),
        check_vma=False,
    )
```

profile of v0, /device:TPU:0, one launch (start us, length us, event | category | flops | bytes accessed | tf_op | source)
XLA Modules:
  0.0 593.3 jit_solution(1535676170303104737)
XLA Ops:
  7.2 0.0 all-gather.7.cloned.1.call-start
  7.2 0.7 all-gather.7.cloned.1.call-update
  7.9 0.0 all-gather.5.cloned.1.call-start
  7.9 1.9 copy.22
  9.9 0.0 reduce-scatter.4.cloned.1.call-start
  9.9 30.9 %all-gather.7.cloned.1.call-done = bf16[1,512,3072]{2,1,0:T(8,128)(2,1)} async-done(((bf16[1,128,3072]{2,1,0:T(8,128)(2,1)}), bf16[1,512,3072]{2,1,0:T(8,128)(2,1)}) %all-gather.7.cloned.1.call-update) | async-done | bytes 3145744 | tf_op jit(solution)/shard_map/all_gather | solution.py:39
  40.8 10.6 %fusion.2 = f32[512,1536]{1,0:T(8,128)} fusion(bf16[1536,3072]{1,0:T(8,128)(2,1)} %param.10, bf16[1,512,3072]{2,1,0:T(8,128)(2,1)} %all-gather.7.cloned.1.call-done), kind=kOutput, calls=%fused_computation.4 | convolution fusion | flops 4831838208 | bytes 15728640 | tf_op jit(solution)/shard_map/dot_general | solution.py:41
  51.4 0.0 reduce-scatter.4.cloned.1.call-update
  51.4 0.0 all-gather.9.cloned.1.call-start
  51.5 0.9 copy-done.3
  52.4 0.9 copy.26
  53.3 0.0 all-gather.9.cloned.1.call-update
  53.4 0.0 all-gather.11.cloned.1.call-start
  53.4 0.2 copy.21
  53.7 27.0 %all-gather.5.cloned.1.call-done = bf16[1,512,1536]{1,2,0:T(8,128)(2,1)} async-done(((bf16[1,128,1536]{1,2,0:T(8,128)(2,1)}), bf16[1,512,1536]{1,2,0:T(8,128)(2,1)}) %all-gather.5.cloned.1.call-update) | async-done | bytes 1572880 | tf_op jit(solution)/shard_map/all_gather | solution.py:21
  80.7 2.1 multiply_reduce_fusion
  82.8 1.0 exponential_reduce_fusion
  83.8 0.5 exponential_convert_fusion
  84.4 57.7 %reduce-scatter.4.cloned.1.call-done = f32[128,1536]{1,0:T(8,128)} async-done(((f32[512,1536]{1,0:T(8,128)}), f32[128,1536]{1,0:T(8,128)}) %reduce-scatter.4.cloned.1.call-update) | async-done | bytes 786448 | tf_op jit(solution)/shard_map/reduce_scatter | solution.py:40
  142.1 1.2 convert_element_type.58
  143.3 0.2 copy.25
  143.5 38.4 %all-gather.9.cloned.1.call-done = bf16[1,512,1536]{1,2,0:T(8,128)(2,1)} async-done(((bf16[1,128,1536]{1,2,0:T(8,128)(2,1)}), bf16[1,512,1536]{1,2,0:T(8,128)(2,1)}) %all-gather.9.cloned.1.call-update) | async-done | bytes 1572880 | tf_op jit(solution)/shard_map/all_gather | solution.py:22
  181.9 2.7 multiply_reduce_fusion.1
  184.6 0.0 reduce-scatter.6.cloned.1.call-start
  184.7 2.0 multiply_convert_fusion.1
  186.7 2.7 multiply_convert_fusion
  189.4 2.7 copy.29
  192.1 0.0 reduce-scatter.6.cloned.1.call-update
  192.1 0.0 reduce-scatter.8.cloned.1.call-start
  192.1 1.7 convolution_convert_fusion.2
  193.8 2.6 copy.30
  196.5 0.0 reduce-scatter.8.cloned.1.call-update
  196.5 0.0 all-reduce.3.cloned.1.call-start
  196.6 20.1 %all_gather.19 = bf16[1,512,364]{1,2,0:T(8,128)(2,1)S(1)} all-gather(bf16[1,128,364]{1,2,0:T(8,128)(2,1)S(1)} %copy-done.5), channel_id=1, replica_groups=mesh['dp'=2,'row'=4,'col'=4] {'col'}, dimensions={1}, use_global_device_ids=true | all-gather | bytes 465920 | tf_op jit(solution)/shard_map/all_gather | solution.py:23
  216.7 4.6 convolution_convert_fusion.1
  221.3 5.5 all-gather.11.cloned.1.call-done
  226.8 9.3 %convolution_convert_fusion = bf16[1536,3072]{1,0:T(8,128)(2,1)} fusion(bf16[1,512,3072]{2,1,0:T(8,128)(2,1)} %all-gather.7.cloned.1.call-done, bf16[1,512,1536]{1,2,0:T(8,128)(2,1)} %all-gather.11.cloned.1.call-done), kind=kOutput, calls=%fused_computation | convolution fusion | flops 4836556800 | bytes 14155776 | tf_op jit(solution)/shard_map/dot_general | solution.py:10
  236.1 0.0 all-reduce.3.cloned.1.call-update
  236.1 1.4 copy-done
  237.5 1.5 convolution_multiply_fusion
  238.9 2.3 copy.31
  241.2 21.2 %reduce-scatter.6.cloned.1.call-done = bf16[128,1536]{1,0:T(8,128)(2,1)} async-done(((bf16[512,1536]{1,0:T(8,128)(2,1)}), bf16[128,1536]{1,0:T(8,128)(2,1)}) %reduce-scatter.6.cloned.1.call-update) | async-done | bytes 393232 | tf_op jit(solution)/shard_map/reduce_scatter | solution.py:69
  262.4 2.0 bitcast_convert_fusion.1
  264.4 34.6 %reduce-scatter.8.cloned.1.call-done = bf16[128,1536]{1,0:T(8,128)(2,1)} async-done(((bf16[512,1536]{1,0:T(8,128)(2,1)}), bf16[128,1536]{1,0:T(8,128)(2,1)}) %reduce-scatter.8.cloned.1.call-update) | async-done | bytes 393232 | tf_op jit(solution)/shard_map/reduce_scatter | solution.py:75
  299.0 2.0 bitcast_convert_fusion
  301.0 270.0 %all-reduce.3.cloned.1.call-done = (bf16[1536,3072]{1,0:T(8,128)(2,1)}, bf16[364,3072]{1,0:T(8,128)(2,1)}) async-done(((bf16[1536,3072]{1,0:T(8,128)(2,1)}, bf16[364,3072]{1,0:T(8,128)(2,1)}), (bf16[1536,3072]{1,0:T(8,128)(2,1)}, bf16[364,3072]{1,0:T(8,128)(2,1)})) %all-reduce.3.cloned.1.call-update) | async-done | bytes 11673616 | tf_op jit(solution)/shard_map/psum | solution.py:85
  571.0 12.9 %convert_element_type.71 = f32[1536,3072]{1,0:T(8,128)} convert(bf16[1536,3072]{1,0:T(8,128)(2,1)} %get-tuple-element.15) | non-fusion elementwise | flops 4718592 | bytes 28311552 | tf_op jit(solution)/shard_map/convert_element_type | solution.py:85
  583.8 2.7 convert_element_type.73
  (13 shorter events, 0.1 us)
Async XLA Ops:
  7.2 33.7 %all-gather.7.cloned.1.call-start = ((), (), s32[]{:S(2)}) async-start(), calls=%async_computation.4 | async-start | bytes 3932160 | tf_op jit(solution)/shard_map/all_gather | solution.py:39
  7.9 72.8 %all-gather.5.cloned.1.call-start = ((), (), s32[]{:S(2)}) async-start(), calls=%async_computation.3 | async-start | bytes 1966080 | tf_op jit(solution)/shard_map/all_gather | solution.py:21
  9.9 132.2 %reduce-scatter.4.cloned.1.call-start = ((), (), s32[]{:S(2)}) async-start(), calls=%async_computation.5 | async-start | bytes 3932160 | tf_op jit(solution)/shard_map/reduce_scatter | solution.py:40
  51.4 1.0 copy-start.3
  51.4 2.0 copy-start.4
  51.4 130.4 %all-gather.9.cloned.1.call-start = ((), (), s32[]{:S(2)}) async-start(), calls=%async_computation.6 | async-start | bytes 1966080 | tf_op jit(solution)/shard_map/all_gather | solution.py:22
  53.4 173.4 %all-gather.11.cloned.1.call-start = ((), (), s32[]{:S(2)}) async-start(), calls=%async_computation.9 | async-start | bytes 1966080 | tf_op jit(solution)/shard_map/all_gather | solution.py:60
  53.6 30.2 %copy-start.1 = (bf16[1,128,1536]{1,2,0:T(8,128)(2,1)}, bf16[1,128,1536]{1,2,0:T(8,128)(2,1)S(1)}, u32[]{:S(2)}) copy-start(bf16[1,128,1536]{1,2,0:T(8,128)(2,1)S(1)} %copy.21) | copy-start | bytes 1179652
  184.6 77.8 %reduce-scatter.6.cloned.1.call-start = ((), (), s32[]{:S(2)}) async-start(), calls=%async_computation.7 | async-start | bytes 1966080 | tf_op jit(solution)/shard_map/reduce_scatter | solution.py:69
  192.1 106.9 %reduce-scatter.8.cloned.1.call-start = ((), (), s32[]{:S(2)}) async-start(), calls=%async_computation.8 | async-start | bytes 1966080 | tf_op jit(solution)/shard_map/reduce_scatter | solution.py:75
  193.8 2.7 copy-start.5
  196.5 374.5 %all-reduce.3.cloned.1.call-start = ((), (), s32[]{:S(2)}) async-start(), calls=%async_computation.10 | async-start | bytes 23396352 | tf_op jit(solution)/shard_map/psum | solution.py:85
  236.1 1.4 copy-start
  571.0 12.9 %copy-start.2 = (bf16[364,3072]{1,0:T(8,128)(2,1)S(1)}, bf16[364,3072]{1,0:T(8,128)(2,1)}, u32[]{:S(2)}) copy-start(bf16[364,3072]{1,0:T(8,128)(2,1)} %get-tuple-element.16) | copy-start | bytes 6709252
Sparse Core Ops, SparseCore 0:
  9.6 31.2 all-gather.6
  43.0 37.7 all-gather.4
  83.6 58.4 reduce-scatter.3
  144.1 37.7 all-gather.8
  184.7 41.9 all-gather.10
  228.9 33.4 reduce-scatter.5
  264.7 34.2 reduce-scatter.7
  302.1 268.8 all-reduce.2
where the time goes:
time: 594 us; the launch traced here: 593 us
  waiting for transfers between devices  486 us (82%)
  matrix products  37.2 us (6%)
  other arithmetic  22.1 us (4%)
  blocking collectives  20.1 us (3%)
  between operations  14.2 us (2%)
  local copies, waits for them, and re-layouts  13.2 us (2%)
    psum x1, waiting for transfers between devices, body(): lax.psum(out_part.astype(jnp.bfloat16), 'dp').astype(jnp.float32)  270 us
    reduce_scatter x1, waiting for transfers between devices, body(): lax.psum_scatter(lax.dot_general(dense_grad, out_weight, (((1,), (1,)), (...  57.7 us
    all_gather x1, waiting for transfers between devices, body(): lax.all_gather(attn_values, 'col', axis=1, tiled=True)  38.4 us
    reduce_scatter x1, waiting for transfers between devices, body(): lax.psum_scatter(value_term.reshape(-1, feature_width).astype(jnp.bfloat1...  34.6 us
    all_gather x1, waiting for transfers between devices, body(): dense_grad = lax.all_gather(output_grad, 'row', axis=1, tiled=True)[0]  30.9 us
    all_gather x1, waiting for transfers between devices, body(): lax.all_gather(attn_keys, 'col', axis=1, tiled=True)  27 us
    reduce_scatter x1, waiting for transfers between devices, body(): lax.psum_scatter(key_term.reshape(-1, feature_width).astype(jnp.bfloat16)...  21.2 us
    all_gather x1, blocking collectives, body(): lax.all_gather(patches, 'col', axis=1, tiled=True)  20.1 us
  transfers between devices with their start and end apart: 8, of which 8 were waited for; matrix products, arithmetic and copies ran while one was open for 9% of the time, Pallas kernels for 0%

commit v1 on v0

--- a/solution.py
+++ b/solution.py
@@ -12,11 +12,17 @@
     )
 
 
+def swap_dp(x):
+    return lax.ppermute(x, "dp", [(0, 1), (1, 0)])
+
+
 def body(patches, queries, attn_keys, attn_values, out_weight, output_grad):
     factor = DH ** (-0.5)
     local_rows = queries.shape[1]
     feature_width = queries.shape[2]
     head_count = feature_width // DH
+    grad_other = swap_dp(output_grad)
+    patch_other = swap_dp(lax.all_gather(patches, "col", axis=1, tiled=True))
     every_key, every_value, every_patch = (
         lax.all_gather(attn_keys, "col", axis=1, tiled=True),
         lax.all_gather(attn_values, "col", axis=1, tiled=True),
@@ -79,11 +85,16 @@
             tiled=True,
         ).astype(jnp.float32),
     )
-    out_part = contract_rows(every_out[0], dense_grad)
-    embed_part = contract_rows(every_patch[0], dense_grad)
-    out_weight_grad, embed_weight_grad = (
-        lax.psum(out_part.astype(jnp.bfloat16), "dp").astype(jnp.float32),
-        lax.psum(embed_part.astype(jnp.bfloat16), "dp").astype(jnp.float32),
+    out_pair = jnp.concatenate([every_out, swap_dp(every_out)], axis=0)
+    grad_pair = lax.all_gather(
+        jnp.concatenate([output_grad, grad_other], axis=0), "row", axis=1, tiled=True
+    )
+    patch_pair = jnp.concatenate([every_patch, patch_other], axis=0)
+    out_weight_grad = lax.dot_general(
+        out_pair, grad_pair, (((0, 1), (0, 1)), ((), ())), preferred_element_type=jnp.float32
+    )
+    embed_weight_grad = lax.dot_general(
+        patch_pair, grad_pair, (((0, 1), (0, 1)), ((), ())), preferred_element_type=jnp.float32
     )
     return (
         query_grad.reshape(1, local_rows, feature_width),

time: 594 us -> 367 us (0.62)
  waiting for transfers between devices: 486 us -> 267 us
  other arithmetic: 22.1 us -> 7.92 us
  matrix products: 37.2 us -> 47.1 us
    psum x1 -> x0, waiting for transfers between devices: 270 us -> none  [body(): lax.psum(out_part.astype(jnp.bfloat16), 'dp').astype(jnp.float32)]
    ppermute x0 -> x3, waiting for transfers between devices: none -> 27.5 us  [swap_dp(): return lax.ppermute(x, 'dp', [(0, 1), (1, 0)])]
    all_gather x0 -> x1, waiting for transfers between devices: none -> 23.4 us  [body(): lax.all_gather(jnp.concatenate([output_grad, grad_other], axis=0), 'row',...]
    convert_element_type x2 -> x0, other arithmetic: 15.5 us -> none  [the longest x1 12.9 us: body(): lax.psum(out_part.astype(jnp.bfloat16), 'dp').astype(jnp.float32)]
    dot_general x2, matrix products: 13.9 us -> 23.8 us  [the longest x1 16.3 us: body(): lax.dot_general(out_pair, grad_pair, (((0, 1), (0, 1)), ((), ())), prefer...]
  transfers between devices with their start and end apart: 8 -> 11, of which waited for: 8 -> 9; matrix products, arithmetic and copies ran while one was open for 9% -> 13% of each run, Pallas kernels for 0% -> 0%
where the time goes in v1:
time: 367 us
  waiting for transfers between devices  267 us (73%)
  matrix products  47.1 us (13%)
  blocking collectives  14.4 us (4%)
  between operations  14.2 us (4%)
  local copies, waits for them, and re-layouts  11.8 us (3%)
  other arithmetic  7.92 us (2%)
  starting transfers between devices  3.94 us (1%)
    reduce_scatter x1, waiting for transfers between devices, body(): lax.psum_scatter(lax.dot_general(dense_grad, out_weight, (((1,), (1,)), (...  57.7 us
    all_gather x1, waiting for transfers between devices, body(): lax.all_gather(attn_values, 'col', axis=1, tiled=True)  38.4 us
    reduce_scatter x1, waiting for transfers between devices, body(): lax.psum_scatter(value_term.reshape(-1, feature_width).astype(jnp.bfloat1...  34.6 us
    all_gather x1, waiting for transfers between devices, body(): dense_grad = lax.all_gather(output_grad, 'row', axis=1, tiled=True)[0]  30.9 us
    ppermute x3, waiting for transfers between devices, swap_dp(): return lax.ppermute(x, 'dp', [(0, 1), (1, 0)])  27.5 us
    all_gather x1, waiting for transfers between devices, body(): lax.all_gather(attn_keys, 'col', axis=1, tiled=True)  27 us
    reduce_scatter x1, waiting for transfers between devices, body(): lax.psum_scatter(key_term.reshape(-1, feature_width).astype(jnp.bfloat16)...  26.8 us
    all_gather x1, waiting for transfers between devices, body(): lax.all_gather(jnp.concatenate([output_grad, grad_other], axis=0), 'row',...  23.4 us
  transfers between devices with their start and end apart: 11, of which 9 were waited for; matrix products, arithmetic and copies ran while one was open for 13% of the time, Pallas kernels for 0%

profile of v1, /device:TPU:0, one launch (start us, length us, event | category | flops | bytes accessed | tf_op | source)
XLA Modules:
  0.0 366.7 jit_solution(11999108349264509849)
XLA Ops:
  7.2 0.0 all-gather.8.cloned.1.call-start
  7.2 0.7 all-gather.8.cloned.1.call-update
  7.9 0.0 all-gather.6.cloned.1.call-start
  7.9 1.9 copy.22
  9.9 0.0 all-gather.6.cloned.1.call-update
  9.9 0.0 reduce-scatter.4.cloned.1.call-start
  9.9 30.9 %all-gather.8.cloned.1.call-done = bf16[1,512,3072]{2,1,0:T(8,128)(2,1)} async-done(((bf16[1,128,3072]{2,1,0:T(8,128)(2,1)}), bf16[1,512,3072]{2,1,0:T(8,128)(2,1)}) %all-gather.8.cloned.1.call-update) | async-done | bytes 3145744 | tf_op jit(solution)/shard_map/all_gather | solution.py:45
  40.8 10.6 %fusion.3 = f32[512,1536]{1,0:T(8,128)} fusion(bf16[1536,3072]{1,0:T(8,128)(2,1)} %param.10, bf16[1,512,3072]{2,1,0:T(8,128)(2,1)} %all-gather.8.cloned.1.call-done), kind=kOutput, calls=%fused_computation.5 | convolution fusion | flops 4831838208 | bytes 15728640 | tf_op jit(solution)/shard_map/dot_general | solution.py:47
  51.4 0.0 reduce-scatter.4.cloned.1.call-update
  51.4 0.0 all-gather.10.cloned.1.call-start
  51.5 0.9 copy-done.3
  52.4 0.9 copy.26
  53.3 0.0 all-gather.10.cloned.1.call-update
  53.4 0.0 all-gather.12.cloned.1.call-start
  53.4 0.2 copy.21
  53.7 27.0 %all-gather.6.cloned.1.call-done = bf16[1,512,1536]{1,2,0:T(8,128)(2,1)} async-done(((bf16[1,128,1536]{1,2,0:T(8,128)(2,1)}), bf16[1,512,1536]{1,2,0:T(8,128)(2,1)}) %all-gather.6.cloned.1.call-update) | async-done | bytes 1572880 | tf_op jit(solution)/shard_map/all_gather | solution.py:27
  80.7 2.1 multiply_reduce_fusion
  82.8 1.0 exponential_reduce_fusion
  83.8 0.5 exponential_convert_fusion
  84.4 57.7 %reduce-scatter.4.cloned.1.call-done = f32[128,1536]{1,0:T(8,128)} async-done(((f32[512,1536]{1,0:T(8,128)}), f32[128,1536]{1,0:T(8,128)}) %reduce-scatter.4.cloned.1.call-update) | async-done | bytes 786448 | tf_op jit(solution)/shard_map/reduce_scatter | solution.py:46
  142.1 1.2 convert_element_type.46
  143.3 0.2 copy.25
  143.5 38.4 %all-gather.10.cloned.1.call-done = bf16[1,512,1536]{1,2,0:T(8,128)(2,1)} async-done(((bf16[1,128,1536]{1,2,0:T(8,128)(2,1)}), bf16[1,512,1536]{1,2,0:T(8,128)(2,1)}) %all-gather.10.cloned.1.call-update) | async-done | bytes 1572880 | tf_op jit(solution)/shard_map/all_gather | solution.py:28
  181.9 2.7 multiply_reduce_fusion.1
  184.6 0.0 all-gather.14.cloned.1.call-start
  184.7 1.6 collective-permute-start.1
  186.3 17.8 %collective-permute-done.1 = bf16[1,128,3072]{2,1,0:T(8,128)(2,1)S(1)} collective-permute-done((bf16[1,128,3072]{2,1,0:T(8,128)(2,1)S(1)}, bf16[1,128,3072]{2,1,0:T(8,128)(2,1)S(1)}, u32[]{:S(2)}, u32[]{:S(2)}) %collective-permute-start.1) | collective-permute-done | bytes 786464 | tf_op jit(solution)/shard_map/ppermute | solution.py:16
  204.0 1.3 pad_maximum_fusion
  205.4 0.0 reduce-scatter.6.cloned.1.call-start
  205.4 2.0 multiply_convert_fusion.1
  207.5 2.7 multiply_convert_fusion
  210.2 2.6 copy.29
  212.8 0.0 reduce-scatter.8.cloned.1.call-start
  212.8 1.7 convolution_convert_fusion
  214.5 2.6 copy.30
  217.2 14.4 %all_gather.24 = bf16[1,512,364]{1,2,0:T(8,128)(2,1)S(1)} all-gather(bf16[1,128,364]{1,2,0:T(8,128)(2,1)S(1)} %copy-done.5), channel_id=1, replica_groups=mesh['dp'=2,'row'=4,'col'=4] {'col'}, dimensions={1}, use_global_device_ids=true | all-gather | bytes 465920 | tf_op jit(solution)/shard_map/all_gather | solution.py:29
  231.5 1.2 collective-permute-start.2
  232.7 0.8 collective-permute-start
  233.6 9.8 %collective-permute-done.2 = bf16[1,512,364]{1,2,0:T(8,128)(2,1)} collective-permute-done((bf16[1,512,364]{1,2,0:T(8,128)(2,1)S(1)}, bf16[1,512,364]{1,2,0:T(8,128)(2,1)}, u32[]{:S(2)}, u32[]{:S(2)}) %collective-permute-start.2) | collective-permute-done | bytes 372768 | tf_op jit(solution)/shard_map/ppermute | solution.py:16
  243.3 23.4 %all-gather.14.cloned.1.call-done = bf16[2,512,3072]{2,1,0:T(8,128)(2,1)} async-done(((bf16[2,128,3072]{2,1,0:T(8,128)(2,1)}), bf16[2,512,3072]{2,1,0:T(8,128)(2,1)}) %all-gather.14.cloned.1.call-update) | async-done | bytes 6291472 | tf_op jit(solution)/shard_map/all_gather | solution.py:89
  266.8 7.5 %convolution_bitcast_fusion.1 = f32[364,3072]{1,0:T(8,128)} fusion(bf16[2,512,3072]{2,1,0:T(8,128)(2,1)} %all-gather.14.cloned.1.call-done, bf16[1,512,364]{1,2,0:T(8,128)(2,1)} %collective-permute-done.2, bf16[1,512,364]{1,2,0:T(8,128)(2,1)S(1)} %all_gather.24), kind=kOutput, calls=%fused_computation.1 | convolution fusion | flops 2290462720 | bytes 11509760 | tf_op jit(solution)/shard_map/dot_general | solution.py:96
  274.3 1.5 convolution_multiply_fusion
  275.8 2.4 copy.31
  278.2 26.8 %reduce-scatter.6.cloned.1.call-done = bf16[128,1536]{1,0:T(8,128)(2,1)} async-done(((bf16[512,1536]{1,0:T(8,128)(2,1)}), bf16[128,1536]{1,0:T(8,128)(2,1)}) %reduce-scatter.6.cloned.1.call-update) | async-done | bytes 393232 | tf_op jit(solution)/shard_map/reduce_scatter | solution.py:75
  305.0 2.0 bitcast_convert_fusion.1
  306.9 34.6 %reduce-scatter.8.cloned.1.call-done = bf16[128,1536]{1,0:T(8,128)(2,1)} async-done(((bf16[512,1536]{1,0:T(8,128)(2,1)}), bf16[128,1536]{1,0:T(8,128)(2,1)}) %reduce-scatter.8.cloned.1.call-update) | async-done | bytes 393232 | tf_op jit(solution)/shard_map/reduce_scatter | solution.py:81
  341.6 2.0 bitcast_convert_fusion
  343.5 16.3 %convolution_bitcast_fusion = f32[1536,3072]{1,0:T(8,128)} fusion(bf16[2,512,3072]{2,1,0:T(8,128)(2,1)} %all-gather.14.cloned.1.call-done, bf16[1,512,1536]{1,2,0:T(8,128)(2,1)} %collective-permute-done, bf16[1,512,1536]{1,2,0:T(8,128)(2,1)S(1)} %copy-done.6), kind=kOutput, calls=%fused_computation | convolution fusion | flops 9665249280 | bytes 28311552 | tf_op jit(solution)/shard_map/dot_general | solution.py:93
  (20 shorter events, 0.1 us)
Async XLA Ops:
  7.2 33.7 %all-gather.8.cloned.1.call-start = ((), (), s32[]{:S(2)}) async-start(), calls=%async_computation.4 | async-start | bytes 3932160 | tf_op jit(solution)/shard_map/all_gather | solution.py:45
  7.9 72.8 %all-gather.6.cloned.1.call-start = ((), (), s32[]{:S(2)}) async-start(), calls=%async_computation.3 | async-start | bytes 1966080 | tf_op jit(solution)/shard_map/all_gather | solution.py:27
  9.9 132.2 %reduce-scatter.4.cloned.1.call-start = ((), (), s32[]{:S(2)}) async-start(), calls=%async_computation.5 | async-start | bytes 3932160 | tf_op jit(solution)/shard_map/reduce_scatter | solution.py:46
  51.4 1.0 copy-start.3
  51.4 2.0 copy-start.4
  51.4 130.4 %all-gather.10.cloned.1.call-start = ((), (), s32[]{:S(2)}) async-start(), calls=%async_computation.6 | async-start | bytes 1966080 | tf_op jit(solution)/shard_map/all_gather | solution.py:28
  53.4 179.4 %all-gather.12.cloned.1.call-start = ((), (), s32[]{:S(2)}) async-start(), calls=%async_computation.9 | async-start | bytes 1966080 | tf_op jit(solution)/shard_map/all_gather | solution.py:66
  53.6 30.2 %copy-start.1 = (bf16[1,128,1536]{1,2,0:T(8,128)(2,1)}, bf16[1,128,1536]{1,2,0:T(8,128)(2,1)S(1)}, u32[]{:S(2)}) copy-start(bf16[1,128,1536]{1,2,0:T(8,128)(2,1)S(1)} %copy.21) | copy-start | bytes 1179652
  84.4 100.3 %copy-start.2 = (bf16[1,128,3072]{2,1,0:T(8,128)(2,1)S(1)}, bf16[1,128,3072]{2,1,0:T(8,128)(2,1)}, u32[]{:S(2)}) copy-start(bf16[1,128,3072]{2,1,0:T(8,128)(2,1)} %param.11) | copy-start | bytes 2359300
  184.6 82.2 %all-gather.14.cloned.1.call-start = ((), (), s32[]{:S(2)}) async-start(), calls=%async_computation.10 | async-start | bytes 7864320 | tf_op jit(solution)/shard_map/all_gather | solution.py:89
  184.7 19.3 %collective-permute-start.1 = (bf16[1,128,3072]{2,1,0:T(8,128)(2,1)S(1)}, bf16[1,128,3072]{2,1,0:T(8,128)(2,1)S(1)}, u32[]{:S(2)}, u32[]{:S(2)}) collective-permute-start(bf16[1,128,3072]{2,1,0:T(8,128)(2,1)S(1)} %copy-done.2), channel_id=1, source_target_pairs={{0,16},{16,0},{1,17},{17,1},{2,18},{18,2},{3,19},{19,3},{4,20},{20... | collective-permute-start | bytes 2359304 | tf_op jit(solution)/shard_map/ppermute | solution.py:16
  205.4 99.6 %reduce-scatter.6.cloned.1.call-start = ((), (), s32[]{:S(2)}) async-start(), calls=%async_computation.7 | async-start | bytes 1966080 | tf_op jit(solution)/shard_map/reduce_scatter | solution.py:75
  212.8 128.8 %reduce-scatter.8.cloned.1.call-start = ((), (), s32[]{:S(2)}) async-start(), calls=%async_computation.8 | async-start | bytes 1966080 | tf_op jit(solution)/shard_map/reduce_scatter | solution.py:81
  214.5 2.6 copy-start.5
  231.5 42.8 %copy-start = (bf16[1,512,1536]{1,2,0:T(8,128)(2,1)S(1)}, bf16[1,512,1536]{1,2,0:T(8,128)(2,1)}, u32[]{:S(2)}) copy-start(bf16[1,512,1536]{1,2,0:T(8,128)(2,1)} %all-gather.6.cloned.1.call-done) | copy-start | bytes 4718596
  231.5 11.8 %collective-permute-start.2 = (bf16[1,512,364]{1,2,0:T(8,128)(2,1)S(1)}, bf16[1,512,364]{1,2,0:T(8,128)(2,1)}, u32[]{:S(2)}, u32[]{:S(2)}) collective-permute-start(bf16[1,512,364]{1,2,0:T(8,128)(2,1)S(1)} %all_gather.24), channel_id=1, source_target_pairs={{0,16},{16,0},{1,17},{17,1},{2,18},{18,2},{3,19},{19,3},{4,20},{20... | collective-permute-start | bytes 1118216 | tf_op jit(solution)/shard_map/ppermute | solution.py:16
  232.7 110.8 %collective-permute-start = (bf16[1,512,1536]{1,2,0:T(8,128)(2,1)}, bf16[1,512,1536]{1,2,0:T(8,128)(2,1)}, u32[]{:S(2)}, u32[]{:S(2)}) collective-permute-start(bf16[1,512,1536]{1,2,0:T(8,128)(2,1)} %all-gather.12.cloned.1.call-done), channel_id=1, source_target_pairs={{0,16},{16,0},{1,17},{17,1},{2,18},{18,2},{3,19},{19,3},{4,20},{20... | collective-permute-start | bytes 4718600 | tf_op jit(solution)/shard_map/ppermute | solution.py:16
  275.8 67.8 %copy-start.6 = (bf16[1,512,1536]{1,2,0:T(8,128)(2,1)S(1)}, bf16[1,512,1536]{1,2,0:T(8,128)(2,1)}, u32[]{:S(2)}) copy-start(bf16[1,512,1536]{1,2,0:T(8,128)(2,1)} %all-gather.12.cloned.1.call-done) | copy-start | bytes 4718596
Sparse Core Ops, SparseCore 0:
  9.6 31.2 all-gather.7
  43.0 37.7 all-gather.5
  83.6 58.4 reduce-scatter.3
  144.1 37.7 all-gather.9
  184.7 35.9 all-gather.11
  222.1 44.5 all-gather.13
  269.6 35.3 reduce-scatter.5
  307.3 34.2 reduce-scatter.7

commit v2 on v1

--- a/solution.py
+++ b/solution.py
@@ -16,7 +16,7 @@
     return lax.ppermute(x, "dp", [(0, 1), (1, 0)])
 
 
-def body(patches, queries, attn_keys, attn_values, out_weight, output_grad):
+def body_tokens(patches, queries, attn_keys, attn_values, out_weight, output_grad):
     factor = DH ** (-0.5)
     local_rows = queries.shape[1]
     feature_width = queries.shape[2]
@@ -105,6 +105,132 @@
     )
 
 
+def axis_size(axis):
+    return lax.psum(1, axis)
+
+
+def shifted(x, axis, step):
+    n = axis_size(axis)
+    return lax.ppermute(x, axis, [(j, (j + step) % n) for j in range(n)])
+
+
+def natural(pieces, axis):
+    n = len(pieces)
+    order = (lax.axis_index(axis) - jnp.arange(n)) % n
+    return jnp.take(jnp.stack(pieces, 0), order, axis=0)
+
+
+def gather_rows(x, axis):
+    n = axis_size(axis)
+    pieces = [x] + [shifted(x, axis, s) for s in range(1, n)]
+    stacked = natural(pieces, axis)
+    return stacked.reshape((n * x.shape[0],) + x.shape[1:])
+
+
+def group_cols(x, axis, group):
+    width = x.shape[1] // axis_size(axis)
+    return lax.dynamic_slice_in_dim(x, group * width, width, 1)
+
+
+def to_heads(x, axis):
+    n, me = axis_size(axis), lax.axis_index(axis)
+    pieces = [group_cols(x, axis, me)] + [
+        shifted(group_cols(x, axis, (me + s) % n), axis, s) for s in range(1, n)
+    ]
+    stacked = natural(pieces, axis)
+    return stacked.reshape((n * x.shape[0],) + stacked.shape[2:])
+
+
+def from_heads(x, axis):
+    n, me = axis_size(axis), lax.axis_index(axis)
+    rows = x.shape[0] // n
+    block = lambda k: lax.dynamic_slice_in_dim(x, k * rows, rows, 0)
+    pieces = [block(me)] + [
+        shifted(block((me + s) % n).astype(jnp.bfloat16), axis, s).astype(jnp.float32)
+        for s in range(1, n)
+    ]
+    stacked = natural(pieces, axis)
+    return jnp.transpose(stacked, (1, 0, 2)).reshape(rows, n * x.shape[1])
+
+
+def sum_to_heads(partial, axis):
+    n, me = axis_size(axis), lax.axis_index(axis)
+    total = group_cols(partial, axis, me)
+    for s in range(1, n):
+        sent = group_cols(partial, axis, (me - s) % n).astype(jnp.bfloat16)
+        total = total + shifted(sent, axis, -s % n).astype(jnp.float32)
+    return total
+
+
+def body_heads(patches, queries, attn_keys, attn_values, out_weight, output_grad):
+    factor = DH ** (-0.5)
+    ncol = axis_size("col")
+    grad_other = swap_dp(output_grad)
+    dense_grad = gather_rows(output_grad[0], "row")
+    other_grad = gather_rows(grad_other[0], "row")
+    query_h, key_h, value_h = (to_heads(a[0], "col") for a in (queries, attn_keys, attn_values))
+    rows, width = query_h.shape
+    heads = width // DH
+    local_query = query_h.reshape(rows, heads, DH)
+    all_keys = key_h.reshape(rows, heads, DH)
+    all_values = value_h.reshape(rows, heads, DH)
+    scores = (
+        jnp.einsum("qhd,khd->hqk", local_query, all_keys, preferred_element_type=jnp.float32)
+        * factor
+    )
+    row_max = jnp.max(scores, axis=2, keepdims=True)
+    log_total = row_max + jnp.log(jnp.sum(jnp.exp(scores - row_max), axis=2, keepdims=True))
+    attn_probs = jnp.exp(scores - log_total).astype(jnp.bfloat16)
+    attn_out = jnp.einsum(
+        "hqk,khd->qhd", attn_probs, all_values, preferred_element_type=jnp.float32
+    ).astype(jnp.bfloat16)
+    grad_partial = lax.dot_general(
+        dense_grad, out_weight, (((1,), (1,)), ((), ())), preferred_element_type=jnp.float32
+    )
+    attn_grad = sum_to_heads(grad_partial, "col").astype(jnp.bfloat16)
+    grad_heads = attn_grad.reshape(rows, heads, DH)
+    prob_grad = jnp.einsum(
+        "qhd,khd->hqk", grad_heads, all_values, preferred_element_type=jnp.float32
+    )
+    row_dot = jnp.transpose(
+        jnp.sum(grad_heads.astype(jnp.float32) * attn_out.astype(jnp.float32), axis=2)
+    )[:, :, None]
+    score_grad = (attn_probs.astype(jnp.float32) * (prob_grad - row_dot)).astype(jnp.bfloat16)
+    query_grad = (
+        jnp.einsum("hqk,khd->qhd", score_grad, all_keys, preferred_element_type=jnp.float32)
+        * factor
+    )
+    key_grad = (
+        jnp.einsum("hqk,qhd->khd", score_grad, local_query, preferred_element_type=jnp.float32)
+        * factor
+    )
+    value_grad = jnp.einsum(
+        "hqk,qhd->khd", attn_probs, grad_heads, preferred_element_type=jnp.float32
+    )
+    outs = [from_heads(g.reshape(rows, width), "col")[None] for g in (query_grad, key_grad, value_grad)]
+    out_groups = natural(
+        [attn_out.reshape(rows, width)]
+        + [shifted(attn_out.reshape(rows, width), "col", s) for s in range(1, ncol)],
+        "col",
+    )
+    every_out = jnp.transpose(out_groups, (1, 0, 2)).reshape(rows, ncol * width)
+    other_out = swap_dp(every_out)
+    every_patch = gather_rows(patches[0], "col")
+    other_patch = swap_dp(every_patch)
+    out_weight_grad = contract_rows(every_out, dense_grad) + contract_rows(other_out, other_grad)
+    embed_weight_grad = contract_rows(every_patch, dense_grad) + contract_rows(
+        other_patch, other_grad
+    )
+    return (*outs, out_weight_grad, embed_weight_grad)
+
+
+def body(patches, queries, attn_keys, attn_values, out_weight, output_grad):
+    heads_here = queries.shape[2] // DH
+    if heads_here % axis_size("col") == 0 and queries.shape[1] == output_grad.shape[1]:
+        return body_heads(patches, queries, attn_keys, attn_values, out_weight, output_grad)
+    return body_tokens(patches, queries, attn_keys, attn_values, out_weight, output_grad)
+
+
 def solution(mesh):
     placed = (
         P("dp", "col", "row"),

time: 367 us -> 300 us (0.82)
  waiting for transfers between devices: 267 us -> 118 us
  starting transfers between devices: 3.94 us -> 68.9 us
  local copies, waits for them, and re-layouts: 11.8 us -> 37.4 us
  other arithmetic: 7.92 us -> 26.3 us
  blocking collectives: 14.4 us -> 0 us
  between operations: 14.2 us -> 1.13 us
    all_gather x5 -> x0, waiting for transfers between devices: 120 us -> none  [the longest x1 38.4 us: body(): lax.all_gather(attn_values, 'col', axis=1, tiled=True)]
    reduce_scatter x3 -> x0, waiting for transfers between devices: 119 us -> none  [the longest x1 57.7 us: body(): lax.psum_scatter(lax.dot_general(dense_grad, out_weight, (((1,), (1,)), (...]
    ppermute x0 -> x33, waiting for transfers between devices: none -> 101 us  [shifted(): return lax.ppermute(x, axis, [(j, (j + step) % n) for j in range(n)])]
    ppermute x0 -> x33, starting transfers between devices: none -> 64.3 us  [shifted(): return lax.ppermute(x, axis, [(j, (j + step) % n) for j in range(n)])]
    gather x0 -> x11, local copies, waits for them, and re-layouts: none -> 18.6 us  [natural(): return jnp.take(jnp.stack(pieces, 0), order, axis=0)]
    all_gather x1 -> x0, blocking collectives: 14.4 us -> none  [body(): lax.all_gather(patches, 'col', axis=1, tiled=True)]
    another operation x0 -> x19, other arithmetic: none -> 13.3 us  [natural(): return jnp.take(jnp.stack(pieces, 0), order, axis=0)]
    ppermute x3, waiting for transfers between devices: 27.5 us -> 16.2 us  [swap_dp(): return lax.ppermute(x, 'dp', [(0, 1), (1, 0)])]
  transfers between devices with their start and end apart: 11 -> 36, of which waited for: 9 -> 18; matrix products, arithmetic and copies ran while one was open for 13% -> 28% of each run, Pallas kernels for 0% -> 0%
where the time goes in v2:
time: 300 us; the launch traced here: 299 us
  waiting for transfers between devices  118 us (39%)
  starting transfers between devices  68.9 us (23%)
  matrix products  47.5 us (16%)
  local copies, waits for them, and re-layouts  37.4 us (12%)
  other arithmetic  26.3 us (9%)
    ppermute x33, waiting for transfers between devices, shifted(): return lax.ppermute(x, axis, [(j, (j + step) % n) for j in range(n)])  101 us
    ppermute x33, starting transfers between devices, shifted(): return lax.ppermute(x, axis, [(j, (j + step) % n) for j in range(n)])  64.3 us
    dot_general x4, matrix products, contract_rows(): lax.dot_general(left, right, (((0,), (0,)), ((), ())), preferred_element_...  30.9 us
    gather x11, local copies, waits for them, and re-layouts, natural(): return jnp.take(jnp.stack(pieces, 0), order, axis=0)  18.6 us
    ppermute x3, waiting for transfers between devices, swap_dp(): return lax.ppermute(x, 'dp', [(0, 1), (1, 0)])  16.2 us
    another operation x19, other arithmetic, natural(): return jnp.take(jnp.stack(pieces, 0), order, axis=0)  13.3 us
    select_n x8, other arithmetic, natural(): return jnp.take(jnp.stack(pieces, 0), order, axis=0)  9.83 us
    dot_general x1, matrix products, body_heads(): lax.dot_general(dense_grad, out_weight, (((1,), (1,)), ((), ())), preferr...  8.79 us
  transfers between devices with their start and end apart: 36, of which 18 were waited for; matrix products, arithmetic and copies ran while one was open for 28% of the time, Pallas kernels for 0%

profile of v2, /device:TPU:0, one launch (start us, length us, event | category | flops | bytes accessed | tf_op | source)
XLA Modules:
  0.0 298.8 jit_solution(13334916575255587597)
XLA Ops:
  0.6 3.1 %collective-permute-start.32 = (bf16[128,364]{0,1:T(8,128)(2,1)}, bf16[128,364]{0,1:T(8,128)(2,1)S(1)}, u32[]{:S(2)}, u32[]{:S(2)}) collective-permute-start(bf16[128,364]{0,1:T(8,128)(2,1)} %bitcast.166), channel_id=1, source_target_pairs={{0,1},{1,2},{2,3},{3,0},{4,5},{5,6},{6,7},{7,4},{8,9},{9,10},{10,1... | collective-permute-start | bytes 279560 | tf_op jit(solution)/shard_map/ppermute | solution.py:114
  3.7 2.6 collective-permute-start.33
  12.3 2.9 collective-permute-start.2
  15.7 7.1 %collective-permute-start.5 = (bf16[128,384]{1,0:T(8,128)(2,1)S(1)}, bf16[128,384]{1,0:T(8,128)(2,1)S(1)}, u32[]{:S(2)}, u32[]{:S(2)}) collective-permute-start(bf16[128,384]{1,0:T(8,128)(2,1)S(1)} %get-tuple-element.26), channel_id=1, source_target_pairs={{0,3},{1,0},{2,1},{3,2},{4,7},{5,4},{6,5},{7,6},{8,11},{9,8},{10,9... | collective-permute-start | bytes 294920 | tf_op jit(solution)/shard_map/ppermute | solution.py:114
  26.0 3.8 %collective-permute-start.12 = (bf16[128,384]{1,0:T(8,128)(2,1)S(1)}, bf16[128,384]{1,0:T(8,128)(2,1)S(1)}, u32[]{:S(2)}, u32[]{:S(2)}) collective-permute-start(bf16[128,384]{1,0:T(8,128)(2,1)S(1)} %get-tuple-element.21), channel_id=1, source_target_pairs={{0,1},{1,2},{2,3},{3,0},{4,5},{5,6},{6,7},{7,4},{8,9},{9,10},{10,1... | collective-permute-start | bytes 294920 | tf_op jit(solution)/shard_map/ppermute | solution.py:114
  30.6 2.4 collective-permute-start.14
  43.8 1.7 multiply_reduce_fusion
  48.8 6.0 %collective-permute-done.6 = bf16[128,3072]{1,0:T(8,128)(2,1)} collective-permute-done((bf16[128,3072]{1,0:T(8,128)(2,1)}, bf16[128,3072]{1,0:T(8,128)(2,1)}, u32[]{:S(2)}, u32[]{:S(2)}) %collective-permute-start.6) | collective-permute-done | bytes 786464 | tf_op jit(solution)/shard_map/ppermute | solution.py:114
  54.8 2.0 copy.33
  56.8 1.9 reshape_reshape.11
  61.9 11.6 %collective-permute-done.8 = bf16[128,3072]{1,0:T(8,128)(2,1)} collective-permute-done((bf16[128,3072]{1,0:T(8,128)(2,1)}, bf16[128,3072]{1,0:T(8,128)(2,1)}, u32[]{:S(2)}, u32[]{:S(2)}) %collective-permute-start.8) | collective-permute-done | bytes 786464 | tf_op jit(solution)/shard_map/ppermute | solution.py:114
  73.5 2.0 pad_maximum_fusion
  75.5 2.4 gather_fusion.4
  77.9 10.6 %collective-permute-done.29 = bf16[128,3072]{1,0:T(8,128)(2,1)} collective-permute-done((bf16[128,3072]{1,0:T(8,128)(2,1)}, bf16[128,3072]{1,0:T(8,128)(2,1)}, u32[]{:S(2)}, u32[]{:S(2)}) %collective-permute-start.29) | collective-permute-done | bytes 786464 | tf_op jit(solution)/shard_map/ppermute | solution.py:114
  88.5 2.8 collective-permute-done.30
  91.3 14.5 %collective-permute-done.31 = bf16[128,3072]{1,0:T(8,128)(2,1)} collective-permute-done((bf16[128,3072]{1,0:T(8,128)(2,1)}, bf16[128,3072]{1,0:T(8,128)(2,1)}, u32[]{:S(2)}, u32[]{:S(2)}) %collective-permute-start.31) | collective-permute-done | bytes 786464 | tf_op jit(solution)/shard_map/ppermute | solution.py:114
  105.8 2.0 pad_maximum_fusion.1
  107.8 2.4 gather_fusion.9
  110.2 3.5 %broadcast_select_fusion = (bf16[4,128,3072]{2,1,0:T(8,128)(2,1)S(1)}, bf16[4,128,3072]{2,1,0:T(8,128)(2,1)S(1)}) fusion(bf16[4,128,3072]{2,1,0:T(8,128)(2,1)} %gather_fusion.9, pred[4]{0:T(512)(128)(4,1)S(1)} %compare_and_fusion.1, bf16[4,128,3072]{2,1,0:T(8,128)(2,1)} %gather_fusion.4), kind=kLoop, calls=%fused_computation.17 | loop fusion | flops 3145728 | bytes 12582916 | tf_op jit(solution)/shard_map/jit(_take)/select_n | solution.py:120
  113.7 8.8 %fusion.9 = f32[512,1536]{1,0:T(8,128)S(1)} fusion(bf16[512,3072]{1,0:T(8,128)(2,1)S(1)} %bitcast.143, bf16[1536,3072]{1,0:T(8,128)(2,1)} %param.16), kind=kOutput, calls=%fused_computation.105 | convolution fusion | flops 4831838208 | bytes 15728640 | tf_op jit(solution)/shard_map/dot_general | solution.py:187
  122.8 2.0 collective-permute-start.11
  124.8 1.9 collective-permute-start.9
  128.1 4.6 %bitcast_add_fusion = f32[364,3072]{1,0:T(8,128)} fusion(f32[364,3072,1]{1,0,2:T(8,128)S(1)} %fusion, bf16[512,364]{1,0:T(8,128)(2,1)} %collective-permute-done.35, bf16[512,3072]{1,0:T(8,128)(2,1)S(1)} %bitcast.141), kind=kOutput, calls=%fused_computation.11 | convolution fusion | flops 1146163200 | bytes 12464128 | tf_op jit(solution)/shard_map/dot_general | solution.py:10
  132.7 18.5 %collective-permute-done.10 = bf16[512,384]{1,0:T(8,128)(2,1)S(1)} collective-permute-done((bf16[512,384]{1,0:T(8,128)(2,1)S(1)}, bf16[512,384]{1,0:T(8,128)(2,1)S(1)}, u32[]{:S(2)}, u32[]{:S(2)}) %collective-permute-start.10) | collective-permute-done | bytes 393248 | tf_op jit(solution)/shard_map/ppermute | solution.py:114
  155.0 2.8 multiply_reduce_fusion.1
  157.8 7.3 %collective-permute-start.24 = (bf16[512,384]{0,1:T(8,128)(2,1)}, bf16[512,384]{0,1:T(8,128)(2,1)}, u32[]{:S(2)}, u32[]{:S(2)}) collective-permute-start(bf16[512,384]{0,1:T(8,128)(2,1)} %bitcast.54), channel_id=1, source_target_pairs={{0,1},{1,2},{2,3},{3,0},{4,5},{5,6},{6,7},{7,4},{8,9},{9,10},{10,1... | collective-permute-start | bytes 1179656 | tf_op jit(solution)/shard_map/ppermute | solution.py:114
  166.0 2.9 collective-permute-start.26
  173.9 19.8 %collective-permute-done.17 = bf16[128,384]{0,1:T(8,128)(2,1)S(1)} collective-permute-done((bf16[128,384]{0,1:T(8,128)(2,1)S(1)}, bf16[128,384]{0,1:T(8,128)(2,1)S(1)}, u32[]{:S(2)}, u32[]{:S(2)}) %collective-permute-start.17) | collective-permute-done | bytes 98336 | tf_op jit(solution)/shard_map/ppermute | solution.py:114
  193.7 8.9 %collective-permute-start.15 = (bf16[128,384]{0,1:T(8,128)(2,1)S(1)}, bf16[128,384]{0,1:T(8,128)(2,1)S(1)}, u32[]{:S(2)}, u32[]{:S(2)}) collective-permute-start(bf16[128,384]{0,1:T(8,128)(2,1)S(1)} %get-tuple-element.17), channel_id=1, source_target_pairs={{0,1},{1,2},{2,3},{3,0},{4,5},{5,6},{6,7},{7,4},{8,9},{9,10},{10,1... | collective-permute-start | bytes 294920 | tf_op jit(solution)/shard_map/ppermute | solution.py:114
  204.0 6.6 %collective-permute-start.20 = (bf16[128,384]{0,1:T(8,128)(2,1)S(1)}, bf16[128,384]{0,1:T(8,128)(2,1)S(1)}, u32[]{:S(2)}, u32[]{:S(2)}) collective-permute-start(bf16[128,384]{0,1:T(8,128)(2,1)S(1)} %get-tuple-element.15), channel_id=1, source_target_pairs={{0,3},{1,0},{2,1},{3,2},{4,7},{5,4},{6,5},{7,6},{8,11},{9,8},{10,9... | collective-permute-start | bytes 294920 | tf_op jit(solution)/shard_map/ppermute | solution.py:114
  211.1 2.2 collective-permute-done.20
  213.3 4.4 %collective-permute-done.19 = bf16[128,384]{0,1:T(8,128)(2,1)S(1)} collective-permute-done((bf16[128,384]{0,1:T(8,128)(2,1)S(1)}, bf16[128,384]{0,1:T(8,128)(2,1)S(1)}, u32[]{:S(2)}, u32[]{:S(2)}) %collective-permute-start.19) | collective-permute-done | bytes 98336 | tf_op jit(solution)/shard_map/ppermute | solution.py:114
  217.7 2.6 collective-permute-start.23
  221.2 2.2 collective-permute-done.23
  224.4 3.5 %collective-permute-done.22 = bf16[128,384]{0,1:T(8,128)(2,1)S(1)} collective-permute-done((bf16[128,384]{0,1:T(8,128)(2,1)S(1)}, bf16[128,384]{0,1:T(8,128)(2,1)S(1)}, u32[]{:S(2)}, u32[]{:S(2)}) %collective-permute-start.22) | collective-permute-done | bytes 98336 | tf_op jit(solution)/shard_map/ppermute | solution.py:114
  229.5 2.6 gather_fusion.6
  232.1 2.6 gather_fusion.7
  235.6 1.9 pad_maximum_fusion.5
  237.4 2.6 gather_fusion.8
  240.1 2.7 pad_maximum_fusion.2
  242.8 3.2 %gather_fusion = bf16[4,512,384]{1,2,0:T(8,128)(2,1)} fusion(bf16[4,512,384]{1,2,0:T(8,128)(2,1)} %pad_maximum_fusion.2, s32[1024]{0:T(1024)S(1)} %pad_clamp_fusion), kind=kCustom, calls=%fused_computation.8 | custom fusion | bytes 3145744 | tf_op jit(solution)/shard_map/jit(_take)/gather | solution.py:120
  246.0 3.0 broadcast_select_fusion.2
  252.0 2.3 copy.54
  254.3 2.3 copy.55
  256.6 2.3 copy.56
  258.9 11.3 %fusion.11 = f32[1536,3072]{1,0:T(8,128)} fusion(bf16[512,1536]{0,1:T(8,128)(2,1)} %bitcast.61, bf16[512,3072]{1,0:T(8,128)(2,1)} %bitcast.144), kind=kOutput, calls=%fused_computation.107 | convolution fusion | flops 4831838208 | bytes 23592960 | tf_op jit(solution)/shard_map/dot_general | solution.py:10
  270.2 15.1 %collective-permute-done.27 = bf16[512,1536]{0,1:T(8,128)(2,1)} collective-permute-done((bf16[512,1536]{0,1:T(8,128)(2,1)}, bf16[512,1536]{0,1:T(8,128)(2,1)}, u32[]{:S(2)}, u32[]{:S(2)}) %collective-permute-start.27) | collective-permute-done | bytes 1572896 | tf_op jit(solution)/shard_map/ppermute | solution.py:16
  285.3 13.6 %convolution_add_fusion = f32[1536,3072]{1,0:T(8,128)} fusion(f32[1536,3072]{1,0:T(8,128)} %fusion.11, bf16[512,1536]{0,1:T(8,128)(2,1)} %collective-permute-done.27, bf16[512,3072]{1,0:T(8,128)(2,1)S(1)} %bitcast.142), kind=kOutput, calls=%fused_computation.10 | convolution fusion | flops 4836556800 | bytes 42467328 | tf_op jit(solution)/shard_map/dot_general | solution.py:10
  (117 shorter events, 48.1 us)
Async XLA Ops:
  0.6 11.6 %collective-permute-start.32 = (bf16[128,364]{0,1:T(8,128)(2,1)}, bf16[128,364]{0,1:T(8,128)(2,1)S(1)}, u32[]{:S(2)}, u32[]{:S(2)}) collective-permute-start(bf16[128,364]{0,1:T(8,128)(2,1)} %bitcast.166), channel_id=1, source_target_pairs={{0,1},{1,2},{2,3},{3,0},{4,5},{5,6},{6,7},{7,4},{8,9},{9,10},{10,1... | collective-permute-start | bytes 279560 | tf_op jit(solution)/shard_map/ppermute | solution.py:114
  3.7 12.0 %collective-permute-start.33 = (bf16[128,364]{0,1:T(8,128)(2,1)}, bf16[128,364]{0,1:T(8,128)(2,1)S(1)}, u32[]{:S(2)}, u32[]{:S(2)}) collective-permute-start(bf16[128,364]{0,1:T(8,128)(2,1)} %bitcast.167), channel_id=1, source_target_pairs={{0,2},{1,3},{2,0},{3,1},{4,6},{5,7},{6,4},{7,5},{8,10},{9,11},{10,... | collective-permute-start | bytes 279560 | tf_op jit(solution)/shard_map/ppermute | solution.py:114
  6.3 16.4 %collective-permute-start.34 = (bf16[128,364]{0,1:T(8,128)(2,1)}, bf16[128,364]{0,1:T(8,128)(2,1)S(1)}, u32[]{:S(2)}, u32[]{:S(2)}) collective-permute-start(bf16[128,364]{0,1:T(8,128)(2,1)} %bitcast.168), channel_id=1, source_target_pairs={{0,3},{1,0},{2,1},{3,2},{4,7},{5,4},{6,5},{7,6},{8,11},{9,8},{10,9... | collective-permute-start | bytes 279560 | tf_op jit(solution)/shard_map/ppermute | solution.py:114
  8.7 16.7 %collective-permute-start = (bf16[128,384]{1,0:T(8,128)(2,1)S(1)}, bf16[128,384]{1,0:T(8,128)(2,1)S(1)}, u32[]{:S(2)}, u32[]{:S(2)}) collective-permute-start(bf16[128,384]{1,0:T(8,128)(2,1)S(1)} %get-tuple-element.29), channel_id=1, source_target_pairs={{0,1},{1,2},{2,3},{3,0},{4,5},{5,6},{6,7},{7,4},{8,9},{9,10},{10,1... | collective-permute-start | bytes 294920 | tf_op jit(solution)/shard_map/ppermute | solution.py:114
  9.5 16.5 %collective-permute-start.1 = (bf16[128,384]{1,0:T(8,128)(2,1)S(1)}, bf16[128,384]{1,0:T(8,128)(2,1)S(1)}, u32[]{:S(2)}, u32[]{:S(2)}) collective-permute-start(bf16[128,384]{1,0:T(8,128)(2,1)S(1)} %get-tuple-element.31), channel_id=1, source_target_pairs={{0,2},{1,3},{2,0},{3,1},{4,6},{5,7},{6,4},{7,5},{8,10},{9,11},{10,... | collective-permute-start | bytes 294920 | tf_op jit(solution)/shard_map/ppermute | solution.py:114
  12.3 17.5 %collective-permute-start.2 = (bf16[128,384]{1,0:T(8,128)(2,1)S(1)}, bf16[128,384]{1,0:T(8,128)(2,1)S(1)}, u32[]{:S(2)}, u32[]{:S(2)}) collective-permute-start(bf16[128,384]{1,0:T(8,128)(2,1)S(1)} %get-tuple-element.30), channel_id=1, source_target_pairs={{0,3},{1,0},{2,1},{3,2},{4,7},{5,4},{6,5},{7,6},{8,11},{9,8},{10,9... | collective-permute-start | bytes 294920 | tf_op jit(solution)/shard_map/ppermute | solution.py:114
  15.7 14.9 %collective-permute-start.5 = (bf16[128,384]{1,0:T(8,128)(2,1)S(1)}, bf16[128,384]{1,0:T(8,128)(2,1)S(1)}, u32[]{:S(2)}, u32[]{:S(2)}) collective-permute-start(bf16[128,384]{1,0:T(8,128)(2,1)S(1)} %get-tuple-element.26), channel_id=1, source_target_pairs={{0,3},{1,0},{2,1},{3,2},{4,7},{5,4},{6,5},{7,6},{8,11},{9,8},{10,9... | collective-permute-start | bytes 294920 | tf_op jit(solution)/shard_map/ppermute | solution.py:114
  22.7 10.3 %collective-permute-start.3 = (bf16[128,384]{1,0:T(8,128)(2,1)S(1)}, bf16[128,384]{1,0:T(8,128)(2,1)S(1)}, u32[]{:S(2)}, u32[]{:S(2)}) collective-permute-start(bf16[128,384]{1,0:T(8,128)(2,1)S(1)} %get-tuple-element.25), channel_id=1, source_target_pairs={{0,1},{1,2},{2,3},{3,0},{4,5},{5,6},{6,7},{7,4},{8,9},{9,10},{10,1... | collective-permute-start | bytes 294920 | tf_op jit(solution)/shard_map/ppermute | solution.py:114
  25.4 10.6 %collective-permute-start.4 = (bf16[128,384]{1,0:T(8,128)(2,1)S(1)}, bf16[128,384]{1,0:T(8,128)(2,1)S(1)}, u32[]{:S(2)}, u32[]{:S(2)}) collective-permute-start(bf16[128,384]{1,0:T(8,128)(2,1)S(1)} %get-tuple-element.27), channel_id=1, source_target_pairs={{0,2},{1,3},{2,0},{3,1},{4,6},{5,7},{6,4},{7,5},{8,10},{9,11},{10,... | collective-permute-start | bytes 294920 | tf_op jit(solution)/shard_map/ppermute | solution.py:114
  26.0 10.8 %collective-permute-start.12 = (bf16[128,384]{1,0:T(8,128)(2,1)S(1)}, bf16[128,384]{1,0:T(8,128)(2,1)S(1)}, u32[]{:S(2)}, u32[]{:S(2)}) collective-permute-start(bf16[128,384]{1,0:T(8,128)(2,1)S(1)} %get-tuple-element.21), channel_id=1, source_target_pairs={{0,1},{1,2},{2,3},{3,0},{4,5},{5,6},{6,7},{7,4},{8,9},{9,10},{10,1... | collective-permute-start | bytes 294920 | tf_op jit(solution)/shard_map/ppermute | solution.py:114
  29.8 8.5 %collective-permute-start.13 = (bf16[128,384]{1,0:T(8,128)(2,1)S(1)}, bf16[128,384]{1,0:T(8,128)(2,1)S(1)}, u32[]{:S(2)}, u32[]{:S(2)}) collective-permute-start(bf16[128,384]{1,0:T(8,128)(2,1)S(1)} %get-tuple-element.23), channel_id=1, source_target_pairs={{0,2},{1,3},{2,0},{3,1},{4,6},{5,7},{6,4},{7,5},{8,10},{9,11},{10,... | collective-permute-start | bytes 294920 | tf_op jit(solution)/shard_map/ppermute | solution.py:114
  30.6 9.2 %collective-permute-start.14 = (bf16[128,384]{1,0:T(8,128)(2,1)S(1)}, bf16[128,384]{1,0:T(8,128)(2,1)S(1)}, u32[]{:S(2)}, u32[]{:S(2)}) collective-permute-start(bf16[128,384]{1,0:T(8,128)(2,1)S(1)} %get-tuple-element.22), channel_id=1, source_target_pairs={{0,3},{1,0},{2,1},{3,2},{4,7},{5,4},{6,5},{7,6},{8,11},{9,8},{10,9... | collective-permute-start | bytes 294920 | tf_op jit(solution)/shard_map/ppermute | solution.py:114
  33.0 14.2 %collective-permute-start.28 = (bf16[1,128,3072]{2,1,0:T(8,128)(2,1)}, bf16[1,128,3072]{2,1,0:T(8,128)(2,1)}, u32[]{:S(2)}, u32[]{:S(2)}) collective-permute-start(bf16[1,128,3072]{2,1,0:T(8,128)(2,1)} %param.17), channel_id=1, source_target_pairs={{0,16},{16,0},{1,17},{17,1},{2,18},{18,2},{3,19},{19,3},{4,20},{20... | collective-permute-start | bytes 2359304 | tf_op jit(solution)/shard_map/ppermute | solution.py:16
  36.1 18.7 %collective-permute-start.6 = (bf16[128,3072]{1,0:T(8,128)(2,1)}, bf16[128,3072]{1,0:T(8,128)(2,1)}, u32[]{:S(2)}, u32[]{:S(2)}) collective-permute-start(bf16[128,3072]{1,0:T(8,128)(2,1)} %bitcast.12), channel_id=1, source_target_pairs={{0,4},{4,8},{8,12},{12,0},{1,5},{5,9},{9,13},{13,1},{2,6},{6,10},{... | collective-permute-start | bytes 2359304 | tf_op jit(solution)/shard_map/ppermute | solution.py:114
  36.8 23.6 %collective-permute-start.7 = (bf16[128,3072]{1,0:T(8,128)(2,1)}, bf16[128,3072]{1,0:T(8,128)(2,1)}, u32[]{:S(2)}, u32[]{:S(2)}) collective-permute-start(bf16[128,3072]{1,0:T(8,128)(2,1)} %bitcast.12), channel_id=1, source_target_pairs={{0,8},{4,12},{8,0},{12,4},{1,9},{5,13},{9,1},{13,5},{2,10},{6,14},... | collective-permute-start | bytes 2359304 | tf_op jit(solution)/shard_map/ppermute | solution.py:114
  38.3 35.1 %collective-permute-start.8 = (bf16[128,3072]{1,0:T(8,128)(2,1)}, bf16[128,3072]{1,0:T(8,128)(2,1)}, u32[]{:S(2)}, u32[]{:S(2)}) collective-permute-start(bf16[128,3072]{1,0:T(8,128)(2,1)} %bitcast.12), channel_id=1, source_target_pairs={{0,12},{4,0},{8,4},{12,8},{1,13},{5,1},{9,5},{13,9},{2,14},{6,2},{... | collective-permute-start | bytes 2359304 | tf_op jit(solution)/shard_map/ppermute | solution.py:114
  47.2 41.3 %collective-permute-start.29 = (bf16[128,3072]{1,0:T(8,128)(2,1)}, bf16[128,3072]{1,0:T(8,128)(2,1)}, u32[]{:S(2)}, u32[]{:S(2)}) collective-permute-start(bf16[128,3072]{1,0:T(8,128)(2,1)} %bitcast.63), channel_id=1, source_target_pairs={{0,4},{4,8},{8,12},{12,0},{1,5},{5,9},{9,13},{13,1},{2,6},{6,10},{... | collective-permute-start | bytes 2359304 | tf_op jit(solution)/shard_map/ppermute | solution.py:114
  47.2 44.1 %collective-permute-start.30 = (bf16[128,3072]{1,0:T(8,128)(2,1)}, bf16[128,3072]{1,0:T(8,128)(2,1)}, u32[]{:S(2)}, u32[]{:S(2)}) collective-permute-start(bf16[128,3072]{1,0:T(8,128)(2,1)} %bitcast.63), channel_id=1, source_target_pairs={{0,8},{4,12},{8,0},{12,4},{1,9},{5,13},{9,1},{13,5},{2,10},{6,14},... | collective-permute-start | bytes 2359304 | tf_op jit(solution)/shard_map/ppermute | solution.py:114
  54.8 51.0 %collective-permute-start.31 = (bf16[128,3072]{1,0:T(8,128)(2,1)}, bf16[128,3072]{1,0:T(8,128)(2,1)}, u32[]{:S(2)}, u32[]{:S(2)}) collective-permute-start(bf16[128,3072]{1,0:T(8,128)(2,1)} %bitcast.63), channel_id=1, source_target_pairs={{0,12},{4,0},{8,4},{12,8},{1,13},{5,1},{9,5},{13,9},{2,14},{6,2},{... | collective-permute-start | bytes 2359304 | tf_op jit(solution)/shard_map/ppermute | solution.py:114
  60.4 67.7 %collective-permute-start.35 = (bf16[512,364]{1,0:T(8,128)(2,1)}, bf16[512,364]{1,0:T(8,128)(2,1)}, u32[]{:S(2)}, u32[]{:S(2)}) collective-permute-start(bf16[512,364]{1,0:T(8,128)(2,1)} %bitcast_select_fusion), channel_id=1, source_target_pairs={{0,16},{16,0},{1,17},{17,1},{2,18},{18,2},{3,19},{19,3},{4,20},{20... | collective-permute-start | bytes 1118216 | tf_op jit(solution)/shard_map/ppermute | solution.py:16
  113.7 13.0 %copy-start.1 = (bf16[4,128,3072]{2,1,0:T(8,128)(2,1)}, bf16[4,128,3072]{2,1,0:T(8,128)(2,1)S(1)}, u32[]{:S(2)}) copy-start(bf16[4,128,3072]{2,1,0:T(8,128)(2,1)S(1)} %get-tuple-element.33) | copy-start | bytes 9437188
  122.7 28.4 %collective-permute-start.10 = (bf16[512,384]{1,0:T(8,128)(2,1)S(1)}, bf16[512,384]{1,0:T(8,128)(2,1)S(1)}, u32[]{:S(2)}, u32[]{:S(2)}) collective-permute-start(bf16[512,384]{1,0:T(8,128)(2,1)S(1)} %get-tuple-element.10), channel_id=1, source_target_pairs={{0,2},{1,3},{2,0},{3,1},{4,6},{5,7},{6,4},{7,5},{8,10},{9,11},{10,... | collective-permute-start | bytes 1179656 | tf_op jit(solution)/shard_map/ppermute | solution.py:114
  122.8 28.3 %collective-permute-start.11 = (bf16[512,384]{1,0:T(8,128)(2,1)S(1)}, bf16[512,384]{1,0:T(8,128)(2,1)S(1)}, u32[]{:S(2)}, u32[]{:S(2)}) collective-permute-start(bf16[512,384]{1,0:T(8,128)(2,1)S(1)} %get-tuple-element.9), channel_id=1, source_target_pairs={{0,1},{1,2},{2,3},{3,0},{4,5},{5,6},{6,7},{7,4},{8,9},{9,10},{10,1... | collective-permute-start | bytes 1179656 | tf_op jit(solution)/shard_map/ppermute | solution.py:114
  124.8 28.1 %collective-permute-start.9 = (bf16[512,384]{1,0:T(8,128)(2,1)S(1)}, bf16[512,384]{1,0:T(8,128)(2,1)S(1)}, u32[]{:S(2)}, u32[]{:S(2)}) collective-permute-start(bf16[512,384]{1,0:T(8,128)(2,1)S(1)} %get-tuple-element.8), channel_id=1, source_target_pairs={{0,3},{1,0},{2,1},{3,2},{4,7},{5,4},{6,5},{7,6},{8,11},{9,8},{10,9... | collective-permute-start | bytes 1179656 | tf_op jit(solution)/shard_map/ppermute | solution.py:114
  154.9 13.9 %copy-start = (bf16[3,512,512]{1,2,0:T(8,128)(2,1)S(1)}, bf16[3,512,512]{1,2,0:T(8,128)(2,1)}, u32[]{:S(2)}) copy-start(bf16[3,512,512]{1,2,0:T(8,128)(2,1)} %exponential_convert_fusion) | copy-start | bytes 4718596
  155.0 15.6 %copy-start.3 = (bf16[512,3,128]{0,2,1:T(8,128)(2,1)S(1)}, bf16[512,3,128]{0,2,1:T(8,128)(2,1)}, u32[]{:S(2)}) copy-start(bf16[512,3,128]{0,2,1:T(8,128)(2,1)} %reshape_reshape.9) | copy-start | bytes 1179652
  157.8 82.3 %collective-permute-start.24 = (bf16[512,384]{0,1:T(8,128)(2,1)}, bf16[512,384]{0,1:T(8,128)(2,1)}, u32[]{:S(2)}, u32[]{:S(2)}) collective-permute-start(bf16[512,384]{0,1:T(8,128)(2,1)} %bitcast.54), channel_id=1, source_target_pairs={{0,1},{1,2},{2,3},{3,0},{4,5},{5,6},{6,7},{7,4},{8,9},{9,10},{10,1... | collective-permute-start | bytes 1179656 | tf_op jit(solution)/shard_map/ppermute | solution.py:114
  165.0 75.0 %collective-permute-start.25 = (bf16[512,384]{0,1:T(8,128)(2,1)}, bf16[512,384]{0,1:T(8,128)(2,1)}, u32[]{:S(2)}, u32[]{:S(2)}) collective-permute-start(bf16[512,384]{0,1:T(8,128)(2,1)} %bitcast.54), channel_id=1, source_target_pairs={{0,2},{1,3},{2,0},{3,1},{4,6},{5,7},{6,4},{7,5},{8,10},{9,11},{10,... | collective-permute-start | bytes 1179656 | tf_op jit(solution)/shard_map/ppermute | solution.py:114
  166.0 74.1 %collective-permute-start.26 = (bf16[512,384]{0,1:T(8,128)(2,1)}, bf16[512,384]{0,1:T(8,128)(2,1)}, u32[]{:S(2)}, u32[]{:S(2)}) collective-permute-start(bf16[512,384]{0,1:T(8,128)(2,1)} %bitcast.54), channel_id=1, source_target_pairs={{0,3},{1,0},{2,1},{3,2},{4,7},{5,4},{6,5},{7,6},{8,11},{9,8},{10,9... | collective-permute-start | bytes 1179656 | tf_op jit(solution)/shard_map/ppermute | solution.py:114
  168.9 2.1 copy-start.2
  172.5 21.2 %collective-permute-start.17 = (bf16[128,384]{0,1:T(8,128)(2,1)S(1)}, bf16[128,384]{0,1:T(8,128)(2,1)S(1)}, u32[]{:S(2)}, u32[]{:S(2)}) collective-permute-start(bf16[128,384]{0,1:T(8,128)(2,1)S(1)} %get-tuple-element.18), channel_id=1, source_target_pairs={{0,3},{1,0},{2,1},{3,2},{4,7},{5,4},{6,5},{7,6},{8,11},{9,8},{10,9... | collective-permute-start | bytes 294920 | tf_op jit(solution)/shard_map/ppermute | solution.py:114
  173.1 30.9 %collective-permute-start.16 = (bf16[128,384]{0,1:T(8,128)(2,1)S(1)}, bf16[128,384]{0,1:T(8,128)(2,1)S(1)}, u32[]{:S(2)}, u32[]{:S(2)}) collective-permute-start(bf16[128,384]{0,1:T(8,128)(2,1)S(1)} %get-tuple-element.19), channel_id=1, source_target_pairs={{0,2},{1,3},{2,0},{3,1},{4,6},{5,7},{6,4},{7,5},{8,10},{9,11},{10,... | collective-permute-start | bytes 294920 | tf_op jit(solution)/shard_map/ppermute | solution.py:114
  193.7 17.0 %collective-permute-start.15 = (bf16[128,384]{0,1:T(8,128)(2,1)S(1)}, bf16[128,384]{0,1:T(8,128)(2,1)S(1)}, u32[]{:S(2)}, u32[]{:S(2)}) collective-permute-start(bf16[128,384]{0,1:T(8,128)(2,1)S(1)} %get-tuple-element.17), channel_id=1, source_target_pairs={{0,1},{1,2},{2,3},{3,0},{4,5},{5,6},{6,7},{7,4},{8,9},{9,10},{10,1... | collective-permute-start | bytes 294920 | tf_op jit(solution)/shard_map/ppermute | solution.py:114
  204.0 9.2 %collective-permute-start.20 = (bf16[128,384]{0,1:T(8,128)(2,1)S(1)}, bf16[128,384]{0,1:T(8,128)(2,1)S(1)}, u32[]{:S(2)}, u32[]{:S(2)}) collective-permute-start(bf16[128,384]{0,1:T(8,128)(2,1)S(1)} %get-tuple-element.15), channel_id=1, source_target_pairs={{0,3},{1,0},{2,1},{3,2},{4,7},{5,4},{6,5},{7,6},{8,11},{9,8},{10,9... | collective-permute-start | bytes 294920 | tf_op jit(solution)/shard_map/ppermute | solution.py:114
  210.7 7.0 %collective-permute-start.19 = (bf16[128,384]{0,1:T(8,128)(2,1)S(1)}, bf16[128,384]{0,1:T(8,128)(2,1)S(1)}, u32[]{:S(2)}, u32[]{:S(2)}) collective-permute-start(bf16[128,384]{0,1:T(8,128)(2,1)S(1)} %get-tuple-element.16), channel_id=1, source_target_pairs={{0,2},{1,3},{2,0},{3,1},{4,6},{5,7},{6,4},{7,5},{8,10},{9,11},{10,... | collective-permute-start | bytes 294920 | tf_op jit(solution)/shard_map/ppermute | solution.py:114
  213.2 7.1 %collective-permute-start.18 = (bf16[128,384]{0,1:T(8,128)(2,1)S(1)}, bf16[128,384]{0,1:T(8,128)(2,1)S(1)}, u32[]{:S(2)}, u32[]{:S(2)}) collective-permute-start(bf16[128,384]{0,1:T(8,128)(2,1)S(1)} %get-tuple-element.14), channel_id=1, source_target_pairs={{0,1},{1,2},{2,3},{3,0},{4,5},{5,6},{6,7},{7,4},{8,9},{9,10},{10,1... | collective-permute-start | bytes 294920 | tf_op jit(solution)/shard_map/ppermute | solution.py:114
  217.7 5.8 %collective-permute-start.23 = (bf16[128,384]{0,1:T(8,128)(2,1)S(1)}, bf16[128,384]{0,1:T(8,128)(2,1)S(1)}, u32[]{:S(2)}, u32[]{:S(2)}) collective-permute-start(bf16[128,384]{0,1:T(8,128)(2,1)S(1)} %get-tuple-element.12), channel_id=1, source_target_pairs={{0,3},{1,0},{2,1},{3,2},{4,7},{5,4},{6,5},{7,6},{8,11},{9,8},{10,9... | collective-permute-start | bytes 294920 | tf_op jit(solution)/shard_map/ppermute | solution.py:114
  220.4 7.5 %collective-permute-start.22 = (bf16[128,384]{0,1:T(8,128)(2,1)S(1)}, bf16[128,384]{0,1:T(8,128)(2,1)S(1)}, u32[]{:S(2)}, u32[]{:S(2)}) collective-permute-start(bf16[128,384]{0,1:T(8,128)(2,1)S(1)} %get-tuple-element.13), channel_id=1, source_target_pairs={{0,2},{1,3},{2,0},{3,1},{4,6},{5,7},{6,4},{7,5},{8,10},{9,11},{10,... | collective-permute-start | bytes 294920 | tf_op jit(solution)/shard_map/ppermute | solution.py:114
  223.4 11.2 %collective-permute-start.21 = (bf16[128,384]{0,1:T(8,128)(2,1)}, bf16[128,384]{0,1:T(8,128)(2,1)}, u32[]{:S(2)}, u32[]{:S(2)}) collective-permute-start(bf16[128,384]{0,1:T(8,128)(2,1)} %get-tuple-element.11), channel_id=1, source_target_pairs={{0,1},{1,2},{2,3},{3,0},{4,5},{5,6},{6,7},{7,4},{8,9},{9,10},{10,1... | collective-permute-start | bytes 294920 | tf_op jit(solution)/shard_map/ppermute | solution.py:114
  246.0 4.5 %copy-start.4 = (f32[4,128,384]{1,2,0:T(8,128)S(1)}, f32[4,128,384]{1,2,0:T(8,128)}, u32[]{:S(2)}) copy-start(f32[4,128,384]{1,2,0:T(8,128)} %gather_fusion.6) | copy-start | bytes 2359300
  246.0 4.5 %copy-start.5 = (f32[4,128,384]{1,2,0:T(8,128)S(1)}, f32[4,128,384]{1,2,0:T(8,128)}, u32[]{:S(2)}) copy-start(f32[4,128,384]{1,2,0:T(8,128)} %gather_fusion.7) | copy-start | bytes 2359300
  246.0 4.5 %copy-start.6 = (f32[4,128,384]{1,2,0:T(8,128)S(1)}, f32[4,128,384]{1,2,0:T(8,128)}, u32[]{:S(2)}) copy-start(f32[4,128,384]{1,2,0:T(8,128)} %gather_fusion.8) | copy-start | bytes 2359300
  249.0 36.3 %collective-permute-start.27 = (bf16[512,1536]{0,1:T(8,128)(2,1)}, bf16[512,1536]{0,1:T(8,128)(2,1)}, u32[]{:S(2)}, u32[]{:S(2)}) collective-permute-start(bf16[512,1536]{0,1:T(8,128)(2,1)} %bitcast.61), channel_id=1, source_target_pairs={{0,16},{16,0},{1,17},{17,1},{2,18},{18,2},{3,19},{19,3},{4,20},{20... | collective-permute-start | bytes 4718600 | tf_op jit(solution)/shard_map/ppermute | solution.py:16

commit v3 on v2

--- a/solution.py
+++ b/solution.py
@@ -1,4 +1,5 @@
 import jax
+import numpy as np
 import jax.numpy as jnp
 from jax import lax
 from jax.sharding import PartitionSpec as P
@@ -162,18 +163,61 @@
     return total
 
 
+def flat(*arrays):
+    return jnp.concatenate([a.reshape(-1) for a in arrays])
+
+
+def unflat(vector, shapes):
+    out, at = [], 0
+    for shape in shapes:
+        size = int(np.prod(shape))
+        out.append(vector[..., at:at + size].reshape(vector.shape[:-1] + shape))
+        at += size
+    return out
+
+
+def gather_rows_relayed(x, axis):
+    n, me = axis_size(axis), lax.axis_index(axis)
+    chips = n // 2
+    cross = [x] + [
+        lax.ppermute(x, axis, [(j, (j + 2 * s) % n) for j in range(n)]) for s in range(1, chips)
+    ]
+    partner_own = lax.ppermute(x, axis, [(j, j ^ 1) for j in range(n)])
+    if chips > 1:
+        relayed = lax.ppermute(jnp.stack(cross[1:], 0), axis, [(j, j ^ 1) for j in range(n)])
+        partner = [partner_own] + [relayed[k] for k in range(chips - 1)]
+    else:
+        partner = [partner_own]
+    pieces = jnp.stack(cross + partner, 0)
+    j = jnp.arange(n)
+    mine = (j % 2) == (me % 2)
+    order = jnp.where(mine, ((me - j) % n) // 2, chips + (((me ^ 1) - j) % n) // 2)
+    stacked = jnp.take(pieces, order, axis=0)
+    return stacked.reshape((n * x.shape[0],) + x.shape[1:])
+
+
 def body_heads(patches, queries, attn_keys, attn_values, out_weight, output_grad):
     factor = DH ** (-0.5)
-    ncol = axis_size("col")
+    n, me = axis_size("col"), lax.axis_index("col")
+    tokens, width_all = queries.shape[1], queries.shape[2]
+    width = width_all // n
+    heads = width // DH
+    patch_here = patches[0]
+    dense_grad = gather_rows_relayed(output_grad[0], "row")
     grad_other = swap_dp(output_grad)
-    dense_grad = gather_rows(output_grad[0], "row")
-    other_grad = gather_rows(grad_other[0], "row")
-    query_h, key_h, value_h = (to_heads(a[0], "col") for a in (queries, attn_keys, attn_values))
-    rows, width = query_h.shape
-    heads = width // DH
-    local_query = query_h.reshape(rows, heads, DH)
-    all_keys = key_h.reshape(rows, heads, DH)
-    all_values = value_h.reshape(rows, heads, DH)
+    other_grad = gather_rows_relayed(grad_other[0], "row")
+    qkv = jnp.stack([queries[0], attn_keys[0], attn_values[0]], 0)
+    part = lambda g: lax.dynamic_slice_in_dim(qkv, g * width, width, 2)
+    shapes = [(3, tokens, width), patch_here.shape]
+    pieces = [(part(me), patch_here)]
+    for s in range(1, n):
+        got = shifted(flat(part((me + s) % n), patch_here), "col", s)
+        pieces.append(tuple(unflat(got, shapes)))
+    qkv_h = natural([p[0] for p in pieces], "col")
+    every_patch = natural([p[1] for p in pieces], "col").reshape(n * tokens, -1)
+    rows = n * tokens
+    qkv_h = jnp.transpose(qkv_h, (1, 0, 2, 3)).reshape(3, rows, heads, DH)
+    local_query, all_keys, all_values = qkv_h[0], qkv_h[1], qkv_h[2]
     scores = (
         jnp.einsum("qhd,khd->hqk", local_query, all_keys, preferred_element_type=jnp.float32)
         * factor
@@ -207,21 +251,23 @@
     value_grad = jnp.einsum(
         "hqk,qhd->khd", attn_probs, grad_heads, preferred_element_type=jnp.float32
     )
-    outs = [from_heads(g.reshape(rows, width), "col")[None] for g in (query_grad, key_grad, value_grad)]
-    out_groups = natural(
-        [attn_out.reshape(rows, width)]
-        + [shifted(attn_out.reshape(rows, width), "col", s) for s in range(1, ncol)],
-        "col",
-    )
-    every_out = jnp.transpose(out_groups, (1, 0, 2)).reshape(rows, ncol * width)
-    other_out = swap_dp(every_out)
-    every_patch = gather_rows(patches[0], "col")
-    other_patch = swap_dp(every_patch)
+    grads = jnp.stack([g.reshape(n, tokens, width) for g in (query_grad, key_grad, value_grad)], 1)
+    back = [grads[me]] + [
+        shifted(grads[(me + s) % n].astype(jnp.bfloat16), "col", s).astype(jnp.float32)
+        for s in range(1, n)
+    ]
+    back = jnp.transpose(natural(back, "col"), (1, 2, 0, 3)).reshape(3, 1, tokens, width_all)
+    out_flat = attn_out.reshape(rows, width)
+    out_groups = natural([out_flat] + [shifted(out_flat, "col", s) for s in range(1, n)], "col")
+    every_out = jnp.transpose(out_groups, (1, 0, 2)).reshape(rows, width_all)
+    other_out, other_patch = unflat(
+        swap_dp(flat(every_out, every_patch)), [every_out.shape, every_patch.shape]
+    )
     out_weight_grad = contract_rows(every_out, dense_grad) + contract_rows(other_out, other_grad)
     embed_weight_grad = contract_rows(every_patch, dense_grad) + contract_rows(
         other_patch, other_grad
     )
-    return (*outs, out_weight_grad, embed_weight_grad)
+    return (back[0], back[1], back[2], out_weight_grad, embed_weight_grad)
 
 
 def body(patches, queries, attn_keys, attn_values, out_weight, output_grad):

time: 300 us -> 320 us (1.067)
  local copies, waits for them, and re-layouts: 37.4 us -> 85.9 us
  starting transfers between devices: 68.9 us -> 33.2 us
  matrix products: 47.5 us -> 51.3 us
    ppermute x33 -> x12, starting transfers between devices: 64.3 us -> 26.9 us  [shifted(): return lax.ppermute(x, axis, [(j, (j + step) % n) for j in range(n)])]
    slice x0 -> x18, local copies, waits for them, and re-layouts: none -> 16.1 us  [the longest x4 8.29 us: body_heads(): return (back[0], back[1], back[2], out_weight_grad, embed_weight_grad)]
    ppermute x0 -> x6, waiting for transfers between devices: none -> 12.8 us  [the longest x2 12.8 us: gather_rows_relayed(): lax.ppermute(x, axis, [(j, (j + 2 * s) % n) for j in range(n)])]
    unnamed x14 -> x54, local copies, waits for them, and re-layouts: 0.03 us -> 12.8 us
    ppermute x33 -> x12, waiting for transfers between devices: 101 us -> 90.7 us  [shifted(): return lax.ppermute(x, axis, [(j, (j + step) % n) for j in range(n)])]
    gather x11 -> x4, local copies, waits for them, and re-layouts: 18.6 us -> 8.82 us  [natural(): return jnp.take(jnp.stack(pieces, 0), order, axis=0)]
    another operation x6 -> x9, local copies, waits for them, and re-layouts: 10.6 us -> 18.8 us  [the longest x6 13.6 us: body_heads(): jnp.stack([g.reshape(n, tokens, width) for g in (query_grad, key_grad, va...]
    reshape x0 -> x6, local copies, waits for them, and re-layouts: none -> 7.63 us  [the longest x2 6.29 us: unflat(): out.append(vector[..., at:at + size].reshape(vector.shape[:-1] + shape))]
  transfers between devices with their start and end apart: 36 -> 20, of which waited for: 18 -> 6; matrix products, arithmetic and copies ran while one was open for 28% -> 22% of each run, Pallas kernels for 0% -> 0%
where the time goes in v3:
time: 320 us; the launch traced here: 318 us
  waiting for transfers between devices  117 us (37%)
  local copies, waits for them, and re-layouts  85.9 us (27%)
  matrix products  51.3 us (16%)
  starting transfers between devices  33.2 us (10%)
  other arithmetic  29.4 us (9%)
    ppermute x12, waiting for transfers between devices, shifted(): return lax.ppermute(x, axis, [(j, (j + step) % n) for j in range(n)])  90.7 us
    dot_general x4, matrix products, contract_rows(): lax.dot_general(left, right, (((0,), (0,)), ((), ())), preferred_element_...  34.3 us
    ppermute x12, starting transfers between devices, shifted(): return lax.ppermute(x, axis, [(j, (j + step) % n) for j in range(n)])  26.9 us
    ppermute x2, waiting for transfers between devices, swap_dp(): return lax.ppermute(x, 'dp', [(0, 1), (1, 0)])  13.9 us
    another operation x6, local copies, waits for them, and re-layouts, body_heads(): jnp.stack([g.reshape(n, tokens, width) for g in (query_grad, key_grad, va...  13.6 us
    ppermute x2, waiting for transfers between devices, gather_rows_relayed(): lax.ppermute(x, axis, [(j, (j + 2 * s) % n) for j in range(n)])  12.8 us
    unnamed x54, local copies, waits for them, and re-layouts  12.8 us
    gather x4, local copies, waits for them, and re-layouts, natural(): return jnp.take(jnp.stack(pieces, 0), order, axis=0)  8.82 us
  transfers between devices with their start and end apart: 20, of which 6 were waited for; matrix products, arithmetic and copies ran while one was open for 22% of the time, Pallas kernels for 0%

profile of v3, /device:TPU:0, one launch (start us, length us, event | category | flops | bytes accessed | tf_op | source)
XLA Modules:
  0.0 318.5 jit_solution(10074039420962976482)
XLA Ops:
  0.6 3.0 collective-permute-start.16
  10.2 3.7 %collective-permute-start.2 = (bf16[194048]{0:T(1024)(128)(2,1)S(1)}, bf16[194048]{0:T(1024)(128)(2,1)S(1)}, u32[]{:S(2)}, u32[]{:S(2)}) collective-permute-start(bf16[194048]{0:T(1024)(128)(2,1)S(1)} %get-tuple-element.36), channel_id=1, source_target_pairs={{0,3},{1,0},{2,1},{3,2},{4,7},{5,4},{6,5},{7,6},{8,11},{9,8},{10,9... | collective-permute-start | bytes 1164296 | tf_op jit(solution)/shard_map/ppermute | solution.py:115
  16.2 7.2 %collective-permute-done.2 = bf16[194048]{0:T(1024)(128)(2,1)S(1)} collective-permute-done((bf16[194048]{0:T(1024)(128)(2,1)S(1)}, bf16[194048]{0:T(1024)(128)(2,1)S(1)}, u32[]{:S(2)}, u32[]{:S(2)}) %collective-permute-start.2) | collective-permute-done | bytes 388128 | tf_op jit(solution)/shard_map/ppermute | solution.py:115
  23.6 22.9 %collective-permute-done.1 = bf16[194048]{0:T(1024)(128)(2,1)S(1)} collective-permute-done((bf16[194048]{0:T(1024)(128)(2,1)S(1)}, bf16[194048]{0:T(1024)(128)(2,1)S(1)}, u32[]{:S(2)}, u32[]{:S(2)}) %collective-permute-start.1) | collective-permute-done | bytes 388128 | tf_op jit(solution)/shard_map/ppermute | solution.py:115
  53.9 12.8 %collective-permute-done.17 = bf16[128,3072]{1,0:T(8,128)(2,1)} collective-permute-done((bf16[128,3072]{1,0:T(8,128)(2,1)}, bf16[128,3072]{1,0:T(8,128)(2,1)}, u32[]{:S(2)}, u32[]{:S(2)}) %collective-permute-start.17) | collective-permute-done | bytes 786464 | tf_op jit(solution)/shard_map/ppermute | solution.py:183
  69.1 2.5 gather_fusion.4
  71.7 2.0 pad_maximum_fusion.1
  73.7 2.5 gather_fusion.5
  76.3 3.5 %broadcast_select_fusion = (bf16[4,128,3072]{2,1,0:T(8,128)(2,1)S(1)}, bf16[4,128,3072]{2,1,0:T(8,128)(2,1)S(1)}) fusion(bf16[4,128,3072]{2,1,0:T(8,128)(2,1)} %gather_fusion.5, pred[4]{0:T(512)(128)(4,1)} %get-tuple-element.16, bf16[4,128,3072]{2,1,0:T(8,128)(2,1)} %gather_fusion.4), kind=kLoop, calls=%fused_computation.13 | loop fusion | flops 3145728 | bytes 12582916 | tf_op jit(solution)/shard_map/jit(_take)/select_n | solution.py:195
  79.8 8.8 %fusion.12 = f32[512,1536]{1,0:T(8,128)S(1)} fusion(bf16[512,3072]{1,0:T(8,128)(2,1)S(1)} %bitcast.92, bf16[1536,3072]{1,0:T(8,128)(2,1)} %param.12), kind=kOutput, calls=%fused_computation.94 | convolution fusion | flops 4831838208 | bytes 15728640 | tf_op jit(solution)/shard_map/dot_general | solution.py:231
  94.1 2.9 collective-permute-start.6
  97.6 1.9 copy.83
  99.6 1.9 squeeze.30
  103.2 3.5 %exponential_convert_fusion = bf16[3,512,512]{1,2,0:T(8,128)(2,1)} fusion(f32[3,512,512]{1,2,0:T(8,128)} %copy-done, f32[3,512]{1,0:T(4,128)} %log_add_fusion), kind=kLoop, calls=%fused_computation.11 | loop fusion | flops 2359296 | bytes 4724736 | tf_op jit(solution)/shard_map/convert_element_type | solution.py:227
  106.7 14.5 %collective-permute-done.7 = bf16[512,384]{1,0:T(8,128)(2,1)} collective-permute-done((bf16[512,384]{1,0:T(8,128)(2,1)}, bf16[512,384]{1,0:T(8,128)(2,1)}, u32[]{:S(2)}, u32[]{:S(2)}) %collective-permute-start.7) | collective-permute-done | bytes 393248 | tf_op jit(solution)/shard_map/ppermute | solution.py:115
  121.2 2.4 add_convert_fusion
  124.8 3.1 convolution_bitcast_fusion
  132.8 2.3 stack_reshape.35
  135.1 2.3 copy.93
  137.4 2.3 stack_reshape.34
  139.6 2.3 copy.92
  141.9 2.3 stack_reshape.33
  144.2 2.3 copy.91
  149.5 10.9 %collective-permute-start.11 = (bf16[3,128,384]{2,1,0:T(8,128)(2,1)}, bf16[3,128,384]{2,1,0:T(8,128)(2,1)}, u32[]{:S(2)}, u32[]{:S(2)}) collective-permute-start(bf16[3,128,384]{2,1,0:T(8,128)(2,1)} %get-tuple-element.25), channel_id=1, source_target_pairs={{0,3},{1,0},{2,1},{3,2},{4,7},{5,4},{6,5},{7,6},{8,11},{9,8},{10,9... | collective-permute-start | bytes 884744 | tf_op jit(solution)/shard_map/ppermute | solution.py:115
  160.4 3.5 %fusion.14 = f32[364,3072,1]{1,0,2:T(8,128)} fusion(bf16[4,128,364]{2,1,0:T(8,128)(2,1)S(1)} %copy-done.8, bf16[4,128,3072]{2,1,0:T(8,128)(2,1)S(1)} %copy-done.4), kind=kOutput, calls=%fused_computation.96 | convolution fusion | flops 1145044992 | bytes 7991296 | tf_op jit(solution)/shard_map/dot_general | solution.py:11
  164.8 2.0 collective-permute-start.12
  166.9 2.9 collective-permute-start.10
  173.7 46.1 %collective-permute-done.10 = bf16[3,128,384]{2,1,0:T(8,128)(2,1)} collective-permute-done((bf16[3,128,384]{2,1,0:T(8,128)(2,1)}, bf16[3,128,384]{2,1,0:T(8,128)(2,1)}, u32[]{:S(2)}, u32[]{:S(2)}) %collective-permute-start.10) | collective-permute-done | bytes 294944 | tf_op jit(solution)/shard_map/ppermute | solution.py:115
  222.4 3.9 %gather_fusion.1 = f32[4,3,128,384]{3,2,1,0:T(8,128)} fusion(f32[4,3,128,384]{3,2,1,0:T(8,128)} %pad_maximum_fusion.3, s32[1024]{0:T(1024)} %copy-done.21), kind=kCustom, calls=%fused_computation.3 | custom fusion | bytes 4718608 | tf_op jit(solution)/shard_map/jit(_take)/gather | solution.py:121
  226.4 2.6 pad_maximum_fusion.5
  229.0 3.5 %gather_fusion.2 = bf16[4,512,384]{2,1,0:T(8,128)(2,1)} fusion(bf16[4,512,384]{2,1,0:T(8,128)(2,1)} %pad_maximum_fusion.5, s32[1024]{0:T(1024)} %copy-done.21), kind=kCustom, calls=%fused_computation.4 | custom fusion | bytes 3145744 | tf_op jit(solution)/shard_map/jit(_take)/gather | solution.py:121
  235.3 2.4 copy.102
  237.7 3.9 %reshape_reshape.4 = bf16[786432]{0:T(1024)(128)(2,1)} reshape(bf16[512,4,384]{2,1,0:T(4,128)(2,1)} %copy.102) | data formatting | bytes 3145728 | tf_op jit(solution)/shard_map/reshape;reshape | solution.py:167
  241.6 3.0 pad_maximum_fusion.4
  246.8 2.3 copy.94
  249.1 2.3 copy.105
  251.4 2.3 copy.95
  253.7 2.3 copy.106
  256.0 2.3 copy.96
  258.2 2.3 copy.107
  260.5 2.6 copy.101
  263.1 11.3 %fusion.13 = f32[1536,3072]{1,0:T(8,128)} fusion(bf16[512,1536]{0,1:T(8,128)(2,1)} %bitcast.102, bf16[512,3072]{1,0:T(8,128)(2,1)} %bitcast.93), kind=kOutput, calls=%fused_computation.95 | convolution fusion | flops 4831838208 | bytes 23592960 | tf_op jit(solution)/shard_map/dot_general | solution.py:11
  274.5 13.9 %collective-permute-done.15 = bf16[972800]{0:T(1024)(128)(2,1)} collective-permute-done((bf16[972800]{0:T(1024)(128)(2,1)}, bf16[972800]{0:T(1024)(128)(2,1)}, u32[]{:S(2)}, u32[]{:S(2)}) %collective-permute-start.15) | collective-permute-done | bytes 1945632 | tf_op jit(solution)/shard_map/ppermute | solution.py:17
  288.4 2.7 slice.86
  291.1 4.3 %reshape.138 = bf16[512,1536]{1,0:T(8,128)(2,1)} reshape(bf16[786432]{0:T(1024)(128)(2,1)} %slice.86) | data formatting | bytes 3145728 | tf_op jit(solution)/shard_map/reshape | solution.py:174
  297.1 2.0 reshape.140
  299.1 13.6 %convolution_add_fusion = f32[1536,3072]{1,0:T(8,128)} fusion(f32[1536,3072]{1,0:T(8,128)} %fusion.13, bf16[512,1536]{1,0:T(8,128)(2,1)} %reshape.138, bf16[512,3072]{1,0:T(8,128)(2,1)S(1)} %bitcast.90), kind=kOutput, calls=%fused_computation.6 | convolution fusion | flops 4836556800 | bytes 42467328 | tf_op jit(solution)/shard_map/dot_general | solution.py:11
  312.7 5.8 %bitcast_add_fusion = f32[364,3072]{1,0:T(8,128)} fusion(f32[364,3072,1]{1,0,2:T(8,128)} %fusion.14, bf16[512,364]{1,0:T(8,128)(2,1)S(1)} %reshape.140, bf16[512,3072]{1,0:T(8,128)(2,1)S(1)} %bitcast.91), kind=kOutput, calls=%fused_computation.7 | convolution fusion | flops 1146163200 | bytes 12464128 | tf_op jit(solution)/shard_map/dot_general | solution.py:11
  (140 shorter events, 49.6 us)
Async XLA Ops:
  0.6 47.8 %collective-permute-start.16 = (bf16[1,128,3072]{2,1,0:T(8,128)(2,1)}, bf16[1,128,3072]{2,1,0:T(8,128)(2,1)}, u32[]{:S(2)}, u32[]{:S(2)}) collective-permute-start(bf16[1,128,3072]{2,1,0:T(8,128)(2,1)} %param.13), channel_id=1, source_target_pairs={{0,16},{16,0},{1,17},{17,1},{2,18},{18,2},{3,19},{19,3},{4,20},{20... | collective-permute-start | bytes 2359304 | tf_op jit(solution)/shard_map/ppermute | solution.py:17
  3.7 48.9 %collective-permute-start.3 = (bf16[128,3072]{1,0:T(8,128)(2,1)}, bf16[128,3072]{1,0:T(8,128)(2,1)}, u32[]{:S(2)}, u32[]{:S(2)}) collective-permute-start(bf16[128,3072]{1,0:T(8,128)(2,1)} %bitcast.3), channel_id=1, source_target_pairs={{0,8},{4,12},{8,0},{12,4},{1,9},{5,13},{9,1},{13,5},{2,10},{6,14},... | collective-permute-start | bytes 2359304 | tf_op jit(solution)/shard_map/ppermute | solution.py:183
  10.2 13.2 %collective-permute-start.2 = (bf16[194048]{0:T(1024)(128)(2,1)S(1)}, bf16[194048]{0:T(1024)(128)(2,1)S(1)}, u32[]{:S(2)}, u32[]{:S(2)}) collective-permute-start(bf16[194048]{0:T(1024)(128)(2,1)S(1)} %get-tuple-element.36), channel_id=1, source_target_pairs={{0,3},{1,0},{2,1},{3,2},{4,7},{5,4},{6,5},{7,6},{8,11},{9,8},{10,9... | collective-permute-start | bytes 1164296 | tf_op jit(solution)/shard_map/ppermute | solution.py:115
  13.9 32.6 %collective-permute-start.1 = (bf16[194048]{0:T(1024)(128)(2,1)S(1)}, bf16[194048]{0:T(1024)(128)(2,1)S(1)}, u32[]{:S(2)}, u32[]{:S(2)}) collective-permute-start(bf16[194048]{0:T(1024)(128)(2,1)S(1)} %get-tuple-element.35), channel_id=1, source_target_pairs={{0,2},{1,3},{2,0},{3,1},{4,6},{5,7},{6,4},{7,5},{8,10},{9,11},{10,... | collective-permute-start | bytes 1164296 | tf_op jit(solution)/shard_map/ppermute | solution.py:115
  13.9 32.8 %collective-permute-start = (bf16[194048]{0:T(1024)(128)(2,1)S(1)}, bf16[194048]{0:T(1024)(128)(2,1)S(1)}, u32[]{:S(2)}, u32[]{:S(2)}) collective-permute-start(bf16[194048]{0:T(1024)(128)(2,1)S(1)} %get-tuple-element.34), channel_id=1, source_target_pairs={{0,1},{1,2},{2,3},{3,0},{4,5},{5,6},{6,7},{7,4},{8,9},{9,10},{10,1... | collective-permute-start | bytes 1164296 | tf_op jit(solution)/shard_map/ppermute | solution.py:115
  14.9 51.7 %copy-start.22 = (pred[4]{0:T(512)(128)(4,1)}, pred[4]{0:T(512)(128)(4,1)S(1)}, u32[]{:S(2)}) copy-start(pred[4]{0:T(512)(128)(4,1)S(1)} %compare_and_fusion.1) | copy-start | bytes 16
  16.2 35.7 %copy-start.21 = (s32[1024]{0:T(1024)}, s32[1024]{0:T(1024)S(1)}, u32[]{:S(2)}) copy-start(s32[1024]{0:T(1024)S(1)} %pad_clamp_fusion.1) | copy-start | bytes 12292
  23.4 43.9 %collective-permute-start.4 = (bf16[128,3072]{1,0:T(8,128)(2,1)}, bf16[128,3072]{1,0:T(8,128)(2,1)}, u32[]{:S(2)}, u32[]{:S(2)}) collective-permute-start(bf16[128,3072]{1,0:T(8,128)(2,1)} %bitcast.3), channel_id=1, source_target_pairs={{0,4},{4,0},{8,12},{12,8},{1,5},{5,1},{9,13},{13,9},{2,6},{6,2},{1... | collective-permute-start | bytes 2359304 | tf_op jit(solution)/shard_map/ppermute | solution.py:185
  46.5 0.7 copy-start.19
  46.7 0.7 copy-start.20
  48.4 18.2 %collective-permute-start.17 = (bf16[128,3072]{1,0:T(8,128)(2,1)}, bf16[128,3072]{1,0:T(8,128)(2,1)}, u32[]{:S(2)}, u32[]{:S(2)}) collective-permute-start(bf16[128,3072]{1,0:T(8,128)(2,1)} %bitcast.31), channel_id=1, source_target_pairs={{0,8},{4,12},{8,0},{12,4},{1,9},{5,13},{9,1},{13,5},{2,10},{6,14},... | collective-permute-start | bytes 2359304 | tf_op jit(solution)/shard_map/ppermute | solution.py:183
  50.1 1.1 slice-start
  50.1 1.4 slice-start.1
  50.6 2.7 copy-start.10
  51.0 2.3 copy-start.12
  52.6 14.8 %collective-permute-start.5 = (bf16[1,128,3072]{2,1,0:T(8,128)(2,1)}, bf16[1,128,3072]{2,1,0:T(8,128)(2,1)S(1)}, u32[]{:S(2)}, u32[]{:S(2)}) collective-permute-start(bf16[1,128,3072]{2,1,0:T(8,128)(2,1)} %bitcast.4), channel_id=1, source_target_pairs={{0,4},{4,0},{8,12},{12,8},{1,5},{5,1},{9,13},{13,9},{2,6},{6,2},{1... | collective-permute-start | bytes 2359304 | tf_op jit(solution)/shard_map/ppermute | solution.py:187
  53.3 13.5 %copy-start = (f32[3,512,512]{1,2,0:T(8,128)}, f32[3,512,512]{1,2,0:T(8,128)S(1)}, u32[]{:S(2)}) copy-start(f32[3,512,512]{1,2,0:T(8,128)S(1)} %get-tuple-element.40) | copy-start | bytes 9437188
  53.3 18.4 %collective-permute-start.18 = (bf16[128,3072]{1,0:T(8,128)(2,1)}, bf16[128,3072]{1,0:T(8,128)(2,1)}, u32[]{:S(2)}, u32[]{:S(2)}) collective-permute-start(bf16[128,3072]{1,0:T(8,128)(2,1)} %bitcast.31), channel_id=1, source_target_pairs={{0,4},{4,0},{8,12},{12,8},{1,5},{5,1},{9,13},{13,9},{2,6},{6,2},{1... | collective-permute-start | bytes 2359304 | tf_op jit(solution)/shard_map/ppermute | solution.py:185
  66.6 5.1 %collective-permute-start.19 = (bf16[1,128,3072]{2,1,0:T(8,128)(2,1)}, bf16[1,128,3072]{2,1,0:T(8,128)(2,1)}, u32[]{:S(2)}, u32[]{:S(2)}) collective-permute-start(bf16[1,128,3072]{2,1,0:T(8,128)(2,1)} %bitcast.32), channel_id=1, source_target_pairs={{0,4},{4,0},{8,12},{12,8},{1,5},{5,1},{9,13},{13,9},{2,6},{6,2},{1... | collective-permute-start | bytes 2359304 | tf_op jit(solution)/shard_map/ppermute | solution.py:187
  66.7 34.8 %copy-start.7 = (bf16[4,128,364]{2,1,0:T(8,128)(2,1)}, bf16[4,128,364]{2,1,0:T(8,128)(2,1)S(1)}, u32[]{:S(2)}) copy-start(bf16[4,128,364]{2,1,0:T(8,128)(2,1)S(1)} %broadcast_select_fusion.2) | copy-start | bytes 1118212
  79.7 8.8 %copy-start.3 = (bf16[4,128,3072]{2,1,0:T(8,128)(2,1)}, bf16[4,128,3072]{2,1,0:T(8,128)(2,1)S(1)}, u32[]{:S(2)}) copy-start(bf16[4,128,3072]{2,1,0:T(8,128)(2,1)S(1)} %get-tuple-element.38) | copy-start | bytes 9437188
  88.6 2.1 copy-start.18
  90.6 16.1 %collective-permute-start.8 = (bf16[512,384]{1,0:T(8,128)(2,1)}, bf16[512,384]{1,0:T(8,128)(2,1)}, u32[]{:S(2)}, u32[]{:S(2)}) collective-permute-start(bf16[512,384]{1,0:T(8,128)(2,1)} %get-tuple-element.19), channel_id=1, source_target_pairs={{0,1},{1,2},{2,3},{3,0},{4,5},{5,6},{6,7},{7,4},{8,9},{9,10},{10,1... | collective-permute-start | bytes 1179656 | tf_op jit(solution)/shard_map/ppermute | solution.py:115
  92.2 29.0 %collective-permute-start.7 = (bf16[512,384]{1,0:T(8,128)(2,1)}, bf16[512,384]{1,0:T(8,128)(2,1)}, u32[]{:S(2)}, u32[]{:S(2)}) collective-permute-start(bf16[512,384]{1,0:T(8,128)(2,1)} %get-tuple-element.20), channel_id=1, source_target_pairs={{0,2},{1,3},{2,0},{3,1},{4,6},{5,7},{6,4},{7,5},{8,10},{9,11},{10,... | collective-permute-start | bytes 1179656 | tf_op jit(solution)/shard_map/ppermute | solution.py:115
  94.1 27.1 %collective-permute-start.6 = (bf16[512,384]{1,0:T(8,128)(2,1)}, bf16[512,384]{1,0:T(8,128)(2,1)}, u32[]{:S(2)}, u32[]{:S(2)}) collective-permute-start(bf16[512,384]{1,0:T(8,128)(2,1)} %get-tuple-element.18), channel_id=1, source_target_pairs={{0,3},{1,0},{2,1},{3,2},{4,7},{5,4},{6,5},{7,6},{8,11},{9,8},{10,9... | collective-permute-start | bytes 1179656 | tf_op jit(solution)/shard_map/ppermute | solution.py:115
  124.8 3.1 copy-start.1
  124.8 3.1 copy-start.14
  129.0 1.0 copy-start.11
  130.0 1.5 copy-start.13
  146.5 13.9 %copy-start.4 = (bf16[4,128,3072]{2,1,0:T(8,128)(2,1)S(1)}, bf16[4,128,3072]{2,1,0:T(8,128)(2,1)}, u32[]{:S(2)}) copy-start(bf16[4,128,3072]{2,1,0:T(8,128)(2,1)} %copy-done.3) | copy-start | bytes 9437188
  146.5 13.9 %copy-start.8 = (bf16[4,128,364]{2,1,0:T(8,128)(2,1)S(1)}, bf16[4,128,364]{2,1,0:T(8,128)(2,1)}, u32[]{:S(2)}) copy-start(bf16[4,128,364]{2,1,0:T(8,128)(2,1)} %copy-done.7) | copy-start | bytes 1118212
  148.4 15.5 %copy-start.6 = (f32[4,3,128,384]{3,2,1,0:T(8,128)}, f32[4,3,128,384]{3,2,1,0:T(8,128)S(1)}, u32[]{:S(2)}) copy-start(f32[4,3,128,384]{3,2,1,0:T(8,128)S(1)} %pad_maximum_fusion.2) | copy-start | bytes 7077892
  149.5 14.4 %copy-start.9 = (bf16[3,128,512]{2,1,0:T(8,128)(2,1)S(1)}, bf16[3,128,512]{2,1,0:T(8,128)(2,1)}, u32[]{:S(2)}) copy-start(bf16[3,128,512]{2,1,0:T(8,128)(2,1)} %get-tuple-element.42) | copy-start | bytes 1179652
  149.5 23.2 %collective-permute-start.11 = (bf16[3,128,384]{2,1,0:T(8,128)(2,1)}, bf16[3,128,384]{2,1,0:T(8,128)(2,1)}, u32[]{:S(2)}, u32[]{:S(2)}) collective-permute-start(bf16[3,128,384]{2,1,0:T(8,128)(2,1)} %get-tuple-element.25), channel_id=1, source_target_pairs={{0,3},{1,0},{2,1},{3,2},{4,7},{5,4},{6,5},{7,6},{8,11},{9,8},{10,9... | collective-permute-start | bytes 884744 | tf_op jit(solution)/shard_map/ppermute | solution.py:115
  164.8 61.5 %collective-permute-start.14 = (bf16[512,384]{1,0:T(8,128)(2,1)}, bf16[512,384]{1,0:T(8,128)(2,1)}, u32[]{:S(2)}, u32[]{:S(2)}) collective-permute-start(bf16[512,384]{1,0:T(8,128)(2,1)} %copy.97), channel_id=1, source_target_pairs={{0,3},{1,0},{2,1},{3,2},{4,7},{5,4},{6,5},{7,6},{8,11},{9,8},{10,9... | collective-permute-start | bytes 1179656 | tf_op jit(solution)/shard_map/ppermute | solution.py:115
  164.8 61.5 %collective-permute-start.13 = (bf16[512,384]{1,0:T(8,128)(2,1)}, bf16[512,384]{1,0:T(8,128)(2,1)}, u32[]{:S(2)}, u32[]{:S(2)}) collective-permute-start(bf16[512,384]{1,0:T(8,128)(2,1)} %copy.97), channel_id=1, source_target_pairs={{0,2},{1,3},{2,0},{3,1},{4,6},{5,7},{6,4},{7,5},{8,10},{9,11},{10,... | collective-permute-start | bytes 1179656 | tf_op jit(solution)/shard_map/ppermute | solution.py:115
  164.8 61.5 %collective-permute-start.12 = (bf16[512,384]{1,0:T(8,128)(2,1)}, bf16[512,384]{1,0:T(8,128)(2,1)}, u32[]{:S(2)}, u32[]{:S(2)}) collective-permute-start(bf16[512,384]{1,0:T(8,128)(2,1)} %copy.97), channel_id=1, source_target_pairs={{0,1},{1,2},{2,3},{3,0},{4,5},{5,6},{6,7},{7,4},{8,9},{9,10},{10,1... | collective-permute-start | bytes 1179656 | tf_op jit(solution)/shard_map/ppermute | solution.py:115
  166.9 52.9 %collective-permute-start.10 = (bf16[3,128,384]{2,1,0:T(8,128)(2,1)}, bf16[3,128,384]{2,1,0:T(8,128)(2,1)}, u32[]{:S(2)}, u32[]{:S(2)}) collective-permute-start(bf16[3,128,384]{2,1,0:T(8,128)(2,1)} %get-tuple-element.26), channel_id=1, source_target_pairs={{0,2},{1,3},{2,0},{3,1},{4,6},{5,7},{6,4},{7,5},{8,10},{9,11},{10,... | collective-permute-start | bytes 884744 | tf_op jit(solution)/shard_map/ppermute | solution.py:115
  172.6 48.2 %copy-start.15 = (f32[1,3,128,384]{3,2,1,0:T(8,128)S(1)}, f32[1,3,128,384]{3,2,1,0:T(8,128)}, u32[]{:S(2)}) copy-start(f32[1,3,128,384]{3,2,1,0:T(8,128)} %constant_dynamic-slice_fusion) | copy-start | bytes 1769476
  172.6 48.1 %collective-permute-start.9 = (bf16[3,128,384]{2,1,0:T(8,128)(2,1)}, bf16[3,128,384]{2,1,0:T(8,128)(2,1)S(1)}, u32[]{:S(2)}, u32[]{:S(2)}) collective-permute-start(bf16[3,128,384]{2,1,0:T(8,128)(2,1)} %get-tuple-element.24), channel_id=1, source_target_pairs={{0,1},{1,2},{2,3},{3,0},{4,5},{5,6},{6,7},{7,4},{8,9},{9,10},{10,1... | collective-permute-start | bytes 884744 | tf_op jit(solution)/shard_map/ppermute | solution.py:115
  222.4 4.0 %copy-start.16 = (bf16[1,512,384]{2,1,0:T(8,128)(2,1)S(1)}, bf16[1,512,384]{2,1,0:T(8,128)(2,1)}, u32[]{:S(2)}) copy-start(bf16[1,512,384]{2,1,0:T(8,128)(2,1)} %copy.100) | copy-start | bytes 1179652
  229.0 3.5 %copy-start.23 = (pred[4]{0:T(512)(128)(4,1)S(1)}, pred[4]{0:T(512)(128)(4,1)}, u32[]{:S(2)}) copy-start(pred[4]{0:T(512)(128)(4,1)} %copy-done.22) | copy-start | bytes 16
  234.1 1.1 copy-start.2
  237.7 3.9 %copy-start.17 = (bf16[186368]{0:T(1024)(128)(2,1)S(1)}, bf16[186368]{0:T(1024)(128)(2,1)}, u32[]{:S(2)}) copy-start(bf16[186368]{0:T(1024)(128)(2,1)} %select_n.222) | copy-start | bytes 1118212
  241.6 3.5 %copy-start.5 = (f32[4,3,128,384]{3,2,1,0:T(8,128)S(1)}, f32[4,3,128,384]{3,2,1,0:T(8,128)}, u32[]{:S(2)}) copy-start(f32[4,3,128,384]{3,2,1,0:T(8,128)} %gather_fusion.1) | copy-start | bytes 7077892
  244.6 43.8 %collective-permute-start.15 = (bf16[972800]{0:T(1024)(128)(2,1)}, bf16[972800]{0:T(1024)(128)(2,1)}, u32[]{:S(2)}, u32[]{:S(2)}) collective-permute-start(bf16[972800]{0:T(1024)(128)(2,1)} %pad_maximum_fusion.4), channel_id=1, source_target_pairs={{0,16},{16,0},{1,17},{17,1},{2,18},{18,2},{3,19},{19,3},{4,20},{20... | collective-permute-start | bytes 5836808 | tf_op jit(solution)/shard_map/ppermute | solution.py:17

commit v4 on v3

--- a/solution.py
+++ b/solution.py
@@ -251,22 +251,29 @@
     value_grad = jnp.einsum(
         "hqk,qhd->khd", attn_probs, grad_heads, preferred_element_type=jnp.float32
     )
+    other_patch = swap_dp(every_patch)
+    embed_weight_grad = contract_rows(every_patch, dense_grad) + contract_rows(
+        other_patch, other_grad
+    )
+    out_flat = attn_out.reshape(rows, width)
+    own_pair = (out_flat, swap_dp(out_flat))
+    attn_grad, sent_out = lax.optimization_barrier((attn_grad, out_flat))
+    out_pieces = [own_pair] + [
+        (got, swap_dp(got)) for got in (shifted(sent_out, "col", s) for s in range(1, n))
+    ]
+    out_own = natural([p[0] for p in out_pieces], "col")
+    out_other = natural([p[1] for p in out_pieces], "col")
+    out_weight_grad = (
+        lax.dot_general(out_own, dense_grad, (((1,), (0,)), ((), ())), preferred_element_type=jnp.float32)
+        + lax.dot_general(out_other, other_grad, (((1,), (0,)), ((), ())), preferred_element_type=jnp.float32)
+    ).reshape(width_all, -1)
     grads = jnp.stack([g.reshape(n, tokens, width) for g in (query_grad, key_grad, value_grad)], 1)
+    grads, out_own = lax.optimization_barrier((grads, out_own))
     back = [grads[me]] + [
         shifted(grads[(me + s) % n].astype(jnp.bfloat16), "col", s).astype(jnp.float32)
         for s in range(1, n)
     ]
     back = jnp.transpose(natural(back, "col"), (1, 2, 0, 3)).reshape(3, 1, tokens, width_all)
-    out_flat = attn_out.reshape(rows, width)
-    out_groups = natural([out_flat] + [shifted(out_flat, "col", s) for s in range(1, n)], "col")
-    every_out = jnp.transpose(out_groups, (1, 0, 2)).reshape(rows, width_all)
-    other_out, other_patch = unflat(
-        swap_dp(flat(every_out, every_patch)), [every_out.shape, every_patch.shape]
-    )
-    out_weight_grad = contract_rows(every_out, dense_grad) + contract_rows(other_out, other_grad)
-    embed_weight_grad = contract_rows(every_patch, dense_grad) + contract_rows(
-        other_patch, other_grad
-    )
     return (back[0], back[1], back[2], out_weight_grad, embed_weight_grad)
 
 

time: 320 us -> 264 us (0.82)
  waiting for transfers between devices: 117 us -> 78.7 us
  local copies, waits for them, and re-layouts: 85.9 us -> 66.3 us
  starting transfers between devices: 33.2 us -> 38.3 us
    dot_general x4 -> x2, matrix products: 34.3 us -> 6.05 us  [contract_rows(): lax.dot_general(left, right, (((0,), (0,)), ((), ())), preferred_element_...]
    ppermute x12, waiting for transfers between devices: 90.7 us -> 64.9 us  [shifted(): return lax.ppermute(x, axis, [(j, (j + step) % n) for j in range(n)])]
    dot_general x0 -> x2, matrix products: none -> 23.1 us  [the longest x1 13.6 us: body_heads(): lax.dot_general(out_other, other_grad, (((1,), (0,)), ((), ())), preferre...]
    ppermute x2 -> x6, waiting for transfers between devices: 13.9 us -> 0.02 us  [swap_dp(): return lax.ppermute(x, 'dp', [(0, 1), (1, 0)])]
    reshape x3 -> x0, local copies, waits for them, and re-layouts: 7.2 us -> none  [the longest x2 6.29 us: unflat(): out.append(vector[..., at:at + size].reshape(vector.shape[:-1] + shape))]
    select_n x3 -> x0, local copies, waits for them, and re-layouts: 6.71 us -> none  [natural(): return jnp.take(jnp.stack(pieces, 0), order, axis=0)]
    ppermute x2 -> x6, starting transfers between devices: 3.54 us -> 8.67 us  [swap_dp(): return lax.ppermute(x, 'dp', [(0, 1), (1, 0)])]
    another operation x2 -> x1, local copies, waits for them, and re-layouts: 4.14 us -> 0.26 us  [flat(): return jnp.concatenate([a.reshape(-1) for a in arrays])]
  transfers between devices with their start and end apart: 20 -> 24, of which waited for: 6 -> 7; matrix products, arithmetic and copies ran while one was open for 22% -> 45% of each run, Pallas kernels for 0% -> 0%
where the time goes in v4:
time: 264 us; the launch traced here: 263 us
  waiting for transfers between devices  78.7 us (30%)
  local copies, waits for them, and re-layouts  66.3 us (25%)
  matrix products  50.3 us (19%)
  starting transfers between devices  38.3 us (15%)
  other arithmetic  27.8 us (11%)
    ppermute x12, waiting for transfers between devices, shifted(): return lax.ppermute(x, axis, [(j, (j + step) % n) for j in range(n)])  64.9 us
    ppermute x12, starting transfers between devices, shifted(): return lax.ppermute(x, axis, [(j, (j + step) % n) for j in range(n)])  27 us
    ppermute x2, waiting for transfers between devices, gather_rows_relayed(): lax.ppermute(x, axis, [(j, (j + 2 * s) % n) for j in range(n)])  13.8 us
    another operation x6, local copies, waits for them, and re-layouts, body_heads(): jnp.stack([g.reshape(n, tokens, width) for g in (query_grad, key_grad, va...  13.7 us
    dot_general x1, matrix products, body_heads(): lax.dot_general(out_other, other_grad, (((1,), (0,)), ((), ())), preferre...  13.6 us
    gather x5, local copies, waits for them, and re-layouts, natural(): return jnp.take(jnp.stack(pieces, 0), order, axis=0)  11.9 us
    unnamed x22, local copies, waits for them, and re-layouts  11.1 us
    dot_general x1, matrix products, body_heads(): lax.dot_general(out_own, dense_grad, (((1,), (0,)), ((), ())), preferred_...  9.47 us
  transfers between devices with their start and end apart: 24, of which 7 were waited for; matrix products, arithmetic and copies ran while one was open for 45% of the time, Pallas kernels for 0%

profile of v4, /device:TPU:0, one launch (start us, length us, event | category | flops | bytes accessed | tf_op | source)
XLA Modules:
  0.0 262.5 jit_solution(14643573074390289531)
XLA Ops:
  0.6 3.0 %collective-permute-start.19 = (bf16[1,128,3072]{2,1,0:T(8,128)(2,1)}, bf16[1,128,3072]{2,1,0:T(8,128)(2,1)}, u32[]{:S(2)}, u32[]{:S(2)}) collective-permute-start(bf16[1,128,3072]{2,1,0:T(8,128)(2,1)} %param.15), channel_id=1, source_target_pairs={{0,16},{16,0},{1,17},{17,1},{2,18},{18,2},{3,19},{19,3},{4,20},{20... | collective-permute-start | bytes 2359304 | tf_op jit(solution)/shard_map/ppermute | solution.py:17
  10.2 3.7 %collective-permute-start.2 = (bf16[194048]{0:T(1024)(128)(2,1)S(1)}, bf16[194048]{0:T(1024)(128)(2,1)S(1)}, u32[]{:S(2)}, u32[]{:S(2)}) collective-permute-start(bf16[194048]{0:T(1024)(128)(2,1)S(1)} %get-tuple-element.36), channel_id=1, source_target_pairs={{0,3},{1,0},{2,1},{3,2},{4,7},{5,4},{6,5},{7,6},{8,11},{9,8},{10,9... | collective-permute-start | bytes 1164296 | tf_op jit(solution)/shard_map/ppermute | solution.py:115
  16.8 6.6 %collective-permute-done.2 = bf16[194048]{0:T(1024)(128)(2,1)S(1)} collective-permute-done((bf16[194048]{0:T(1024)(128)(2,1)S(1)}, bf16[194048]{0:T(1024)(128)(2,1)S(1)}, u32[]{:S(2)}, u32[]{:S(2)}) %collective-permute-start.2) | collective-permute-done | bytes 388128 | tf_op jit(solution)/shard_map/ppermute | solution.py:115
  23.6 22.9 %collective-permute-done.1 = bf16[194048]{0:T(1024)(128)(2,1)S(1)} collective-permute-done((bf16[194048]{0:T(1024)(128)(2,1)S(1)}, bf16[194048]{0:T(1024)(128)(2,1)S(1)}, u32[]{:S(2)}, u32[]{:S(2)}) %collective-permute-start.1) | collective-permute-done | bytes 388128 | tf_op jit(solution)/shard_map/ppermute | solution.py:115
  55.3 1.7 multiply_reduce_fusion
  59.0 13.8 %collective-permute-done.20 = bf16[128,3072]{1,0:T(8,128)(2,1)} collective-permute-done((bf16[128,3072]{1,0:T(8,128)(2,1)}, bf16[128,3072]{1,0:T(8,128)(2,1)}, u32[]{:S(2)}, u32[]{:S(2)}) %collective-permute-start.20) | collective-permute-done | bytes 786464 | tf_op jit(solution)/shard_map/ppermute | solution.py:183
  72.9 2.0 copy.53
  74.8 1.9 squeeze.30
  79.0 2.0 pad_maximum_fusion
  81.0 2.5 gather_fusion.3
  83.6 2.0 pad_maximum_fusion.1
  85.6 2.5 gather_fusion.6
  88.2 3.5 %broadcast_select_fusion = (bf16[4,128,3072]{2,1,0:T(8,128)(2,1)S(1)}, bf16[4,128,3072]{2,1,0:T(8,128)(2,1)S(1)}) fusion(bf16[4,128,3072]{2,1,0:T(8,128)(2,1)} %gather_fusion.6, pred[4]{0:T(512)(128)(4,1)S(1)} %copy-done.7, bf16[4,128,3072]{2,1,0:T(8,128)(2,1)} %gather_fusion.3), kind=kLoop, calls=%fused_computation.14 | loop fusion | flops 3145728 | bytes 12582916 | tf_op jit(solution)/shard_map/jit(_take)/select_n | solution.py:195
  91.6 8.8 %fusion.21 = f32[512,1536]{1,0:T(8,128)S(1)} fusion(bf16[512,3072]{1,0:T(8,128)(2,1)S(1)} %bitcast.101, bf16[1536,3072]{1,0:T(8,128)(2,1)} %param.14), kind=kOutput, calls=%fused_computation.106 | convolution fusion | flops 4831838208 | bytes 15728640 | tf_op jit(solution)/shard_map/dot_general | solution.py:231
  102.3 2.1 collective-permute-start.7
  104.4 2.8 %collective-permute-start.6 = (bf16[512,384]{1,0:T(8,128)(2,1)S(1)}, bf16[512,384]{1,0:T(8,128)(2,1)S(1)}, u32[]{:S(2)}, u32[]{:S(2)}) collective-permute-start(bf16[512,384]{1,0:T(8,128)(2,1)S(1)} %get-tuple-element.18), channel_id=1, source_target_pairs={{0,3},{1,0},{2,1},{3,2},{4,7},{5,4},{6,5},{7,6},{8,11},{9,8},{10,9... | collective-permute-start | bytes 1179656 | tf_op jit(solution)/shard_map/ppermute | solution.py:115
  108.7 4.6 %bitcast_add_fusion = f32[364,3072]{1,0:T(8,128)} fusion(f32[364,3072,1]{1,0,2:T(8,128)S(1)} %fusion.5, bf16[512,364]{1,0:T(8,128)(2,1)} %collective-permute-done.23, bf16[512,3072]{1,0:T(8,128)(2,1)S(1)} %bitcast.98), kind=kOutput, calls=%fused_computation.8 | convolution fusion | flops 1146163200 | bytes 12464128 | tf_op jit(solution)/shard_map/dot_general | solution.py:11
  114.6 16.1 %collective-permute-done.7 = bf16[512,384]{1,0:T(8,128)(2,1)S(1)} collective-permute-done((bf16[512,384]{1,0:T(8,128)(2,1)S(1)}, bf16[512,384]{1,0:T(8,128)(2,1)S(1)}, u32[]{:S(2)}, u32[]{:S(2)}) %collective-permute-start.7) | collective-permute-done | bytes 393248 | tf_op jit(solution)/shard_map/ppermute | solution.py:115
  132.9 3.1 %convolution_bitcast_fusion = f32[512,3,128]{0,2,1:T(8,128)} fusion(bf16[512,3,128]{0,2,1:T(8,128)(2,1)S(1)} %bitcast.103, bf16[3,512,512]{1,2,0:T(8,128)(2,1)} %exponential_convert_fusion), kind=kOutput, calls=%fused_computation.29 | convolution fusion | flops 201326592 | bytes 2752512 | tf_op jit(solution)/shard_map/hqk,qhd->khd/dot_general | solution.py:251
  137.1 11.0 %collective-permute-start.11 = (bf16[512,384]{0,1:T(8,128)(2,1)}, bf16[512,384]{0,1:T(8,128)(2,1)}, u32[]{:S(2)}, u32[]{:S(2)}) collective-permute-start(bf16[512,384]{0,1:T(8,128)(2,1)} %bitcast.14), channel_id=1, source_target_pairs={{0,3},{1,0},{2,1},{3,2},{4,7},{5,4},{6,5},{7,6},{8,11},{9,8},{10,9... | collective-permute-start | bytes 1179656 | tf_op jit(solution)/shard_map/ppermute | solution.py:115
  150.2 2.3 stack_reshape.35
  152.4 2.3 copy.63
  154.7 2.2 multiply_convert_fusion
  159.6 2.3 stack_reshape.34
  161.9 2.3 copy.62
  164.2 2.7 %fusion.3 = f32[512,3,128]{0,2,1:T(8,128)} fusion(bf16[512,3,128]{0,2,1:T(8,128)(2,1)S(1)} %copy-done.4, bf16[3,512,512]{1,2,0:T(8,128)(2,1)} %copy-done.1), kind=kOutput, calls=%fused_computation.28 | convolution fusion | flops 201523200 | bytes 2752512 | tf_op jit(solution)/shard_map/hqk,khd->qhd/dot_general | solution.py:244
  166.9 2.3 stack_reshape.33
  169.2 2.3 copy.61
  171.4 3.2 %pad_maximum_fusion.2 = f32[4,3,128,384]{3,2,1,0:T(8,128)} fusion(f32[4,1,128,384]{3,2,1,0:T(8,128)} %copy.63, f32[4,1,128,384]{3,2,1,0:T(8,128)} %copy.62, f32[4,1,128,384]{3,2,1,0:T(8,128)} %copy.61), kind=kLoop, calls=%fused_computation.17 | loop fusion | flops 1179648 | bytes 4718592 | tf_op jit(solution)/shard_map/stack | solution.py:270
  174.6 7.5 %collective-permute-done.10 = bf16[512,384]{0,1:T(8,128)(2,1)} collective-permute-done((bf16[512,384]{0,1:T(8,128)(2,1)}, bf16[512,384]{0,1:T(8,128)(2,1)}, u32[]{:S(2)}, u32[]{:S(2)}) %collective-permute-start.10) | collective-permute-done | bytes 393248 | tf_op jit(solution)/shard_map/ppermute | solution.py:115
  182.1 2.7 %pad_maximum_fusion.4 = bf16[4,512,384]{1,2,0:T(8,128)(2,1)} fusion(bf16[1,512,384]{1,2,0:T(8,128)(2,1)} %bitcast.17, bf16[1,512,384]{1,2,0:T(8,128)(2,1)} %bitcast.16, bf16[1,512,384]{1,2,0:T(8,128)(2,1)} %bitcast.15, bf16[1,512,384]{1,2,0:T(8,128)(2,1)} %bitcast.13), kind=kLoop, calls=%fused_computation.20 | loop fusion | flops 2359296 | bytes 3145728 | tf_op jit(solution)/shard_map/stack | solution.py:121
  184.8 3.4 %gather_fusion.4 = bf16[4,512,384]{1,2,0:T(8,128)(2,1)} fusion(bf16[4,512,384]{1,2,0:T(8,128)(2,1)} %pad_maximum_fusion.4, s32[1024]{0:T(1024)} %pad_clamp_fusion), kind=kCustom, calls=%fused_computation.1.clone | custom fusion | bytes 3145744 | tf_op jit(solution)/shard_map/jit(_take)/gather | solution.py:121
  188.2 1.8 broadcast_select_fusion.2
  191.5 2.2 collective-permute-start.13
  193.7 1.9 collective-permute-start.12
  195.7 9.5 %fusion.22 = f32[4,384,3072]{2,1,0:T(8,128)} fusion(bf16[4,512,384]{1,2,0:T(8,128)(2,1)S(1)} %broadcast_select_fusion.2, bf16[512,3072,1]{1,0,2:T(8,128)(2,1)S(1)} %bitcast.102), kind=kOutput, calls=%fused_computation.107 | convolution fusion | flops 4831838208 | bytes 23592960 | tf_op jit(solution)/shard_map/dot_general | solution.py:267
  208.4 10.4 %collective-permute-done.13 = bf16[3,128,384]{2,1,0:T(8,128)(2,1)S(1)} collective-permute-done((bf16[3,128,384]{2,1,0:T(8,128)(2,1)S(1)}, bf16[3,128,384]{2,1,0:T(8,128)(2,1)S(1)}, u32[]{:S(2)}, u32[]{:S(2)}) %collective-permute-start.13) | collective-permute-done | bytes 294944 | tf_op jit(solution)/shard_map/ppermute | solution.py:115
  222.0 3.8 %gather_fusion.1 = f32[4,3,128,384]{3,2,1,0:T(8,128)} fusion(f32[4,3,128,384]{3,2,1,0:T(8,128)} %pad_maximum_fusion.3, s32[1024]{0:T(1024)S(1)} %pad_clamp_fusion.2), kind=kCustom, calls=%fused_computation.5 | custom fusion | bytes 4718608 | tf_op jit(solution)/shard_map/jit(_take)/gather | solution.py:121
  225.8 1.9 select_bitcast_fusion
  229.2 2.3 copy.64
  231.5 2.3 copy.69
  233.8 2.3 copy.65
  236.1 2.3 copy.70
  238.4 2.3 copy.66
  240.7 2.3 copy.71
  243.0 2.6 pad_maximum_fusion.5
  245.6 3.3 %gather_fusion.5 = bf16[4,512,384]{1,2,0:T(8,128)(2,1)} fusion(bf16[4,512,384]{1,2,0:T(8,128)(2,1)} %pad_maximum_fusion.5, s32[1024]{0:T(1024)} %pad_clamp_fusion), kind=kCustom, calls=%fused_computation.3.clone | custom fusion | bytes 3145744 | tf_op jit(solution)/shard_map/jit(_take)/gather | solution.py:121
  248.9 13.6 %convolution_add_fusion = f32[4,384,3072]{2,1,0:T(8,128)} fusion(f32[4,384,3072]{2,1,0:T(8,128)} %fusion.22, bf16[512,3072,1]{1,0,2:T(8,128)(2,1)S(1)} %bitcast.99, bf16[4,512,384]{1,2,0:T(8,128)(2,1)} %gather_fusion.5, pred[4]{0:T(512)(128)(4,1)S(1)} %compare_and_fusion.1), kind=kOutput, calls=%fused_computation.7 | convolution fusion | flops 4837343232 | bytes 42467332 | tf_op jit(solution)/shard_map/dot_general | solution.py:268
  (108 shorter events, 44.5 us)
Async XLA Ops:
  0.6 54.0 %collective-permute-start.19 = (bf16[1,128,3072]{2,1,0:T(8,128)(2,1)}, bf16[1,128,3072]{2,1,0:T(8,128)(2,1)}, u32[]{:S(2)}, u32[]{:S(2)}) collective-permute-start(bf16[1,128,3072]{2,1,0:T(8,128)(2,1)} %param.15), channel_id=1, source_target_pairs={{0,16},{16,0},{1,17},{17,1},{2,18},{18,2},{3,19},{19,3},{4,20},{20... | collective-permute-start | bytes 2359304 | tf_op jit(solution)/shard_map/ppermute | solution.py:17
  3.7 53.9 %collective-permute-start.3 = (bf16[128,3072]{1,0:T(8,128)(2,1)}, bf16[128,3072]{1,0:T(8,128)(2,1)}, u32[]{:S(2)}, u32[]{:S(2)}) collective-permute-start(bf16[128,3072]{1,0:T(8,128)(2,1)} %bitcast.3), channel_id=1, source_target_pairs={{0,8},{4,12},{8,0},{12,4},{1,9},{5,13},{9,1},{13,5},{2,10},{6,14},... | collective-permute-start | bytes 2359304 | tf_op jit(solution)/shard_map/ppermute | solution.py:183
  10.2 13.2 %collective-permute-start.2 = (bf16[194048]{0:T(1024)(128)(2,1)S(1)}, bf16[194048]{0:T(1024)(128)(2,1)S(1)}, u32[]{:S(2)}, u32[]{:S(2)}) collective-permute-start(bf16[194048]{0:T(1024)(128)(2,1)S(1)} %get-tuple-element.36), channel_id=1, source_target_pairs={{0,3},{1,0},{2,1},{3,2},{4,7},{5,4},{6,5},{7,6},{8,11},{9,8},{10,9... | collective-permute-start | bytes 1164296 | tf_op jit(solution)/shard_map/ppermute | solution.py:115
  13.9 32.6 %collective-permute-start.1 = (bf16[194048]{0:T(1024)(128)(2,1)S(1)}, bf16[194048]{0:T(1024)(128)(2,1)S(1)}, u32[]{:S(2)}, u32[]{:S(2)}) collective-permute-start(bf16[194048]{0:T(1024)(128)(2,1)S(1)} %get-tuple-element.35), channel_id=1, source_target_pairs={{0,2},{1,3},{2,0},{3,1},{4,6},{5,7},{6,4},{7,5},{8,10},{9,11},{10,... | collective-permute-start | bytes 1164296 | tf_op jit(solution)/shard_map/ppermute | solution.py:115
  13.9 32.8 %collective-permute-start = (bf16[194048]{0:T(1024)(128)(2,1)S(1)}, bf16[194048]{0:T(1024)(128)(2,1)}, u32[]{:S(2)}, u32[]{:S(2)}) collective-permute-start(bf16[194048]{0:T(1024)(128)(2,1)S(1)} %get-tuple-element.34), channel_id=1, source_target_pairs={{0,1},{1,2},{2,3},{3,0},{4,5},{5,6},{6,7},{7,4},{8,9},{9,10},{10,1... | collective-permute-start | bytes 1164296 | tf_op jit(solution)/shard_map/ppermute | solution.py:115
  23.4 55.6 %collective-permute-start.4 = (bf16[128,3072]{1,0:T(8,128)(2,1)}, bf16[128,3072]{1,0:T(8,128)(2,1)}, u32[]{:S(2)}, u32[]{:S(2)}) collective-permute-start(bf16[128,3072]{1,0:T(8,128)(2,1)} %bitcast.3), channel_id=1, source_target_pairs={{0,4},{4,0},{8,12},{12,8},{1,5},{5,1},{9,13},{13,9},{2,6},{6,2},{1... | collective-permute-start | bytes 2359304 | tf_op jit(solution)/shard_map/ppermute | solution.py:185
  54.7 18.2 %collective-permute-start.20 = (bf16[128,3072]{1,0:T(8,128)(2,1)}, bf16[128,3072]{1,0:T(8,128)(2,1)}, u32[]{:S(2)}, u32[]{:S(2)}) collective-permute-start(bf16[128,3072]{1,0:T(8,128)(2,1)} %bitcast.34), channel_id=1, source_target_pairs={{0,8},{4,12},{8,0},{12,4},{1,9},{5,13},{9,1},{13,5},{2,10},{6,14},... | collective-permute-start | bytes 2359304 | tf_op jit(solution)/shard_map/ppermute | solution.py:183
  57.6 21.4 %collective-permute-start.5 = (bf16[1,128,3072]{2,1,0:T(8,128)(2,1)}, bf16[1,128,3072]{2,1,0:T(8,128)(2,1)}, u32[]{:S(2)}, u32[]{:S(2)}) collective-permute-start(bf16[1,128,3072]{2,1,0:T(8,128)(2,1)} %bitcast.4), channel_id=1, source_target_pairs={{0,4},{4,0},{8,12},{12,8},{1,5},{5,1},{9,13},{13,9},{2,6},{6,2},{1... | collective-permute-start | bytes 2359304 | tf_op jit(solution)/shard_map/ppermute | solution.py:187
  58.5 25.0 %collective-permute-start.21 = (bf16[128,3072]{1,0:T(8,128)(2,1)}, bf16[128,3072]{1,0:T(8,128)(2,1)}, u32[]{:S(2)}, u32[]{:S(2)}) collective-permute-start(bf16[128,3072]{1,0:T(8,128)(2,1)} %bitcast.34), channel_id=1, source_target_pairs={{0,4},{4,0},{8,12},{12,8},{1,5},{5,1},{9,13},{13,9},{2,6},{6,2},{1... | collective-permute-start | bytes 2359304 | tf_op jit(solution)/shard_map/ppermute | solution.py:185
  72.9 10.7 %collective-permute-start.22 = (bf16[1,128,3072]{2,1,0:T(8,128)(2,1)}, bf16[1,128,3072]{2,1,0:T(8,128)(2,1)}, u32[]{:S(2)}, u32[]{:S(2)}) collective-permute-start(bf16[1,128,3072]{2,1,0:T(8,128)(2,1)} %bitcast.35), channel_id=1, source_target_pairs={{0,4},{4,0},{8,12},{12,8},{1,5},{5,1},{9,13},{13,9},{2,6},{6,2},{1... | collective-permute-start | bytes 2359304 | tf_op jit(solution)/shard_map/ppermute | solution.py:187
  76.8 31.9 %collective-permute-start.23 = (bf16[512,364]{1,0:T(8,128)(2,1)}, bf16[512,364]{1,0:T(8,128)(2,1)}, u32[]{:S(2)}, u32[]{:S(2)}) collective-permute-start(bf16[512,364]{1,0:T(8,128)(2,1)} %bitcast_select_fusion), channel_id=1, source_target_pairs={{0,16},{16,0},{1,17},{17,1},{2,18},{18,2},{3,19},{19,3},{4,20},{20... | collective-permute-start | bytes 1118216 | tf_op jit(solution)/shard_map/ppermute | solution.py:17
  85.6 2.5 copy-start.7
  91.6 15.6 %copy-start.2 = (bf16[4,128,3072]{2,1,0:T(8,128)(2,1)}, bf16[4,128,3072]{2,1,0:T(8,128)(2,1)S(1)}, u32[]{:S(2)}) copy-start(bf16[4,128,3072]{2,1,0:T(8,128)(2,1)S(1)} %get-tuple-element.38) | copy-start | bytes 9437188
  100.7 13.9 %collective-permute-start.8 = (bf16[512,384]{1,0:T(8,128)(2,1)S(1)}, bf16[512,384]{1,0:T(8,128)(2,1)S(1)}, u32[]{:S(2)}, u32[]{:S(2)}) collective-permute-start(bf16[512,384]{1,0:T(8,128)(2,1)S(1)} %get-tuple-element.19), channel_id=1, source_target_pairs={{0,1},{1,2},{2,3},{3,0},{4,5},{5,6},{6,7},{7,4},{8,9},{9,10},{10,1... | collective-permute-start | bytes 1179656 | tf_op jit(solution)/shard_map/ppermute | solution.py:115
  102.3 28.5 %collective-permute-start.7 = (bf16[512,384]{1,0:T(8,128)(2,1)S(1)}, bf16[512,384]{1,0:T(8,128)(2,1)S(1)}, u32[]{:S(2)}, u32[]{:S(2)}) collective-permute-start(bf16[512,384]{1,0:T(8,128)(2,1)S(1)} %get-tuple-element.20), channel_id=1, source_target_pairs={{0,2},{1,3},{2,0},{3,1},{4,6},{5,7},{6,4},{7,5},{8,10},{9,11},{10,... | collective-permute-start | bytes 1179656 | tf_op jit(solution)/shard_map/ppermute | solution.py:115
  104.4 26.4 %collective-permute-start.6 = (bf16[512,384]{1,0:T(8,128)(2,1)S(1)}, bf16[512,384]{1,0:T(8,128)(2,1)S(1)}, u32[]{:S(2)}, u32[]{:S(2)}) collective-permute-start(bf16[512,384]{1,0:T(8,128)(2,1)S(1)} %get-tuple-element.18), channel_id=1, source_target_pairs={{0,3},{1,0},{2,1},{3,2},{4,7},{5,4},{6,5},{7,6},{8,11},{9,8},{10,9... | collective-permute-start | bytes 1179656 | tf_op jit(solution)/shard_map/ppermute | solution.py:115
  132.8 3.1 %copy-start = (bf16[3,512,512]{1,2,0:T(8,128)(2,1)S(1)}, bf16[3,512,512]{1,2,0:T(8,128)(2,1)}, u32[]{:S(2)}) copy-start(bf16[3,512,512]{1,2,0:T(8,128)(2,1)} %exponential_convert_fusion) | copy-start | bytes 4718596
  132.8 3.1 %copy-start.6 = (bf16[512,3,128]{0,2,1:T(8,128)(2,1)S(1)}, bf16[512,3,128]{0,2,1:T(8,128)(2,1)}, u32[]{:S(2)}) copy-start(bf16[512,3,128]{0,2,1:T(8,128)(2,1)} %squeeze.30) | copy-start | bytes 1179652
  137.1 37.5 %collective-permute-start.11 = (bf16[512,384]{0,1:T(8,128)(2,1)}, bf16[512,384]{0,1:T(8,128)(2,1)}, u32[]{:S(2)}, u32[]{:S(2)}) collective-permute-start(bf16[512,384]{0,1:T(8,128)(2,1)} %bitcast.14), channel_id=1, source_target_pairs={{0,3},{1,0},{2,1},{3,2},{4,7},{5,4},{6,5},{7,6},{8,11},{9,8},{10,9... | collective-permute-start | bytes 1179656 | tf_op jit(solution)/shard_map/ppermute | solution.py:115
  148.1 34.0 %collective-permute-start.10 = (bf16[512,384]{0,1:T(8,128)(2,1)}, bf16[512,384]{0,1:T(8,128)(2,1)}, u32[]{:S(2)}, u32[]{:S(2)}) collective-permute-start(bf16[512,384]{0,1:T(8,128)(2,1)} %bitcast.14), channel_id=1, source_target_pairs={{0,2},{1,3},{2,0},{3,1},{4,6},{5,7},{6,4},{7,5},{8,10},{9,11},{10,... | collective-permute-start | bytes 1179656 | tf_op jit(solution)/shard_map/ppermute | solution.py:115
  148.1 34.0 %collective-permute-start.9 = (bf16[512,384]{0,1:T(8,128)(2,1)}, bf16[512,384]{0,1:T(8,128)(2,1)}, u32[]{:S(2)}, u32[]{:S(2)}) collective-permute-start(bf16[512,384]{0,1:T(8,128)(2,1)} %bitcast.14), channel_id=1, source_target_pairs={{0,1},{1,2},{2,3},{3,0},{4,5},{5,6},{6,7},{7,4},{8,9},{9,10},{10,1... | collective-permute-start | bytes 1179656 | tf_op jit(solution)/shard_map/ppermute | solution.py:115
  148.7 94.3 %collective-permute-start.15 = (bf16[512,384]{0,1:T(8,128)(2,1)}, bf16[512,384]{0,1:T(8,128)(2,1)}, u32[]{:S(2)}, u32[]{:S(2)}) collective-permute-start(bf16[512,384]{0,1:T(8,128)(2,1)} %bitcast.14), channel_id=1, source_target_pairs={{0,16},{16,0},{1,17},{17,1},{2,18},{18,2},{3,19},{19,3},{4,20},{20... | collective-permute-start | bytes 1179656 | tf_op jit(solution)/shard_map/ppermute | solution.py:17
  154.7 3.4 %copy-start.5 = (bf16[512,3,128]{0,2,1:T(8,128)(2,1)S(1)}, bf16[512,3,128]{0,2,1:T(8,128)(2,1)}, u32[]{:S(2)}) copy-start(bf16[512,3,128]{0,2,1:T(8,128)(2,1)} %squeeze.28) | copy-start | bytes 1179652
  156.9 1.2 copy-start.1
  158.1 6.1 %copy-start.4 = (bf16[512,3,128]{0,2,1:T(8,128)(2,1)S(1)}, bf16[512,3,128]{0,2,1:T(8,128)(2,1)}, u32[]{:S(2)}) copy-start(bf16[512,3,128]{0,2,1:T(8,128)(2,1)} %squeeze.27) | copy-start | bytes 1179652
  188.2 7.5 %copy-start.3 = (bf16[4,128,3072]{2,1,0:T(8,128)(2,1)S(1)}, bf16[4,128,3072]{2,1,0:T(8,128)(2,1)}, u32[]{:S(2)}) copy-start(bf16[4,128,3072]{2,1,0:T(8,128)(2,1)} %copy-done.2) | copy-start | bytes 9437188
  191.5 16.3 %collective-permute-start.14 = (bf16[3,128,384]{2,1,0:T(8,128)(2,1)S(1)}, bf16[3,128,384]{2,1,0:T(8,128)(2,1)S(1)}, u32[]{:S(2)}, u32[]{:S(2)}) collective-permute-start(bf16[3,128,384]{2,1,0:T(8,128)(2,1)S(1)} %get-tuple-element.25), channel_id=1, source_target_pairs={{0,3},{1,0},{2,1},{3,2},{4,7},{5,4},{6,5},{7,6},{8,11},{9,8},{10,9... | collective-permute-start | bytes 884744 | tf_op jit(solution)/shard_map/ppermute | solution.py:115
  191.5 27.3 %collective-permute-start.13 = (bf16[3,128,384]{2,1,0:T(8,128)(2,1)S(1)}, bf16[3,128,384]{2,1,0:T(8,128)(2,1)S(1)}, u32[]{:S(2)}, u32[]{:S(2)}) collective-permute-start(bf16[3,128,384]{2,1,0:T(8,128)(2,1)S(1)} %get-tuple-element.26), channel_id=1, source_target_pairs={{0,2},{1,3},{2,0},{3,1},{4,6},{5,7},{6,4},{7,5},{8,10},{9,11},{10,... | collective-permute-start | bytes 884744 | tf_op jit(solution)/shard_map/ppermute | solution.py:115
  193.7 26.7 %collective-permute-start.12 = (bf16[3,128,384]{2,1,0:T(8,128)(2,1)S(1)}, bf16[3,128,384]{2,1,0:T(8,128)(2,1)S(1)}, u32[]{:S(2)}, u32[]{:S(2)}) collective-permute-start(bf16[3,128,384]{2,1,0:T(8,128)(2,1)S(1)} %get-tuple-element.24), channel_id=1, source_target_pairs={{0,1},{1,2},{2,3},{3,0},{4,5},{5,6},{6,7},{7,4},{8,9},{9,10},{10,1... | collective-permute-start | bytes 884744 | tf_op jit(solution)/shard_map/ppermute | solution.py:115
  206.2 36.7 %collective-permute-start.18 = (bf16[512,384]{0,1:T(8,128)(2,1)}, bf16[512,384]{0,1:T(8,128)(2,1)S(1)}, u32[]{:S(2)}, u32[]{:S(2)}) collective-permute-start(bf16[512,384]{0,1:T(8,128)(2,1)} %collective-permute-done.11), channel_id=1, source_target_pairs={{0,16},{16,0},{1,17},{17,1},{2,18},{18,2},{3,19},{19,3},{4,20},{20... | collective-permute-start | bytes 1179656 | tf_op jit(solution)/shard_map/ppermute | solution.py:17
  207.8 35.2 %collective-permute-start.17 = (bf16[512,384]{0,1:T(8,128)(2,1)}, bf16[512,384]{0,1:T(8,128)(2,1)}, u32[]{:S(2)}, u32[]{:S(2)}) collective-permute-start(bf16[512,384]{0,1:T(8,128)(2,1)} %collective-permute-done.10), channel_id=1, source_target_pairs={{0,16},{16,0},{1,17},{17,1},{2,18},{18,2},{3,19},{19,3},{4,20},{20... | collective-permute-start | bytes 1179656 | tf_op jit(solution)/shard_map/ppermute | solution.py:17
  218.8 24.2 %collective-permute-start.16 = (bf16[512,384]{0,1:T(8,128)(2,1)}, bf16[512,384]{0,1:T(8,128)(2,1)}, u32[]{:S(2)}, u32[]{:S(2)}) collective-permute-start(bf16[512,384]{0,1:T(8,128)(2,1)} %collective-permute-done.9), channel_id=1, source_target_pairs={{0,16},{16,0},{1,17},{17,1},{2,18},{18,2},{3,19},{19,3},{4,20},{20... | collective-permute-start | bytes 1179656 | tf_op jit(solution)/shard_map/ppermute | solution.py:17

commit v5 on v4

--- a/solution.py
+++ b/solution.py
@@ -203,9 +203,9 @@
     width = width_all // n
     heads = width // DH
     patch_here = patches[0]
-    dense_grad = gather_rows_relayed(output_grad[0], "row")
+    dense_grad = gather_rows(output_grad[0], "row")
     grad_other = swap_dp(output_grad)
-    other_grad = gather_rows_relayed(grad_other[0], "row")
+    other_grad = gather_rows(grad_other[0], "row")
     qkv = jnp.stack([queries[0], attn_keys[0], attn_values[0]], 0)
     part = lambda g: lax.dynamic_slice_in_dim(qkv, g * width, width, 2)
     shapes = [(3, tokens, width), patch_here.shape]
@@ -256,24 +256,36 @@
         other_patch, other_grad
     )
     out_flat = attn_out.reshape(rows, width)
-    own_pair = (out_flat, swap_dp(out_flat))
+    cols = dense_grad.shape[1]
+
+    def weight_rows(own, other):
+        return lax.dot_general(
+            own, dense_grad, (((0,), (0,)), ((), ())), preferred_element_type=jnp.float32
+        ) + lax.dot_general(
+            other, other_grad, (((0,), (0,)), ((), ())), preferred_element_type=jnp.float32
+        )
+
+    out_weight_grad = jnp.zeros((width_all, cols), jnp.float32)
+    out_weight_grad = lax.dynamic_update_slice_in_dim(
+        out_weight_grad, weight_rows(out_flat, swap_dp(out_flat)), me * width, 0
+    )
     attn_grad, sent_out = lax.optimization_barrier((attn_grad, out_flat))
-    out_pieces = [own_pair] + [
-        (got, swap_dp(got)) for got in (shifted(sent_out, "col", s) for s in range(1, n))
-    ]
-    out_own = natural([p[0] for p in out_pieces], "col")
-    out_other = natural([p[1] for p in out_pieces], "col")
-    out_weight_grad = (
-        lax.dot_general(out_own, dense_grad, (((1,), (0,)), ((), ())), preferred_element_type=jnp.float32)
-        + lax.dot_general(out_other, other_grad, (((1,), (0,)), ((), ())), preferred_element_type=jnp.float32)
-    ).reshape(width_all, -1)
+    arrived = []
+    for s in range(1, n):
+        got = shifted(sent_out, "col", s)
+        arrived.append(got)
+        out_weight_grad = lax.dynamic_update_slice_in_dim(
+            out_weight_grad, weight_rows(got, swap_dp(got)), ((me - s) % n) * width, 0
+        )
     grads = jnp.stack([g.reshape(n, tokens, width) for g in (query_grad, key_grad, value_grad)], 1)
-    grads, out_own = lax.optimization_barrier((grads, out_own))
-    back = [grads[me]] + [
-        shifted(grads[(me + s) % n].astype(jnp.bfloat16), "col", s).astype(jnp.float32)
-        for s in range(1, n)
-    ]
-    back = jnp.transpose(natural(back, "col"), (1, 2, 0, 3)).reshape(3, 1, tokens, width_all)
+    grads, arrived = lax.optimization_barrier((grads, arrived))
+    pick = lambda k: lax.dynamic_index_in_dim(grads, k, 0, keepdims=False)
+    back = jnp.zeros((3, tokens, width_all), jnp.float32)
+    back = lax.dynamic_update_slice_in_dim(back, pick(me), me * width, 2)
+    for s in range(1, n):
+        got = shifted(pick((me + s) % n).astype(jnp.bfloat16), "col", s).astype(jnp.float32)
+        back = lax.dynamic_update_slice_in_dim(back, got, ((me - s) % n) * width, 2)
+    back = back.reshape(3, 1, tokens, width_all)
     return (back[0], back[1], back[2], out_weight_grad, embed_weight_grad)
 
 

time: 264 us -> 239 us (0.905)
  local copies, waits for them, and re-layouts: 66.3 us -> 49.1 us
  other arithmetic: 27.8 us -> 17.8 us
  waiting for transfers between devices: 78.7 us -> 74.4 us
  starting transfers between devices: 38.3 us -> 42.3 us
    ppermute x6 -> x0, waiting for transfers between devices: 13.8 us -> none  [the longest x2 13.8 us: gather_rows_relayed(): lax.ppermute(x, axis, [(j, (j + 2 * s) % n) for j in range(n)])]
    ppermute x12 -> x18, waiting for transfers between devices: 64.9 us -> 74.4 us  [shifted(): return lax.ppermute(x, axis, [(j, (j + step) % n) for j in range(n)])]
    broadcast_in_dim x0 -> x1, local copies, waits for them, and re-layouts: none -> 9.24 us  [body_heads(): out_weight_grad = jnp.zeros((width_all, cols), jnp.float32)]
    ppermute x12 -> x18, starting transfers between devices: 27 us -> 35.5 us  [shifted(): return lax.ppermute(x, axis, [(j, (j + step) % n) for j in range(n)])]
    slice x4 -> x0, local copies, waits for them, and re-layouts: 8.37 us -> none  [body_heads(): return (back[0], back[1], back[2], out_weight_grad, embed_weight_grad)]
    unnamed x22 -> x17, local copies, waits for them, and re-layouts: 11.1 us -> 3.76 us
    gather x5 -> x4, local copies, waits for them, and re-layouts: 11.9 us -> 6.26 us  [natural(): return jnp.take(jnp.stack(pieces, 0), order, axis=0)]
    gather x2 -> x0, local copies, waits for them, and re-layouts: 5.07 us -> none  [gather_rows_relayed(): stacked = jnp.take(pieces, order, axis=0)]
  transfers between devices with their start and end apart: 24 -> 24, of which waited for: 7 -> 7; matrix products, arithmetic and copies ran while one was open for 45% -> 44% of each run, Pallas kernels for 0% -> 0%
where the time goes in v5:
time: 239 us; the launch traced here: 238 us
  waiting for transfers between devices  74.4 us (31%)
  matrix products  52.9 us (22%)
  local copies, waits for them, and re-layouts  49.1 us (21%)
  starting transfers between devices  42.3 us (18%)
  other arithmetic  17.8 us (7%)
    ppermute x18, waiting for transfers between devices, shifted(): return lax.ppermute(x, axis, [(j, (j + step) % n) for j in range(n)])  74.4 us
    ppermute x18, starting transfers between devices, shifted(): return lax.ppermute(x, axis, [(j, (j + step) % n) for j in range(n)])  35.5 us
    dot_general x4, matrix products, weight_rows(): lax.dot_general(other, other_grad, (((0,), (0,)), ((), ())), preferred_el...  17 us
    another operation x6, local copies, waits for them, and re-layouts, body_heads(): jnp.stack([g.reshape(n, tokens, width) for g in (query_grad, key_grad, va...  13.7 us
    dot_general x4, matrix products, weight_rows(): lax.dot_general(own, dense_grad, (((0,), (0,)), ((), ())), preferred_elem...  10.7 us
    broadcast_in_dim x1, local copies, waits for them, and re-layouts, body_heads(): out_weight_grad = jnp.zeros((width_all, cols), jnp.float32)  9.24 us
    dot_general x1, matrix products, body_heads(): lax.dot_general(dense_grad, out_weight, (((1,), (1,)), ((), ())), preferr...  8.79 us
    ppermute x6, starting transfers between devices, swap_dp(): return lax.ppermute(x, 'dp', [(0, 1), (1, 0)])  6.78 us
  transfers between devices with their start and end apart: 24, of which 7 were waited for; matrix products, arithmetic and copies ran while one was open for 44% of the time, Pallas kernels for 0%

profile of v5, /device:TPU:0, one launch (start us, length us, event | category | flops | bytes accessed | tf_op | source)
XLA Modules:
  0.0 237.6 jit_solution(14512275212802448632)
XLA Ops:
  0.6 3.0 %collective-permute-start.16 = (bf16[1,128,3072]{2,1,0:T(8,128)(2,1)}, bf16[1,128,3072]{2,1,0:T(8,128)(2,1)}, u32[]{:S(2)}, u32[]{:S(2)}) collective-permute-start(bf16[1,128,3072]{2,1,0:T(8,128)(2,1)} %param.13), channel_id=1, source_target_pairs={{0,16},{16,0},{1,17},{17,1},{2,18},{18,2},{3,19},{19,3},{4,20},{20... | collective-permute-start | bytes 2359304 | tf_op jit(solution)/shard_map/ppermute | solution.py:17
  9.4 3.7 %collective-permute-start.2 = (bf16[194048]{0:T(1024)(128)(2,1)S(1)}, bf16[194048]{0:T(1024)(128)(2,1)S(1)}, u32[]{:S(2)}, u32[]{:S(2)}) collective-permute-start(bf16[194048]{0:T(1024)(128)(2,1)S(1)} %get-tuple-element.28), channel_id=1, source_target_pairs={{0,3},{1,0},{2,1},{3,2},{4,7},{5,4},{6,5},{7,6},{8,11},{9,8},{10,9... | collective-permute-start | bytes 1164296 | tf_op jit(solution)/shard_map/ppermute | solution.py:115
  14.8 7.7 %collective-permute-done.2 = bf16[194048]{0:T(1024)(128)(2,1)S(1)} collective-permute-done((bf16[194048]{0:T(1024)(128)(2,1)S(1)}, bf16[194048]{0:T(1024)(128)(2,1)S(1)}, u32[]{:S(2)}, u32[]{:S(2)}) %collective-permute-start.2) | collective-permute-done | bytes 388128 | tf_op jit(solution)/shard_map/ppermute | solution.py:115
  23.5 22.8 %collective-permute-done.1 = bf16[194048]{0:T(1024)(128)(2,1)S(1)} collective-permute-done((bf16[194048]{0:T(1024)(128)(2,1)S(1)}, bf16[194048]{0:T(1024)(128)(2,1)S(1)}, u32[]{:S(2)}, u32[]{:S(2)}) %collective-permute-start.1) | collective-permute-done | bytes 388128 | tf_op jit(solution)/shard_map/ppermute | solution.py:115
  54.4 1.7 multiply_reduce_fusion
  57.6 1.7 collective-permute-start.19
  59.3 1.5 collective-permute-start.18
  60.9 2.0 copy.51
  62.8 1.9 squeeze.32
  64.7 1.7 exponential_convert_fusion
  66.9 2.0 pad_maximum_fusion
  69.0 2.4 %gather_fusion.2 = bf16[4,128,3072]{2,1,0:T(8,128)(2,1)} fusion(bf16[4,128,3072]{2,1,0:T(8,128)(2,1)S(1)} %pad_maximum_fusion, s32[1024]{0:T(1024)S(1)} %pad_clamp_fusion), kind=kCustom, calls=%fused_computation.clone | custom fusion | bytes 6291472 | tf_op jit(solution)/shard_map/jit(_take)/gather | solution.py:121
  71.4 6.1 %collective-permute-done.19 = bf16[128,3072]{1,0:T(8,128)(2,1)} collective-permute-done((bf16[128,3072]{1,0:T(8,128)(2,1)}, bf16[128,3072]{1,0:T(8,128)(2,1)}, u32[]{:S(2)}, u32[]{:S(2)}) %collective-permute-start.19) | collective-permute-done | bytes 786464 | tf_op jit(solution)/shard_map/ppermute | solution.py:115
  77.5 18.3 %collective-permute-done.18 = bf16[128,3072]{1,0:T(8,128)(2,1)} collective-permute-done((bf16[128,3072]{1,0:T(8,128)(2,1)}, bf16[128,3072]{1,0:T(8,128)(2,1)}, u32[]{:S(2)}, u32[]{:S(2)}) %collective-permute-start.18) | collective-permute-done | bytes 786464 | tf_op jit(solution)/shard_map/ppermute | solution.py:115
  95.9 2.0 pad_maximum_fusion.1
  97.9 2.4 %gather_fusion.3 = bf16[4,128,3072]{2,1,0:T(8,128)(2,1)} fusion(bf16[4,128,3072]{2,1,0:T(8,128)(2,1)S(1)} %pad_maximum_fusion.1, s32[1024]{0:T(1024)S(1)} %pad_clamp_fusion), kind=kCustom, calls=%fused_computation.1.clone | custom fusion | bytes 6291472 | tf_op jit(solution)/shard_map/jit(_take)/gather | solution.py:121
  100.3 3.5 %broadcast_select_fusion = (bf16[4,128,3072]{2,1,0:T(8,128)(2,1)S(1)}, bf16[4,128,3072]{2,1,0:T(8,128)(2,1)S(1)}) fusion(bf16[4,128,3072]{2,1,0:T(8,128)(2,1)} %gather_fusion.3, pred[4]{0:T(512)(128)(4,1)S(1)} %copy-done.6, bf16[4,128,3072]{2,1,0:T(8,128)(2,1)} %gather_fusion.2), kind=kLoop, calls=%fused_computation.14 | loop fusion | flops 3145728 | bytes 12582916 | tf_op jit(solution)/shard_map/jit(_take)/select_n | solution.py:121
  103.8 8.8 %fusion.15 = f32[512,1536]{1,0:T(8,128)S(1)} fusion(bf16[512,3072]{1,0:T(8,128)(2,1)S(1)} %bitcast.113, bf16[1536,3072]{1,0:T(8,128)(2,1)} %param.12), kind=kOutput, calls=%fused_computation.84 | convolution fusion | flops 4831838208 | bytes 15728640 | tf_op jit(solution)/shard_map/dot_general | solution.py:231
  112.9 1.6 collective-permute-start.7
  114.5 2.8 %collective-permute-start.6 = (bf16[512,384]{1,0:T(8,128)(2,1)S(1)}, bf16[512,384]{1,0:T(8,128)(2,1)S(1)}, u32[]{:S(2)}, u32[]{:S(2)}) collective-permute-start(bf16[512,384]{1,0:T(8,128)(2,1)S(1)} %get-tuple-element.10), channel_id=1, source_target_pairs={{0,3},{1,0},{2,1},{3,2},{4,7},{5,4},{6,5},{7,6},{8,11},{9,8},{10,9... | collective-permute-start | bytes 1179656 | tf_op jit(solution)/shard_map/ppermute | solution.py:115
  118.8 4.6 %bitcast_add_fusion = f32[364,3072]{1,0:T(8,128)} fusion(f32[364,3072,1]{1,0,2:T(8,128)S(1)} %fusion.2, bf16[512,364]{1,0:T(8,128)(2,1)} %collective-permute-done.23, bf16[512,3072]{1,0:T(8,128)(2,1)S(1)} %bitcast.108), kind=kOutput, calls=%fused_computation.8 | convolution fusion | flops 1146163200 | bytes 12464128 | tf_op jit(solution)/shard_map/dot_general | solution.py:11
  123.4 3.4 %collective-permute-done.8 = bf16[512,384]{1,0:T(8,128)(2,1)S(1)} collective-permute-done((bf16[512,384]{1,0:T(8,128)(2,1)S(1)}, bf16[512,384]{1,0:T(8,128)(2,1)S(1)}, u32[]{:S(2)}, u32[]{:S(2)}) %collective-permute-start.8) | collective-permute-done | bytes 393248 | tf_op jit(solution)/shard_map/ppermute | solution.py:115
  126.8 13.7 %collective-permute-done.7 = bf16[512,384]{1,0:T(8,128)(2,1)S(1)} collective-permute-done((bf16[512,384]{1,0:T(8,128)(2,1)S(1)}, bf16[512,384]{1,0:T(8,128)(2,1)S(1)}, u32[]{:S(2)}, u32[]{:S(2)}) %collective-permute-start.7) | collective-permute-done | bytes 393248 | tf_op jit(solution)/shard_map/ppermute | solution.py:115
  142.6 3.1 %convolution_bitcast_fusion = f32[512,3,128]{0,2,1:T(8,128)} fusion(bf16[512,3,128]{0,2,1:T(8,128)(2,1)S(1)} %bitcast.118, bf16[3,512,512]{1,2,0:T(8,128)(2,1)} %exponential_convert_fusion), kind=kOutput, calls=%fused_computation.22 | convolution fusion | flops 201326592 | bytes 2752512 | tf_op jit(solution)/shard_map/hqk,qhd->khd/dot_general | solution.py:251
  145.6 2.2 multiply_reduce_fusion.1
  148.5 1.5 fusion
  151.3 8.2 %collective-permute-start.9 = (bf16[512,384]{0,1:T(8,128)(2,1)}, bf16[512,384]{0,1:T(8,128)(2,1)}, u32[]{:S(2)}, u32[]{:S(2)}) collective-permute-start(bf16[512,384]{0,1:T(8,128)(2,1)} %bitcast.14), channel_id=1, source_target_pairs={{0,1},{1,2},{2,3},{3,0},{4,5},{5,6},{6,7},{7,4},{8,9},{9,10},{10,1... | collective-permute-start | bytes 1179656 | tf_op jit(solution)/shard_map/ppermute | solution.py:115
  159.4 2.3 collective-permute-start.10
  162.3 2.3 stack_reshape.32
  164.6 2.3 copy.61
  166.8 2.3 stack_reshape.31
  169.1 2.3 copy.60
  171.4 2.3 stack_reshape.30
  173.6 2.3 copy.59
  175.9 1.9 pad_maximum_fusion.2
  178.5 4.5 %fusion.16 = f32[384,3072]{1,0:T(8,128)} fusion(bf16[512,384]{0,1:T(8,128)(2,1)} %bitcast.14, bf16[512,3072]{1,0:T(8,128)(2,1)S(1)} %bitcast.114), kind=kOutput, calls=%fused_computation.85 | convolution fusion | flops 1207959552 | bytes 8257536 | tf_op jit(solution)/shard_map/dot_general | solution.py:262
  183.1 2.4 %collective-permute-done.10 = bf16[512,384]{0,1:T(8,128)(2,1)} collective-permute-done((bf16[512,384]{0,1:T(8,128)(2,1)}, bf16[512,384]{0,1:T(8,128)(2,1)}, u32[]{:S(2)}, u32[]{:S(2)}) %collective-permute-start.10) | collective-permute-done | bytes 393248 | tf_op jit(solution)/shard_map/ppermute | solution.py:115
  186.4 8.8 %collective-permute-start.12 = (bf16[3,128,384]{2,1,0:T(8,128)(2,1)}, bf16[3,128,384]{2,1,0:T(8,128)(2,1)}, u32[]{:S(2)}, u32[]{:S(2)}) collective-permute-start(bf16[3,128,384]{2,1,0:T(8,128)(2,1)} %get-tuple-element.18), channel_id=1, source_target_pairs={{0,1},{1,2},{2,3},{3,0},{4,5},{5,6},{6,7},{7,4},{8,9},{9,10},{10,1... | collective-permute-start | bytes 884744 | tf_op jit(solution)/shard_map/ppermute | solution.py:115
  195.2 2.2 collective-permute-start.13
  197.9 2.4 %fusion.17 = f32[384,3072]{1,0:T(8,128)S(1)} fusion(bf16[512,384]{0,1:T(8,128)(2,1)} %collective-permute-done.9, bf16[512,3072]{1,0:T(8,128)(2,1)S(1)} %bitcast.115), kind=kOutput, calls=%fused_computation.86 | convolution fusion | flops 1207959552 | bytes 8257536 | tf_op jit(solution)/shard_map/dot_general | solution.py:262
  200.9 2.4 %fusion.18 = f32[384,3072]{1,0:T(8,128)S(1)} fusion(bf16[512,384]{0,1:T(8,128)(2,1)} %collective-permute-done.10, bf16[512,3072]{1,0:T(8,128)(2,1)S(1)} %bitcast.116), kind=kOutput, calls=%fused_computation.87 | convolution fusion | flops 1207959552 | bytes 8257536 | tf_op jit(solution)/shard_map/dot_general | solution.py:262
  203.3 1.6 collective-permute-start.21
  204.9 9.2 %broadcast_in_dim.46 = f32[1536,3072]{1,0:T(8,128)} broadcast(f32[]{:T(128)} %constant.137.clone.1), dimensions={} | broadcast | bytes 18874372 | tf_op jit(solution)/shard_map/broadcast_in_dim | solution.py:268
  214.1 6.0 %add_dynamic-update-slice_fusion.3 = f32[1536,3072]{1,0:T(8,128)} fusion(f32[1536,3072]{1,0:T(8,128)} %broadcast_in_dim.46, s32[]{:T(128)S(6)} %select_n.154, f32[384,3072]{1,0:T(8,128)} %fusion.16, bf16[512,384]{0,1:T(8,128)(2,1)} %collective-permute-done.15, bf16[512,3072]{1,0:T(8,128)(2,1)S(1)} %bitcast.109), kind=kOutput, calls=%fused_computation.7 | convolution fusion | flops 1209139200 | bytes 12976132 | tf_op jit(solution)/shard_map/dot_general | solution.py:264
  225.3 1.5 slice_bitcast_fusion
  226.7 3.6 %add_dynamic-update-slice_fusion.2 = f32[1536,3072]{1,0:T(8,128)} fusion(f32[1536,3072]{1,0:T(8,128)} %add_dynamic-update-slice_fusion.3, s32[]{:T(128)S(6)} %select_n.167, f32[384,3072]{1,0:T(8,128)S(1)} %fusion.17, bf16[512,384]{0,1:T(8,128)(2,1)S(1)} %collective-permute-done.20, bf16[512,3072]{1,0:T(8,128)(2,1)S(1)} %bitcast.110), kind=kOutput, calls=%fused_computation.6 | convolution fusion | flops 1209139200 | bytes 12976132 | tf_op jit(solution)/shard_map/dot_general | solution.py:264
  230.3 3.6 %add_dynamic-update-slice_fusion.1 = f32[1536,3072]{1,0:T(8,128)} fusion(f32[1536,3072]{1,0:T(8,128)} %add_dynamic-update-slice_fusion.2, s32[]{:T(128)S(6)} %select_n.169, f32[384,3072]{1,0:T(8,128)S(1)} %fusion.18, bf16[512,384]{0,1:T(8,128)(2,1)S(1)} %collective-permute-done.21, bf16[512,3072]{1,0:T(8,128)(2,1)S(1)} %bitcast.111), kind=kOutput, calls=%fused_computation.5 | convolution fusion | flops 1209139200 | bytes 12976132 | tf_op jit(solution)/shard_map/dot_general | solution.py:264
  234.0 3.7 %add_dynamic-update-slice_fusion = f32[1536,3072]{1,0:T(8,128)} fusion(f32[1536,3072]{1,0:T(8,128)} %add_dynamic-update-slice_fusion.1, s32[]{:T(128)S(6)} %select_n.171, f32[384,3072]{1,0:T(8,128)S(1)} %fusion.19, bf16[512,384]{0,1:T(8,128)(2,1)S(1)} %collective-permute-done.22, bf16[512,3072]{1,0:T(8,128)(2,1)S(1)} %bitcast.112), kind=kOutput, calls=%fused_computation.4 | convolution fusion | flops 1209139200 | bytes 12976132 | tf_op jit(solution)/shard_map/dot_general | solution.py:264
  (99 shorter events, 32.4 us)
Async XLA Ops:
  0.6 57.0 %collective-permute-start.16 = (bf16[1,128,3072]{2,1,0:T(8,128)(2,1)}, bf16[1,128,3072]{2,1,0:T(8,128)(2,1)}, u32[]{:S(2)}, u32[]{:S(2)}) collective-permute-start(bf16[1,128,3072]{2,1,0:T(8,128)(2,1)} %param.13), channel_id=1, source_target_pairs={{0,16},{16,0},{1,17},{17,1},{2,18},{18,2},{3,19},{19,3},{4,20},{20... | collective-permute-start | bytes 2359304 | tf_op jit(solution)/shard_map/ppermute | solution.py:17
  3.7 57.2 %collective-permute-start.5 = (bf16[128,3072]{1,0:T(8,128)(2,1)}, bf16[128,3072]{1,0:T(8,128)(2,1)}, u32[]{:S(2)}, u32[]{:S(2)}) collective-permute-start(bf16[128,3072]{1,0:T(8,128)(2,1)} %bitcast.3), channel_id=1, source_target_pairs={{0,12},{4,0},{8,4},{12,8},{1,13},{5,1},{9,5},{13,9},{2,14},{6,2},{... | collective-permute-start | bytes 2359304 | tf_op jit(solution)/shard_map/ppermute | solution.py:115
  9.4 13.1 %collective-permute-start.2 = (bf16[194048]{0:T(1024)(128)(2,1)S(1)}, bf16[194048]{0:T(1024)(128)(2,1)S(1)}, u32[]{:S(2)}, u32[]{:S(2)}) collective-permute-start(bf16[194048]{0:T(1024)(128)(2,1)S(1)} %get-tuple-element.28), channel_id=1, source_target_pairs={{0,3},{1,0},{2,1},{3,2},{4,7},{5,4},{6,5},{7,6},{8,11},{9,8},{10,9... | collective-permute-start | bytes 1164296 | tf_op jit(solution)/shard_map/ppermute | solution.py:115
  13.0 33.2 %collective-permute-start.1 = (bf16[194048]{0:T(1024)(128)(2,1)S(1)}, bf16[194048]{0:T(1024)(128)(2,1)S(1)}, u32[]{:S(2)}, u32[]{:S(2)}) collective-permute-start(bf16[194048]{0:T(1024)(128)(2,1)S(1)} %get-tuple-element.27), channel_id=1, source_target_pairs={{0,2},{1,3},{2,0},{3,1},{4,6},{5,7},{6,4},{7,5},{8,10},{9,11},{10,... | collective-permute-start | bytes 1164296 | tf_op jit(solution)/shard_map/ppermute | solution.py:115
  13.0 33.4 %collective-permute-start = (bf16[194048]{0:T(1024)(128)(2,1)S(1)}, bf16[194048]{0:T(1024)(128)(2,1)}, u32[]{:S(2)}, u32[]{:S(2)}) collective-permute-start(bf16[194048]{0:T(1024)(128)(2,1)S(1)} %get-tuple-element.26), channel_id=1, source_target_pairs={{0,1},{1,2},{2,3},{3,0},{4,5},{5,6},{6,7},{7,4},{8,9},{9,10},{10,1... | collective-permute-start | bytes 1164296 | tf_op jit(solution)/shard_map/ppermute | solution.py:115
  22.5 43.9 %collective-permute-start.4 = (bf16[128,3072]{1,0:T(8,128)(2,1)}, bf16[128,3072]{1,0:T(8,128)(2,1)}, u32[]{:S(2)}, u32[]{:S(2)}) collective-permute-start(bf16[128,3072]{1,0:T(8,128)(2,1)} %bitcast.3), channel_id=1, source_target_pairs={{0,8},{4,12},{8,0},{12,4},{1,9},{5,13},{9,1},{13,5},{2,10},{6,14},... | collective-permute-start | bytes 2359304 | tf_op jit(solution)/shard_map/ppermute | solution.py:115
  46.2 20.7 %collective-permute-start.3 = (bf16[128,3072]{1,0:T(8,128)(2,1)}, bf16[128,3072]{1,0:T(8,128)(2,1)}, u32[]{:S(2)}, u32[]{:S(2)}) collective-permute-start(bf16[128,3072]{1,0:T(8,128)(2,1)} %bitcast.3), channel_id=1, source_target_pairs={{0,4},{4,8},{8,12},{12,0},{1,5},{5,9},{9,13},{13,1},{2,6},{6,10},{... | collective-permute-start | bytes 2359304 | tf_op jit(solution)/shard_map/ppermute | solution.py:115
  57.6 19.9 %collective-permute-start.19 = (bf16[128,3072]{1,0:T(8,128)(2,1)}, bf16[128,3072]{1,0:T(8,128)(2,1)}, u32[]{:S(2)}, u32[]{:S(2)}) collective-permute-start(bf16[128,3072]{1,0:T(8,128)(2,1)} %bitcast.28), channel_id=1, source_target_pairs={{0,12},{4,0},{8,4},{12,8},{1,13},{5,1},{9,5},{13,9},{2,14},{6,2},{... | collective-permute-start | bytes 2359304 | tf_op jit(solution)/shard_map/ppermute | solution.py:115
  59.3 36.5 %collective-permute-start.18 = (bf16[128,3072]{1,0:T(8,128)(2,1)}, bf16[128,3072]{1,0:T(8,128)(2,1)}, u32[]{:S(2)}, u32[]{:S(2)}) collective-permute-start(bf16[128,3072]{1,0:T(8,128)(2,1)} %bitcast.28), channel_id=1, source_target_pairs={{0,8},{4,12},{8,0},{12,4},{1,9},{5,13},{9,1},{13,5},{2,10},{6,14},... | collective-permute-start | bytes 2359304 | tf_op jit(solution)/shard_map/ppermute | solution.py:115
  60.8 35.0 %collective-permute-start.17 = (bf16[128,3072]{1,0:T(8,128)(2,1)}, bf16[128,3072]{1,0:T(8,128)(2,1)}, u32[]{:S(2)}, u32[]{:S(2)}) collective-permute-start(bf16[128,3072]{1,0:T(8,128)(2,1)} %bitcast.28), channel_id=1, source_target_pairs={{0,4},{4,8},{8,12},{12,0},{1,5},{5,9},{9,13},{13,1},{2,6},{6,10},{... | collective-permute-start | bytes 2359304 | tf_op jit(solution)/shard_map/ppermute | solution.py:115
  66.4 52.4 %collective-permute-start.23 = (bf16[512,364]{1,0:T(8,128)(2,1)}, bf16[512,364]{1,0:T(8,128)(2,1)}, u32[]{:S(2)}, u32[]{:S(2)}) collective-permute-start(bf16[512,364]{1,0:T(8,128)(2,1)} %bitcast_select_fusion), channel_id=1, source_target_pairs={{0,16},{16,0},{1,17},{17,1},{2,18},{18,2},{3,19},{19,3},{4,20},{20... | collective-permute-start | bytes 1118216 | tf_op jit(solution)/shard_map/ppermute | solution.py:17
  97.9 2.4 %copy-start.6 = (pred[4]{0:T(512)(128)(4,1)S(1)}, pred[4]{0:T(512)(128)(4,1)}, u32[]{:S(2)}) copy-start(pred[4]{0:T(512)(128)(4,1)} %compare_and_fusion) | copy-start | bytes 16
  103.8 13.5 %copy-start = (bf16[4,128,3072]{2,1,0:T(8,128)(2,1)}, bf16[4,128,3072]{2,1,0:T(8,128)(2,1)S(1)}, u32[]{:S(2)}) copy-start(bf16[4,128,3072]{2,1,0:T(8,128)(2,1)S(1)} %get-tuple-element.30) | copy-start | bytes 9437188
  112.8 14.0 %collective-permute-start.8 = (bf16[512,384]{1,0:T(8,128)(2,1)S(1)}, bf16[512,384]{1,0:T(8,128)(2,1)S(1)}, u32[]{:S(2)}, u32[]{:S(2)}) collective-permute-start(bf16[512,384]{1,0:T(8,128)(2,1)S(1)} %get-tuple-element.11), channel_id=1, source_target_pairs={{0,1},{1,2},{2,3},{3,0},{4,5},{5,6},{6,7},{7,4},{8,9},{9,10},{10,1... | collective-permute-start | bytes 1179656 | tf_op jit(solution)/shard_map/ppermute | solution.py:115
  112.9 27.6 %collective-permute-start.7 = (bf16[512,384]{1,0:T(8,128)(2,1)S(1)}, bf16[512,384]{1,0:T(8,128)(2,1)S(1)}, u32[]{:S(2)}, u32[]{:S(2)}) collective-permute-start(bf16[512,384]{1,0:T(8,128)(2,1)S(1)} %get-tuple-element.12), channel_id=1, source_target_pairs={{0,2},{1,3},{2,0},{3,1},{4,6},{5,7},{6,4},{7,5},{8,10},{9,11},{10,... | collective-permute-start | bytes 1179656 | tf_op jit(solution)/shard_map/ppermute | solution.py:115
  114.5 26.0 %collective-permute-start.6 = (bf16[512,384]{1,0:T(8,128)(2,1)S(1)}, bf16[512,384]{1,0:T(8,128)(2,1)S(1)}, u32[]{:S(2)}, u32[]{:S(2)}) collective-permute-start(bf16[512,384]{1,0:T(8,128)(2,1)S(1)} %get-tuple-element.10), channel_id=1, source_target_pairs={{0,3},{1,0},{2,1},{3,2},{4,7},{5,4},{6,5},{7,6},{8,11},{9,8},{10,9... | collective-permute-start | bytes 1179656 | tf_op jit(solution)/shard_map/ppermute | solution.py:115
  142.5 3.1 %copy-start.2 = (bf16[3,512,512]{1,2,0:T(8,128)(2,1)S(1)}, bf16[3,512,512]{1,2,0:T(8,128)(2,1)}, u32[]{:S(2)}) copy-start(bf16[3,512,512]{1,2,0:T(8,128)(2,1)} %exponential_convert_fusion) | copy-start | bytes 4718596
  142.6 5.3 %copy-start.5 = (bf16[512,3,128]{0,2,1:T(8,128)(2,1)S(1)}, bf16[512,3,128]{0,2,1:T(8,128)(2,1)}, u32[]{:S(2)}) copy-start(bf16[512,3,128]{0,2,1:T(8,128)(2,1)} %squeeze.32) | copy-start | bytes 1179652
  145.6 2.8 %copy-start.3 = (bf16[512,3,128]{0,2,1:T(8,128)(2,1)S(1)}, bf16[512,3,128]{0,2,1:T(8,128)(2,1)}, u32[]{:S(2)}) copy-start(bf16[512,3,128]{0,2,1:T(8,128)(2,1)} %squeeze.30) | copy-start | bytes 1179652
  147.8 2.2 copy-start.4
  151.3 31.8 %collective-permute-start.9 = (bf16[512,384]{0,1:T(8,128)(2,1)}, bf16[512,384]{0,1:T(8,128)(2,1)}, u32[]{:S(2)}, u32[]{:S(2)}) collective-permute-start(bf16[512,384]{0,1:T(8,128)(2,1)} %bitcast.14), channel_id=1, source_target_pairs={{0,1},{1,2},{2,3},{3,0},{4,5},{5,6},{6,7},{7,4},{8,9},{9,10},{10,1... | collective-permute-start | bytes 1179656 | tf_op jit(solution)/shard_map/ppermute | solution.py:115
  159.4 26.1 %collective-permute-start.10 = (bf16[512,384]{0,1:T(8,128)(2,1)}, bf16[512,384]{0,1:T(8,128)(2,1)}, u32[]{:S(2)}, u32[]{:S(2)}) collective-permute-start(bf16[512,384]{0,1:T(8,128)(2,1)} %bitcast.14), channel_id=1, source_target_pairs={{0,2},{1,3},{2,0},{3,1},{4,6},{5,7},{6,4},{7,5},{8,10},{9,11},{10,... | collective-permute-start | bytes 1179656 | tf_op jit(solution)/shard_map/ppermute | solution.py:115
  161.7 23.8 %collective-permute-start.11 = (bf16[512,384]{0,1:T(8,128)(2,1)}, bf16[512,384]{0,1:T(8,128)(2,1)S(1)}, u32[]{:S(2)}, u32[]{:S(2)}) collective-permute-start(bf16[512,384]{0,1:T(8,128)(2,1)} %bitcast.14), channel_id=1, source_target_pairs={{0,3},{1,0},{2,1},{3,2},{4,7},{5,4},{6,5},{7,6},{8,11},{9,8},{10,9... | collective-permute-start | bytes 1179656 | tf_op jit(solution)/shard_map/ppermute | solution.py:115
  161.8 41.5 %collective-permute-start.15 = (bf16[512,384]{0,1:T(8,128)(2,1)}, bf16[512,384]{0,1:T(8,128)(2,1)}, u32[]{:S(2)}, u32[]{:S(2)}) collective-permute-start(bf16[512,384]{0,1:T(8,128)(2,1)} %bitcast.14), channel_id=1, source_target_pairs={{0,16},{16,0},{1,17},{17,1},{2,18},{18,2},{3,19},{19,3},{4,20},{20... | collective-permute-start | bytes 1179656 | tf_op jit(solution)/shard_map/ppermute | solution.py:17
  175.9 2.6 %copy-start.1 = (bf16[4,128,3072]{2,1,0:T(8,128)(2,1)S(1)}, bf16[4,128,3072]{2,1,0:T(8,128)(2,1)}, u32[]{:S(2)}) copy-start(bf16[4,128,3072]{2,1,0:T(8,128)(2,1)} %copy-done) | copy-start | bytes 9437188
  186.4 35.1 %collective-permute-start.12 = (bf16[3,128,384]{2,1,0:T(8,128)(2,1)}, bf16[3,128,384]{2,1,0:T(8,128)(2,1)}, u32[]{:S(2)}, u32[]{:S(2)}) collective-permute-start(bf16[3,128,384]{2,1,0:T(8,128)(2,1)} %get-tuple-element.18), channel_id=1, source_target_pairs={{0,1},{1,2},{2,3},{3,0},{4,5},{5,6},{6,7},{7,4},{8,9},{9,10},{10,1... | collective-permute-start | bytes 884744 | tf_op jit(solution)/shard_map/ppermute | solution.py:115
  195.2 28.0 %collective-permute-start.13 = (bf16[3,128,384]{2,1,0:T(8,128)(2,1)}, bf16[3,128,384]{2,1,0:T(8,128)(2,1)}, u32[]{:S(2)}, u32[]{:S(2)}) collective-permute-start(bf16[3,128,384]{2,1,0:T(8,128)(2,1)} %get-tuple-element.17), channel_id=1, source_target_pairs={{0,2},{1,3},{2,0},{3,1},{4,6},{5,7},{6,4},{7,5},{8,10},{9,11},{10,... | collective-permute-start | bytes 884744 | tf_op jit(solution)/shard_map/ppermute | solution.py:115
  197.4 26.8 %collective-permute-start.14 = (bf16[3,128,384]{2,1,0:T(8,128)(2,1)}, bf16[3,128,384]{2,1,0:T(8,128)(2,1)}, u32[]{:S(2)}, u32[]{:S(2)}) collective-permute-start(bf16[3,128,384]{2,1,0:T(8,128)(2,1)} %get-tuple-element.16), channel_id=1, source_target_pairs={{0,3},{1,0},{2,1},{3,2},{4,7},{5,4},{6,5},{7,6},{8,11},{9,8},{10,9... | collective-permute-start | bytes 884744 | tf_op jit(solution)/shard_map/ppermute | solution.py:115
  200.3 26.4 %collective-permute-start.20 = (bf16[512,384]{0,1:T(8,128)(2,1)}, bf16[512,384]{0,1:T(8,128)(2,1)S(1)}, u32[]{:S(2)}, u32[]{:S(2)}) collective-permute-start(bf16[512,384]{0,1:T(8,128)(2,1)} %collective-permute-done.9), channel_id=1, source_target_pairs={{0,16},{16,0},{1,17},{17,1},{2,18},{18,2},{3,19},{19,3},{4,20},{20... | collective-permute-start | bytes 1179656 | tf_op jit(solution)/shard_map/ppermute | solution.py:17
  203.3 27.0 %collective-permute-start.21 = (bf16[512,384]{0,1:T(8,128)(2,1)}, bf16[512,384]{0,1:T(8,128)(2,1)S(1)}, u32[]{:S(2)}, u32[]{:S(2)}) collective-permute-start(bf16[512,384]{0,1:T(8,128)(2,1)} %collective-permute-done.10), channel_id=1, source_target_pairs={{0,16},{16,0},{1,17},{17,1},{2,18},{18,2},{3,19},{19,3},{4,20},{20... | collective-permute-start | bytes 1179656 | tf_op jit(solution)/shard_map/ppermute | solution.py:17
  221.6 12.4 %collective-permute-start.22 = (bf16[512,384]{0,1:T(8,128)(2,1)S(1)}, bf16[512,384]{0,1:T(8,128)(2,1)S(1)}, u32[]{:S(2)}, u32[]{:S(2)}) collective-permute-start(bf16[512,384]{0,1:T(8,128)(2,1)S(1)} %collective-permute-done.11), channel_id=1, source_target_pairs={{0,16},{16,0},{1,17},{17,1},{2,18},{18,2},{3,19},{19,3},{4,20},{20... | collective-permute-start | bytes 1179656 | tf_op jit(solution)/shard_map/ppermute | solution.py:17

commit v6 on v4

--- a/solution.py
+++ b/solution.py
@@ -203,9 +203,8 @@
     width = width_all // n
     heads = width // DH
     patch_here = patches[0]
-    dense_grad = gather_rows_relayed(output_grad[0], "row")
+    dense_grad = gather_rows(output_grad[0], "row")
     grad_other = swap_dp(output_grad)
-    other_grad = gather_rows_relayed(grad_other[0], "row")
     qkv = jnp.stack([queries[0], attn_keys[0], attn_values[0]], 0)
     part = lambda g: lax.dynamic_slice_in_dim(qkv, g * width, width, 2)
     shapes = [(3, tokens, width), patch_here.shape]
@@ -231,6 +230,8 @@
     grad_partial = lax.dot_general(
         dense_grad, out_weight, (((1,), (1,)), ((), ())), preferred_element_type=jnp.float32
     )
+    grad_partial, grad_other = lax.optimization_barrier((grad_partial, grad_other))
+    other_grad = gather_rows(grad_other[0], "row")
     attn_grad = sum_to_heads(grad_partial, "col").astype(jnp.bfloat16)
     grad_heads = attn_grad.reshape(rows, heads, DH)
     prob_grad = jnp.einsum(
@@ -267,13 +268,17 @@
         lax.dot_general(out_own, dense_grad, (((1,), (0,)), ((), ())), preferred_element_type=jnp.float32)
         + lax.dot_general(out_other, other_grad, (((1,), (0,)), ((), ())), preferred_element_type=jnp.float32)
     ).reshape(width_all, -1)
-    grads = jnp.stack([g.reshape(n, tokens, width) for g in (query_grad, key_grad, value_grad)], 1)
-    grads, out_own = lax.optimization_barrier((grads, out_own))
-    back = [grads[me]] + [
-        shifted(grads[(me + s) % n].astype(jnp.bfloat16), "col", s).astype(jnp.float32)
-        for s in range(1, n)
-    ]
-    back = jnp.transpose(natural(back, "col"), (1, 2, 0, 3)).reshape(3, 1, tokens, width_all)
+    grad_list = [g.reshape(n, tokens, width) for g in (query_grad, key_grad, value_grad)]
+    sendable = jnp.stack([g.astype(jnp.bfloat16) for g in grad_list], 1)
+    sendable, out_own = lax.optimization_barrier((sendable, out_own))
+    back = jnp.zeros((3, tokens, width_all), jnp.float32)
+    mine = jnp.stack([lax.dynamic_index_in_dim(g, me, 0, keepdims=False) for g in grad_list], 0)
+    back = lax.dynamic_update_slice_in_dim(back, mine, me * width, 2)
+    for s in range(1, n):
+        piece = lax.dynamic_index_in_dim(sendable, (me + s) % n, 0, keepdims=False)
+        got = shifted(piece, "col", s).astype(jnp.float32)
+        back = lax.dynamic_update_slice_in_dim(back, got, ((me - s) % n) * width, 2)
+    back = back.reshape(3, 1, tokens, width_all)
     return (back[0], back[1], back[2], out_weight_grad, embed_weight_grad)
 
 

time: 264 us -> 239 us (0.905)
  local copies, waits for them, and re-layouts: 66.3 us -> 46.5 us
  starting transfers between devices: 38.3 us -> 31.8 us
  waiting for transfers between devices: 78.7 us -> 85 us
    ppermute x6 -> x0, waiting for transfers between devices: 13.8 us -> none  [the longest x2 13.8 us: gather_rows_relayed(): lax.ppermute(x, axis, [(j, (j + 2 * s) % n) for j in range(n)])]
    another operation x6 -> x0, local copies, waits for them, and re-layouts: 13.7 us -> none  [body_heads(): jnp.stack([g.reshape(n, tokens, width) for g in (query_grad, key_grad, va...]
    ppermute x12 -> x18, waiting for transfers between devices: 64.9 us -> 77.8 us  [shifted(): return lax.ppermute(x, axis, [(j, (j + step) % n) for j in range(n)])]
    dynamic_slice x1 -> x7, local copies, waits for them, and re-layouts: 1.1 us -> 13.9 us  [the longest x4 11.2 us: body_heads(): piece = lax.dynamic_index_in_dim(sendable, (me + s) % n, 0, keepdims=False)]
    slice x4 -> x0, local copies, waits for them, and re-layouts: 8.37 us -> none  [body_heads(): return (back[0], back[1], back[2], out_weight_grad, embed_weight_grad)]
    ppermute x6, waiting for transfers between devices: 0.02 us -> 7.15 us  [swap_dp(): return lax.ppermute(x, 'dp', [(0, 1), (1, 0)])]
    unnamed x22 -> x20, local copies, waits for them, and re-layouts: 11.1 us -> 4.33 us
    dynamic_update_slice x0 -> x4, other arithmetic: none -> 6.52 us  [the longest x3 5.57 us: body_heads(): back = lax.dynamic_update_slice_in_dim(back, got, (me - s) % n * width, 2)]
  transfers between devices with their start and end apart: 24 -> 24, of which waited for: 7 -> 8; matrix products, arithmetic and copies ran while one was open for 45% -> 43% of each run, Pallas kernels for 0% -> 0%
where the time goes in v6:
time: 239 us; the launch traced here: 238 us
  waiting for transfers between devices  85 us (36%)
  matrix products  47.8 us (20%)
  local copies, waits for them, and re-layouts  46.5 us (19%)
  starting transfers between devices  31.8 us (13%)
  other arithmetic  25.3 us (11%)
    ppermute x18, waiting for transfers between devices, shifted(): return lax.ppermute(x, axis, [(j, (j + step) % n) for j in range(n)])  77.8 us
    ppermute x18, starting transfers between devices, shifted(): return lax.ppermute(x, axis, [(j, (j + step) % n) for j in range(n)])  25.7 us
    dot_general x1, matrix products, body_heads(): lax.dot_general(out_other, other_grad, (((1,), (0,)), ((), ())), preferre...  13.6 us
    gather x6, local copies, waits for them, and re-layouts, natural(): return jnp.take(jnp.stack(pieces, 0), order, axis=0)  12.1 us
    dynamic_slice x4, local copies, waits for them, and re-layouts, body_heads(): piece = lax.dynamic_index_in_dim(sendable, (me + s) % n, 0, keepdims=False)  11.2 us
    dot_general x1, matrix products, body_heads(): lax.dot_general(out_own, dense_grad, (((1,), (0,)), ((), ())), preferred_...  10.9 us
    dot_general x2, matrix products, contract_rows(): lax.dot_general(left, right, (((0,), (0,)), ((), ())), preferred_element_...  9.51 us
    dot_general x1, matrix products, body_heads(): lax.dot_general(dense_grad, out_weight, (((1,), (1,)), ((), ())), preferr...  8.79 us
  transfers between devices with their start and end apart: 24, of which 8 were waited for; matrix products, arithmetic and copies ran while one was open for 43% of the time, Pallas kernels for 0%

profile of v6, /device:TPU:0, one launch (start us, length us, event | category | flops | bytes accessed | tf_op | source)
XLA Modules:
  0.0 237.7 jit_solution(11792724446154493863)
XLA Ops:
  0.6 2.4 %collective-permute-start.5 = (bf16[128,3072]{1,0:T(8,128)(2,1)}, bf16[128,3072]{1,0:T(8,128)(2,1)}, u32[]{:S(2)}, u32[]{:S(2)}) collective-permute-start(bf16[128,3072]{1,0:T(8,128)(2,1)} %bitcast.3), channel_id=1, source_target_pairs={{0,12},{4,0},{8,4},{12,8},{1,13},{5,1},{9,5},{13,9},{2,14},{6,2},{... | collective-permute-start | bytes 2359304 | tf_op jit(solution)/shard_map/ppermute | solution.py:115
  5.0 1.0 constant_dynamic-update-slice_fusion.2
  8.8 3.7 %collective-permute-start.2 = (bf16[194048]{0:T(1024)(128)(2,1)S(1)}, bf16[194048]{0:T(1024)(128)(2,1)S(1)}, u32[]{:S(2)}, u32[]{:S(2)}) collective-permute-start(bf16[194048]{0:T(1024)(128)(2,1)S(1)} %get-tuple-element.33), channel_id=1, source_target_pairs={{0,3},{1,0},{2,1},{3,2},{4,7},{5,4},{6,5},{7,6},{8,11},{9,8},{10,9... | collective-permute-start | bytes 1164296 | tf_op jit(solution)/shard_map/ppermute | solution.py:115
  13.7 8.2 %collective-permute-done.2 = bf16[194048]{0:T(1024)(128)(2,1)S(1)} collective-permute-done((bf16[194048]{0:T(1024)(128)(2,1)S(1)}, bf16[194048]{0:T(1024)(128)(2,1)S(1)}, u32[]{:S(2)}, u32[]{:S(2)}) %collective-permute-start.2) | collective-permute-done | bytes 388128 | tf_op jit(solution)/shard_map/ppermute | solution.py:115
  22.1 24.0 %collective-permute-done.1 = bf16[194048]{0:T(1024)(128)(2,1)} collective-permute-done((bf16[194048]{0:T(1024)(128)(2,1)S(1)}, bf16[194048]{0:T(1024)(128)(2,1)}, u32[]{:S(2)}, u32[]{:S(2)}) %collective-permute-start.1) | collective-permute-done | bytes 388128 | tf_op jit(solution)/shard_map/ppermute | solution.py:115
  46.0 1.5 collective-permute-start.6
  58.9 3.2 %pad_maximum_fusion = bf16[4,128,3072]{2,1,0:T(8,128)(2,1)} fusion(bf16[1,128,3072]{2,1,0:T(8,128)(2,1)} %bitcast.6, bf16[1,128,3072]{2,1,0:T(8,128)(2,1)} %bitcast.5, bf16[1,128,3072]{2,1,0:T(8,128)(2,1)} %bitcast.4, bf16[1,128,3072]{2,1,0:T(8,128)(2,1)} %param.15), kind=kLoop, calls=%fused_computation.8 | loop fusion | flops 4718592 | bytes 6291456 | tf_op jit(solution)/shard_map/stack | solution.py:121
  62.1 4.3 %gather_fusion.2 = bf16[4,128,3072]{2,1,0:T(8,128)(2,1)} fusion(bf16[4,128,3072]{2,1,0:T(8,128)(2,1)} %pad_maximum_fusion, s32[1024]{0:T(1024)S(1)} %pad_clamp_fusion.1), kind=kCustom, calls=%fused_computation.clone | custom fusion | bytes 6291472 | tf_op jit(solution)/shard_map/jit(_take)/gather | solution.py:121
  66.4 2.3 broadcast_select_fusion.1
  68.7 8.8 %fusion.20 = f32[512,1536]{1,0:T(8,128)S(1)} fusion(bf16[512,3072]{1,0:T(8,128)(2,1)S(1)} %bitcast.111, bf16[1536,3072]{1,0:T(8,128)(2,1)} %param.14), kind=kOutput, calls=%fused_computation.95 | convolution fusion | flops 4831838208 | bytes 15728640 | tf_op jit(solution)/shard_map/dot_general | solution.py:230
  77.8 1.2 collective-permute-start.8
  79.0 2.8 %collective-permute-start.7 = (bf16[512,384]{1,0:T(8,128)(2,1)S(1)}, bf16[512,384]{1,0:T(8,128)(2,1)S(1)}, u32[]{:S(2)}, u32[]{:S(2)}) collective-permute-start(bf16[512,384]{1,0:T(8,128)(2,1)S(1)} %get-tuple-element.15), channel_id=1, source_target_pairs={{0,3},{1,0},{2,1},{3,2},{4,7},{5,4},{6,5},{7,6},{8,11},{9,8},{10,9... | collective-permute-start | bytes 1179656 | tf_op jit(solution)/shard_map/ppermute | solution.py:115
  81.8 3.6 %fusion.6 = f32[364,3072,1]{1,0,2:T(8,128)} fusion(bf16[4,128,3072]{2,1,0:T(8,128)(2,1)S(1)} %broadcast_select_fusion.1, bf16[4,128,364]{2,1,0:T(8,128)(2,1)S(1)} %gather_fusion.1, pred[4]{0:T(512)(128)(4,1)S(1)} %get-tuple-element.45), kind=kOutput, calls=%fused_computation.49 | convolution fusion | flops 1145231360 | bytes 7991300 | tf_op jit(solution)/shard_map/dot_general | solution.py:11
  85.4 6.3 %collective-permute-done.9 = bf16[512,384]{1,0:T(8,128)(2,1)S(1)} collective-permute-done((bf16[512,384]{1,0:T(8,128)(2,1)S(1)}, bf16[512,384]{1,0:T(8,128)(2,1)S(1)}, u32[]{:S(2)}, u32[]{:S(2)}) %collective-permute-start.9) | collective-permute-done | bytes 393248 | tf_op jit(solution)/shard_map/ppermute | solution.py:115
  91.7 14.7 %collective-permute-done.8 = bf16[512,384]{1,0:T(8,128)(2,1)S(1)} collective-permute-done((bf16[512,384]{1,0:T(8,128)(2,1)S(1)}, bf16[512,384]{1,0:T(8,128)(2,1)S(1)}, u32[]{:S(2)}, u32[]{:S(2)}) %collective-permute-start.8) | collective-permute-done | bytes 393248 | tf_op jit(solution)/shard_map/ppermute | solution.py:115
  106.8 1.6 fusion.17
  108.4 1.1 multiply_reduce_fusion.1
  111.2 8.8 %collective-permute-start.12 = (bf16[512,384]{0,1:T(8,128)(2,1)}, bf16[512,384]{0,1:T(8,128)(2,1)}, u32[]{:S(2)}, u32[]{:S(2)}) collective-permute-start(bf16[512,384]{0,1:T(8,128)(2,1)} %bitcast.16), channel_id=1, source_target_pairs={{0,3},{1,0},{2,1},{3,2},{4,7},{5,4},{6,5},{7,6},{8,11},{9,8},{10,9... | collective-permute-start | bytes 1179656 | tf_op jit(solution)/shard_map/ppermute | solution.py:115
  120.8 1.1 reshape.196
  121.9 1.3 constant_dynamic-slice_fusion.3
  124.0 1.1 reshape.195
  125.2 1.3 constant_dynamic-slice_fusion.4
  127.5 1.7 reshape.188
  130.2 2.0 pad_maximum_fusion.5
  132.5 22.0 %collective-permute-done.11 = bf16[512,384]{0,1:T(8,128)(2,1)} collective-permute-done((bf16[512,384]{0,1:T(8,128)(2,1)}, bf16[512,384]{0,1:T(8,128)(2,1)}, u32[]{:S(2)}, u32[]{:S(2)}) %collective-permute-start.11) | collective-permute-done | bytes 393248 | tf_op jit(solution)/shard_map/ppermute | solution.py:115
  154.5 1.5 collective-permute-start.16
  156.0 1.5 pad_maximum_fusion.2
  158.2 1.4 broadcast_select_fusion.2
  159.8 2.8 %constant_dynamic-slice_fusion = (bf16[1,3,128,384]{2,0,3,1:T(2,128)(2,1)}, bf16[1,3,128,384]{2,0,3,1:T(2,128)(2,1)}, bf16[1,3,128,384]{2,0,3,1:T(2,128)(2,1)}) fusion(bf16[4,3,128,384]{2,0,3,1:T(4,128)(2,1)S(1)} %copy-done.2, s32[]{:T(128)S(6)} %select_n.178, s32[]{:T(128)S(6)} %select_n.177, s32[]{:T(128)S(6)} %select_n.176), kind=kLoop, calls=%fused_computation.58 | loop fusion | bytes 1769484 | tf_op jit(solution)/shard_map/jit(dynamic_index_in_dim)/dynamic_slice | solution.py:278
  162.6 2.8 %copy.64 = bf16[1,3,128,384]{3,2,1,0:T(8,128)(2,1)} copy(bf16[1,3,128,384]{2,0,3,1:T(2,128)(2,1)} %get-tuple-element.23) | data formatting | bytes 589824 | tf_op jit(solution)/shard_map/jit(dynamic_index_in_dim)/dynamic_slice | solution.py:278
  165.4 2.8 %copy.65 = bf16[1,3,128,384]{3,2,1,0:T(8,128)(2,1)} copy(bf16[1,3,128,384]{2,0,3,1:T(2,128)(2,1)} %get-tuple-element.22) | data formatting | bytes 589824 | tf_op jit(solution)/shard_map/jit(dynamic_index_in_dim)/dynamic_slice | solution.py:278
  168.2 2.8 %copy.66 = bf16[1,3,128,384]{3,2,1,0:T(8,128)(2,1)} copy(bf16[1,3,128,384]{2,0,3,1:T(2,128)(2,1)} %get-tuple-element.21) | data formatting | bytes 589824 | tf_op jit(solution)/shard_map/jit(dynamic_index_in_dim)/dynamic_slice | solution.py:278
  170.9 10.9 %fusion.21 = f32[4,384,3072]{2,1,0:T(8,128)} fusion(bf16[4,512,384]{1,2,0:T(8,128)(2,1)} %broadcast_select_fusion.2, bf16[512,3072,1]{1,0,2:T(8,128)(2,1)S(1)} %bitcast.112), kind=kOutput, calls=%fused_computation.96 | convolution fusion | flops 4831838208 | bytes 23592960 | tf_op jit(solution)/shard_map/dot_general | solution.py:268
  182.0 3.7 %collective-permute-start.15 = (bf16[3,128,384]{2,1,0:T(8,128)(2,1)}, bf16[3,128,384]{2,1,0:T(8,128)(2,1)}, u32[]{:S(2)}, u32[]{:S(2)}) collective-permute-start(bf16[3,128,384]{2,1,0:T(8,128)(2,1)} %bitcast.24), channel_id=1, source_target_pairs={{0,3},{1,0},{2,1},{3,2},{4,7},{5,4},{6,5},{7,6},{8,11},{9,8},{10,9... | collective-permute-start | bytes 884744 | tf_op jit(solution)/shard_map/ppermute | solution.py:115
  185.7 2.0 pad_maximum_fusion.1
  187.8 2.5 %gather_fusion.5 = bf16[4,128,3072]{2,1,0:T(8,128)(2,1)} fusion(bf16[4,128,3072]{2,1,0:T(8,128)(2,1)S(1)} %pad_maximum_fusion.1, s32[1024]{0:T(1024)S(1)} %pad_clamp_fusion.1), kind=kCustom, calls=%fused_computation.2.clone | custom fusion | bytes 6291472 | tf_op jit(solution)/shard_map/jit(_take)/gather | solution.py:121
  190.3 2.3 broadcast_select_fusion
  193.1 5.9 %bitcast_add_fusion = f32[364,3072]{1,0:T(8,128)} fusion(f32[364,3072,1]{1,0,2:T(8,128)} %fusion.6, bf16[512,364]{1,0:T(8,128)(2,1)} %collective-permute-done.23, bf16[512,3072]{1,0:T(8,128)(2,1)S(1)} %bitcast.108), kind=kOutput, calls=%fused_computation.7 | convolution fusion | flops 1146163200 | bytes 12464128 | tf_op jit(solution)/shard_map/dot_general | solution.py:11
  199.0 1.5 collective-permute-start.18
  200.5 1.9 convert_dynamic-update-slice_fusion.2
  202.4 2.7 %collective-permute-done.14 = bf16[3,128,384]{2,1,0:T(8,128)(2,1)} collective-permute-done((bf16[3,128,384]{2,1,0:T(8,128)(2,1)}, bf16[3,128,384]{2,1,0:T(8,128)(2,1)}, u32[]{:S(2)}, u32[]{:S(2)}) %collective-permute-start.14) | collective-permute-done | bytes 294944 | tf_op jit(solution)/shard_map/ppermute | solution.py:115
  205.6 1.9 convert_dynamic-update-slice_fusion.1
  207.5 1.8 convert_dynamic-update-slice_fusion
  209.3 3.1 %slice_bitcast_fusion = (f32[1,128,1536]{2,1,0:T(8,128)}, f32[1,128,1536]{2,1,0:T(8,128)}, f32[1,128,1536]{2,1,0:T(8,128)}) fusion(f32[3,1,128,1536]{3,2,1,0:T(8,128)} %convert_dynamic-update-slice_fusion), kind=kLoop, calls=%fused_computation.30 | loop fusion | bytes 4718592 | tf_op jit(solution)/shard_map/squeeze | solution.py:282
  213.3 6.2 %collective-permute-done.17 = bf16[512,384]{0,1:T(8,128)(2,1)S(1)} collective-permute-done((bf16[512,384]{0,1:T(8,128)(2,1)}, bf16[512,384]{0,1:T(8,128)(2,1)S(1)}, u32[]{:S(2)}, u32[]{:S(2)}) %collective-permute-start.17) | collective-permute-done | bytes 393248 | tf_op jit(solution)/shard_map/ppermute | solution.py:17
  219.5 1.4 pad_maximum_fusion.3
  220.9 3.2 %gather_fusion.4 = bf16[4,512,384]{1,2,0:T(8,128)(2,1)} fusion(bf16[4,512,384]{1,2,0:T(8,128)(2,1)} %pad_maximum_fusion.3, s32[1024]{0:T(1024)S(1)} %pad_clamp_fusion), kind=kCustom, calls=%fused_computation.3.clone | custom fusion | bytes 3145744 | tf_op jit(solution)/shard_map/jit(_take)/gather | solution.py:121
  224.1 13.6 %convolution_add_fusion = f32[4,384,3072]{2,1,0:T(8,128)} fusion(f32[4,384,3072]{2,1,0:T(8,128)} %fusion.21, bf16[512,3072,1]{1,0,2:T(8,128)(2,1)S(1)} %bitcast.109, bf16[4,512,384]{1,2,0:T(8,128)(2,1)} %gather_fusion.4, pred[4]{0:T(512)(128)(4,1)S(1)} %get-tuple-element.45), kind=kOutput, calls=%fused_computation.6 | convolution fusion | flops 4837343232 | bytes 42467332 | tf_op jit(solution)/shard_map/dot_general | solution.py:269
  (109 shorter events, 26.3 us)
Async XLA Ops:
  0.6 58.2 %collective-permute-start.5 = (bf16[128,3072]{1,0:T(8,128)(2,1)}, bf16[128,3072]{1,0:T(8,128)(2,1)}, u32[]{:S(2)}, u32[]{:S(2)}) collective-permute-start(bf16[128,3072]{1,0:T(8,128)(2,1)} %bitcast.3), channel_id=1, source_target_pairs={{0,12},{4,0},{8,4},{12,8},{1,13},{5,1},{9,5},{13,9},{2,14},{6,2},{... | collective-permute-start | bytes 2359304 | tf_op jit(solution)/shard_map/ppermute | solution.py:115
  3.1 55.8 %collective-permute-start.4 = (bf16[128,3072]{1,0:T(8,128)(2,1)}, bf16[128,3072]{1,0:T(8,128)(2,1)}, u32[]{:S(2)}, u32[]{:S(2)}) collective-permute-start(bf16[128,3072]{1,0:T(8,128)(2,1)} %bitcast.3), channel_id=1, source_target_pairs={{0,8},{4,12},{8,0},{12,4},{1,9},{5,13},{9,1},{13,5},{2,10},{6,14},... | collective-permute-start | bytes 2359304 | tf_op jit(solution)/shard_map/ppermute | solution.py:115
  8.8 13.1 %collective-permute-start.2 = (bf16[194048]{0:T(1024)(128)(2,1)S(1)}, bf16[194048]{0:T(1024)(128)(2,1)S(1)}, u32[]{:S(2)}, u32[]{:S(2)}) collective-permute-start(bf16[194048]{0:T(1024)(128)(2,1)S(1)} %get-tuple-element.33), channel_id=1, source_target_pairs={{0,3},{1,0},{2,1},{3,2},{4,7},{5,4},{6,5},{7,6},{8,11},{9,8},{10,9... | collective-permute-start | bytes 1164296 | tf_op jit(solution)/shard_map/ppermute | solution.py:115
  12.4 33.6 %collective-permute-start.1 = (bf16[194048]{0:T(1024)(128)(2,1)S(1)}, bf16[194048]{0:T(1024)(128)(2,1)}, u32[]{:S(2)}, u32[]{:S(2)}) collective-permute-start(bf16[194048]{0:T(1024)(128)(2,1)S(1)} %get-tuple-element.32), channel_id=1, source_target_pairs={{0,2},{1,3},{2,0},{3,1},{4,6},{5,7},{6,4},{7,5},{8,10},{9,11},{10,... | collective-permute-start | bytes 1164296 | tf_op jit(solution)/shard_map/ppermute | solution.py:115
  12.4 36.3 %collective-permute-start = (bf16[194048]{0:T(1024)(128)(2,1)S(1)}, bf16[194048]{0:T(1024)(128)(2,1)}, u32[]{:S(2)}, u32[]{:S(2)}) collective-permute-start(bf16[194048]{0:T(1024)(128)(2,1)S(1)} %get-tuple-element.31), channel_id=1, source_target_pairs={{0,1},{1,2},{2,3},{3,0},{4,5},{5,6},{6,7},{7,4},{8,9},{9,10},{10,1... | collective-permute-start | bytes 1164296 | tf_op jit(solution)/shard_map/ppermute | solution.py:115
  21.9 27.9 %copy-start.6 = (bf16[194048]{0:T(1024)(128)(2,1)}, bf16[194048]{0:T(1024)(128)(2,1)S(1)}, u32[]{:S(2)}) copy-start(bf16[194048]{0:T(1024)(128)(2,1)S(1)} %collective-permute-done.2) | copy-start | bytes 1164292
  21.9 37.0 %collective-permute-start.3 = (bf16[128,3072]{1,0:T(8,128)(2,1)}, bf16[128,3072]{1,0:T(8,128)(2,1)}, u32[]{:S(2)}, u32[]{:S(2)}) collective-permute-start(bf16[128,3072]{1,0:T(8,128)(2,1)} %bitcast.3), channel_id=1, source_target_pairs={{0,4},{4,8},{8,12},{12,0},{1,5},{5,9},{9,13},{13,1},{2,6},{6,10},{... | collective-permute-start | bytes 2359304 | tf_op jit(solution)/shard_map/ppermute | solution.py:115
  46.0 31.5 %collective-permute-start.6 = (bf16[1,128,3072]{2,1,0:T(8,128)(2,1)}, bf16[1,128,3072]{2,1,0:T(8,128)(2,1)}, u32[]{:S(2)}, u32[]{:S(2)}) collective-permute-start(bf16[1,128,3072]{2,1,0:T(8,128)(2,1)} %param.15), channel_id=1, source_target_pairs={{0,16},{16,0},{1,17},{17,1},{2,18},{18,2},{3,19},{19,3},{4,20},{20... | collective-permute-start | bytes 2359304 | tf_op jit(solution)/shard_map/ppermute | solution.py:17
  51.2 1.3 slice-start
  56.7 135.9 %collective-permute-start.23 = (bf16[512,364]{1,0:T(8,128)(2,1)}, bf16[512,364]{1,0:T(8,128)(2,1)}, u32[]{:S(2)}, u32[]{:S(2)}) collective-permute-start(bf16[512,364]{1,0:T(8,128)(2,1)} %bitcast_select_fusion), channel_id=1, source_target_pairs={{0,16},{16,0},{1,17},{17,1},{2,18},{18,2},{3,19},{19,3},{4,20},{20... | collective-permute-start | bytes 1118216 | tf_op jit(solution)/shard_map/ppermute | solution.py:17
  68.7 13.2 %copy-start = (bf16[4,128,3072]{2,1,0:T(8,128)(2,1)}, bf16[4,128,3072]{2,1,0:T(8,128)(2,1)S(1)}, u32[]{:S(2)}) copy-start(bf16[4,128,3072]{2,1,0:T(8,128)(2,1)S(1)} %broadcast_select_fusion.1) | copy-start | bytes 9437188
  77.7 14.0 %collective-permute-start.9 = (bf16[512,384]{1,0:T(8,128)(2,1)S(1)}, bf16[512,384]{1,0:T(8,128)(2,1)S(1)}, u32[]{:S(2)}, u32[]{:S(2)}) collective-permute-start(bf16[512,384]{1,0:T(8,128)(2,1)S(1)} %get-tuple-element.16), channel_id=1, source_target_pairs={{0,1},{1,2},{2,3},{3,0},{4,5},{5,6},{6,7},{7,4},{8,9},{9,10},{10,1... | collective-permute-start | bytes 1179656 | tf_op jit(solution)/shard_map/ppermute | solution.py:115
  77.8 28.6 %collective-permute-start.8 = (bf16[512,384]{1,0:T(8,128)(2,1)S(1)}, bf16[512,384]{1,0:T(8,128)(2,1)S(1)}, u32[]{:S(2)}, u32[]{:S(2)}) collective-permute-start(bf16[512,384]{1,0:T(8,128)(2,1)S(1)} %get-tuple-element.17), channel_id=1, source_target_pairs={{0,2},{1,3},{2,0},{3,1},{4,6},{5,7},{6,4},{7,5},{8,10},{9,11},{10,... | collective-permute-start | bytes 1179656 | tf_op jit(solution)/shard_map/ppermute | solution.py:115
  79.0 27.4 %collective-permute-start.7 = (bf16[512,384]{1,0:T(8,128)(2,1)S(1)}, bf16[512,384]{1,0:T(8,128)(2,1)S(1)}, u32[]{:S(2)}, u32[]{:S(2)}) collective-permute-start(bf16[512,384]{1,0:T(8,128)(2,1)S(1)} %get-tuple-element.15), channel_id=1, source_target_pairs={{0,3},{1,0},{2,1},{3,2},{4,7},{5,4},{6,5},{7,6},{8,11},{9,8},{10,9... | collective-permute-start | bytes 1179656 | tf_op jit(solution)/shard_map/ppermute | solution.py:115
  81.8 100.0 %collective-permute-start.22 = (bf16[128,3072]{1,0:T(8,128)(2,1)}, bf16[128,3072]{1,0:T(8,128)(2,1)}, u32[]{:S(2)}, u32[]{:S(2)}) collective-permute-start(bf16[128,3072]{1,0:T(8,128)(2,1)} %bitcast.35), channel_id=1, source_target_pairs={{0,12},{4,0},{8,4},{12,8},{1,13},{5,1},{9,5},{13,9},{2,14},{6,2},{... | collective-permute-start | bytes 2359304 | tf_op jit(solution)/shard_map/ppermute | solution.py:115
  110.8 10.0 %copy-start.3 = (f32[512,3,128]{0,2,1:T(8,128)S(1)}, f32[512,3,128]{0,2,1:T(8,128)}, u32[]{:S(2)}) copy-start(f32[512,3,128]{0,2,1:T(8,128)} %get-tuple-element.39) | copy-start | bytes 2359300
  111.2 20.9 %collective-permute-start.12 = (bf16[512,384]{0,1:T(8,128)(2,1)}, bf16[512,384]{0,1:T(8,128)(2,1)}, u32[]{:S(2)}, u32[]{:S(2)}) collective-permute-start(bf16[512,384]{0,1:T(8,128)(2,1)} %bitcast.16), channel_id=1, source_target_pairs={{0,3},{1,0},{2,1},{3,2},{4,7},{5,4},{6,5},{7,6},{8,11},{9,8},{10,9... | collective-permute-start | bytes 1179656 | tf_op jit(solution)/shard_map/ppermute | solution.py:115
  120.0 34.5 %collective-permute-start.11 = (bf16[512,384]{0,1:T(8,128)(2,1)}, bf16[512,384]{0,1:T(8,128)(2,1)}, u32[]{:S(2)}, u32[]{:S(2)}) collective-permute-start(bf16[512,384]{0,1:T(8,128)(2,1)} %bitcast.16), channel_id=1, source_target_pairs={{0,2},{1,3},{2,0},{3,1},{4,6},{5,7},{6,4},{7,5},{8,10},{9,11},{10,... | collective-permute-start | bytes 1179656 | tf_op jit(solution)/shard_map/ppermute | solution.py:115
  120.8 33.7 %collective-permute-start.10 = (bf16[512,384]{0,1:T(8,128)(2,1)}, bf16[512,384]{0,1:T(8,128)(2,1)}, u32[]{:S(2)}, u32[]{:S(2)}) collective-permute-start(bf16[512,384]{0,1:T(8,128)(2,1)} %bitcast.16), channel_id=1, source_target_pairs={{0,1},{1,2},{2,3},{3,0},{4,5},{5,6},{6,7},{7,4},{8,9},{9,10},{10,1... | collective-permute-start | bytes 1179656 | tf_op jit(solution)/shard_map/ppermute | solution.py:115
  124.0 3.2 %copy-start.4 = (bf16[512,3,128]{0,2,1:T(8,128)(2,1)S(1)}, bf16[512,3,128]{0,2,1:T(8,128)(2,1)}, u32[]{:S(2)}) copy-start(bf16[512,3,128]{0,2,1:T(8,128)(2,1)} %get-tuple-element.38) | copy-start | bytes 1179652
  127.2 2.0 copy-start.5
  132.2 49.7 %collective-permute-start.21 = (bf16[128,3072]{1,0:T(8,128)(2,1)}, bf16[128,3072]{1,0:T(8,128)(2,1)}, u32[]{:S(2)}, u32[]{:S(2)}) collective-permute-start(bf16[128,3072]{1,0:T(8,128)(2,1)} %bitcast.35), channel_id=1, source_target_pairs={{0,8},{4,12},{8,0},{12,4},{1,9},{5,13},{9,1},{13,5},{2,10},{6,14},... | collective-permute-start | bytes 2359304 | tf_op jit(solution)/shard_map/ppermute | solution.py:115
  154.5 27.5 %collective-permute-start.20 = (bf16[128,3072]{1,0:T(8,128)(2,1)}, bf16[128,3072]{1,0:T(8,128)(2,1)}, u32[]{:S(2)}, u32[]{:S(2)}) collective-permute-start(bf16[128,3072]{1,0:T(8,128)(2,1)} %bitcast.35), channel_id=1, source_target_pairs={{0,4},{4,8},{8,12},{12,0},{1,5},{5,9},{9,13},{13,1},{2,6},{6,10},{... | collective-permute-start | bytes 2359304 | tf_op jit(solution)/shard_map/ppermute | solution.py:115
  154.5 57.9 %collective-permute-start.16 = (bf16[512,384]{0,1:T(8,128)(2,1)}, bf16[512,384]{0,1:T(8,128)(2,1)S(1)}, u32[]{:S(2)}, u32[]{:S(2)}) collective-permute-start(bf16[512,384]{0,1:T(8,128)(2,1)} %bitcast.16), channel_id=1, source_target_pairs={{0,16},{16,0},{1,17},{17,1},{2,18},{18,2},{3,19},{19,3},{4,20},{20... | collective-permute-start | bytes 1179656 | tf_op jit(solution)/shard_map/ppermute | solution.py:17
  158.2 1.6 copy-start.2
  159.8 11.2 %copy-start.1 = (bf16[4,128,3072]{2,1,0:T(8,128)(2,1)S(1)}, bf16[4,128,3072]{2,1,0:T(8,128)(2,1)}, u32[]{:S(2)}) copy-start(bf16[4,128,3072]{2,1,0:T(8,128)(2,1)} %copy-done) | copy-start | bytes 9437188
  181.8 17.2 %collective-permute-start.13 = (bf16[3,128,384]{2,1,0:T(8,128)(2,1)}, bf16[3,128,384]{2,1,0:T(8,128)(2,1)}, u32[]{:S(2)}, u32[]{:S(2)}) collective-permute-start(bf16[3,128,384]{2,1,0:T(8,128)(2,1)} %bitcast.20), channel_id=1, source_target_pairs={{0,1},{1,2},{2,3},{3,0},{4,5},{5,6},{6,7},{7,4},{8,9},{9,10},{10,1... | collective-permute-start | bytes 884744 | tf_op jit(solution)/shard_map/ppermute | solution.py:115
  181.8 23.3 %collective-permute-start.14 = (bf16[3,128,384]{2,1,0:T(8,128)(2,1)}, bf16[3,128,384]{2,1,0:T(8,128)(2,1)}, u32[]{:S(2)}, u32[]{:S(2)}) collective-permute-start(bf16[3,128,384]{2,1,0:T(8,128)(2,1)} %bitcast.22), channel_id=1, source_target_pairs={{0,2},{1,3},{2,0},{3,1},{4,6},{5,7},{6,4},{7,5},{8,10},{9,11},{10,... | collective-permute-start | bytes 884744 | tf_op jit(solution)/shard_map/ppermute | solution.py:115
  182.0 25.4 %collective-permute-start.15 = (bf16[3,128,384]{2,1,0:T(8,128)(2,1)}, bf16[3,128,384]{2,1,0:T(8,128)(2,1)}, u32[]{:S(2)}, u32[]{:S(2)}) collective-permute-start(bf16[3,128,384]{2,1,0:T(8,128)(2,1)} %bitcast.24), channel_id=1, source_target_pairs={{0,3},{1,0},{2,1},{3,2},{4,7},{5,4},{6,5},{7,6},{8,11},{9,8},{10,9... | collective-permute-start | bytes 884744 | tf_op jit(solution)/shard_map/ppermute | solution.py:115
  192.5 19.9 %collective-permute-start.19 = (bf16[512,384]{0,1:T(8,128)(2,1)}, bf16[512,384]{0,1:T(8,128)(2,1)S(1)}, u32[]{:S(2)}, u32[]{:S(2)}) collective-permute-start(bf16[512,384]{0,1:T(8,128)(2,1)} %collective-permute-done.12), channel_id=1, source_target_pairs={{0,16},{16,0},{1,17},{17,1},{2,18},{18,2},{3,19},{19,3},{4,20},{20... | collective-permute-start | bytes 1179656 | tf_op jit(solution)/shard_map/ppermute | solution.py:17
  199.0 14.3 %collective-permute-start.18 = (bf16[512,384]{0,1:T(8,128)(2,1)}, bf16[512,384]{0,1:T(8,128)(2,1)S(1)}, u32[]{:S(2)}, u32[]{:S(2)}) collective-permute-start(bf16[512,384]{0,1:T(8,128)(2,1)} %collective-permute-done.11), channel_id=1, source_target_pairs={{0,16},{16,0},{1,17},{17,1},{2,18},{18,2},{3,19},{19,3},{4,20},{20... | collective-permute-start | bytes 1179656 | tf_op jit(solution)/shard_map/ppermute | solution.py:17
  205.1 14.4 %collective-permute-start.17 = (bf16[512,384]{0,1:T(8,128)(2,1)}, bf16[512,384]{0,1:T(8,128)(2,1)S(1)}, u32[]{:S(2)}, u32[]{:S(2)}) collective-permute-start(bf16[512,384]{0,1:T(8,128)(2,1)} %collective-permute-done.10), channel_id=1, source_target_pairs={{0,16},{16,0},{1,17},{17,1},{2,18},{18,2},{3,19},{19,3},{4,20},{20... | collective-permute-start | bytes 1179656 | tf_op jit(solution)/shard_map/ppermute | solution.py:17

commit v7 on v6

--- a/solution.py
+++ b/solution.py
@@ -196,14 +196,21 @@
     return stacked.reshape((n * x.shape[0],) + x.shape[1:])
 
 
+def roll_blocks(x, shift):
+    n = x.shape[0]
+    return lax.dynamic_slice_in_dim(jnp.concatenate([x, x], 0), shift % n, n, 0)
+
+
 def body_heads(patches, queries, attn_keys, attn_values, out_weight, output_grad):
     factor = DH ** (-0.5)
     n, me = axis_size("col"), lax.axis_index("col")
+    rank = lax.axis_index("row")
     tokens, width_all = queries.shape[1], queries.shape[2]
     width = width_all // n
     heads = width // DH
     patch_here = patches[0]
-    dense_grad = gather_rows(output_grad[0], "row")
+    grad_blocks = [output_grad[0]] + [shifted(output_grad[0], "row", s) for s in range(1, n)]
+    dense_grad = jnp.concatenate(grad_blocks, 0)
     grad_other = swap_dp(output_grad)
     qkv = jnp.stack([queries[0], attn_keys[0], attn_values[0]], 0)
     part = lambda g: lax.dynamic_slice_in_dim(qkv, g * width, width, 2)
@@ -212,11 +219,17 @@
     for s in range(1, n):
         got = shifted(flat(part((me + s) % n), patch_here), "col", s)
         pieces.append(tuple(unflat(got, shapes)))
-    qkv_h = natural([p[0] for p in pieces], "col")
-    every_patch = natural([p[1] for p in pieces], "col").reshape(n * tokens, -1)
+    order = me - rank
+    qkv_h = roll_blocks(jnp.stack([p[0] for p in pieces], 0), order)
+    every_patch = roll_blocks(jnp.stack([p[1] for p in pieces], 0), order).reshape(n * tokens, -1)
     rows = n * tokens
     qkv_h = jnp.transpose(qkv_h, (1, 0, 2, 3)).reshape(3, rows, heads, DH)
     local_query, all_keys, all_values = qkv_h[0], qkv_h[1], qkv_h[2]
+    grad_partial = lax.dot_general(
+        dense_grad, out_weight, (((1,), (1,)), ((), ())), preferred_element_type=jnp.float32
+    )
+    grad_partial, grad_other = lax.optimization_barrier((grad_partial, grad_other))
+    other_blocks = [grad_other[0]] + [shifted(grad_other[0], "row", s) for s in range(1, n)]
     scores = (
         jnp.einsum("qhd,khd->hqk", local_query, all_keys, preferred_element_type=jnp.float32)
         * factor
@@ -227,11 +240,6 @@
     attn_out = jnp.einsum(
         "hqk,khd->qhd", attn_probs, all_values, preferred_element_type=jnp.float32
     ).astype(jnp.bfloat16)
-    grad_partial = lax.dot_general(
-        dense_grad, out_weight, (((1,), (1,)), ((), ())), preferred_element_type=jnp.float32
-    )
-    grad_partial, grad_other = lax.optimization_barrier((grad_partial, grad_other))
-    other_grad = gather_rows(grad_other[0], "row")
     attn_grad = sum_to_heads(grad_partial, "col").astype(jnp.bfloat16)
     grad_heads = attn_grad.reshape(rows, heads, DH)
     prob_grad = jnp.einsum(
@@ -253,38 +261,44 @@
         "hqk,qhd->khd", attn_probs, grad_heads, preferred_element_type=jnp.float32
     )
     other_patch = swap_dp(every_patch)
-    embed_weight_grad = contract_rows(every_patch, dense_grad) + contract_rows(
-        other_patch, other_grad
-    )
     out_flat = attn_out.reshape(rows, width)
     own_pair = (out_flat, swap_dp(out_flat))
     attn_grad, sent_out = lax.optimization_barrier((attn_grad, out_flat))
     out_pieces = [own_pair] + [
-        (got, swap_dp(got)) for got in (shifted(sent_out, "col", s) for s in range(1, n))
+        (got, swap_dp(got)) for got in (shifted(sent_out, "col", -s % n) for s in range(1, n))
     ]
-    out_own = natural([p[0] for p in out_pieces], "col")
-    out_other = natural([p[1] for p in out_pieces], "col")
-    out_weight_grad = (
-        lax.dot_general(out_own, dense_grad, (((1,), (0,)), ((), ())), preferred_element_type=jnp.float32)
-        + lax.dot_general(out_other, other_grad, (((1,), (0,)), ((), ())), preferred_element_type=jnp.float32)
+    out_both = roll_blocks(
+        jnp.stack([jnp.concatenate(p, 0) for p in out_pieces], 0), -me
+    )
+    grad_both = jnp.concatenate([dense_grad] + other_blocks, 0)
+    out_weight_grad = lax.dot_general(
+        out_both, grad_both, (((1,), (0,)), ((), ())), preferred_element_type=jnp.float32
     ).reshape(width_all, -1)
+    embed_weight_grad = contract_rows(jnp.concatenate([every_patch, other_patch], 0), grad_both)
     grad_list = [g.reshape(n, tokens, width) for g in (query_grad, key_grad, value_grad)]
-    sendable = jnp.stack([g.astype(jnp.bfloat16) for g in grad_list], 1)
-    sendable, out_own = lax.optimization_barrier((sendable, out_own))
+    sendable = roll_blocks(
+        jnp.stack([g.astype(jnp.bfloat16) for g in grad_list], 1), rank - me
+    )
+    sendable, out_both = lax.optimization_barrier((sendable, out_both))
+    mine = jnp.stack(
+        [lax.dynamic_index_in_dim(g, (rank - me) % n, 0, keepdims=False) for g in grad_list], 0
+    )
     back = jnp.zeros((3, tokens, width_all), jnp.float32)
-    mine = jnp.stack([lax.dynamic_index_in_dim(g, me, 0, keepdims=False) for g in grad_list], 0)
     back = lax.dynamic_update_slice_in_dim(back, mine, me * width, 2)
     for s in range(1, n):
-        piece = lax.dynamic_index_in_dim(sendable, (me + s) % n, 0, keepdims=False)
-        got = shifted(piece, "col", s).astype(jnp.float32)
-        back = lax.dynamic_update_slice_in_dim(back, got, ((me - s) % n) * width, 2)
+        got = shifted(sendable[s], "col", -s % n).astype(jnp.float32)
+        back = lax.dynamic_update_slice_in_dim(back, got, ((me + s) % n) * width, 2)
     back = back.reshape(3, 1, tokens, width_all)
     return (back[0], back[1], back[2], out_weight_grad, embed_weight_grad)
 
 
 def body(patches, queries, attn_keys, attn_values, out_weight, output_grad):
     heads_here = queries.shape[2] // DH
-    if heads_here % axis_size("col") == 0 and queries.shape[1] == output_grad.shape[1]:
+    if (
+        heads_here % axis_size("col") == 0
+        and queries.shape[1] == output_grad.shape[1]
+        and axis_size("row") == axis_size("col")
+    ):
         return body_heads(patches, queries, attn_keys, attn_values, out_weight, output_grad)
     return body_tokens(patches, queries, attn_keys, attn_values, out_weight, output_grad)
 

time: 239 us -> 219 us (0.916)
  other arithmetic: 25.3 us -> 10 us
  matrix products: 47.8 us -> 39.4 us
  starting transfers between devices: 31.8 us -> 39.5 us
  waiting for transfers between devices: 85 us -> 77.9 us
  local copies, waits for them, and re-layouts: 46.5 us -> 49.6 us
    unnamed x20 -> x45, local copies, waits for them, and re-layouts: 4.33 us -> 26.7 us
    gather x6 -> x0, local copies, waits for them, and re-layouts: 12.1 us -> none  [natural(): return jnp.take(jnp.stack(pieces, 0), order, axis=0)]
    ppermute x18, waiting for transfers between devices: 77.8 us -> 65.9 us  [shifted(): return lax.ppermute(x, axis, [(j, (j + step) % n) for j in range(n)])]
    another operation x7 -> x0, other arithmetic: 10.5 us -> none  [the longest x6 8.45 us: natural(): return jnp.take(jnp.stack(pieces, 0), order, axis=0)]
    dynamic_slice x7 -> x5, local copies, waits for them, and re-layouts: 13.9 us -> 4.15 us  [the longest x2 2.1 us: roll_blocks(): return lax.dynamic_slice_in_dim(jnp.concatenate([x, x], 0), shift % n, n, 0)]
    dot_general x2 -> x1, matrix products: 24.5 us -> 15.8 us  [body_heads(): lax.dot_general(out_both, grad_both, (((1,), (0,)), ((), ())), preferred_...]
    ppermute x18, starting transfers between devices: 25.7 us -> 33.4 us  [shifted(): return lax.ppermute(x, axis, [(j, (j + step) % n) for j in range(n)])]
    select_n x8 -> x0, other arithmetic: 7.01 us -> none  [natural(): return jnp.take(jnp.stack(pieces, 0), order, axis=0)]
  transfers between devices with their start and end apart: 24 -> 24, of which waited for: 8 -> 9; matrix products, arithmetic and copies ran while one was open for 43% -> 43% of each run, Pallas kernels for 0% -> 0%
where the time goes in v7:
time: 219 us; the launch traced here: 218 us
  waiting for transfers between devices  77.9 us (36%)
  local copies, waits for them, and re-layouts  49.6 us (23%)
  starting transfers between devices  39.5 us (18%)
  matrix products  39.4 us (18%)
  other arithmetic  10 us (5%)
    ppermute x18, waiting for transfers between devices, shifted(): return lax.ppermute(x, axis, [(j, (j + step) % n) for j in range(n)])  65.9 us
    ppermute x18, starting transfers between devices, shifted(): return lax.ppermute(x, axis, [(j, (j + step) % n) for j in range(n)])  33.4 us
    unnamed x45, local copies, waits for them, and re-layouts  26.7 us
    dot_general x1, matrix products, body_heads(): lax.dot_general(out_both, grad_both, (((1,), (0,)), ((), ())), preferred_...  15.8 us
    ppermute x6, waiting for transfers between devices, swap_dp(): return lax.ppermute(x, 'dp', [(0, 1), (1, 0)])  11.9 us
    dot_general x1, matrix products, body_heads(): lax.dot_general(dense_grad, out_weight, (((1,), (1,)), ((), ())), preferr...  10.3 us
    dot_general x1, matrix products, contract_rows(): lax.dot_general(left, right, (((0,), (0,)), ((), ())), preferred_element_...  7.48 us
    unnamed x7, other arithmetic  6.61 us
  transfers between devices with their start and end apart: 24, of which 9 were waited for; matrix products, arithmetic and copies ran while one was open for 43% of the time, Pallas kernels for 0%

profile of v7, /device:TPU:0, one launch (start us, length us, event | category | flops | bytes accessed | tf_op | source)
XLA Modules:
  0.0 217.6 jit_solution(1686410725318223633)
XLA Ops:
  0.6 2.4 %collective-permute-start.5 = (bf16[128,3072]{1,0:T(8,128)(2,1)}, bf16[128,3072]{1,0:T(8,128)(2,1)}, u32[]{:S(2)}, u32[]{:S(2)}) collective-permute-start(bf16[128,3072]{1,0:T(8,128)(2,1)} %bitcast.119), channel_id=1, source_target_pairs={{0,12},{4,0},{8,4},{12,8},{1,13},{5,1},{9,5},{13,9},{2,14},{6,2},{... | collective-permute-start | bytes 2359304 | tf_op jit(solution)/shard_map/ppermute | solution.py:115
  6.0 1.0 constant_dynamic-update-slice_fusion.1
  7.0 1.0 constant_dynamic-update-slice_fusion
  8.6 1.0 pad_maximum_fusion
  9.7 1.6 collective-permute-start
  11.3 2.6 %collective-permute-start.1 = (bf16[194048]{0:T(1024)(128)(2,1)}, bf16[194048]{0:T(1024)(128)(2,1)}, u32[]{:S(2)}, u32[]{:S(2)}) collective-permute-start(bf16[194048]{0:T(1024)(128)(2,1)} %get-tuple-element.29), channel_id=1, source_target_pairs={{0,2},{1,3},{2,0},{3,1},{4,6},{5,7},{6,4},{7,5},{8,10},{9,11},{10,... | collective-permute-start | bytes 1164296 | tf_op jit(solution)/shard_map/ppermute | solution.py:115
  13.9 1.3 collective-permute-start.2
  17.5 6.2 %collective-permute-done = bf16[194048]{0:T(1024)(128)(2,1)S(1)} collective-permute-done((bf16[194048]{0:T(1024)(128)(2,1)}, bf16[194048]{0:T(1024)(128)(2,1)S(1)}, u32[]{:S(2)}, u32[]{:S(2)}) %collective-permute-start) | collective-permute-done | bytes 388128 | tf_op jit(solution)/shard_map/ppermute | solution.py:115
  23.9 15.9 %collective-permute-done.1 = bf16[194048]{0:T(1024)(128)(2,1)} collective-permute-done((bf16[194048]{0:T(1024)(128)(2,1)}, bf16[194048]{0:T(1024)(128)(2,1)}, u32[]{:S(2)}, u32[]{:S(2)}) %collective-permute-start.1) | collective-permute-done | bytes 388128 | tf_op jit(solution)/shard_map/ppermute | solution.py:115
  39.8 1.5 collective-permute-start.6
  48.8 1.4 dynamic-slice_bitcast_fusion
  58.7 1.8 constant_dynamic-slice_fusion
  62.3 10.3 %fusion.2 = f32[512,1536]{1,0:T(8,128)S(1)} fusion(bf16[1536,3072]{1,0:T(8,128)(2,1)} %param.10, bf16[128,3072]{1,0:T(8,128)(2,1)} %collective-permute-done.5, bf16[128,3072]{1,0:T(8,128)(2,1)} %collective-permute-done.4, bf16[128,3072]{1,0:T(8,128)(2,1)} %collective-permute-done.3, bf16[128,3072]{1,0:T(8,128)(2,1)S(1)} %bitcast.122), kind=kOutput, calls=%fused_computation.2 | convolution fusion | flops 4844421120 | bytes 15728640 | tf_op jit(solution)/shard_map/dot_general | solution.py:228
  73.4 7.0 %collective-permute-start.9 = (bf16[512,384]{1,0:T(8,128)(2,1)S(1)}, bf16[512,384]{1,0:T(8,128)(2,1)S(1)}, u32[]{:S(2)}, u32[]{:S(2)}) collective-permute-start(bf16[512,384]{1,0:T(8,128)(2,1)S(1)} %get-tuple-element.14), channel_id=1, source_target_pairs={{0,1},{1,2},{2,3},{3,0},{4,5},{5,6},{6,7},{7,4},{8,9},{9,10},{10,1... | collective-permute-start | bytes 1179656 | tf_op jit(solution)/shard_map/ppermute | solution.py:115
  80.4 3.4 %collective-permute-start.8 = (bf16[512,384]{1,0:T(8,128)(2,1)S(1)}, bf16[512,384]{1,0:T(8,128)(2,1)S(1)}, u32[]{:S(2)}, u32[]{:S(2)}) collective-permute-start(bf16[512,384]{1,0:T(8,128)(2,1)S(1)} %get-tuple-element.15), channel_id=1, source_target_pairs={{0,2},{1,3},{2,0},{3,1},{4,6},{5,7},{6,4},{7,5},{8,10},{9,11},{10,... | collective-permute-start | bytes 1179656 | tf_op jit(solution)/shard_map/ppermute | solution.py:115
  83.8 2.1 constant_dynamic-update-slice_fusion.15
  85.9 2.1 constant_dynamic-update-slice_fusion.14
  88.0 2.1 constant_dynamic-update-slice_fusion.13
  90.1 2.1 constant_dynamic-update-slice_fusion.12
  93.8 16.3 %collective-permute-done.8 = bf16[512,384]{1,0:T(8,128)(2,1)S(1)} collective-permute-done((bf16[512,384]{1,0:T(8,128)(2,1)S(1)}, bf16[512,384]{1,0:T(8,128)(2,1)S(1)}, u32[]{:S(2)}, u32[]{:S(2)}) %collective-permute-start.8) | collective-permute-done | bytes 393248 | tf_op jit(solution)/shard_map/ppermute | solution.py:115
  110.5 1.4 fusion.35
  111.9 1.1 multiply_reduce_fusion.1
  113.0 7.5 %collective-permute-start.11 = (bf16[512,384]{0,1:T(8,128)(2,1)}, bf16[512,384]{0,1:T(8,128)(2,1)}, u32[]{:S(2)}, u32[]{:S(2)}) collective-permute-start(bf16[512,384]{0,1:T(8,128)(2,1)} %bitcast.10), channel_id=1, source_target_pairs={{0,3},{1,0},{2,1},{3,2},{4,7},{5,4},{6,5},{7,6},{8,11},{9,8},{10,9... | collective-permute-start | bytes 1179656 | tf_op jit(solution)/shard_map/ppermute | solution.py:115
  120.5 3.0 %collective-permute-start.13 = (bf16[512,384]{0,1:T(8,128)(2,1)}, bf16[512,384]{0,1:T(8,128)(2,1)}, u32[]{:S(2)}, u32[]{:S(2)}) collective-permute-start(bf16[512,384]{0,1:T(8,128)(2,1)} %bitcast.10), channel_id=1, source_target_pairs={{0,2},{1,3},{2,0},{3,1},{4,6},{5,7},{6,4},{7,5},{8,10},{9,11},{10,... | collective-permute-start | bytes 1179656 | tf_op jit(solution)/shard_map/ppermute | solution.py:115
  123.5 1.1 reshape.125
  124.6 1.7 multiply_convert_fusion
  126.9 1.1 reshape.124
  128.8 1.8 constant_dynamic-slice_fusion.2
  133.6 2.1 constant_dynamic-update-slice_fusion.11
  136.2 2.1 constant_dynamic-update-slice_fusion.10
  138.3 1.5 collective-permute-start.10
  139.8 18.4 %collective-permute-done.13 = bf16[512,384]{0,1:T(8,128)(2,1)} collective-permute-done((bf16[512,384]{0,1:T(8,128)(2,1)}, bf16[512,384]{0,1:T(8,128)(2,1)}, u32[]{:S(2)}, u32[]{:S(2)}) %collective-permute-start.13) | collective-permute-done | bytes 393248 | tf_op jit(solution)/shard_map/ppermute | solution.py:115
  158.7 1.5 collective-permute-start.14
  160.7 2.1 constant_dynamic-update-slice_fusion.9
  162.8 7.5 %fusion.17 = f32[364,3072]{1,0:T(8,128)} fusion(bf16[1024,3072]{1,0:T(8,128)(2,1)} %constant_dynamic-update-slice_fusion.9, bf16[512,364]{1,0:T(8,128)(2,1)S(1)} %collective-permute-done.23, bf16[512,364]{1,0:T(8,128)(2,1)S(1)} %bitcast.118), kind=kOutput, calls=%fused_computation.39 | convolution fusion | flops 2291580928 | bytes 11509760 | tf_op jit(solution)/shard_map/dot_general | solution.py:11
  170.3 1.1 fusion.28
  171.4 1.1 fusion.26
  172.5 6.4 %collective-permute-done.14 = bf16[512,384]{0,1:T(8,128)(2,1)S(1)} collective-permute-done((bf16[512,384]{0,1:T(8,128)(2,1)}, bf16[512,384]{0,1:T(8,128)(2,1)S(1)}, u32[]{:S(2)}, u32[]{:S(2)}) %collective-permute-start.14) | collective-permute-done | bytes 393248 | tf_op jit(solution)/shard_map/ppermute | solution.py:17
  178.9 1.1 fusion.24
  180.0 5.6 %collective-permute-done.16 = bf16[512,384]{0,1:T(8,128)(2,1)S(1)} collective-permute-done((bf16[512,384]{0,1:T(8,128)(2,1)S(1)}, bf16[512,384]{0,1:T(8,128)(2,1)S(1)}, u32[]{:S(2)}, u32[]{:S(2)}) %collective-permute-start.16) | collective-permute-done | bytes 393248 | tf_op jit(solution)/shard_map/ppermute | solution.py:17
  185.6 1.1 fusion.29
  186.7 1.1 fusion.27
  187.8 1.1 fusion.25
  189.7 2.0 collective-permute-start.18
  191.7 15.8 %fusion = f32[4,384,3072]{2,1,0:T(8,128)} fusion(bf16[4,1024,384]{1,2,0:T(8,128)(2,1)S(1)} %constant_dynamic-slice_fusion.1, bf16[1024,3072]{1,0:T(8,128)(2,1)} %constant_dynamic-update-slice_fusion.9), kind=kOutput, calls=%fused_computation | convolution fusion | flops 9663676416 | bytes 28311552 | tf_op jit(solution)/shard_map/dot_general | solution.py:274
  207.6 1.2 collective-permute-done.18
  208.9 7.2 %collective-permute-done.19 = bf16[3,128,384]{2,1,0:T(8,128)(2,1)S(1)} collective-permute-done((bf16[3,128,384]{2,1,0:T(8,128)(2,1)S(1)}, bf16[3,128,384]{2,1,0:T(8,128)(2,1)S(1)}, u32[]{:S(2)}, u32[]{:S(2)}) %collective-permute-start.19) | collective-permute-done | bytes 294944 | tf_op jit(solution)/shard_map/ppermute | solution.py:115
  216.1 1.5 slice_bitcast_fusion
  (120 shorter events, 33.3 us)
Async XLA Ops:
  0.6 61.6 %collective-permute-start.5 = (bf16[128,3072]{1,0:T(8,128)(2,1)}, bf16[128,3072]{1,0:T(8,128)(2,1)}, u32[]{:S(2)}, u32[]{:S(2)}) collective-permute-start(bf16[128,3072]{1,0:T(8,128)(2,1)} %bitcast.119), channel_id=1, source_target_pairs={{0,12},{4,0},{8,4},{12,8},{1,13},{5,1},{9,5},{13,9},{2,14},{6,2},{... | collective-permute-start | bytes 2359304 | tf_op jit(solution)/shard_map/ppermute | solution.py:115
  3.1 59.2 %collective-permute-start.4 = (bf16[128,3072]{1,0:T(8,128)(2,1)}, bf16[128,3072]{1,0:T(8,128)(2,1)}, u32[]{:S(2)}, u32[]{:S(2)}) collective-permute-start(bf16[128,3072]{1,0:T(8,128)(2,1)} %bitcast.120), channel_id=1, source_target_pairs={{0,8},{4,12},{8,0},{12,4},{1,9},{5,13},{9,1},{13,5},{2,10},{6,14},... | collective-permute-start | bytes 2359304 | tf_op jit(solution)/shard_map/ppermute | solution.py:115
  8.2 7.0 %copy-start.7 = (bf16[1,128,3072]{2,1,0:T(8,128)(2,1)S(1)}, bf16[1,128,3072]{2,1,0:T(8,128)(2,1)}, u32[]{:S(2)}) copy-start(bf16[1,128,3072]{2,1,0:T(8,128)(2,1)} %param.11) | copy-start | bytes 2359300
  9.7 14.0 %collective-permute-start = (bf16[194048]{0:T(1024)(128)(2,1)}, bf16[194048]{0:T(1024)(128)(2,1)S(1)}, u32[]{:S(2)}, u32[]{:S(2)}) collective-permute-start(bf16[194048]{0:T(1024)(128)(2,1)} %get-tuple-element.30), channel_id=1, source_target_pairs={{0,1},{1,2},{2,3},{3,0},{4,5},{5,6},{6,7},{7,4},{8,9},{9,10},{10,1... | collective-permute-start | bytes 1164296 | tf_op jit(solution)/shard_map/ppermute | solution.py:115
  11.3 28.5 %collective-permute-start.1 = (bf16[194048]{0:T(1024)(128)(2,1)}, bf16[194048]{0:T(1024)(128)(2,1)}, u32[]{:S(2)}, u32[]{:S(2)}) collective-permute-start(bf16[194048]{0:T(1024)(128)(2,1)} %get-tuple-element.29), channel_id=1, source_target_pairs={{0,2},{1,3},{2,0},{3,1},{4,6},{5,7},{6,4},{7,5},{8,10},{9,11},{10,... | collective-permute-start | bytes 1164296 | tf_op jit(solution)/shard_map/ppermute | solution.py:115
  13.9 28.6 %collective-permute-start.2 = (bf16[194048]{0:T(1024)(128)(2,1)}, bf16[194048]{0:T(1024)(128)(2,1)}, u32[]{:S(2)}, u32[]{:S(2)}) collective-permute-start(bf16[194048]{0:T(1024)(128)(2,1)} %get-tuple-element.28), channel_id=1, source_target_pairs={{0,3},{1,0},{2,1},{3,2},{4,7},{5,4},{6,5},{7,6},{8,11},{9,8},{10,9... | collective-permute-start | bytes 1164296 | tf_op jit(solution)/shard_map/ppermute | solution.py:115
  23.7 16.1 %copy-start.8 = (bf16[194048]{0:T(1024)(128)(2,1)}, bf16[194048]{0:T(1024)(128)(2,1)S(1)}, u32[]{:S(2)}) copy-start(bf16[194048]{0:T(1024)(128)(2,1)S(1)} %collective-permute-done) | copy-start | bytes 1164292
  23.7 38.5 %collective-permute-start.3 = (bf16[128,3072]{1,0:T(8,128)(2,1)S(1)}, bf16[128,3072]{1,0:T(8,128)(2,1)}, u32[]{:S(2)}, u32[]{:S(2)}) collective-permute-start(bf16[128,3072]{1,0:T(8,128)(2,1)S(1)} %bitcast.121), channel_id=1, source_target_pairs={{0,4},{4,8},{8,12},{12,0},{1,5},{5,9},{9,13},{13,1},{2,6},{6,10},{... | collective-permute-start | bytes 2359304 | tf_op jit(solution)/shard_map/ppermute | solution.py:115
  39.8 32.8 %collective-permute-start.6 = (bf16[1,128,3072]{2,1,0:T(8,128)(2,1)S(1)}, bf16[1,128,3072]{2,1,0:T(8,128)(2,1)}, u32[]{:S(2)}, u32[]{:S(2)}) collective-permute-start(bf16[1,128,3072]{2,1,0:T(8,128)(2,1)S(1)} %copy-done.7), channel_id=1, source_target_pairs={{0,16},{16,0},{1,17},{17,1},{2,18},{18,2},{3,19},{19,3},{4,20},{20... | collective-permute-start | bytes 2359304 | tf_op jit(solution)/shard_map/ppermute | solution.py:17
  50.3 1.3 slice-start
  50.7 9.8 %copy-start.2 = (bf16[512,3,128]{0,2,1:T(8,128)(2,1)}, bf16[512,3,128]{0,2,1:T(8,128)(2,1)S(1)}, u32[]{:S(2)}) copy-start(bf16[512,3,128]{0,2,1:T(8,128)(2,1)S(1)} %squeeze.44) | copy-start | bytes 1179652
  51.2 9.4 %copy-start = (bf16[512,3,128]{0,2,1:T(8,128)(2,1)}, bf16[512,3,128]{0,2,1:T(8,128)(2,1)S(1)}, u32[]{:S(2)}) copy-start(bf16[512,3,128]{0,2,1:T(8,128)(2,1)S(1)} %squeeze.43) | copy-start | bytes 1179652
  51.6 60.3 %copy-start.4 = (bf16[512,3,128]{0,2,1:T(8,128)(2,1)}, bf16[512,3,128]{0,2,1:T(8,128)(2,1)S(1)}, u32[]{:S(2)}) copy-start(bf16[512,3,128]{0,2,1:T(8,128)(2,1)S(1)} %squeeze.46) | copy-start | bytes 1179652
  72.6 61.0 %collective-permute-start.20 = (bf16[128,3072]{1,0:T(8,128)(2,1)}, bf16[128,3072]{1,0:T(8,128)(2,1)}, u32[]{:S(2)}, u32[]{:S(2)}) collective-permute-start(bf16[128,3072]{1,0:T(8,128)(2,1)} %bitcast.27), channel_id=1, source_target_pairs={{0,4},{4,8},{8,12},{12,0},{1,5},{5,9},{9,13},{13,1},{2,6},{6,10},{... | collective-permute-start | bytes 2359304 | tf_op jit(solution)/shard_map/ppermute | solution.py:115
  72.6 63.0 %collective-permute-start.21 = (bf16[128,3072]{1,0:T(8,128)(2,1)}, bf16[128,3072]{1,0:T(8,128)(2,1)}, u32[]{:S(2)}, u32[]{:S(2)}) collective-permute-start(bf16[128,3072]{1,0:T(8,128)(2,1)} %bitcast.27), channel_id=1, source_target_pairs={{0,8},{4,12},{8,0},{12,4},{1,9},{5,13},{9,1},{13,5},{2,10},{6,14},... | collective-permute-start | bytes 2359304 | tf_op jit(solution)/shard_map/ppermute | solution.py:115
  73.4 19.5 %collective-permute-start.9 = (bf16[512,384]{1,0:T(8,128)(2,1)S(1)}, bf16[512,384]{1,0:T(8,128)(2,1)S(1)}, u32[]{:S(2)}, u32[]{:S(2)}) collective-permute-start(bf16[512,384]{1,0:T(8,128)(2,1)S(1)} %get-tuple-element.14), channel_id=1, source_target_pairs={{0,1},{1,2},{2,3},{3,0},{4,5},{5,6},{6,7},{7,4},{8,9},{9,10},{10,1... | collective-permute-start | bytes 1179656 | tf_op jit(solution)/shard_map/ppermute | solution.py:115
  80.4 29.7 %collective-permute-start.8 = (bf16[512,384]{1,0:T(8,128)(2,1)S(1)}, bf16[512,384]{1,0:T(8,128)(2,1)S(1)}, u32[]{:S(2)}, u32[]{:S(2)}) collective-permute-start(bf16[512,384]{1,0:T(8,128)(2,1)S(1)} %get-tuple-element.15), channel_id=1, source_target_pairs={{0,2},{1,3},{2,0},{3,1},{4,6},{5,7},{6,4},{7,5},{8,10},{9,11},{10,... | collective-permute-start | bytes 1179656 | tf_op jit(solution)/shard_map/ppermute | solution.py:115
  83.8 26.3 %collective-permute-start.7 = (bf16[512,384]{1,0:T(8,128)(2,1)S(1)}, bf16[512,384]{1,0:T(8,128)(2,1)S(1)}, u32[]{:S(2)}, u32[]{:S(2)}) collective-permute-start(bf16[512,384]{1,0:T(8,128)(2,1)S(1)} %get-tuple-element.13), channel_id=1, source_target_pairs={{0,3},{1,0},{2,1},{3,2},{4,7},{5,4},{6,5},{7,6},{8,11},{9,8},{10,9... | collective-permute-start | bytes 1179656 | tf_op jit(solution)/shard_map/ppermute | solution.py:115
  92.9 67.3 %collective-permute-start.22 = (bf16[128,3072]{1,0:T(8,128)(2,1)}, bf16[128,3072]{1,0:T(8,128)(2,1)}, u32[]{:S(2)}, u32[]{:S(2)}) collective-permute-start(bf16[128,3072]{1,0:T(8,128)(2,1)} %bitcast.27), channel_id=1, source_target_pairs={{0,12},{4,0},{8,4},{12,8},{1,13},{5,1},{9,5},{13,9},{2,14},{6,2},{... | collective-permute-start | bytes 2359304 | tf_op jit(solution)/shard_map/ppermute | solution.py:115
  113.0 25.3 %collective-permute-start.11 = (bf16[512,384]{0,1:T(8,128)(2,1)}, bf16[512,384]{0,1:T(8,128)(2,1)}, u32[]{:S(2)}, u32[]{:S(2)}) collective-permute-start(bf16[512,384]{0,1:T(8,128)(2,1)} %bitcast.10), channel_id=1, source_target_pairs={{0,3},{1,0},{2,1},{3,2},{4,7},{5,4},{6,5},{7,6},{8,11},{9,8},{10,9... | collective-permute-start | bytes 1179656 | tf_op jit(solution)/shard_map/ppermute | solution.py:115
  120.5 37.7 %collective-permute-start.13 = (bf16[512,384]{0,1:T(8,128)(2,1)}, bf16[512,384]{0,1:T(8,128)(2,1)}, u32[]{:S(2)}, u32[]{:S(2)}) collective-permute-start(bf16[512,384]{0,1:T(8,128)(2,1)} %bitcast.10), channel_id=1, source_target_pairs={{0,2},{1,3},{2,0},{3,1},{4,6},{5,7},{6,4},{7,5},{8,10},{9,11},{10,... | collective-permute-start | bytes 1179656 | tf_op jit(solution)/shard_map/ppermute | solution.py:115
  124.6 1.7 copy-start.3
  126.3 1.8 copy-start.1
  130.5 1.4 copy-start.5
  133.1 2.5 %copy-start.6 = (bf16[4,128,364]{2,1,0:T(8,128)(2,1)S(1)}, bf16[4,128,364]{2,1,0:T(8,128)(2,1)}, u32[]{:S(2)}) copy-start(bf16[4,128,364]{2,1,0:T(8,128)(2,1)} %constant_dynamic-slice_fusion) | copy-start | bytes 1118212
  133.5 25.2 %collective-permute-start.15 = (bf16[512,384]{0,1:T(8,128)(2,1)}, bf16[512,384]{0,1:T(8,128)(2,1)S(1)}, u32[]{:S(2)}, u32[]{:S(2)}) collective-permute-start(bf16[512,384]{0,1:T(8,128)(2,1)} %bitcast.10), channel_id=1, source_target_pairs={{0,1},{1,2},{2,3},{3,0},{4,5},{5,6},{6,7},{7,4},{8,9},{9,10},{10,1... | collective-permute-start | bytes 1179656 | tf_op jit(solution)/shard_map/ppermute | solution.py:115
  135.7 27.2 %collective-permute-start.23 = (bf16[512,364]{1,0:T(8,128)(2,1)S(1)}, bf16[512,364]{1,0:T(8,128)(2,1)S(1)}, u32[]{:S(2)}, u32[]{:S(2)}) collective-permute-start(bf16[512,364]{1,0:T(8,128)(2,1)S(1)} %bitcast.117), channel_id=1, source_target_pairs={{0,16},{16,0},{1,17},{17,1},{2,18},{18,2},{3,19},{19,3},{4,20},{20... | collective-permute-start | bytes 1118216 | tf_op jit(solution)/shard_map/ppermute | solution.py:17
  138.3 32.0 %collective-permute-start.10 = (bf16[512,384]{0,1:T(8,128)(2,1)}, bf16[512,384]{0,1:T(8,128)(2,1)S(1)}, u32[]{:S(2)}, u32[]{:S(2)}) collective-permute-start(bf16[512,384]{0,1:T(8,128)(2,1)} %bitcast.10), channel_id=1, source_target_pairs={{0,16},{16,0},{1,17},{17,1},{2,18},{18,2},{3,19},{19,3},{4,20},{20... | collective-permute-start | bytes 1179656 | tf_op jit(solution)/shard_map/ppermute | solution.py:17
  158.2 13.2 %collective-permute-start.12 = (bf16[512,384]{0,1:T(8,128)(2,1)}, bf16[512,384]{0,1:T(8,128)(2,1)S(1)}, u32[]{:S(2)}, u32[]{:S(2)}) collective-permute-start(bf16[512,384]{0,1:T(8,128)(2,1)} %collective-permute-done.11), channel_id=1, source_target_pairs={{0,16},{16,0},{1,17},{17,1},{2,18},{18,2},{3,19},{19,3},{4,20},{20... | collective-permute-start | bytes 1179656 | tf_op jit(solution)/shard_map/ppermute | solution.py:17
  158.7 20.2 %collective-permute-start.14 = (bf16[512,384]{0,1:T(8,128)(2,1)}, bf16[512,384]{0,1:T(8,128)(2,1)S(1)}, u32[]{:S(2)}, u32[]{:S(2)}) collective-permute-start(bf16[512,384]{0,1:T(8,128)(2,1)} %collective-permute-done.13), channel_id=1, source_target_pairs={{0,16},{16,0},{1,17},{17,1},{2,18},{18,2},{3,19},{19,3},{4,20},{20... | collective-permute-start | bytes 1179656 | tf_op jit(solution)/shard_map/ppermute | solution.py:17
  160.2 25.3 %collective-permute-start.16 = (bf16[512,384]{0,1:T(8,128)(2,1)S(1)}, bf16[512,384]{0,1:T(8,128)(2,1)S(1)}, u32[]{:S(2)}, u32[]{:S(2)}) collective-permute-start(bf16[512,384]{0,1:T(8,128)(2,1)S(1)} %collective-permute-done.15), channel_id=1, source_target_pairs={{0,16},{16,0},{1,17},{17,1},{2,18},{18,2},{3,19},{19,3},{4,20},{20... | collective-permute-start | bytes 1179656 | tf_op jit(solution)/shard_map/ppermute | solution.py:17
  189.4 18.1 %collective-permute-start.17 = (bf16[3,128,384]{2,1,0:T(8,128)(2,1)S(1)}, bf16[3,128,384]{2,1,0:T(8,128)(2,1)S(1)}, u32[]{:S(2)}, u32[]{:S(2)}) collective-permute-start(bf16[3,128,384]{2,1,0:T(8,128)(2,1)S(1)} %get-tuple-element.21), channel_id=1, source_target_pairs={{0,3},{1,0},{2,1},{3,2},{4,7},{5,4},{6,5},{7,6},{8,11},{9,8},{10,9... | collective-permute-start | bytes 884744 | tf_op jit(solution)/shard_map/ppermute | solution.py:115
  189.7 19.1 %collective-permute-start.18 = (bf16[3,128,384]{2,1,0:T(8,128)(2,1)S(1)}, bf16[3,128,384]{2,1,0:T(8,128)(2,1)S(1)}, u32[]{:S(2)}, u32[]{:S(2)}) collective-permute-start(bf16[3,128,384]{2,1,0:T(8,128)(2,1)S(1)} %get-tuple-element.20), channel_id=1, source_target_pairs={{0,2},{1,3},{2,0},{3,1},{4,6},{5,7},{6,4},{7,5},{8,10},{9,11},{10,... | collective-permute-start | bytes 884744 | tf_op jit(solution)/shard_map/ppermute | solution.py:115
  207.5 8.5 %collective-permute-start.19 = (bf16[3,128,384]{2,1,0:T(8,128)(2,1)S(1)}, bf16[3,128,384]{2,1,0:T(8,128)(2,1)S(1)}, u32[]{:S(2)}, u32[]{:S(2)}) collective-permute-start(bf16[3,128,384]{2,1,0:T(8,128)(2,1)S(1)} %get-tuple-element.19), channel_id=1, source_target_pairs={{0,1},{1,2},{2,3},{3,0},{4,5},{5,6},{6,7},{7,4},{8,9},{9,10},{10,1... | collective-permute-start | bytes 884744 | tf_op jit(solution)/shard_map/ppermute | solution.py:115

commit v8 on v7

--- a/solution.py
+++ b/solution.py
@@ -1,7 +1,11 @@
+import functools
+
 import jax
 import numpy as np
 import jax.numpy as jnp
 from jax import lax
+from jax.experimental import pallas as pl
+from jax.experimental.pallas import tpu as pltpu
 from jax.sharding import PartitionSpec as P
 
 DH = 128
@@ -196,6 +200,41 @@
     return stacked.reshape((n * x.shape[0],) + x.shape[1:])
 
 
+def _wg_kernel(nblk, blk, shift_ref, lhs_ref, *refs):
+    grads, out_ref = refs[:nblk], refs[nblk]
+    acc = None
+    for k in range(nblk):
+        part = lax.dot_general(
+            lhs_ref[0, k * blk:(k + 1) * blk, :], grads[k][...],
+            (((0,), (0,)), ((), ())), preferred_element_type=jnp.float32,
+        )
+        acc = part if acc is None else acc + part
+    out_ref[...] = acc
+
+
+def weight_grad(lhs, grads, shift, tile=768):
+    slots, toks, m = lhs.shape
+    nblk = len(grads)
+    blk, cols = grads[0].shape
+    tile = tile if cols % tile == 0 else cols
+    grid = (slots, cols // tile)
+    in_specs = [pl.BlockSpec((1, toks, m), lambda s, j, sh: (s, 0, 0))] + [
+        pl.BlockSpec((blk, tile), lambda s, j, sh: (0, j)) for _ in range(nblk)
+    ]
+    out_spec = pl.BlockSpec((m, tile), lambda s, j, sh: ((s + sh[0]) % slots, j))
+    return pl.pallas_call(
+        functools.partial(_wg_kernel, nblk, blk),
+        out_shape=jax.ShapeDtypeStruct((slots * m, cols), jnp.float32),
+        grid_spec=pltpu.PrefetchScalarGridSpec(
+            num_scalar_prefetch=1, grid=grid, in_specs=in_specs, out_specs=out_spec
+        ),
+        cost_estimate=pl.CostEstimate(
+            flops=2 * slots * toks * m * cols, transcendentals=0,
+            bytes_accessed=2 * slots * toks * m + 2 * toks * cols + 4 * slots * m * cols,
+        ),
+    )(jnp.reshape(shift, (1,)).astype(jnp.int32), lhs, *grads)
+
+
 def roll_blocks(x, shift):
     n = x.shape[0]
     return lax.dynamic_slice_in_dim(jnp.concatenate([x, x], 0), shift % n, n, 0)
@@ -210,7 +249,6 @@
     heads = width // DH
     patch_here = patches[0]
     grad_blocks = [output_grad[0]] + [shifted(output_grad[0], "row", s) for s in range(1, n)]
-    dense_grad = jnp.concatenate(grad_blocks, 0)
     grad_other = swap_dp(output_grad)
     qkv = jnp.stack([queries[0], attn_keys[0], attn_values[0]], 0)
     part = lambda g: lax.dynamic_slice_in_dim(qkv, g * width, width, 2)
@@ -225,9 +263,10 @@
     rows = n * tokens
     qkv_h = jnp.transpose(qkv_h, (1, 0, 2, 3)).reshape(3, rows, heads, DH)
     local_query, all_keys, all_values = qkv_h[0], qkv_h[1], qkv_h[2]
-    grad_partial = lax.dot_general(
-        dense_grad, out_weight, (((1,), (1,)), ((), ())), preferred_element_type=jnp.float32
-    )
+    grad_partial = [
+        lax.dot_general(g, out_weight, (((1,), (1,)), ((), ())), preferred_element_type=jnp.float32)
+        for g in grad_blocks
+    ]
     grad_partial, grad_other = lax.optimization_barrier((grad_partial, grad_other))
     other_blocks = [grad_other[0]] + [shifted(grad_other[0], "row", s) for s in range(1, n)]
     scores = (
@@ -240,7 +279,12 @@
     attn_out = jnp.einsum(
         "hqk,khd->qhd", attn_probs, all_values, preferred_element_type=jnp.float32
     ).astype(jnp.bfloat16)
-    attn_grad = sum_to_heads(grad_partial, "col").astype(jnp.bfloat16)
+    group_rows = lambda g: jnp.concatenate([group_cols(p, "col", g) for p in grad_partial], 0)
+    attn_grad = group_rows(me)
+    for s in range(1, n):
+        sent = group_rows((me - s) % n).astype(jnp.bfloat16)
+        attn_grad = attn_grad + shifted(sent, "col", -s % n).astype(jnp.float32)
+    attn_grad = attn_grad.astype(jnp.bfloat16)
     grad_heads = attn_grad.reshape(rows, heads, DH)
     prob_grad = jnp.einsum(
         "qhd,khd->hqk", grad_heads, all_values, preferred_element_type=jnp.float32
@@ -267,14 +311,12 @@
     out_pieces = [own_pair] + [
         (got, swap_dp(got)) for got in (shifted(sent_out, "col", -s % n) for s in range(1, n))
     ]
-    out_both = roll_blocks(
-        jnp.stack([jnp.concatenate(p, 0) for p in out_pieces], 0), -me
-    )
-    grad_both = jnp.concatenate([dense_grad] + other_blocks, 0)
-    out_weight_grad = lax.dot_general(
-        out_both, grad_both, (((1,), (0,)), ((), ())), preferred_element_type=jnp.float32
-    ).reshape(width_all, -1)
-    embed_weight_grad = contract_rows(jnp.concatenate([every_patch, other_patch], 0), grad_both)
+    out_both = jnp.stack([jnp.concatenate(p, 0) for p in out_pieces], 0)
+    grad_both = grad_blocks + other_blocks
+    out_weight_grad = weight_grad(out_both, grad_both, me)
+    embed_weight_grad = weight_grad(
+        jnp.concatenate([every_patch, other_patch], 0)[None], grad_both, jnp.int32(0)
+    )
     grad_list = [g.reshape(n, tokens, width) for g in (query_grad, key_grad, value_grad)]
     sendable = roll_blocks(
         jnp.stack([g.astype(jnp.bfloat16) for g in grad_list], 1), rank - me

time: 219 us -> 267 us (1.22)
  Pallas kernels: 0 us -> 38.3 us
  waiting for transfers between devices: 77.9 us -> 58.9 us
  local copies, waits for them, and re-layouts: 49.6 us -> 67.6 us
  starting transfers between devices: 39.5 us -> 49.6 us
  matrix products: 39.4 us -> 32.3 us
  other arithmetic: 10 us -> 16.9 us
    pallas_call x0 -> x2, Pallas kernels: none -> 38.3 us  [weight_grad(): pl.pallas_call(functools.partial(_wg_kernel, nblk, blk), out_shape=jax.Sh...]
    ppermute x18, waiting for transfers between devices: 65.9 us -> 43.5 us  [shifted(): return lax.ppermute(x, axis, [(j, (j + step) % n) for j in range(n)])]
    ppermute x18, starting transfers between devices: 33.4 us -> 43.2 us  [shifted(): return lax.ppermute(x, axis, [(j, (j + step) % n) for j in range(n)])]
    dot_general x3 -> x4, matrix products: 33.6 us -> 24.3 us  [body_heads(): lax.dot_general(g, out_weight, (((1,), (1,)), ((), ())), preferred_elemen...]
    another operation x0 -> x5, other arithmetic: none -> 6.68 us  [body_heads(): out_both = jnp.stack([jnp.concatenate(p, 0) for p in out_pieces], 0)]
    unnamed x7 -> x1, other arithmetic: 6.61 us -> 0.01 us
    slice x7 -> x6, local copies, waits for them, and re-layouts: 3.79 us -> 9.13 us  [unflat(): out.append(vector[..., at:at + size].reshape(vector.shape[:-1] + shape))]
    unnamed x45 -> x76, local copies, waits for them, and re-layouts: 26.7 us -> 22 us
  transfers between devices with their start and end apart: 24 -> 24, of which waited for: 9 -> 8; matrix products, arithmetic and copies ran while one was open for 43% -> 41% of each run, Pallas kernels for 0% -> 14%
where the time goes in v8:
time: 267 us; the launch traced here: 265 us
  local copies, waits for them, and re-layouts  67.6 us (25%)
  waiting for transfers between devices  58.9 us (22%)
  starting transfers between devices  49.6 us (19%)
  Pallas kernels  38.3 us (14%)
  matrix products  32.3 us (12%)
  other arithmetic  16.9 us (6%)
    ppermute x18, waiting for transfers between devices, shifted(): return lax.ppermute(x, axis, [(j, (j + step) % n) for j in range(n)])  43.5 us
    ppermute x18, starting transfers between devices, shifted(): return lax.ppermute(x, axis, [(j, (j + step) % n) for j in range(n)])  43.2 us
    pallas_call x2, Pallas kernels, weight_grad(): pl.pallas_call(functools.partial(_wg_kernel, nblk, blk), out_shape=jax.Sh...  38.3 us
    dot_general x4, matrix products, body_heads(): lax.dot_general(g, out_weight, (((1,), (1,)), ((), ())), preferred_elemen...  24.3 us
    unnamed x76, local copies, waits for them, and re-layouts  22 us
    ppermute x6, waiting for transfers between devices, swap_dp(): return lax.ppermute(x, 'dp', [(0, 1), (1, 0)])  15.4 us
    slice x6, local copies, waits for them, and re-layouts, unflat(): out.append(vector[..., at:at + size].reshape(vector.shape[:-1] + shape))  9.13 us
    another operation x5, other arithmetic, body_heads(): out_both = jnp.stack([jnp.concatenate(p, 0) for p in out_pieces], 0)  6.68 us
  transfers between devices with their start and end apart: 24, of which 8 were waited for; matrix products, arithmetic and copies ran while one was open for 41% of the time, Pallas kernels for 14%

profile of v8, /device:TPU:0, one launch (start us, length us, event | category | flops | bytes accessed | tf_op | source)
XLA Modules:
  0.0 264.8 jit_solution(4951356921563347416)
XLA Ops:
  1.1 2.6 collective-permute-start.4
  9.5 1.9 reshape.121
  12.4 2.1 pad_maximum_fusion.1
  14.6 1.6 collective-permute-start
  16.1 2.6 collective-permute-start.1
  21.5 7.8 %fusion.11 = f32[128,1536]{1,0:T(8,128)} fusion(bf16[1536,3072]{1,0:T(8,128)(2,1)} %param.10, bf16[1,128,3072]{2,1,0:T(8,128)(2,1)S(1)} %copy-done.9), kind=kOutput, calls=%fused_computation.93 | convolution fusion | flops 1207959552 | bytes 11010048 | tf_op jit(solution)/shard_map/dot_general | solution.py:267
  31.7 13.1 %collective-permute-done.1 = bf16[194048]{0:T(1024)(128)(2,1)} collective-permute-done((bf16[194048]{0:T(1024)(128)(2,1)}, bf16[194048]{0:T(1024)(128)(2,1)}, u32[]{:S(2)}, u32[]{:S(2)}) %collective-permute-start.1) | collective-permute-done | bytes 388128 | tf_op jit(solution)/shard_map/ppermute | solution.py:119
  44.8 1.5 collective-permute-start.6
  46.3 1.7 slice.64
  49.1 1.7 slice.65
  50.8 1.8 stack_reshape.20
  54.1 1.7 constant_dynamic-update-slice_fusion.6
  61.9 1.7 slice.72
  63.6 1.8 stack_reshape.21
  65.4 1.5 slice.73
  66.9 1.8 stack_reshape.22
  68.7 1.5 slice.74
  70.2 1.8 stack_reshape.23
  72.0 1.5 constant_dynamic-update-slice_fusion.15
  73.6 1.5 constant_dynamic-update-slice_fusion.14
  75.1 1.5 constant_dynamic-update-slice_fusion.13
  77.3 1.5 constant_dynamic-update-slice_fusion.11
  78.8 1.5 constant_dynamic-update-slice_fusion.10
  80.4 1.5 constant_dynamic-update-slice_fusion.9
  81.9 1.8 constant_dynamic-slice_fusion
  85.5 7.2 %fusion.17 = f32[128,1536]{1,0:T(8,128)S(1)} fusion(bf16[128,3072]{1,0:T(8,128)(2,1)S(1)} %collective-permute-done.3.refs_1_, bf16[1536,3072]{1,0:T(8,128)(2,1)} %param.10), kind=kOutput, calls=%fused_computation.99 | convolution fusion | flops 1207959552 | bytes 11010048 | tf_op jit(solution)/shard_map/dot_general | solution.py:267
  92.8 4.6 %fusion.18 = f32[128,1536]{1,0:T(8,128)S(1)} fusion(bf16[128,3072]{1,0:T(8,128)(2,1)} %collective-permute-done.4.refs_2_, bf16[1536,3072]{1,0:T(8,128)(2,1)S(1)} %bitcast.102), kind=kOutput, calls=%fused_computation.100 | convolution fusion | flops 1207959552 | bytes 11010048 | tf_op jit(solution)/shard_map/dot_general | solution.py:267
  97.4 4.7 %fusion.19 = f32[128,1536]{1,0:T(8,128)S(1)} fusion(bf16[128,3072]{1,0:T(8,128)(2,1)} %collective-permute-done.5.refs_3_, bf16[1536,3072]{1,0:T(8,128)(2,1)S(1)} %bitcast.102), kind=kOutput, calls=%fused_computation.101 | convolution fusion | flops 1207959552 | bytes 11010048 | tf_op jit(solution)/shard_map/dot_general | solution.py:267
  103.1 7.0 %collective-permute-start.9 = (bf16[512,384]{1,0:T(8,128)(2,1)}, bf16[512,384]{1,0:T(8,128)(2,1)}, u32[]{:S(2)}, u32[]{:S(2)}) collective-permute-start(bf16[512,384]{1,0:T(8,128)(2,1)} %pad_maximum_fusion.6), channel_id=1, source_target_pairs={{0,1},{1,2},{2,3},{3,0},{4,5},{5,6},{6,7},{7,4},{8,9},{9,10},{10,1... | collective-permute-start | bytes 1179656 | tf_op jit(solution)/shard_map/ppermute | solution.py:119
  110.9 3.4 %collective-permute-start.8 = (bf16[512,384]{1,0:T(8,128)(2,1)}, bf16[512,384]{1,0:T(8,128)(2,1)}, u32[]{:S(2)}, u32[]{:S(2)}) collective-permute-start(bf16[512,384]{1,0:T(8,128)(2,1)} %pad_maximum_fusion.5), channel_id=1, source_target_pairs={{0,2},{1,3},{2,0},{3,1},{4,6},{5,7},{6,4},{7,5},{8,10},{9,11},{10,... | collective-permute-start | bytes 1179656 | tf_op jit(solution)/shard_map/ppermute | solution.py:119
  116.6 2.2 maximum_bitcast_fusion.4.lhs_ref
  121.8 1.7 collective-permute-done.9
  123.5 15.0 %collective-permute-done.8 = bf16[512,384]{1,0:T(8,128)(2,1)} collective-permute-done((bf16[512,384]{1,0:T(8,128)(2,1)}, bf16[512,384]{1,0:T(8,128)(2,1)}, u32[]{:S(2)}, u32[]{:S(2)}) %collective-permute-start.8) | collective-permute-done | bytes 393248 | tf_op jit(solution)/shard_map/ppermute | solution.py:119
  140.1 1.6 fusion.16
  142.9 1.7 multiply_convert_fusion
  144.6 1.5 fusion.15
  147.1 8.9 %collective-permute-start.15 = (bf16[512,384]{1,0:T(8,128)(2,1)}, bf16[512,384]{1,0:T(8,128)(2,1)}, u32[]{:S(2)}, u32[]{:S(2)}) collective-permute-start(bf16[512,384]{1,0:T(8,128)(2,1)} %copy.80), channel_id=1, source_target_pairs={{0,1},{1,2},{2,3},{3,0},{4,5},{5,6},{6,7},{7,4},{8,9},{9,10},{10,1... | collective-permute-start | bytes 1179656 | tf_op jit(solution)/shard_map/ppermute | solution.py:119
  158.5 2.1 constant_dynamic-slice_fusion.1
  160.8 4.9 %collective-permute-done.15 = bf16[512,384]{1,0:T(8,128)(2,1)} collective-permute-done((bf16[512,384]{1,0:T(8,128)(2,1)}, bf16[512,384]{1,0:T(8,128)(2,1)}, u32[]{:S(2)}, u32[]{:S(2)}) %collective-permute-start.15) | collective-permute-done | bytes 393248 | tf_op jit(solution)/shard_map/ppermute | solution.py:119
  171.0 8.8 %collective-permute-done.13 = bf16[512,384]{1,0:T(8,128)(2,1)} collective-permute-done((bf16[512,384]{1,0:T(8,128)(2,1)}, bf16[512,384]{1,0:T(8,128)(2,1)}, u32[]{:S(2)}, u32[]{:S(2)}) %collective-permute-start.13) | collective-permute-done | bytes 393248 | tf_op jit(solution)/shard_map/ppermute | solution.py:119
  179.7 1.5 collective-permute-start.10
  188.3 9.0 %shard_map.102 = f32[364,3072]{1,0:T(8,128)} custom-call(s32[1]{0:T(128)} %constant.101.clone.1.shift_ref, bf16[1,1024,364]{2,1,0:T(8,128)(2,1)} %maximum_bitcast_fusion.4.lhs_ref, bf16[128,3072]{1,0:T(8,128)(2,1)} %bitcast.110, bf16[128,3072]{1,0:T(8,128)(2,1)} %copy-done.10, bf16[128,3072]{1,0:T(8,128)(2,1)} %collective-permute-done.4.refs_2_, ...), custom_call_target="tpu_custom_call" | custom-call | flops 2290089984 | bytes 11509760 | tf_op jit(solution)/shard_map/pallas_call | solution.py:225
  198.5 1.9 collective-permute-done.16
  201.7 7.2 %collective-permute-done.14 = bf16[512,384]{1,0:T(8,128)(2,1)} collective-permute-done((bf16[512,384]{1,0:T(8,128)(2,1)}, bf16[512,384]{1,0:T(8,128)(2,1)}, u32[]{:S(2)}, u32[]{:S(2)}) %collective-permute-start.14) | collective-permute-done | bytes 393248 | tf_op jit(solution)/shard_map/ppermute | solution.py:21
  210.1 6.2 %collective-permute-done.12 = bf16[512,384]{1,0:T(8,128)(2,1)} collective-permute-done((bf16[512,384]{1,0:T(8,128)(2,1)}, bf16[512,384]{1,0:T(8,128)(2,1)}, u32[]{:S(2)}, u32[]{:S(2)}) %collective-permute-start.12) | collective-permute-done | bytes 393248 | tf_op jit(solution)/shard_map/ppermute | solution.py:21
  217.5 1.9 pad_maximum_fusion.lhs_ref
  220.3 13.0 %collective-permute-start.17 = (bf16[3,128,384]{2,1,0:T(8,128)(2,1)}, bf16[3,128,384]{2,1,0:T(8,128)(2,1)S(1)}, u32[]{:S(2)}, u32[]{:S(2)}) collective-permute-start(bf16[3,128,384]{2,1,0:T(8,128)(2,1)} %get-tuple-element.24), channel_id=1, source_target_pairs={{0,3},{1,0},{2,1},{3,2},{4,7},{5,4},{6,5},{7,6},{8,11},{9,8},{10,9... | collective-permute-start | bytes 884744 | tf_op jit(solution)/shard_map/ppermute | solution.py:119
  233.8 29.3 %shard_map.101 = f32[1536,3072]{1,0:T(8,128)} custom-call(s32[1]{0:T(128)} %bitcast.27.shift_ref, bf16[4,1024,384]{2,1,0:T(8,128)(2,1)} %pad_maximum_fusion.lhs_ref, bf16[128,3072]{1,0:T(8,128)(2,1)} %bitcast.111, bf16[128,3072]{1,0:T(8,128)(2,1)} %copy-done.10, bf16[128,3072]{1,0:T(8,128)(2,1)} %collective-permute-done.4.refs_2_, ...), custom_call_target="tpu_custom_call" | custom-call | flops 9663676416 | bytes 28311552 | tf_op jit(solution)/shard_map/pallas_call | solution.py:225
  (159 shorter events, 57.0 us)
Async XLA Ops:
  0.6 84.8 %collective-permute-start.3 = (bf16[128,3072]{1,0:T(8,128)(2,1)}, bf16[128,3072]{1,0:T(8,128)(2,1)S(1)}, u32[]{:S(2)}, u32[]{:S(2)}) collective-permute-start(bf16[128,3072]{1,0:T(8,128)(2,1)} %bitcast.108), channel_id=1, source_target_pairs={{0,4},{4,8},{8,12},{12,0},{1,5},{5,9},{9,13},{13,1},{2,6},{6,10},{... | collective-permute-start | bytes 2359304 | tf_op jit(solution)/shard_map/ppermute | solution.py:119
  1.1 91.6 %collective-permute-start.4 = (bf16[128,3072]{1,0:T(8,128)(2,1)}, bf16[128,3072]{1,0:T(8,128)(2,1)}, u32[]{:S(2)}, u32[]{:S(2)}) collective-permute-start(bf16[128,3072]{1,0:T(8,128)(2,1)} %bitcast.109), channel_id=1, source_target_pairs={{0,8},{4,12},{8,0},{12,4},{1,9},{5,13},{9,1},{13,5},{2,10},{6,14},... | collective-permute-start | bytes 2359304 | tf_op jit(solution)/shard_map/ppermute | solution.py:119
  9.5 11.9 %copy-start.9 = (bf16[1,128,3072]{2,1,0:T(8,128)(2,1)S(1)}, bf16[1,128,3072]{2,1,0:T(8,128)(2,1)}, u32[]{:S(2)}) copy-start(bf16[1,128,3072]{2,1,0:T(8,128)(2,1)} %param.11) | copy-start | bytes 2359300
  14.6 14.7 %collective-permute-start = (bf16[194048]{0:T(1024)(128)(2,1)}, bf16[194048]{0:T(1024)(128)(2,1)S(1)}, u32[]{:S(2)}, u32[]{:S(2)}) collective-permute-start(bf16[194048]{0:T(1024)(128)(2,1)} %get-tuple-element.45), channel_id=1, source_target_pairs={{0,1},{1,2},{2,3},{3,0},{4,5},{5,6},{6,7},{7,4},{8,9},{9,10},{10,1... | collective-permute-start | bytes 1164296 | tf_op jit(solution)/shard_map/ppermute | solution.py:119
  16.1 28.6 %collective-permute-start.1 = (bf16[194048]{0:T(1024)(128)(2,1)}, bf16[194048]{0:T(1024)(128)(2,1)}, u32[]{:S(2)}, u32[]{:S(2)}) collective-permute-start(bf16[194048]{0:T(1024)(128)(2,1)} %get-tuple-element.44), channel_id=1, source_target_pairs={{0,2},{1,3},{2,0},{3,1},{4,6},{5,7},{6,4},{7,5},{8,10},{9,11},{10,... | collective-permute-start | bytes 1164296 | tf_op jit(solution)/shard_map/ppermute | solution.py:119
  18.7 30.4 %collective-permute-start.2 = (bf16[194048]{0:T(1024)(128)(2,1)}, bf16[194048]{0:T(1024)(128)(2,1)}, u32[]{:S(2)}, u32[]{:S(2)}) collective-permute-start(bf16[194048]{0:T(1024)(128)(2,1)} %get-tuple-element.43), channel_id=1, source_target_pairs={{0,3},{1,0},{2,1},{3,2},{4,7},{5,4},{6,5},{7,6},{8,11},{9,8},{10,9... | collective-permute-start | bytes 1164296 | tf_op jit(solution)/shard_map/ppermute | solution.py:119
  30.0 67.4 %collective-permute-start.5 = (bf16[128,3072]{1,0:T(8,128)(2,1)S(1)}, bf16[128,3072]{1,0:T(8,128)(2,1)}, u32[]{:S(2)}, u32[]{:S(2)}) collective-permute-start(bf16[128,3072]{1,0:T(8,128)(2,1)S(1)} %bitcast.112), channel_id=1, source_target_pairs={{0,12},{4,0},{8,4},{12,8},{1,13},{5,1},{9,5},{13,9},{2,14},{6,2},{... | collective-permute-start | bytes 2359304 | tf_op jit(solution)/shard_map/ppermute | solution.py:119
  44.8 57.3 %collective-permute-start.6 = (bf16[1,128,3072]{2,1,0:T(8,128)(2,1)S(1)}, bf16[1,128,3072]{2,1,0:T(8,128)(2,1)}, u32[]{:S(2)}, u32[]{:S(2)}) collective-permute-start(bf16[1,128,3072]{2,1,0:T(8,128)(2,1)S(1)} %copy-done.9), channel_id=1, source_target_pairs={{0,16},{16,0},{1,17},{17,1},{2,18},{18,2},{3,19},{19,3},{4,20},{20... | collective-permute-start | bytes 2359304 | tf_op jit(solution)/shard_map/ppermute | solution.py:21
  52.6 5.4 %copy-start.11 = (bf16[1,3,128,384]{3,2,1,0:T(8,128)(2,1)S(1)}, bf16[1,3,128,384]{3,2,1,0:T(8,128)(2,1)}, u32[]{:S(2)}) copy-start(bf16[1,3,128,384]{3,2,1,0:T(8,128)(2,1)} %stack_reshape.20) | copy-start | bytes 884740
  61.5 22.8 %copy-start.3 = (bf16[512,3,128]{0,2,1:T(8,128)(2,1)}, bf16[512,3,128]{0,2,1:T(8,128)(2,1)S(1)}, u32[]{:S(2)}) copy-start(bf16[512,3,128]{0,2,1:T(8,128)(2,1)S(1)} %squeeze.44) | copy-start | bytes 1179652
  61.9 23.0 %copy-start.1 = (bf16[512,3,128]{0,2,1:T(8,128)(2,1)}, bf16[512,3,128]{0,2,1:T(8,128)(2,1)S(1)}, u32[]{:S(2)}) copy-start(bf16[512,3,128]{0,2,1:T(8,128)(2,1)S(1)} %squeeze.43) | copy-start | bytes 1179652
  61.9 30.8 %slice-start = ((s8[9437184]{0:T(1024)(128)(4,1)}), s8[1048576]{0:T(1024)(128)(4,1)S(1)}, s32[]{:S(2)}) async-start(s8[9437184]{0:T(1024)(128)(4,1)} %bitcast.101), calls=%async_computation | async-start | bytes 2097152
  83.7 9.0 %slice-start.1 = ((s8[9437184]{0:T(1024)(128)(4,1)}), s8[4194304]{0:T(1024)(128)(4,1)S(1)}, s32[]{:S(2)}) async-start(s8[9437184]{0:T(1024)(128)(4,1)} %bitcast.101), calls=%async_computation.1 | async-start | bytes 8388608
  83.7 32.8 %collective-permute-start.23 = (bf16[512,364]{1,0:T(8,128)(2,1)}, bf16[512,364]{1,0:T(8,128)(2,1)}, u32[]{:S(2)}, u32[]{:S(2)}) collective-permute-start(bf16[512,364]{1,0:T(8,128)(2,1)} %bitcast.29), channel_id=1, source_target_pairs={{0,16},{16,0},{1,17},{17,1},{2,18},{18,2},{3,19},{19,3},{4,20},{20... | collective-permute-start | bytes 1118216 | tf_op jit(solution)/shard_map/ppermute | solution.py:21
  85.4 7.3 %slice-start.2 = ((s8[9437184]{0:T(1024)(128)(4,1)}), s8[4194304]{0:T(1024)(128)(4,1)S(1)}, s32[]{:S(2)}) async-start(s8[9437184]{0:T(1024)(128)(4,1)} %bitcast.101), calls=%async_computation.2 | async-start | bytes 8388608
  85.4 7.3 %copy-start.10 = (bf16[128,3072]{1,0:T(8,128)(2,1)}, bf16[128,3072]{1,0:T(8,128)(2,1)S(1)}, u32[]{:S(2)}) copy-start(bf16[128,3072]{1,0:T(8,128)(2,1)S(1)} %collective-permute-done.3.refs_1_) | copy-start | bytes 2359300
  92.7 9.5 %copy-start.13 = (f32[128,1536]{1,0:T(8,128)}, f32[128,1536]{1,0:T(8,128)S(1)}, u32[]{:S(2)}) copy-start(f32[128,1536]{1,0:T(8,128)S(1)} %fusion.17) | copy-start | bytes 2359300
  97.4 4.7 %copy-start.14 = (f32[128,1536]{1,0:T(8,128)}, f32[128,1536]{1,0:T(8,128)S(1)}, u32[]{:S(2)}) copy-start(f32[128,1536]{1,0:T(8,128)S(1)} %fusion.18) | copy-start | bytes 2359300
  97.4 4.8 %copy-start.12 = (f32[128,1536]{1,0:T(8,128)S(1)}, f32[128,1536]{1,0:T(8,128)}, u32[]{:S(2)}) copy-start(f32[128,1536]{1,0:T(8,128)} %fusion.11) | copy-start | bytes 2359300
  102.1 13.1 %copy-start.15 = (f32[128,1536]{1,0:T(8,128)}, f32[128,1536]{1,0:T(8,128)S(1)}, u32[]{:S(2)}) copy-start(f32[128,1536]{1,0:T(8,128)S(1)} %fusion.19) | copy-start | bytes 2359300
  103.1 20.3 %collective-permute-start.9 = (bf16[512,384]{1,0:T(8,128)(2,1)}, bf16[512,384]{1,0:T(8,128)(2,1)}, u32[]{:S(2)}, u32[]{:S(2)}) collective-permute-start(bf16[512,384]{1,0:T(8,128)(2,1)} %pad_maximum_fusion.6), channel_id=1, source_target_pairs={{0,1},{1,2},{2,3},{3,0},{4,5},{5,6},{6,7},{7,4},{8,9},{9,10},{10,1... | collective-permute-start | bytes 1179656 | tf_op jit(solution)/shard_map/ppermute | solution.py:119
  110.9 27.5 %collective-permute-start.8 = (bf16[512,384]{1,0:T(8,128)(2,1)}, bf16[512,384]{1,0:T(8,128)(2,1)}, u32[]{:S(2)}, u32[]{:S(2)}) collective-permute-start(bf16[512,384]{1,0:T(8,128)(2,1)} %pad_maximum_fusion.5), channel_id=1, source_target_pairs={{0,2},{1,3},{2,0},{3,1},{4,6},{5,7},{6,4},{7,5},{8,10},{9,11},{10,... | collective-permute-start | bytes 1179656 | tf_op jit(solution)/shard_map/ppermute | solution.py:119
  115.1 23.4 %collective-permute-start.7 = (bf16[512,384]{1,0:T(8,128)(2,1)}, bf16[512,384]{1,0:T(8,128)(2,1)}, u32[]{:S(2)}, u32[]{:S(2)}) collective-permute-start(bf16[512,384]{1,0:T(8,128)(2,1)} %pad_maximum_fusion.4), channel_id=1, source_target_pairs={{0,3},{1,0},{2,1},{3,2},{4,7},{5,4},{6,5},{7,6},{8,11},{9,8},{10,9... | collective-permute-start | bytes 1179656 | tf_op jit(solution)/shard_map/ppermute | solution.py:119
  116.5 25.2 %copy-start.5 = (bf16[512,3,128]{0,2,1:T(8,128)(2,1)}, bf16[512,3,128]{0,2,1:T(8,128)(2,1)S(1)}, u32[]{:S(2)}) copy-start(bf16[512,3,128]{0,2,1:T(8,128)(2,1)S(1)} %squeeze.46) | copy-start | bytes 1179652
  118.8 67.4 %collective-permute-start.20 = (bf16[128,3072]{1,0:T(8,128)(2,1)}, bf16[128,3072]{1,0:T(8,128)(2,1)}, u32[]{:S(2)}, u32[]{:S(2)}) collective-permute-start(bf16[128,3072]{1,0:T(8,128)(2,1)} %bitcast.28.refs_4_), channel_id=1, source_target_pairs={{0,4},{4,8},{8,12},{12,0},{1,5},{5,9},{9,13},{13,1},{2,6},{6,10},{... | collective-permute-start | bytes 2359304 | tf_op jit(solution)/shard_map/ppermute | solution.py:119
  118.8 68.8 %collective-permute-start.21 = (bf16[128,3072]{1,0:T(8,128)(2,1)}, bf16[128,3072]{1,0:T(8,128)(2,1)}, u32[]{:S(2)}, u32[]{:S(2)}) collective-permute-start(bf16[128,3072]{1,0:T(8,128)(2,1)} %bitcast.28.refs_4_), channel_id=1, source_target_pairs={{0,8},{4,12},{8,0},{12,4},{1,9},{5,13},{9,1},{13,5},{2,10},{6,14},... | collective-permute-start | bytes 2359304 | tf_op jit(solution)/shard_map/ppermute | solution.py:119
  123.5 64.9 %collective-permute-start.22 = (bf16[128,3072]{1,0:T(8,128)(2,1)}, bf16[128,3072]{1,0:T(8,128)(2,1)}, u32[]{:S(2)}, u32[]{:S(2)}) collective-permute-start(bf16[128,3072]{1,0:T(8,128)(2,1)} %bitcast.28.refs_4_), channel_id=1, source_target_pairs={{0,12},{4,0},{8,4},{12,8},{1,13},{5,1},{9,5},{13,9},{2,14},{6,2},{... | collective-permute-start | bytes 2359304 | tf_op jit(solution)/shard_map/ppermute | solution.py:119
  142.9 1.7 copy-start.4
  144.6 1.6 copy-start
  144.6 11.4 %copy-start.2 = (bf16[512,3,128]{0,2,1:T(8,128)(2,1)S(1)}, bf16[512,3,128]{0,2,1:T(8,128)(2,1)}, u32[]{:S(2)}) copy-start(bf16[512,3,128]{0,2,1:T(8,128)(2,1)} %copy-done.1) | copy-start | bytes 1179652
  146.1 11.2 %copy-start.6 = (f32[512,3,128]{0,2,1:T(8,128)S(1)}, f32[512,3,128]{0,2,1:T(8,128)}, u32[]{:S(2)}) copy-start(f32[512,3,128]{0,2,1:T(8,128)} %get-tuple-element.55) | copy-start | bytes 2359300
  147.1 18.7 %collective-permute-start.15 = (bf16[512,384]{1,0:T(8,128)(2,1)}, bf16[512,384]{1,0:T(8,128)(2,1)}, u32[]{:S(2)}, u32[]{:S(2)}) collective-permute-start(bf16[512,384]{1,0:T(8,128)(2,1)} %copy.80), channel_id=1, source_target_pairs={{0,1},{1,2},{2,3},{3,0},{4,5},{5,6},{6,7},{7,4},{8,9},{9,10},{10,1... | collective-permute-start | bytes 1179656 | tf_op jit(solution)/shard_map/ppermute | solution.py:119
  157.3 3.2 %copy-start.8 = (f32[512,3,128]{0,2,1:T(8,128)S(1)}, f32[512,3,128]{0,2,1:T(8,128)}, u32[]{:S(2)}) copy-start(f32[512,3,128]{0,2,1:T(8,128)} %get-tuple-element.53) | copy-start | bytes 2359300
  157.3 22.4 %collective-permute-start.13 = (bf16[512,384]{1,0:T(8,128)(2,1)}, bf16[512,384]{1,0:T(8,128)(2,1)}, u32[]{:S(2)}, u32[]{:S(2)}) collective-permute-start(bf16[512,384]{1,0:T(8,128)(2,1)} %copy.80), channel_id=1, source_target_pairs={{0,2},{1,3},{2,0},{3,1},{4,6},{5,7},{6,4},{7,5},{8,10},{9,11},{10,... | collective-permute-start | bytes 1179656 | tf_op jit(solution)/shard_map/ppermute | solution.py:119
  157.3 10.4 %copy-start.7 = (f32[512,3,128]{0,2,1:T(8,128)S(1)}, f32[512,3,128]{0,2,1:T(8,128)}, u32[]{:S(2)}) copy-start(f32[512,3,128]{0,2,1:T(8,128)} %get-tuple-element.51) | copy-start | bytes 2359300
  158.5 10.4 %copy-start.18 = (bf16[512,3,128]{0,2,1:T(8,128)(2,1)S(1)}, bf16[512,3,128]{0,2,1:T(8,128)(2,1)}, u32[]{:S(2)}) copy-start(bf16[512,3,128]{0,2,1:T(8,128)(2,1)} %get-tuple-element.50) | copy-start | bytes 1179652
  165.8 19.3 %collective-permute-start.11 = (bf16[512,384]{1,0:T(8,128)(2,1)}, bf16[512,384]{1,0:T(8,128)(2,1)}, u32[]{:S(2)}, u32[]{:S(2)}) collective-permute-start(bf16[512,384]{1,0:T(8,128)(2,1)} %copy.80), channel_id=1, source_target_pairs={{0,3},{1,0},{2,1},{3,2},{4,7},{5,4},{6,5},{7,6},{8,11},{9,8},{10,9... | collective-permute-start | bytes 1179656 | tf_op jit(solution)/shard_map/ppermute | solution.py:119
  167.8 1.9 copy-start.17
  169.7 12.9 %copy-start.19 = (f32[1,128,384]{1,0,2:T(1,128)S(1)}, f32[1,128,384]{1,0,2:T(1,128)}, u32[]{:S(2)}) copy-start(f32[1,128,384]{1,0,2:T(1,128)} %constant_dynamic-slice_fusion.1) | copy-start | bytes 589828
  169.7 13.7 %copy-start.20 = (f32[1,128,384]{1,0,2:T(1,128)S(1)}, f32[1,128,384]{1,0,2:T(1,128)}, u32[]{:S(2)}) copy-start(f32[1,128,384]{1,0,2:T(1,128)} %constant_dynamic-slice_fusion.2) | copy-start | bytes 589828
  179.7 17.6 %collective-permute-start.10 = (bf16[512,384]{1,0:T(8,128)(2,1)}, bf16[512,384]{1,0:T(8,128)(2,1)}, u32[]{:S(2)}, u32[]{:S(2)}) collective-permute-start(bf16[512,384]{1,0:T(8,128)(2,1)} %copy.79), channel_id=1, source_target_pairs={{0,16},{16,0},{1,17},{17,1},{2,18},{18,2},{3,19},{19,3},{4,20},{20... | collective-permute-start | bytes 1179656 | tf_op jit(solution)/shard_map/ppermute | solution.py:21
  185.0 1.1 copy-start.23
  185.0 15.5 %collective-permute-start.16 = (bf16[512,384]{1,0:T(8,128)(2,1)}, bf16[512,384]{1,0:T(8,128)(2,1)}, u32[]{:S(2)}, u32[]{:S(2)}) collective-permute-start(bf16[512,384]{1,0:T(8,128)(2,1)} %collective-permute-done.15), channel_id=1, source_target_pairs={{0,16},{16,0},{1,17},{17,1},{2,18},{18,2},{3,19},{19,3},{4,20},{20... | collective-permute-start | bytes 1179656 | tf_op jit(solution)/shard_map/ppermute | solution.py:21
  186.2 22.7 %collective-permute-start.14 = (bf16[512,384]{1,0:T(8,128)(2,1)}, bf16[512,384]{1,0:T(8,128)(2,1)}, u32[]{:S(2)}, u32[]{:S(2)}) collective-permute-start(bf16[512,384]{1,0:T(8,128)(2,1)} %collective-permute-done.13), channel_id=1, source_target_pairs={{0,16},{16,0},{1,17},{17,1},{2,18},{18,2},{3,19},{19,3},{4,20},{20... | collective-permute-start | bytes 1179656 | tf_op jit(solution)/shard_map/ppermute | solution.py:21
  187.6 28.7 %collective-permute-start.12 = (bf16[512,384]{1,0:T(8,128)(2,1)}, bf16[512,384]{1,0:T(8,128)(2,1)}, u32[]{:S(2)}, u32[]{:S(2)}) collective-permute-start(bf16[512,384]{1,0:T(8,128)(2,1)} %collective-permute-done.11), channel_id=1, source_target_pairs={{0,16},{16,0},{1,17},{17,1},{2,18},{18,2},{3,19},{19,3},{4,20},{20... | collective-permute-start | bytes 1179656 | tf_op jit(solution)/shard_map/ppermute | solution.py:21
  220.3 42.8 %collective-permute-start.17 = (bf16[3,128,384]{2,1,0:T(8,128)(2,1)}, bf16[3,128,384]{2,1,0:T(8,128)(2,1)S(1)}, u32[]{:S(2)}, u32[]{:S(2)}) collective-permute-start(bf16[3,128,384]{2,1,0:T(8,128)(2,1)} %get-tuple-element.24), channel_id=1, source_target_pairs={{0,3},{1,0},{2,1},{3,2},{4,7},{5,4},{6,5},{7,6},{8,11},{9,8},{10,9... | collective-permute-start | bytes 884744 | tf_op jit(solution)/shard_map/ppermute | solution.py:119
  233.3 29.9 %collective-permute-start.18 = (bf16[3,128,384]{2,1,0:T(8,128)(2,1)}, bf16[3,128,384]{2,1,0:T(8,128)(2,1)S(1)}, u32[]{:S(2)}, u32[]{:S(2)}) collective-permute-start(bf16[3,128,384]{2,1,0:T(8,128)(2,1)} %get-tuple-element.23), channel_id=1, source_target_pairs={{0,2},{1,3},{2,0},{3,1},{4,6},{5,7},{6,4},{7,5},{8,10},{9,11},{10,... | collective-permute-start | bytes 884744 | tf_op jit(solution)/shard_map/ppermute | solution.py:119
  233.3 30.0 %collective-permute-start.19 = (bf16[3,128,384]{2,1,0:T(8,128)(2,1)}, bf16[3,128,384]{2,1,0:T(8,128)(2,1)S(1)}, u32[]{:S(2)}, u32[]{:S(2)}) collective-permute-start(bf16[3,128,384]{2,1,0:T(8,128)(2,1)} %get-tuple-element.22), channel_id=1, source_target_pairs={{0,1},{1,2},{2,3},{3,0},{4,5},{5,6},{6,7},{7,4},{8,9},{9,10},{10,1... | collective-permute-start | bytes 884744 | tf_op jit(solution)/shard_map/ppermute | solution.py:119
  (4 other events, 4.0 us)

commit v9 on v7

--- a/solution.py
+++ b/solution.py
@@ -219,15 +219,16 @@
     for s in range(1, n):
         got = shifted(flat(part((me + s) % n), patch_here), "col", s)
         pieces.append(tuple(unflat(got, shapes)))
+    grad_partial = lax.dot_general(
+        dense_grad, out_weight, (((1,), (1,)), ((), ())), preferred_element_type=jnp.float32
+    )
+    pieces, grad_partial = lax.optimization_barrier((pieces, grad_partial))
     order = me - rank
     qkv_h = roll_blocks(jnp.stack([p[0] for p in pieces], 0), order)
     every_patch = roll_blocks(jnp.stack([p[1] for p in pieces], 0), order).reshape(n * tokens, -1)
     rows = n * tokens
     qkv_h = jnp.transpose(qkv_h, (1, 0, 2, 3)).reshape(3, rows, heads, DH)
     local_query, all_keys, all_values = qkv_h[0], qkv_h[1], qkv_h[2]
-    grad_partial = lax.dot_general(
-        dense_grad, out_weight, (((1,), (1,)), ((), ())), preferred_element_type=jnp.float32
-    )
     grad_partial, grad_other = lax.optimization_barrier((grad_partial, grad_other))
     other_blocks = [grad_other[0]] + [shifted(grad_other[0], "row", s) for s in range(1, n)]
     scores = (

time: 219 us -> 205 us (0.936)
  local copies, waits for them, and re-layouts: 49.6 us -> 41.9 us
  waiting for transfers between devices: 77.9 us -> 70.2 us
  other arithmetic: 10 us -> 12.9 us
  matrix products: 39.4 us -> 37 us
    unnamed x45 -> x65, local copies, waits for them, and re-layouts: 26.7 us -> 16.3 us
    ppermute x18, waiting for transfers between devices: 65.9 us -> 58.1 us  [shifted(): return lax.ppermute(x, axis, [(j, (j + step) % n) for j in range(n)])]
    reshape x0 -> x6, local copies, waits for them, and re-layouts: none -> 3.13 us  [unflat(): out.append(vector[..., at:at + size].reshape(vector.shape[:-1] + shape))]
    dot_general x1, matrix products: 15.8 us -> 13 us  [body_heads(): lax.dot_general(out_both, grad_both, (((1,), (0,)), ((), ())), preferred_...]
    unnamed x7 -> x8, other arithmetic: 6.61 us -> 6.88 us
  transfers between devices with their start and end apart: 24 -> 24, of which waited for: 9 -> 9; matrix products, arithmetic and copies ran while one was open for 43% -> 39% of each run, Pallas kernels for 0% -> 0%
where the time goes in v9:
time: 205 us; the launch traced here: 204 us
  waiting for transfers between devices  70.2 us (34%)
  local copies, waits for them, and re-layouts  41.9 us (20%)
  starting transfers between devices  40.2 us (20%)
  matrix products  37 us (18%)
  other arithmetic  12.9 us (6%)
    ppermute x18, waiting for transfers between devices, shifted(): return lax.ppermute(x, axis, [(j, (j + step) % n) for j in range(n)])  58.1 us
    ppermute x18, starting transfers between devices, shifted(): return lax.ppermute(x, axis, [(j, (j + step) % n) for j in range(n)])  33.1 us
    unnamed x65, local copies, waits for them, and re-layouts  16.3 us
    dot_general x1, matrix products, body_heads(): lax.dot_general(out_both, grad_both, (((1,), (0,)), ((), ())), preferred_...  13 us
    ppermute x6, waiting for transfers between devices, swap_dp(): return lax.ppermute(x, 'dp', [(0, 1), (1, 0)])  12.1 us
    dot_general x1, matrix products, body_heads(): lax.dot_general(dense_grad, out_weight, (((1,), (1,)), ((), ())), preferr...  9.5 us
    dot_general x1, matrix products, contract_rows(): lax.dot_general(left, right, (((0,), (0,)), ((), ())), preferred_element_...  7.48 us
    ppermute x6, starting transfers between devices, swap_dp(): return lax.ppermute(x, 'dp', [(0, 1), (1, 0)])  7.1 us
  transfers between devices with their start and end apart: 24, of which 9 were waited for; matrix products, arithmetic and copies ran while one was open for 39% of the time, Pallas kernels for 0%

profile of v9, /device:TPU:0, one launch (start us, length us, event | category | flops | bytes accessed | tf_op | source)
XLA Modules:
  0.0 203.6 jit_solution(18185756556525862635)
XLA Ops:
  6.7 3.0 %collective-permute-start = (bf16[194048]{0:T(1024)(128)(2,1)}, bf16[194048]{0:T(1024)(128)(2,1)S(1)}, u32[]{:S(2)}, u32[]{:S(2)}) collective-permute-start(bf16[194048]{0:T(1024)(128)(2,1)} %get-tuple-element.49), channel_id=1, source_target_pairs={{0,1},{1,2},{2,3},{3,0},{4,5},{5,6},{6,7},{7,4},{8,9},{9,10},{10,1... | collective-permute-start | bytes 1164296 | tf_op jit(solution)/shard_map/ppermute | solution.py:115
  11.5 2.6 %collective-permute-start.1 = (bf16[194048]{0:T(1024)(128)(2,1)}, bf16[194048]{0:T(1024)(128)(2,1)}, u32[]{:S(2)}, u32[]{:S(2)}) collective-permute-start(bf16[194048]{0:T(1024)(128)(2,1)} %get-tuple-element.48), channel_id=1, source_target_pairs={{0,2},{1,3},{2,0},{3,1},{4,6},{5,7},{6,4},{7,5},{8,10},{9,11},{10,... | collective-permute-start | bytes 1164296 | tf_op jit(solution)/shard_map/ppermute | solution.py:115
  14.1 7.9 %collective-permute-done = bf16[194048]{0:T(1024)(128)(2,1)S(1)} collective-permute-done((bf16[194048]{0:T(1024)(128)(2,1)}, bf16[194048]{0:T(1024)(128)(2,1)S(1)}, u32[]{:S(2)}, u32[]{:S(2)}) %collective-permute-start) | collective-permute-done | bytes 388128 | tf_op jit(solution)/shard_map/ppermute | solution.py:115
  21.9 1.2 collective-permute-start.2
  25.2 12.6 %collective-permute-done.1 = bf16[194048]{0:T(1024)(128)(2,1)} collective-permute-done((bf16[194048]{0:T(1024)(128)(2,1)}, bf16[194048]{0:T(1024)(128)(2,1)}, u32[]{:S(2)}, u32[]{:S(2)}) %collective-permute-start.1) | collective-permute-done | bytes 388128 | tf_op jit(solution)/shard_map/ppermute | solution.py:115
  37.8 1.5 collective-permute-start.6
  42.2 1.5 collective-permute-done.2
  46.7 9.5 %fusion.2 = f32[512,1536]{1,0:T(8,128)S(1)} fusion(bf16[1536,3072]{1,0:T(8,128)(2,1)} %param.10, bf16[128,3072]{1,0:T(8,128)(2,1)S(1)} %collective-permute-done.5, bf16[128,3072]{1,0:T(8,128)(2,1)} %collective-permute-done.4, bf16[128,3072]{1,0:T(8,128)(2,1)} %collective-permute-done.3, bf16[128,3072]{1,0:T(8,128)(2,1)S(1)} %bitcast.148), kind=kOutput, calls=%fused_computation.2 | convolution fusion | flops 4844421120 | bytes 15728640 | tf_op jit(solution)/shard_map/dot_general | solution.py:222
  56.2 1.2 collective-permute-done.6
  57.4 1.5 collective-permute-start.21
  59.0 1.1 dynamic-slice_convert_fusion.2
  60.1 6.0 %collective-permute-start.9 = (bf16[512,384]{1,0:T(8,128)(2,1)}, bf16[512,384]{1,0:T(8,128)(2,1)}, u32[]{:S(2)}, u32[]{:S(2)}) collective-permute-start(bf16[512,384]{1,0:T(8,128)(2,1)} %get-tuple-element.32), channel_id=1, source_target_pairs={{0,1},{1,2},{2,3},{3,0},{4,5},{5,6},{6,7},{7,4},{8,9},{9,10},{10,1... | collective-permute-start | bytes 1179656 | tf_op jit(solution)/shard_map/ppermute | solution.py:115
  66.1 3.4 %collective-permute-start.8 = (bf16[512,384]{1,0:T(8,128)(2,1)}, bf16[512,384]{1,0:T(8,128)(2,1)}, u32[]{:S(2)}, u32[]{:S(2)}) collective-permute-start(bf16[512,384]{1,0:T(8,128)(2,1)} %get-tuple-element.33), channel_id=1, source_target_pairs={{0,2},{1,3},{2,0},{3,1},{4,6},{5,7},{6,4},{7,5},{8,10},{9,11},{10,... | collective-permute-start | bytes 1179656 | tf_op jit(solution)/shard_map/ppermute | solution.py:115
  72.6 1.8 multiply_reduce_fusion
  74.9 2.1 %constant_dynamic-update-slice_fusion.9 = bf16[1024,3072]{1,0:T(8,128)(2,1)} fusion(bf16[1024,3072]{1,0:T(8,128)(2,1)} %constant_dynamic-update-slice_fusion.10, bf16[128,3072]{1,0:T(8,128)(2,1)} %collective-permute-done.3), kind=kLoop, calls=%fused_computation.92 | loop fusion | bytes 1572864
  77.1 2.1 %constant_dynamic-update-slice_fusion.8 = bf16[1024,3072]{1,0:T(8,128)(2,1)} fusion(bf16[1024,3072]{1,0:T(8,128)(2,1)} %constant_dynamic-update-slice_fusion.9, bf16[128,3072]{1,0:T(8,128)(2,1)} %collective-permute-done.4), kind=kLoop, calls=%fused_computation.91 | loop fusion | bytes 1572864
  80.1 2.1 %constant_dynamic-update-slice_fusion.6 = bf16[1024,3072]{1,0:T(8,128)(2,1)} fusion(bf16[1024,3072]{1,0:T(8,128)(2,1)} %constant_dynamic-update-slice_fusion.7, bf16[1,128,3072]{2,1,0:T(8,128)(2,1)} %collective-permute-done.6), kind=kLoop, calls=%fused_computation.89 | loop fusion | bytes 1572864
  84.2 1.1 squeeze.50
  85.4 1.7 exponential_convert_fusion
  87.9 7.8 %collective-permute-done.8 = bf16[512,384]{1,0:T(8,128)(2,1)} collective-permute-done((bf16[512,384]{1,0:T(8,128)(2,1)}, bf16[512,384]{1,0:T(8,128)(2,1)}, u32[]{:S(2)}, u32[]{:S(2)}) %collective-permute-start.8) | collective-permute-done | bytes 393248 | tf_op jit(solution)/shard_map/ppermute | solution.py:115
  95.8 1.7 add_convert_fusion
  97.7 1.4 fusion.35
  99.1 1.1 multiply_reduce_fusion.1
  100.2 7.9 %collective-permute-start.11 = (bf16[512,384]{0,1:T(8,128)(2,1)}, bf16[512,384]{0,1:T(8,128)(2,1)}, u32[]{:S(2)}, u32[]{:S(2)}) collective-permute-start(bf16[512,384]{0,1:T(8,128)(2,1)} %bitcast.14), channel_id=1, source_target_pairs={{0,3},{1,0},{2,1},{3,2},{4,7},{5,4},{6,5},{7,6},{8,11},{9,8},{10,9... | collective-permute-start | bytes 1179656 | tf_op jit(solution)/shard_map/ppermute | solution.py:115
  108.0 2.5 %collective-permute-start.13 = (bf16[512,384]{0,1:T(8,128)(2,1)}, bf16[512,384]{0,1:T(8,128)(2,1)}, u32[]{:S(2)}, u32[]{:S(2)}) collective-permute-start(bf16[512,384]{0,1:T(8,128)(2,1)} %bitcast.14), channel_id=1, source_target_pairs={{0,2},{1,3},{2,0},{3,1},{4,6},{5,7},{6,4},{7,5},{8,10},{9,11},{10,... | collective-permute-start | bytes 1179656 | tf_op jit(solution)/shard_map/ppermute | solution.py:115
  110.6 1.1 reshape.149
  111.7 1.7 multiply_convert_fusion
  114.0 1.1 reshape.148
  115.8 1.8 constant_dynamic-slice_fusion.2
  120.9 2.1 %constant_dynamic-update-slice_fusion.5 = bf16[1024,3072]{1,0:T(8,128)(2,1)} fusion(bf16[1024,3072]{1,0:T(8,128)(2,1)} %constant_dynamic-update-slice_fusion.6, bf16[128,3072]{1,0:T(8,128)(2,1)} %collective-permute-done.20), kind=kLoop, calls=%fused_computation.88 | loop fusion | bytes 1572864
  123.0 1.5 collective-permute-start.23
  124.5 2.1 %constant_dynamic-update-slice_fusion.4 = bf16[1024,3072]{1,0:T(8,128)(2,1)} fusion(bf16[1024,3072]{1,0:T(8,128)(2,1)} %constant_dynamic-update-slice_fusion.5, bf16[128,3072]{1,0:T(8,128)(2,1)} %collective-permute-done.21), kind=kLoop, calls=%fused_computation.87 | loop fusion | bytes 1572864
  127.0 18.1 %collective-permute-done.13 = bf16[512,384]{0,1:T(8,128)(2,1)} collective-permute-done((bf16[512,384]{0,1:T(8,128)(2,1)}, bf16[512,384]{0,1:T(8,128)(2,1)}, u32[]{:S(2)}, u32[]{:S(2)}) %collective-permute-start.13) | collective-permute-done | bytes 393248 | tf_op jit(solution)/shard_map/ppermute | solution.py:115
  145.2 1.5 collective-permute-start.12
  147.2 1.5 collective-permute-start.16
  148.8 2.1 %constant_dynamic-update-slice_fusion.3 = bf16[1024,3072]{1,0:T(8,128)(2,1)} fusion(bf16[1024,3072]{1,0:T(8,128)(2,1)} %constant_dynamic-update-slice_fusion.4, bf16[128,3072]{1,0:T(8,128)(2,1)} %collective-permute-done.22), kind=kLoop, calls=%fused_computation.86 | loop fusion | bytes 1572864 | tf_op jit(solution)/shard_map/concatenate | solution.py:274
  150.8 7.5 %fusion.17 = f32[364,3072]{1,0:T(8,128)} fusion(bf16[1024,3072]{1,0:T(8,128)(2,1)} %constant_dynamic-update-slice_fusion.3, bf16[512,364]{1,0:T(8,128)(2,1)S(1)} %collective-permute-done.23, bf16[512,364]{1,0:T(8,128)(2,1)S(1)} %bitcast.144), kind=kOutput, calls=%fused_computation.39 | convolution fusion | flops 2291580928 | bytes 11509760 | tf_op jit(solution)/shard_map/dot_general | solution.py:11
  158.3 1.1 fusion.28
  159.4 1.1 fusion.26
  160.5 5.4 %collective-permute-done.14 = bf16[512,384]{0,1:T(8,128)(2,1)S(1)} collective-permute-done((bf16[512,384]{0,1:T(8,128)(2,1)}, bf16[512,384]{0,1:T(8,128)(2,1)S(1)}, u32[]{:S(2)}, u32[]{:S(2)}) %collective-permute-start.14) | collective-permute-done | bytes 393248 | tf_op jit(solution)/shard_map/ppermute | solution.py:17
  167.0 5.5 %collective-permute-done.16 = bf16[512,384]{0,1:T(8,128)(2,1)S(1)} collective-permute-done((bf16[512,384]{0,1:T(8,128)(2,1)S(1)}, bf16[512,384]{0,1:T(8,128)(2,1)S(1)}, u32[]{:S(2)}, u32[]{:S(2)}) %collective-permute-start.16) | collective-permute-done | bytes 393248 | tf_op jit(solution)/shard_map/ppermute | solution.py:17
  172.6 1.1 fusion.29
  173.7 1.2 fusion.27
  174.9 1.2 fusion.25
  176.8 2.0 collective-permute-start.18
  178.8 13.0 %fusion = f32[4,384,3072]{2,1,0:T(8,128)} fusion(bf16[4,1024,384]{1,2,0:T(8,128)(2,1)S(1)} %constant_dynamic-slice_fusion.1, bf16[1024,3072]{1,0:T(8,128)(2,1)S(1)} %bitcast.137), kind=kOutput, calls=%fused_computation | convolution fusion | flops 9663676416 | bytes 28311552 | tf_op jit(solution)/shard_map/dot_general | solution.py:275
  191.9 10.1 %collective-permute-done.18 = bf16[3,128,384]{2,1,0:T(8,128)(2,1)S(1)} collective-permute-done((bf16[3,128,384]{2,1,0:T(8,128)(2,1)S(1)}, bf16[3,128,384]{2,1,0:T(8,128)(2,1)S(1)}, u32[]{:S(2)}, u32[]{:S(2)}) %collective-permute-start.18) | collective-permute-done | bytes 294944 | tf_op jit(solution)/shard_map/ppermute | solution.py:115
  202.2 1.5 slice_bitcast_fusion
  (140 shorter events, 30.5 us)
Async XLA Ops:
  2.7 2.7 %copy-start.7 = (bf16[1,128,364]{2,1,0:T(8,128)(2,1)}, bf16[1,128,364]{2,1,0:T(8,128)(2,1)S(1)}, u32[]{:S(2)}) copy-start(bf16[1,128,364]{2,1,0:T(8,128)(2,1)S(1)} %copy.30) | copy-start | bytes 279556
  5.2 4.5 %copy-start.14 = (bf16[1,128,3072]{2,1,0:T(8,128)(2,1)S(1)}, bf16[1,128,3072]{2,1,0:T(8,128)(2,1)}, u32[]{:S(2)}) copy-start(bf16[1,128,3072]{2,1,0:T(8,128)(2,1)} %param.11) | copy-start | bytes 2359300
  6.7 15.2 %collective-permute-start = (bf16[194048]{0:T(1024)(128)(2,1)}, bf16[194048]{0:T(1024)(128)(2,1)S(1)}, u32[]{:S(2)}, u32[]{:S(2)}) collective-permute-start(bf16[194048]{0:T(1024)(128)(2,1)} %get-tuple-element.49), channel_id=1, source_target_pairs={{0,1},{1,2},{2,3},{3,0},{4,5},{5,6},{6,7},{7,4},{8,9},{9,10},{10,1... | collective-permute-start | bytes 1164296 | tf_op jit(solution)/shard_map/ppermute | solution.py:115
  9.7 37.0 %collective-permute-start.5 = (bf16[128,3072]{1,0:T(8,128)(2,1)S(1)}, bf16[128,3072]{1,0:T(8,128)(2,1)S(1)}, u32[]{:S(2)}, u32[]{:S(2)}) collective-permute-start(bf16[128,3072]{1,0:T(8,128)(2,1)S(1)} %bitcast.145), channel_id=1, source_target_pairs={{0,12},{4,0},{8,4},{12,8},{1,13},{5,1},{9,5},{13,9},{2,14},{6,2},{... | collective-permute-start | bytes 2359304 | tf_op jit(solution)/shard_map/ppermute | solution.py:115
  10.4 36.3 %collective-permute-start.4 = (bf16[128,3072]{1,0:T(8,128)(2,1)S(1)}, bf16[128,3072]{1,0:T(8,128)(2,1)}, u32[]{:S(2)}, u32[]{:S(2)}) collective-permute-start(bf16[128,3072]{1,0:T(8,128)(2,1)S(1)} %bitcast.146), channel_id=1, source_target_pairs={{0,8},{4,12},{8,0},{12,4},{1,9},{5,13},{9,1},{13,5},{2,10},{6,14},... | collective-permute-start | bytes 2359304 | tf_op jit(solution)/shard_map/ppermute | solution.py:115
  11.2 35.5 %collective-permute-start.3 = (bf16[128,3072]{1,0:T(8,128)(2,1)S(1)}, bf16[128,3072]{1,0:T(8,128)(2,1)}, u32[]{:S(2)}, u32[]{:S(2)}) collective-permute-start(bf16[128,3072]{1,0:T(8,128)(2,1)S(1)} %bitcast.147), channel_id=1, source_target_pairs={{0,4},{4,8},{8,12},{12,0},{1,5},{5,9},{9,13},{13,1},{2,6},{6,10},{... | collective-permute-start | bytes 2359304 | tf_op jit(solution)/shard_map/ppermute | solution.py:115
  11.5 26.3 %collective-permute-start.1 = (bf16[194048]{0:T(1024)(128)(2,1)}, bf16[194048]{0:T(1024)(128)(2,1)}, u32[]{:S(2)}, u32[]{:S(2)}) collective-permute-start(bf16[194048]{0:T(1024)(128)(2,1)} %get-tuple-element.48), channel_id=1, source_target_pairs={{0,2},{1,3},{2,0},{3,1},{4,6},{5,7},{6,4},{7,5},{8,10},{9,11},{10,... | collective-permute-start | bytes 1164296 | tf_op jit(solution)/shard_map/ppermute | solution.py:115
  21.9 21.8 %collective-permute-start.2 = (bf16[194048]{0:T(1024)(128)(2,1)}, bf16[194048]{0:T(1024)(128)(2,1)}, u32[]{:S(2)}, u32[]{:S(2)}) collective-permute-start(bf16[194048]{0:T(1024)(128)(2,1)} %get-tuple-element.47), channel_id=1, source_target_pairs={{0,3},{1,0},{2,1},{3,2},{4,7},{5,4},{6,5},{7,6},{8,11},{9,8},{10,9... | collective-permute-start | bytes 1164296 | tf_op jit(solution)/shard_map/ppermute | solution.py:115
  37.8 19.7 %collective-permute-start.6 = (bf16[1,128,3072]{2,1,0:T(8,128)(2,1)S(1)}, bf16[1,128,3072]{2,1,0:T(8,128)(2,1)}, u32[]{:S(2)}, u32[]{:S(2)}) collective-permute-start(bf16[1,128,3072]{2,1,0:T(8,128)(2,1)S(1)} %copy-done.14), channel_id=1, source_target_pairs={{0,16},{16,0},{1,17},{17,1},{2,18},{18,2},{3,19},{19,3},{4,20},{20... | collective-permute-start | bytes 2359304 | tf_op jit(solution)/shard_map/ppermute | solution.py:17
  46.7 9.5 %copy-start.15 = (bf16[128,3072]{1,0:T(8,128)(2,1)}, bf16[128,3072]{1,0:T(8,128)(2,1)S(1)}, u32[]{:S(2)}) copy-start(bf16[128,3072]{1,0:T(8,128)(2,1)S(1)} %collective-permute-done.5) | copy-start | bytes 2359300
  56.2 13.4 %copy-start.10 = (f32[512,1536]{1,0:T(8,128)}, f32[512,1536]{1,0:T(8,128)S(1)}, u32[]{:S(2)}) copy-start(f32[512,1536]{1,0:T(8,128)S(1)} %fusion.2) | copy-start | bytes 9437188
  57.4 63.1 %collective-permute-start.20 = (bf16[128,3072]{1,0:T(8,128)(2,1)}, bf16[128,3072]{1,0:T(8,128)(2,1)}, u32[]{:S(2)}, u32[]{:S(2)}) collective-permute-start(bf16[128,3072]{1,0:T(8,128)(2,1)} %bitcast.31), channel_id=1, source_target_pairs={{0,4},{4,8},{8,12},{12,0},{1,5},{5,9},{9,13},{13,1},{2,6},{6,10},{... | collective-permute-start | bytes 2359304 | tf_op jit(solution)/shard_map/ppermute | solution.py:115
  57.4 65.5 %collective-permute-start.21 = (bf16[128,3072]{1,0:T(8,128)(2,1)}, bf16[128,3072]{1,0:T(8,128)(2,1)}, u32[]{:S(2)}, u32[]{:S(2)}) collective-permute-start(bf16[128,3072]{1,0:T(8,128)(2,1)} %bitcast.31), channel_id=1, source_target_pairs={{0,8},{4,12},{8,0},{12,4},{1,9},{5,13},{9,1},{13,5},{2,10},{6,14},... | collective-permute-start | bytes 2359304 | tf_op jit(solution)/shard_map/ppermute | solution.py:115
  60.1 27.0 %collective-permute-start.9 = (bf16[512,384]{1,0:T(8,128)(2,1)}, bf16[512,384]{1,0:T(8,128)(2,1)}, u32[]{:S(2)}, u32[]{:S(2)}) collective-permute-start(bf16[512,384]{1,0:T(8,128)(2,1)} %get-tuple-element.32), channel_id=1, source_target_pairs={{0,1},{1,2},{2,3},{3,0},{4,5},{5,6},{6,7},{7,4},{8,9},{9,10},{10,1... | collective-permute-start | bytes 1179656 | tf_op jit(solution)/shard_map/ppermute | solution.py:115
  66.1 29.7 %collective-permute-start.8 = (bf16[512,384]{1,0:T(8,128)(2,1)}, bf16[512,384]{1,0:T(8,128)(2,1)}, u32[]{:S(2)}, u32[]{:S(2)}) collective-permute-start(bf16[512,384]{1,0:T(8,128)(2,1)} %get-tuple-element.33), channel_id=1, source_target_pairs={{0,2},{1,3},{2,0},{3,1},{4,6},{5,7},{6,4},{7,5},{8,10},{9,11},{10,... | collective-permute-start | bytes 1179656 | tf_op jit(solution)/shard_map/ppermute | solution.py:115
  69.5 26.3 %collective-permute-start.7 = (bf16[512,384]{1,0:T(8,128)(2,1)}, bf16[512,384]{1,0:T(8,128)(2,1)}, u32[]{:S(2)}, u32[]{:S(2)}) collective-permute-start(bf16[512,384]{1,0:T(8,128)(2,1)} %get-tuple-element.31), channel_id=1, source_target_pairs={{0,3},{1,0},{2,1},{3,2},{4,7},{5,4},{6,5},{7,6},{8,11},{9,8},{10,9... | collective-permute-start | bytes 1179656 | tf_op jit(solution)/shard_map/ppermute | solution.py:115
  72.6 2.3 %copy-start.1 = (bf16[512,3,128]{0,2,1:T(8,128)(2,1)}, bf16[512,3,128]{0,2,1:T(8,128)(2,1)S(1)}, u32[]{:S(2)}) copy-start(bf16[512,3,128]{0,2,1:T(8,128)(2,1)S(1)} %squeeze.48) | copy-start | bytes 1179652
  74.9 4.3 %copy-start.16 = (bf16[128,3072]{1,0:T(8,128)(2,1)S(1)}, bf16[128,3072]{1,0:T(8,128)(2,1)}, u32[]{:S(2)}) copy-start(bf16[128,3072]{1,0:T(8,128)(2,1)} %copy-done.15) | copy-start | bytes 2359300
  77.1 5.2 %copy-start.8 = (bf16[1,128,364]{2,1,0:T(8,128)(2,1)S(1)}, bf16[1,128,364]{2,1,0:T(8,128)(2,1)}, u32[]{:S(2)}) copy-start(bf16[1,128,364]{2,1,0:T(8,128)(2,1)} %copy-done.7) | copy-start | bytes 279556
  77.1 5.2 %copy-start.11 = (bf16[128,364]{1,0:T(8,128)(2,1)S(1)}, bf16[128,364]{1,0:T(8,128)(2,1)}, u32[]{:S(2)}) copy-start(bf16[128,364]{1,0:T(8,128)(2,1)} %reshape.139) | copy-start | bytes 279556
  77.1 5.2 %copy-start.12 = (bf16[128,364]{1,0:T(8,128)(2,1)S(1)}, bf16[128,364]{1,0:T(8,128)(2,1)}, u32[]{:S(2)}) copy-start(bf16[128,364]{1,0:T(8,128)(2,1)} %reshape.142) | copy-start | bytes 279556
  77.1 5.3 %copy-start.13 = (bf16[128,364]{1,0:T(8,128)(2,1)S(1)}, bf16[128,364]{1,0:T(8,128)(2,1)}, u32[]{:S(2)}) copy-start(bf16[128,364]{1,0:T(8,128)(2,1)} %reshape.145) | copy-start | bytes 279556
  80.1 3.1 %copy-start.6 = (bf16[1,4,128,384]{3,2,0,1:T(8,128)(2,1)S(1)}, bf16[1,4,128,384]{3,2,0,1:T(8,128)(2,1)}, u32[]{:S(2)}) copy-start(bf16[1,4,128,384]{3,2,0,1:T(8,128)(2,1)} %get-tuple-element.40) | copy-start | bytes 1179652
  85.4 13.7 %copy-start.4 = (bf16[512,3,128]{0,2,1:T(8,128)(2,1)}, bf16[512,3,128]{0,2,1:T(8,128)(2,1)S(1)}, u32[]{:S(2)}) copy-start(bf16[512,3,128]{0,2,1:T(8,128)(2,1)S(1)} %squeeze.50) | copy-start | bytes 1179652
  87.1 10.6 %copy-start = (bf16[3,512,512]{1,2,0:T(8,128)(2,1)S(1)}, bf16[3,512,512]{1,2,0:T(8,128)(2,1)}, u32[]{:S(2)}) copy-start(bf16[3,512,512]{1,2,0:T(8,128)(2,1)} %exponential_convert_fusion) | copy-start | bytes 4718596
  87.1 60.2 %collective-permute-start.22 = (bf16[128,3072]{1,0:T(8,128)(2,1)}, bf16[128,3072]{1,0:T(8,128)(2,1)}, u32[]{:S(2)}, u32[]{:S(2)}) collective-permute-start(bf16[128,3072]{1,0:T(8,128)(2,1)} %bitcast.31), channel_id=1, source_target_pairs={{0,12},{4,0},{8,4},{12,8},{1,13},{5,1},{9,5},{13,9},{2,14},{6,2},{... | collective-permute-start | bytes 2359304 | tf_op jit(solution)/shard_map/ppermute | solution.py:115
  100.2 26.4 %collective-permute-start.11 = (bf16[512,384]{0,1:T(8,128)(2,1)}, bf16[512,384]{0,1:T(8,128)(2,1)}, u32[]{:S(2)}, u32[]{:S(2)}) collective-permute-start(bf16[512,384]{0,1:T(8,128)(2,1)} %bitcast.14), channel_id=1, source_target_pairs={{0,3},{1,0},{2,1},{3,2},{4,7},{5,4},{6,5},{7,6},{8,11},{9,8},{10,9... | collective-permute-start | bytes 1179656 | tf_op jit(solution)/shard_map/ppermute | solution.py:115
  108.0 37.2 %collective-permute-start.13 = (bf16[512,384]{0,1:T(8,128)(2,1)}, bf16[512,384]{0,1:T(8,128)(2,1)}, u32[]{:S(2)}, u32[]{:S(2)}) collective-permute-start(bf16[512,384]{0,1:T(8,128)(2,1)} %bitcast.14), channel_id=1, source_target_pairs={{0,2},{1,3},{2,0},{3,1},{4,6},{5,7},{6,4},{7,5},{8,10},{9,11},{10,... | collective-permute-start | bytes 1179656 | tf_op jit(solution)/shard_map/ppermute | solution.py:115
  111.7 1.7 copy-start.3
  113.4 1.8 copy-start.2
  117.6 1.4 copy-start.5
  120.2 2.7 %copy-start.9 = (bf16[4,128,364]{2,1,0:T(8,128)(2,1)S(1)}, bf16[4,128,364]{2,1,0:T(8,128)(2,1)}, u32[]{:S(2)}) copy-start(bf16[4,128,364]{2,1,0:T(8,128)(2,1)} %constant_dynamic-slice_fusion) | copy-start | bytes 1118212
  120.6 26.1 %collective-permute-start.15 = (bf16[512,384]{0,1:T(8,128)(2,1)}, bf16[512,384]{0,1:T(8,128)(2,1)S(1)}, u32[]{:S(2)}, u32[]{:S(2)}) collective-permute-start(bf16[512,384]{0,1:T(8,128)(2,1)} %bitcast.14), channel_id=1, source_target_pairs={{0,1},{1,2},{2,3},{3,0},{4,5},{5,6},{6,7},{7,4},{8,9},{9,10},{10,1... | collective-permute-start | bytes 1179656 | tf_op jit(solution)/shard_map/ppermute | solution.py:115
  123.0 27.9 %collective-permute-start.23 = (bf16[512,364]{1,0:T(8,128)(2,1)S(1)}, bf16[512,364]{1,0:T(8,128)(2,1)S(1)}, u32[]{:S(2)}, u32[]{:S(2)}) collective-permute-start(bf16[512,364]{1,0:T(8,128)(2,1)S(1)} %bitcast.143), channel_id=1, source_target_pairs={{0,16},{16,0},{1,17},{17,1},{2,18},{18,2},{3,19},{19,3},{4,20},{20... | collective-permute-start | bytes 1118216 | tf_op jit(solution)/shard_map/ppermute | solution.py:17
  126.5 31.8 %collective-permute-start.10 = (bf16[512,384]{0,1:T(8,128)(2,1)}, bf16[512,384]{0,1:T(8,128)(2,1)S(1)}, u32[]{:S(2)}, u32[]{:S(2)}) collective-permute-start(bf16[512,384]{0,1:T(8,128)(2,1)} %bitcast.14), channel_id=1, source_target_pairs={{0,16},{16,0},{1,17},{17,1},{2,18},{18,2},{3,19},{19,3},{4,20},{20... | collective-permute-start | bytes 1179656 | tf_op jit(solution)/shard_map/ppermute | solution.py:17
  145.2 14.2 %collective-permute-start.12 = (bf16[512,384]{0,1:T(8,128)(2,1)}, bf16[512,384]{0,1:T(8,128)(2,1)S(1)}, u32[]{:S(2)}, u32[]{:S(2)}) collective-permute-start(bf16[512,384]{0,1:T(8,128)(2,1)} %collective-permute-done.11), channel_id=1, source_target_pairs={{0,16},{16,0},{1,17},{17,1},{2,18},{18,2},{3,19},{19,3},{4,20},{20... | collective-permute-start | bytes 1179656 | tf_op jit(solution)/shard_map/ppermute | solution.py:17
  146.7 19.2 %collective-permute-start.14 = (bf16[512,384]{0,1:T(8,128)(2,1)}, bf16[512,384]{0,1:T(8,128)(2,1)S(1)}, u32[]{:S(2)}, u32[]{:S(2)}) collective-permute-start(bf16[512,384]{0,1:T(8,128)(2,1)} %collective-permute-done.13), channel_id=1, source_target_pairs={{0,16},{16,0},{1,17},{17,1},{2,18},{18,2},{3,19},{19,3},{4,20},{20... | collective-permute-start | bytes 1179656 | tf_op jit(solution)/shard_map/ppermute | solution.py:17
  147.2 25.3 %collective-permute-start.16 = (bf16[512,384]{0,1:T(8,128)(2,1)S(1)}, bf16[512,384]{0,1:T(8,128)(2,1)S(1)}, u32[]{:S(2)}, u32[]{:S(2)}) collective-permute-start(bf16[512,384]{0,1:T(8,128)(2,1)S(1)} %collective-permute-done.15), channel_id=1, source_target_pairs={{0,16},{16,0},{1,17},{17,1},{2,18},{18,2},{3,19},{19,3},{4,20},{20... | collective-permute-start | bytes 1179656 | tf_op jit(solution)/shard_map/ppermute | solution.py:17
  173.7 5.1 %slice-start = ((s8[6291456]{0:T(1024)(128)(4,1)}), s8[4194304]{0:T(1024)(128)(4,1)S(1)}, s32[]{:S(2)}) async-start(s8[6291456]{0:T(1024)(128)(4,1)} %bitcast.136), calls=%async_computation | async-start | bytes 8388608
  176.3 2.5 %slice-start.1 = ((s8[6291456]{0:T(1024)(128)(4,1)}), s8[2097152]{0:T(1024)(128)(4,1)S(1)}, s32[]{:S(2)}) async-start(s8[6291456]{0:T(1024)(128)(4,1)} %bitcast.136), calls=%async_computation.1 | async-start | bytes 4194304
  176.7 15.2 %collective-permute-start.17 = (bf16[3,128,384]{2,1,0:T(8,128)(2,1)S(1)}, bf16[3,128,384]{2,1,0:T(8,128)(2,1)S(1)}, u32[]{:S(2)}, u32[]{:S(2)}) collective-permute-start(bf16[3,128,384]{2,1,0:T(8,128)(2,1)S(1)} %get-tuple-element.39), channel_id=1, source_target_pairs={{0,3},{1,0},{2,1},{3,2},{4,7},{5,4},{6,5},{7,6},{8,11},{9,8},{10,9... | collective-permute-start | bytes 884744 | tf_op jit(solution)/shard_map/ppermute | solution.py:115
  176.8 25.2 %collective-permute-start.18 = (bf16[3,128,384]{2,1,0:T(8,128)(2,1)S(1)}, bf16[3,128,384]{2,1,0:T(8,128)(2,1)S(1)}, u32[]{:S(2)}, u32[]{:S(2)}) collective-permute-start(bf16[3,128,384]{2,1,0:T(8,128)(2,1)S(1)} %get-tuple-element.38), channel_id=1, source_target_pairs={{0,2},{1,3},{2,0},{3,1},{4,6},{5,7},{6,4},{7,5},{8,10},{9,11},{10,... | collective-permute-start | bytes 884744 | tf_op jit(solution)/shard_map/ppermute | solution.py:115
  191.8 10.3 %collective-permute-start.19 = (bf16[3,128,384]{2,1,0:T(8,128)(2,1)S(1)}, bf16[3,128,384]{2,1,0:T(8,128)(2,1)S(1)}, u32[]{:S(2)}, u32[]{:S(2)}) collective-permute-start(bf16[3,128,384]{2,1,0:T(8,128)(2,1)S(1)} %get-tuple-element.37), channel_id=1, source_target_pairs={{0,1},{1,2},{2,3},{3,0},{4,5},{5,6},{6,7},{7,4},{8,9},{9,10},{10,1... | collective-permute-start | bytes 884744 | tf_op jit(solution)/shard_map/ppermute | solution.py:115

commit v10 on v9

--- a/solution.py
+++ b/solution.py
@@ -280,7 +280,7 @@
     sendable = roll_blocks(
         jnp.stack([g.astype(jnp.bfloat16) for g in grad_list], 1), rank - me
     )
-    sendable, out_both = lax.optimization_barrier((sendable, out_both))
+    sendable, _ = lax.optimization_barrier((sendable, [p[0] for p in out_pieces]))
     mine = jnp.stack(
         [lax.dynamic_index_in_dim(g, (rank - me) % n, 0, keepdims=False) for g in grad_list], 0
     )

time: 205 us -> 210 us (1.024)
  local copies, waits for them, and re-layouts: 41.9 us -> 46.4 us
    ppermute x6, waiting for transfers between devices: 12.1 us -> 15.9 us  [swap_dp(): return lax.ppermute(x, 'dp', [(0, 1), (1, 0)])]
    ppermute x18, waiting for transfers between devices: 58.1 us -> 55.2 us  [shifted(): return lax.ppermute(x, axis, [(j, (j + step) % n) for j in range(n)])]
    concatenate x2, other arithmetic: 0.89 us -> 2.99 us  [roll_blocks(): return lax.dynamic_slice_in_dim(jnp.concatenate([x, x], 0), shift % n, n, 0)]
    unnamed x65 -> x63, local copies, waits for them, and re-layouts: 16.3 us -> 16.3 us
  transfers between devices with their start and end apart: 24 -> 24, of which waited for: 9 -> 11; matrix products, arithmetic and copies ran while one was open for 39% -> 35% of each run, Pallas kernels for 0% -> 0%
where the time goes in v10:
time: 210 us; the launch traced here: 209 us
  waiting for transfers between devices  71.1 us (34%)
  local copies, waits for them, and re-layouts  46.4 us (22%)
  starting transfers between devices  39.2 us (19%)
  matrix products  36.9 us (18%)
  other arithmetic  14.3 us (7%)
    ppermute x18, waiting for transfers between devices, shifted(): return lax.ppermute(x, axis, [(j, (j + step) % n) for j in range(n)])  55.2 us
    ppermute x18, starting transfers between devices, shifted(): return lax.ppermute(x, axis, [(j, (j + step) % n) for j in range(n)])  32 us
    unnamed x63, local copies, waits for them, and re-layouts  16.3 us
    ppermute x6, waiting for transfers between devices, swap_dp(): return lax.ppermute(x, 'dp', [(0, 1), (1, 0)])  15.9 us
    dot_general x1, matrix products, body_heads(): lax.dot_general(out_both, grad_both, (((1,), (0,)), ((), ())), preferred_...  13.1 us
    dot_general x1, matrix products, body_heads(): lax.dot_general(dense_grad, out_weight, (((1,), (1,)), ((), ())), preferr...  9.4 us
    dot_general x1, matrix products, contract_rows(): lax.dot_general(left, right, (((0,), (0,)), ((), ())), preferred_element_...  7.47 us
    ppermute x6, starting transfers between devices, swap_dp(): return lax.ppermute(x, 'dp', [(0, 1), (1, 0)])  7.16 us
  transfers between devices with their start and end apart: 24, of which 11 were waited for; matrix products, arithmetic and copies ran while one was open for 35% of the time, Pallas kernels for 0%

profile of v10, /device:TPU:0, one launch (start us, length us, event | category | flops | bytes accessed | tf_op | source)
XLA Modules:
  0.0 209.3 jit_solution(16681849053960682802)
XLA Ops:
  6.6 3.0 %collective-permute-start = (bf16[194048]{0:T(1024)(128)(2,1)}, bf16[194048]{0:T(1024)(128)(2,1)S(1)}, u32[]{:S(2)}, u32[]{:S(2)}) collective-permute-start(bf16[194048]{0:T(1024)(128)(2,1)} %get-tuple-element.49), channel_id=1, source_target_pairs={{0,1},{1,2},{2,3},{3,0},{4,5},{5,6},{6,7},{7,4},{8,9},{9,10},{10,1... | collective-permute-start | bytes 1164296 | tf_op jit(solution)/shard_map/ppermute | solution.py:115
  11.4 2.6 %collective-permute-start.1 = (bf16[194048]{0:T(1024)(128)(2,1)}, bf16[194048]{0:T(1024)(128)(2,1)}, u32[]{:S(2)}, u32[]{:S(2)}) collective-permute-start(bf16[194048]{0:T(1024)(128)(2,1)} %get-tuple-element.48), channel_id=1, source_target_pairs={{0,2},{1,3},{2,0},{3,1},{4,6},{5,7},{6,4},{7,5},{8,10},{9,11},{10,... | collective-permute-start | bytes 1164296 | tf_op jit(solution)/shard_map/ppermute | solution.py:115
  14.0 7.9 %collective-permute-done = bf16[194048]{0:T(1024)(128)(2,1)S(1)} collective-permute-done((bf16[194048]{0:T(1024)(128)(2,1)}, bf16[194048]{0:T(1024)(128)(2,1)S(1)}, u32[]{:S(2)}, u32[]{:S(2)}) %collective-permute-start) | collective-permute-done | bytes 388128 | tf_op jit(solution)/shard_map/ppermute | solution.py:115
  21.8 1.2 collective-permute-start.2
  26.9 10.8 %collective-permute-done.1 = bf16[194048]{0:T(1024)(128)(2,1)} collective-permute-done((bf16[194048]{0:T(1024)(128)(2,1)}, bf16[194048]{0:T(1024)(128)(2,1)}, u32[]{:S(2)}, u32[]{:S(2)}) %collective-permute-start.1) | collective-permute-done | bytes 388128 | tf_op jit(solution)/shard_map/ppermute | solution.py:115
  37.7 1.5 collective-permute-start.6
  42.1 1.3 collective-permute-done.2
  46.5 9.4 %fusion.2 = f32[512,1536]{1,0:T(8,128)S(1)} fusion(bf16[1536,3072]{1,0:T(8,128)(2,1)} %param.10, bf16[128,3072]{1,0:T(8,128)(2,1)S(1)} %collective-permute-done.5, bf16[128,3072]{1,0:T(8,128)(2,1)} %collective-permute-done.4, bf16[128,3072]{1,0:T(8,128)(2,1)} %collective-permute-done.3, bf16[128,3072]{1,0:T(8,128)(2,1)S(1)} %bitcast.153), kind=kOutput, calls=%fused_computation.2 | convolution fusion | flops 4844421120 | bytes 15728640 | tf_op jit(solution)/shard_map/dot_general | solution.py:222
  55.9 1.4 collective-permute-done.6
  57.4 1.5 collective-permute-start.21
  58.9 1.1 dynamic-slice_convert_fusion.2
  60.0 6.0 %collective-permute-start.9 = (bf16[512,384]{1,0:T(8,128)(2,1)}, bf16[512,384]{1,0:T(8,128)(2,1)}, u32[]{:S(2)}, u32[]{:S(2)}) collective-permute-start(bf16[512,384]{1,0:T(8,128)(2,1)} %get-tuple-element.32), channel_id=1, source_target_pairs={{0,1},{1,2},{2,3},{3,0},{4,5},{5,6},{6,7},{7,4},{8,9},{9,10},{10,1... | collective-permute-start | bytes 1179656 | tf_op jit(solution)/shard_map/ppermute | solution.py:115
  66.0 3.4 %collective-permute-start.8 = (bf16[512,384]{1,0:T(8,128)(2,1)}, bf16[512,384]{1,0:T(8,128)(2,1)}, u32[]{:S(2)}, u32[]{:S(2)}) collective-permute-start(bf16[512,384]{1,0:T(8,128)(2,1)} %get-tuple-element.33), channel_id=1, source_target_pairs={{0,2},{1,3},{2,0},{3,1},{4,6},{5,7},{6,4},{7,5},{8,10},{9,11},{10,... | collective-permute-start | bytes 1179656 | tf_op jit(solution)/shard_map/ppermute | solution.py:115
  72.4 1.6 multiply_reduce_fusion
  74.6 2.1 %constant_dynamic-update-slice_fusion.9 = bf16[1024,3072]{1,0:T(8,128)(2,1)} fusion(bf16[1024,3072]{1,0:T(8,128)(2,1)} %constant_dynamic-update-slice_fusion.10, bf16[128,3072]{1,0:T(8,128)(2,1)} %collective-permute-done.3), kind=kLoop, calls=%fused_computation.93 | loop fusion | bytes 1572864
  76.8 2.1 %constant_dynamic-update-slice_fusion.8 = bf16[1024,3072]{1,0:T(8,128)(2,1)} fusion(bf16[1024,3072]{1,0:T(8,128)(2,1)} %constant_dynamic-update-slice_fusion.9, bf16[128,3072]{1,0:T(8,128)(2,1)} %collective-permute-done.4), kind=kLoop, calls=%fused_computation.92 | loop fusion | bytes 1572864
  79.8 2.1 constant_dynamic-update-slice_fusion.6
  82.9 1.9 copy.37
  84.9 1.9 squeeze.50
  86.8 1.7 exponential_convert_fusion
  88.4 7.2 %collective-permute-done.8 = bf16[512,384]{1,0:T(8,128)(2,1)} collective-permute-done((bf16[512,384]{1,0:T(8,128)(2,1)}, bf16[512,384]{1,0:T(8,128)(2,1)}, u32[]{:S(2)}, u32[]{:S(2)}) %collective-permute-start.8) | collective-permute-done | bytes 393248 | tf_op jit(solution)/shard_map/ppermute | solution.py:115
  95.7 1.7 add_convert_fusion
  97.6 1.5 fusion.37
  100.1 1.5 fusion.36
  101.7 1.3 fusion.35
  102.9 7.9 %collective-permute-start.10 = (bf16[512,384]{0,1:T(8,128)(2,1)S(1)}, bf16[512,384]{0,1:T(8,128)(2,1)}, u32[]{:S(2)}, u32[]{:S(2)}) collective-permute-start(bf16[512,384]{0,1:T(8,128)(2,1)S(1)} %bitcast.140), channel_id=1, source_target_pairs={{0,3},{1,0},{2,1},{3,2},{4,7},{5,4},{6,5},{7,6},{8,11},{9,8},{10,9... | collective-permute-start | bytes 1179656 | tf_op jit(solution)/shard_map/ppermute | solution.py:115
  110.8 2.5 %collective-permute-start.11 = (bf16[512,384]{0,1:T(8,128)(2,1)S(1)}, bf16[512,384]{0,1:T(8,128)(2,1)}, u32[]{:S(2)}, u32[]{:S(2)}) collective-permute-start(bf16[512,384]{0,1:T(8,128)(2,1)S(1)} %bitcast.141), channel_id=1, source_target_pairs={{0,2},{1,3},{2,0},{3,1},{4,6},{5,7},{6,4},{7,5},{8,10},{9,11},{10,... | collective-permute-start | bytes 1179656 | tf_op jit(solution)/shard_map/ppermute | solution.py:115
  116.0 1.9 fusion.15
  117.9 1.1 reshape.149
  119.0 1.1 reshape.148
  120.1 1.4 reshape.147
  121.5 1.8 constant_dynamic-slice_fusion.1
  124.4 23.4 %collective-permute-done.11 = bf16[512,384]{0,1:T(8,128)(2,1)} collective-permute-done((bf16[512,384]{0,1:T(8,128)(2,1)S(1)}, bf16[512,384]{0,1:T(8,128)(2,1)}, u32[]{:S(2)}, u32[]{:S(2)}) %collective-permute-start.11) | collective-permute-done | bytes 393248 | tf_op jit(solution)/shard_map/ppermute | solution.py:115
  147.7 1.5 collective-permute-start.23
  149.9 2.1 constant_dynamic-update-slice_fusion.5
  152.0 2.1 constant_dynamic-update-slice_fusion.4
  154.1 2.0 collective-permute-start.15
  157.0 2.8 %collective-permute-done.23 = bf16[512,364]{1,0:T(8,128)(2,1)S(1)} collective-permute-done((bf16[512,364]{1,0:T(8,128)(2,1)S(1)}, bf16[512,364]{1,0:T(8,128)(2,1)S(1)}, u32[]{:S(2)}, u32[]{:S(2)}) %collective-permute-start.23) | collective-permute-done | bytes 372768 | tf_op jit(solution)/shard_map/ppermute | solution.py:17
  159.8 1.5 collective-permute-start.17
  161.3 7.5 %fusion.18 = f32[364,3072]{1,0:T(8,128)} fusion(bf16[1024,3072]{1,0:T(8,128)(2,1)} %constant_dynamic-update-slice_fusion.3, bf16[512,364]{1,0:T(8,128)(2,1)S(1)} %collective-permute-done.23, bf16[512,364]{1,0:T(8,128)(2,1)S(1)} %bitcast.149), kind=kOutput, calls=%fused_computation.40 | convolution fusion | flops 2291580928 | bytes 11509760 | tf_op jit(solution)/shard_map/dot_general | solution.py:11
  169.8 1.1 collective-permute-start.19
  171.0 4.5 %collective-permute-done.14 = bf16[3,128,384]{2,1,0:T(8,128)(2,1)S(1)} collective-permute-done((bf16[3,128,384]{2,1,0:T(8,128)(2,1)S(1)}, bf16[3,128,384]{2,1,0:T(8,128)(2,1)S(1)}, u32[]{:S(2)}, u32[]{:S(2)}) %collective-permute-start.14) | collective-permute-done | bytes 294944 | tf_op jit(solution)/shard_map/ppermute | solution.py:115
  175.7 1.5 slice_bitcast_fusion
  177.2 1.7 fusion.27
  178.9 6.2 %collective-permute-done.18 = bf16[512,384]{0,1:T(8,128)(2,1)S(1)} collective-permute-done((bf16[512,384]{0,1:T(8,128)(2,1)}, bf16[512,384]{0,1:T(8,128)(2,1)S(1)}, u32[]{:S(2)}, u32[]{:S(2)}) %collective-permute-start.18) | collective-permute-done | bytes 393248 | tf_op jit(solution)/shard_map/ppermute | solution.py:17
  186.2 5.5 %collective-permute-done.19 = bf16[512,384]{0,1:T(8,128)(2,1)S(1)} collective-permute-done((bf16[512,384]{0,1:T(8,128)(2,1)}, bf16[512,384]{0,1:T(8,128)(2,1)S(1)}, u32[]{:S(2)}, u32[]{:S(2)}) %collective-permute-start.19) | collective-permute-done | bytes 393248 | tf_op jit(solution)/shard_map/ppermute | solution.py:17
  195.1 1.1 fusion.24
  196.2 13.1 %fusion = f32[4,384,3072]{2,1,0:T(8,128)} fusion(bf16[1024,3072]{1,0:T(8,128)(2,1)S(1)} %bitcast.136, bf16[8,1024,384]{1,2,0:T(8,128)(2,1)S(1)} %fusion.24, s32[]{:T(128)S(6)} %select_n.114), kind=kOutput, calls=%fused_computation | convolution fusion | flops 9663676416 | bytes 28311556 | tf_op jit(solution)/shard_map/dot_general | solution.py:275
  (137 shorter events, 34.9 us)
Async XLA Ops:
  2.7 2.7 %copy-start.5 = (bf16[1,128,364]{2,1,0:T(8,128)(2,1)}, bf16[1,128,364]{2,1,0:T(8,128)(2,1)S(1)}, u32[]{:S(2)}) copy-start(bf16[1,128,364]{2,1,0:T(8,128)(2,1)S(1)} %copy.30) | copy-start | bytes 279556
  5.2 4.4 %copy-start.12 = (bf16[1,128,3072]{2,1,0:T(8,128)(2,1)S(1)}, bf16[1,128,3072]{2,1,0:T(8,128)(2,1)}, u32[]{:S(2)}) copy-start(bf16[1,128,3072]{2,1,0:T(8,128)(2,1)} %param.11) | copy-start | bytes 2359300
  6.6 15.2 %collective-permute-start = (bf16[194048]{0:T(1024)(128)(2,1)}, bf16[194048]{0:T(1024)(128)(2,1)S(1)}, u32[]{:S(2)}, u32[]{:S(2)}) collective-permute-start(bf16[194048]{0:T(1024)(128)(2,1)} %get-tuple-element.49), channel_id=1, source_target_pairs={{0,1},{1,2},{2,3},{3,0},{4,5},{5,6},{6,7},{7,4},{8,9},{9,10},{10,1... | collective-permute-start | bytes 1164296 | tf_op jit(solution)/shard_map/ppermute | solution.py:115
  9.7 36.7 %collective-permute-start.5 = (bf16[128,3072]{1,0:T(8,128)(2,1)S(1)}, bf16[128,3072]{1,0:T(8,128)(2,1)S(1)}, u32[]{:S(2)}, u32[]{:S(2)}) collective-permute-start(bf16[128,3072]{1,0:T(8,128)(2,1)S(1)} %bitcast.150), channel_id=1, source_target_pairs={{0,12},{4,0},{8,4},{12,8},{1,13},{5,1},{9,5},{13,9},{2,14},{6,2},{... | collective-permute-start | bytes 2359304 | tf_op jit(solution)/shard_map/ppermute | solution.py:115
  10.3 36.1 %collective-permute-start.4 = (bf16[128,3072]{1,0:T(8,128)(2,1)S(1)}, bf16[128,3072]{1,0:T(8,128)(2,1)}, u32[]{:S(2)}, u32[]{:S(2)}) collective-permute-start(bf16[128,3072]{1,0:T(8,128)(2,1)S(1)} %bitcast.151), channel_id=1, source_target_pairs={{0,8},{4,12},{8,0},{12,4},{1,9},{5,13},{9,1},{13,5},{2,10},{6,14},... | collective-permute-start | bytes 2359304 | tf_op jit(solution)/shard_map/ppermute | solution.py:115
  11.1 35.3 %collective-permute-start.3 = (bf16[128,3072]{1,0:T(8,128)(2,1)S(1)}, bf16[128,3072]{1,0:T(8,128)(2,1)}, u32[]{:S(2)}, u32[]{:S(2)}) collective-permute-start(bf16[128,3072]{1,0:T(8,128)(2,1)S(1)} %bitcast.152), channel_id=1, source_target_pairs={{0,4},{4,8},{8,12},{12,0},{1,5},{5,9},{9,13},{13,1},{2,6},{6,10},{... | collective-permute-start | bytes 2359304 | tf_op jit(solution)/shard_map/ppermute | solution.py:115
  11.4 26.3 %collective-permute-start.1 = (bf16[194048]{0:T(1024)(128)(2,1)}, bf16[194048]{0:T(1024)(128)(2,1)}, u32[]{:S(2)}, u32[]{:S(2)}) collective-permute-start(bf16[194048]{0:T(1024)(128)(2,1)} %get-tuple-element.48), channel_id=1, source_target_pairs={{0,2},{1,3},{2,0},{3,1},{4,6},{5,7},{6,4},{7,5},{8,10},{9,11},{10,... | collective-permute-start | bytes 1164296 | tf_op jit(solution)/shard_map/ppermute | solution.py:115
  21.8 1.2 copy-start.15
  21.8 21.6 %collective-permute-start.2 = (bf16[194048]{0:T(1024)(128)(2,1)S(1)}, bf16[194048]{0:T(1024)(128)(2,1)}, u32[]{:S(2)}, u32[]{:S(2)}) collective-permute-start(bf16[194048]{0:T(1024)(128)(2,1)S(1)} %get-tuple-element.47), channel_id=1, source_target_pairs={{0,3},{1,0},{2,1},{3,2},{4,7},{5,4},{6,5},{7,6},{8,11},{9,8},{10,9... | collective-permute-start | bytes 1164296 | tf_op jit(solution)/shard_map/ppermute | solution.py:115
  37.7 19.7 %collective-permute-start.6 = (bf16[1,128,3072]{2,1,0:T(8,128)(2,1)S(1)}, bf16[1,128,3072]{2,1,0:T(8,128)(2,1)}, u32[]{:S(2)}, u32[]{:S(2)}) collective-permute-start(bf16[1,128,3072]{2,1,0:T(8,128)(2,1)S(1)} %copy-done.12), channel_id=1, source_target_pairs={{0,16},{16,0},{1,17},{17,1},{2,18},{18,2},{3,19},{19,3},{4,20},{20... | collective-permute-start | bytes 2359304 | tf_op jit(solution)/shard_map/ppermute | solution.py:17
  46.4 9.5 %copy-start.13 = (bf16[128,3072]{1,0:T(8,128)(2,1)}, bf16[128,3072]{1,0:T(8,128)(2,1)S(1)}, u32[]{:S(2)}) copy-start(bf16[128,3072]{1,0:T(8,128)(2,1)S(1)} %collective-permute-done.5) | copy-start | bytes 2359300
  55.9 13.7 %copy-start.8 = (f32[512,1536]{1,0:T(8,128)}, f32[512,1536]{1,0:T(8,128)S(1)}, u32[]{:S(2)}) copy-start(f32[512,1536]{1,0:T(8,128)S(1)} %fusion.2) | copy-start | bytes 9437188
  57.4 92.5 %collective-permute-start.20 = (bf16[128,3072]{1,0:T(8,128)(2,1)}, bf16[128,3072]{1,0:T(8,128)(2,1)}, u32[]{:S(2)}, u32[]{:S(2)}) collective-permute-start(bf16[128,3072]{1,0:T(8,128)(2,1)} %bitcast.31), channel_id=1, source_target_pairs={{0,4},{4,8},{8,12},{12,0},{1,5},{5,9},{9,13},{13,1},{2,6},{6,10},{... | collective-permute-start | bytes 2359304 | tf_op jit(solution)/shard_map/ppermute | solution.py:115
  57.4 94.7 %collective-permute-start.21 = (bf16[128,3072]{1,0:T(8,128)(2,1)}, bf16[128,3072]{1,0:T(8,128)(2,1)}, u32[]{:S(2)}, u32[]{:S(2)}) collective-permute-start(bf16[128,3072]{1,0:T(8,128)(2,1)} %bitcast.31), channel_id=1, source_target_pairs={{0,8},{4,12},{8,0},{12,4},{1,9},{5,13},{9,1},{13,5},{2,10},{6,14},... | collective-permute-start | bytes 2359304 | tf_op jit(solution)/shard_map/ppermute | solution.py:115
  60.0 28.5 %collective-permute-start.9 = (bf16[512,384]{1,0:T(8,128)(2,1)}, bf16[512,384]{1,0:T(8,128)(2,1)}, u32[]{:S(2)}, u32[]{:S(2)}) collective-permute-start(bf16[512,384]{1,0:T(8,128)(2,1)} %get-tuple-element.32), channel_id=1, source_target_pairs={{0,1},{1,2},{2,3},{3,0},{4,5},{5,6},{6,7},{7,4},{8,9},{9,10},{10,1... | collective-permute-start | bytes 1179656 | tf_op jit(solution)/shard_map/ppermute | solution.py:115
  66.0 29.7 %collective-permute-start.8 = (bf16[512,384]{1,0:T(8,128)(2,1)}, bf16[512,384]{1,0:T(8,128)(2,1)}, u32[]{:S(2)}, u32[]{:S(2)}) collective-permute-start(bf16[512,384]{1,0:T(8,128)(2,1)} %get-tuple-element.33), channel_id=1, source_target_pairs={{0,2},{1,3},{2,0},{3,1},{4,6},{5,7},{6,4},{7,5},{8,10},{9,11},{10,... | collective-permute-start | bytes 1179656 | tf_op jit(solution)/shard_map/ppermute | solution.py:115
  69.4 26.3 %collective-permute-start.7 = (bf16[512,384]{1,0:T(8,128)(2,1)}, bf16[512,384]{1,0:T(8,128)(2,1)}, u32[]{:S(2)}, u32[]{:S(2)}) collective-permute-start(bf16[512,384]{1,0:T(8,128)(2,1)} %get-tuple-element.31), channel_id=1, source_target_pairs={{0,3},{1,0},{2,1},{3,2},{4,7},{5,4},{6,5},{7,6},{8,11},{9,8},{10,9... | collective-permute-start | bytes 1179656 | tf_op jit(solution)/shard_map/ppermute | solution.py:115
  74.6 4.3 %copy-start.14 = (bf16[128,3072]{1,0:T(8,128)(2,1)S(1)}, bf16[128,3072]{1,0:T(8,128)(2,1)}, u32[]{:S(2)}) copy-start(bf16[128,3072]{1,0:T(8,128)(2,1)} %copy-done.13) | copy-start | bytes 2359300
  76.8 5.1 %copy-start.6 = (bf16[1,128,364]{2,1,0:T(8,128)(2,1)S(1)}, bf16[1,128,364]{2,1,0:T(8,128)(2,1)}, u32[]{:S(2)}) copy-start(bf16[1,128,364]{2,1,0:T(8,128)(2,1)} %copy-done.5) | copy-start | bytes 279556
  76.8 5.1 %copy-start.9 = (bf16[128,364]{1,0:T(8,128)(2,1)S(1)}, bf16[128,364]{1,0:T(8,128)(2,1)}, u32[]{:S(2)}) copy-start(bf16[128,364]{1,0:T(8,128)(2,1)} %reshape.139) | copy-start | bytes 279556
  76.8 5.2 %copy-start.10 = (bf16[128,364]{1,0:T(8,128)(2,1)S(1)}, bf16[128,364]{1,0:T(8,128)(2,1)}, u32[]{:S(2)}) copy-start(bf16[128,364]{1,0:T(8,128)(2,1)} %reshape.142) | copy-start | bytes 279556
  76.8 5.2 %copy-start.11 = (bf16[128,364]{1,0:T(8,128)(2,1)S(1)}, bf16[128,364]{1,0:T(8,128)(2,1)}, u32[]{:S(2)}) copy-start(bf16[128,364]{1,0:T(8,128)(2,1)} %reshape.145) | copy-start | bytes 279556
  88.4 9.1 %copy-start = (bf16[3,512,512]{1,2,0:T(8,128)(2,1)S(1)}, bf16[3,512,512]{1,2,0:T(8,128)(2,1)}, u32[]{:S(2)}) copy-start(bf16[3,512,512]{1,2,0:T(8,128)(2,1)} %exponential_convert_fusion) | copy-start | bytes 4718596
  97.4 1.7 copy-start.2
  100.1 1.5 copy-start.1
  102.9 21.4 %collective-permute-start.10 = (bf16[512,384]{0,1:T(8,128)(2,1)S(1)}, bf16[512,384]{0,1:T(8,128)(2,1)}, u32[]{:S(2)}, u32[]{:S(2)}) collective-permute-start(bf16[512,384]{0,1:T(8,128)(2,1)S(1)} %bitcast.140), channel_id=1, source_target_pairs={{0,3},{1,0},{2,1},{3,2},{4,7},{5,4},{6,5},{7,6},{8,11},{9,8},{10,9... | collective-permute-start | bytes 1179656 | tf_op jit(solution)/shard_map/ppermute | solution.py:115
  110.8 37.0 %collective-permute-start.11 = (bf16[512,384]{0,1:T(8,128)(2,1)S(1)}, bf16[512,384]{0,1:T(8,128)(2,1)}, u32[]{:S(2)}, u32[]{:S(2)}) collective-permute-start(bf16[512,384]{0,1:T(8,128)(2,1)S(1)} %bitcast.141), channel_id=1, source_target_pairs={{0,2},{1,3},{2,0},{3,1},{4,6},{5,7},{6,4},{7,5},{8,10},{9,11},{10,... | collective-permute-start | bytes 1179656 | tf_op jit(solution)/shard_map/ppermute | solution.py:115
  113.3 36.0 %collective-permute-start.12 = (bf16[512,384]{0,1:T(8,128)(2,1)S(1)}, bf16[512,384]{0,1:T(8,128)(2,1)}, u32[]{:S(2)}, u32[]{:S(2)}) collective-permute-start(bf16[512,384]{0,1:T(8,128)(2,1)S(1)} %bitcast.142), channel_id=1, source_target_pairs={{0,1},{1,2},{2,3},{3,0},{4,5},{5,6},{6,7},{7,4},{8,9},{9,10},{10,1... | collective-permute-start | bytes 1179656 | tf_op jit(solution)/shard_map/ppermute | solution.py:115
  113.8 4.1 %copy-start.3 = (f32[512,3,128]{0,2,1:T(8,128)S(1)}, f32[512,3,128]{0,2,1:T(8,128)}, u32[]{:S(2)}) copy-start(f32[512,3,128]{0,2,1:T(8,128)} %get-tuple-element.59) | copy-start | bytes 2359300
  114.9 4.1 %copy-start.4 = (f32[512,3,128]{0,2,1:T(8,128)S(1)}, f32[512,3,128]{0,2,1:T(8,128)}, u32[]{:S(2)}) copy-start(f32[512,3,128]{0,2,1:T(8,128)} %get-tuple-element.57) | copy-start | bytes 2359300
  123.5 24.2 %copy-start.7 = (bf16[4,128,364]{2,1,0:T(8,128)(2,1)S(1)}, bf16[4,128,364]{2,1,0:T(8,128)(2,1)}, u32[]{:S(2)}) copy-start(bf16[4,128,364]{2,1,0:T(8,128)(2,1)} %constant_dynamic-slice_fusion) | copy-start | bytes 1118212
  124.3 29.8 %collective-permute-start.22 = (bf16[128,3072]{1,0:T(8,128)(2,1)}, bf16[128,3072]{1,0:T(8,128)(2,1)S(1)}, u32[]{:S(2)}, u32[]{:S(2)}) collective-permute-start(bf16[128,3072]{1,0:T(8,128)(2,1)} %bitcast.31), channel_id=1, source_target_pairs={{0,12},{4,0},{8,4},{12,8},{1,13},{5,1},{9,5},{13,9},{2,14},{6,2},{... | collective-permute-start | bytes 2359304 | tf_op jit(solution)/shard_map/ppermute | solution.py:115
  147.7 12.1 %collective-permute-start.23 = (bf16[512,364]{1,0:T(8,128)(2,1)S(1)}, bf16[512,364]{1,0:T(8,128)(2,1)S(1)}, u32[]{:S(2)}, u32[]{:S(2)}) collective-permute-start(bf16[512,364]{1,0:T(8,128)(2,1)S(1)} %bitcast.148), channel_id=1, source_target_pairs={{0,16},{16,0},{1,17},{17,1},{2,18},{18,2},{3,19},{19,3},{4,20},{20... | collective-permute-start | bytes 1118216 | tf_op jit(solution)/shard_map/ppermute | solution.py:17
  149.3 19.5 %collective-permute-start.16 = (bf16[512,384]{0,1:T(8,128)(2,1)S(1)}, bf16[512,384]{0,1:T(8,128)(2,1)S(1)}, u32[]{:S(2)}, u32[]{:S(2)}) collective-permute-start(bf16[512,384]{0,1:T(8,128)(2,1)S(1)} %bitcast.143), channel_id=1, source_target_pairs={{0,16},{16,0},{1,17},{17,1},{2,18},{18,2},{3,19},{19,3},{4,20},{20... | collective-permute-start | bytes 1179656 | tf_op jit(solution)/shard_map/ppermute | solution.py:17
  149.9 20.0 %collective-permute-start.13 = (bf16[3,128,384]{2,1,0:T(8,128)(2,1)S(1)}, bf16[3,128,384]{2,1,0:T(8,128)(2,1)S(1)}, u32[]{:S(2)}, u32[]{:S(2)}) collective-permute-start(bf16[3,128,384]{2,1,0:T(8,128)(2,1)S(1)} %get-tuple-element.39), channel_id=1, source_target_pairs={{0,3},{1,0},{2,1},{3,2},{4,7},{5,4},{6,5},{7,6},{8,11},{9,8},{10,9... | collective-permute-start | bytes 884744 | tf_op jit(solution)/shard_map/ppermute | solution.py:115
  152.0 23.5 %collective-permute-start.14 = (bf16[3,128,384]{2,1,0:T(8,128)(2,1)S(1)}, bf16[3,128,384]{2,1,0:T(8,128)(2,1)S(1)}, u32[]{:S(2)}, u32[]{:S(2)}) collective-permute-start(bf16[3,128,384]{2,1,0:T(8,128)(2,1)S(1)} %get-tuple-element.38), channel_id=1, source_target_pairs={{0,2},{1,3},{2,0},{3,1},{4,6},{5,7},{6,4},{7,5},{8,10},{9,11},{10,... | collective-permute-start | bytes 884744 | tf_op jit(solution)/shard_map/ppermute | solution.py:115
  154.1 21.5 %collective-permute-start.15 = (bf16[3,128,384]{2,1,0:T(8,128)(2,1)S(1)}, bf16[3,128,384]{2,1,0:T(8,128)(2,1)S(1)}, u32[]{:S(2)}, u32[]{:S(2)}) collective-permute-start(bf16[3,128,384]{2,1,0:T(8,128)(2,1)S(1)} %get-tuple-element.37), channel_id=1, source_target_pairs={{0,1},{1,2},{2,3},{3,0},{4,5},{5,6},{6,7},{7,4},{8,9},{9,10},{10,1... | collective-permute-start | bytes 884744 | tf_op jit(solution)/shard_map/ppermute | solution.py:115
  159.8 17.4 %collective-permute-start.17 = (bf16[512,384]{0,1:T(8,128)(2,1)}, bf16[512,384]{0,1:T(8,128)(2,1)S(1)}, u32[]{:S(2)}, u32[]{:S(2)}) collective-permute-start(bf16[512,384]{0,1:T(8,128)(2,1)} %collective-permute-done.10), channel_id=1, source_target_pairs={{0,16},{16,0},{1,17},{17,1},{2,18},{18,2},{3,19},{19,3},{4,20},{20... | collective-permute-start | bytes 1179656 | tf_op jit(solution)/shard_map/ppermute | solution.py:17
  168.8 16.3 %collective-permute-start.18 = (bf16[512,384]{0,1:T(8,128)(2,1)}, bf16[512,384]{0,1:T(8,128)(2,1)S(1)}, u32[]{:S(2)}, u32[]{:S(2)}) collective-permute-start(bf16[512,384]{0,1:T(8,128)(2,1)} %collective-permute-done.11), channel_id=1, source_target_pairs={{0,16},{16,0},{1,17},{17,1},{2,18},{18,2},{3,19},{19,3},{4,20},{20... | collective-permute-start | bytes 1179656 | tf_op jit(solution)/shard_map/ppermute | solution.py:17
  169.8 21.8 %collective-permute-start.19 = (bf16[512,384]{0,1:T(8,128)(2,1)}, bf16[512,384]{0,1:T(8,128)(2,1)S(1)}, u32[]{:S(2)}, u32[]{:S(2)}) collective-permute-start(bf16[512,384]{0,1:T(8,128)(2,1)} %collective-permute-done.12), channel_id=1, source_target_pairs={{0,16},{16,0},{1,17},{17,1},{2,18},{18,2},{3,19},{19,3},{4,20},{20... | collective-permute-start | bytes 1179656 | tf_op jit(solution)/shard_map/ppermute | solution.py:17
  175.7 20.5 %slice-start = ((s8[6291456]{0:T(1024)(128)(4,1)}), s8[4194304]{0:T(1024)(128)(4,1)S(1)}, s32[]{:S(2)}) async-start(s8[6291456]{0:T(1024)(128)(4,1)} %bitcast.135), calls=%async_computation | async-start | bytes 8388608
  186.2 10.0 %slice-start.1 = ((s8[6291456]{0:T(1024)(128)(4,1)}), s8[2097152]{0:T(1024)(128)(4,1)S(1)}, s32[]{:S(2)}) async-start(s8[6291456]{0:T(1024)(128)(4,1)} %bitcast.135), calls=%async_computation.1 | async-start | bytes 4194304

commit v11 on v10

--- a/solution.py
+++ b/solution.py
@@ -286,8 +286,10 @@
     )
     back = jnp.zeros((3, tokens, width_all), jnp.float32)
     back = lax.dynamic_update_slice_in_dim(back, mine, me * width, 2)
+    received = [shifted(sendable[s], "col", -s % n) for s in range(1, n)]
+    received, out_weight_grad = lax.optimization_barrier((received, out_weight_grad))
     for s in range(1, n):
-        got = shifted(sendable[s], "col", -s % n).astype(jnp.float32)
+        got = received[s - 1].astype(jnp.float32)
         back = lax.dynamic_update_slice_in_dim(back, got, ((me + s) % n) * width, 2)
     back = back.reshape(3, 1, tokens, width_all)
     return (back[0], back[1], back[2], out_weight_grad, embed_weight_grad)

time: 210 us -> 212 us (level)
  waiting for transfers between devices: 71.1 us -> 74.8 us
    ppermute x6, waiting for transfers between devices: 15.9 us -> 24.1 us  [swap_dp(): return lax.ppermute(x, 'dp', [(0, 1), (1, 0)])]
    ppermute x18, waiting for transfers between devices: 55.2 us -> 50.7 us  [shifted(): return lax.ppermute(x, axis, [(j, (j + step) % n) for j in range(n)])]
  transfers between devices with their start and end apart: 24 -> 24, of which waited for: 11 -> 11; matrix products, arithmetic and copies ran while one was open for 35% -> 42% of each run, Pallas kernels for 0% -> 0%
where the time goes in v11:
time: 212 us; the launch traced here: 211 us
  waiting for transfers between devices  74.8 us (35%)
  local copies, waits for them, and re-layouts  46.4 us (22%)
  starting transfers between devices  37.8 us (18%)
  matrix products  36.9 us (17%)
  other arithmetic  13.7 us (6%)
    ppermute x18, waiting for transfers between devices, shifted(): return lax.ppermute(x, axis, [(j, (j + step) % n) for j in range(n)])  50.7 us
    ppermute x18, starting transfers between devices, shifted(): return lax.ppermute(x, axis, [(j, (j + step) % n) for j in range(n)])  30.2 us
    ppermute x6, waiting for transfers between devices, swap_dp(): return lax.ppermute(x, 'dp', [(0, 1), (1, 0)])  24.1 us
    unnamed x63, local copies, waits for them, and re-layouts  16.3 us
    dot_general x1, matrix products, body_heads(): lax.dot_general(out_both, grad_both, (((1,), (0,)), ((), ())), preferred_...  13.1 us
    dot_general x1, matrix products, body_heads(): lax.dot_general(dense_grad, out_weight, (((1,), (1,)), ((), ())), preferr...  9.4 us
    ppermute x6, starting transfers between devices, swap_dp(): return lax.ppermute(x, 'dp', [(0, 1), (1, 0)])  7.55 us
    dot_general x1, matrix products, contract_rows(): lax.dot_general(left, right, (((0,), (0,)), ((), ())), preferred_element_...  7.47 us
  transfers between devices with their start and end apart: 24, of which 11 were waited for; matrix products, arithmetic and copies ran while one was open for 42% of the time, Pallas kernels for 0%

profile of v11, /device:TPU:0, one launch (start us, length us, event | category | flops | bytes accessed | tf_op | source)
XLA Modules:
  0.0 211.0 jit_solution(11183522780702513626)
XLA Ops:
  6.6 3.0 %collective-permute-start = (bf16[194048]{0:T(1024)(128)(2,1)}, bf16[194048]{0:T(1024)(128)(2,1)S(1)}, u32[]{:S(2)}, u32[]{:S(2)}) collective-permute-start(bf16[194048]{0:T(1024)(128)(2,1)} %get-tuple-element.57), channel_id=1, source_target_pairs={{0,1},{1,2},{2,3},{3,0},{4,5},{5,6},{6,7},{7,4},{8,9},{9,10},{10,1... | collective-permute-start | bytes 1164296 | tf_op jit(solution)/shard_map/ppermute | solution.py:115
  11.4 2.6 %collective-permute-start.1 = (bf16[194048]{0:T(1024)(128)(2,1)}, bf16[194048]{0:T(1024)(128)(2,1)}, u32[]{:S(2)}, u32[]{:S(2)}) collective-permute-start(bf16[194048]{0:T(1024)(128)(2,1)} %get-tuple-element.56), channel_id=1, source_target_pairs={{0,2},{1,3},{2,0},{3,1},{4,6},{5,7},{6,4},{7,5},{8,10},{9,11},{10,... | collective-permute-start | bytes 1164296 | tf_op jit(solution)/shard_map/ppermute | solution.py:115
  14.0 7.9 %collective-permute-done = bf16[194048]{0:T(1024)(128)(2,1)S(1)} collective-permute-done((bf16[194048]{0:T(1024)(128)(2,1)}, bf16[194048]{0:T(1024)(128)(2,1)S(1)}, u32[]{:S(2)}, u32[]{:S(2)}) %collective-permute-start) | collective-permute-done | bytes 388128 | tf_op jit(solution)/shard_map/ppermute | solution.py:115
  21.8 1.2 collective-permute-start.2
  26.9 10.8 %collective-permute-done.1 = bf16[194048]{0:T(1024)(128)(2,1)} collective-permute-done((bf16[194048]{0:T(1024)(128)(2,1)}, bf16[194048]{0:T(1024)(128)(2,1)}, u32[]{:S(2)}, u32[]{:S(2)}) %collective-permute-start.1) | collective-permute-done | bytes 388128 | tf_op jit(solution)/shard_map/ppermute | solution.py:115
  37.7 1.5 collective-permute-start.6
  42.1 1.3 collective-permute-done.2
  46.5 9.4 %fusion.2 = f32[512,1536]{1,0:T(8,128)S(1)} fusion(bf16[1536,3072]{1,0:T(8,128)(2,1)} %param.10, bf16[128,3072]{1,0:T(8,128)(2,1)S(1)} %collective-permute-done.5, bf16[128,3072]{1,0:T(8,128)(2,1)} %collective-permute-done.4, bf16[128,3072]{1,0:T(8,128)(2,1)} %collective-permute-done.3, bf16[128,3072]{1,0:T(8,128)(2,1)S(1)} %bitcast.153), kind=kOutput, calls=%fused_computation.2 | convolution fusion | flops 4844421120 | bytes 15728640 | tf_op jit(solution)/shard_map/dot_general | solution.py:222
  55.9 1.4 collective-permute-done.6
  57.4 1.5 collective-permute-start.21
  58.9 1.1 dynamic-slice_convert_fusion.2
  60.0 6.0 %collective-permute-start.9 = (bf16[512,384]{1,0:T(8,128)(2,1)}, bf16[512,384]{1,0:T(8,128)(2,1)}, u32[]{:S(2)}, u32[]{:S(2)}) collective-permute-start(bf16[512,384]{1,0:T(8,128)(2,1)} %get-tuple-element.40), channel_id=1, source_target_pairs={{0,1},{1,2},{2,3},{3,0},{4,5},{5,6},{6,7},{7,4},{8,9},{9,10},{10,1... | collective-permute-start | bytes 1179656 | tf_op jit(solution)/shard_map/ppermute | solution.py:115
  66.0 3.4 %collective-permute-start.8 = (bf16[512,384]{1,0:T(8,128)(2,1)}, bf16[512,384]{1,0:T(8,128)(2,1)}, u32[]{:S(2)}, u32[]{:S(2)}) collective-permute-start(bf16[512,384]{1,0:T(8,128)(2,1)} %get-tuple-element.41), channel_id=1, source_target_pairs={{0,2},{1,3},{2,0},{3,1},{4,6},{5,7},{6,4},{7,5},{8,10},{9,11},{10,... | collective-permute-start | bytes 1179656 | tf_op jit(solution)/shard_map/ppermute | solution.py:115
  72.4 1.6 multiply_reduce_fusion
  74.6 2.1 %constant_dynamic-update-slice_fusion.9 = bf16[1024,3072]{1,0:T(8,128)(2,1)} fusion(bf16[1024,3072]{1,0:T(8,128)(2,1)} %constant_dynamic-update-slice_fusion.10, bf16[128,3072]{1,0:T(8,128)(2,1)} %collective-permute-done.3), kind=kLoop, calls=%fused_computation.93 | loop fusion | bytes 1572864
  76.8 2.1 %constant_dynamic-update-slice_fusion.8 = bf16[1024,3072]{1,0:T(8,128)(2,1)} fusion(bf16[1024,3072]{1,0:T(8,128)(2,1)} %constant_dynamic-update-slice_fusion.9, bf16[128,3072]{1,0:T(8,128)(2,1)} %collective-permute-done.4), kind=kLoop, calls=%fused_computation.92 | loop fusion | bytes 1572864
  79.8 2.1 constant_dynamic-update-slice_fusion.6
  82.9 1.9 copy.37
  84.9 1.9 squeeze.50
  86.8 1.7 exponential_convert_fusion
  88.4 7.2 %collective-permute-done.8 = bf16[512,384]{1,0:T(8,128)(2,1)} collective-permute-done((bf16[512,384]{1,0:T(8,128)(2,1)}, bf16[512,384]{1,0:T(8,128)(2,1)}, u32[]{:S(2)}, u32[]{:S(2)}) %collective-permute-start.8) | collective-permute-done | bytes 393248 | tf_op jit(solution)/shard_map/ppermute | solution.py:115
  95.7 1.7 add_convert_fusion
  97.6 1.5 fusion.37
  100.1 1.5 fusion.36
  101.7 1.3 fusion.35
  102.9 7.9 %collective-permute-start.10 = (bf16[512,384]{0,1:T(8,128)(2,1)S(1)}, bf16[512,384]{0,1:T(8,128)(2,1)}, u32[]{:S(2)}, u32[]{:S(2)}) collective-permute-start(bf16[512,384]{0,1:T(8,128)(2,1)S(1)} %bitcast.140), channel_id=1, source_target_pairs={{0,3},{1,0},{2,1},{3,2},{4,7},{5,4},{6,5},{7,6},{8,11},{9,8},{10,9... | collective-permute-start | bytes 1179656 | tf_op jit(solution)/shard_map/ppermute | solution.py:115
  110.8 2.5 %collective-permute-start.11 = (bf16[512,384]{0,1:T(8,128)(2,1)S(1)}, bf16[512,384]{0,1:T(8,128)(2,1)}, u32[]{:S(2)}, u32[]{:S(2)}) collective-permute-start(bf16[512,384]{0,1:T(8,128)(2,1)S(1)} %bitcast.141), channel_id=1, source_target_pairs={{0,2},{1,3},{2,0},{3,1},{4,6},{5,7},{6,4},{7,5},{8,10},{9,11},{10,... | collective-permute-start | bytes 1179656 | tf_op jit(solution)/shard_map/ppermute | solution.py:115
  116.0 1.9 fusion.15
  117.9 1.1 reshape.149
  119.0 1.1 reshape.148
  120.1 1.4 reshape.147
  121.5 1.8 constant_dynamic-slice_fusion.1
  124.4 23.4 %collective-permute-done.11 = bf16[512,384]{0,1:T(8,128)(2,1)} collective-permute-done((bf16[512,384]{0,1:T(8,128)(2,1)S(1)}, bf16[512,384]{0,1:T(8,128)(2,1)}, u32[]{:S(2)}, u32[]{:S(2)}) %collective-permute-start.11) | collective-permute-done | bytes 393248 | tf_op jit(solution)/shard_map/ppermute | solution.py:115
  147.7 1.5 collective-permute-start.23
  150.2 2.1 constant_dynamic-update-slice_fusion.5
  152.2 2.1 constant_dynamic-update-slice_fusion.4
  154.3 1.5 collective-permute-start.17
  156.8 3.0 %collective-permute-done.23 = bf16[512,364]{1,0:T(8,128)(2,1)S(1)} collective-permute-done((bf16[512,364]{1,0:T(8,128)(2,1)S(1)}, bf16[512,364]{1,0:T(8,128)(2,1)S(1)}, u32[]{:S(2)}, u32[]{:S(2)}) %collective-permute-start.23) | collective-permute-done | bytes 372768 | tf_op jit(solution)/shard_map/ppermute | solution.py:17
  159.8 1.5 collective-permute-start.18
  161.3 7.5 %fusion.18 = f32[364,3072]{1,0:T(8,128)} fusion(bf16[1024,3072]{1,0:T(8,128)(2,1)} %constant_dynamic-update-slice_fusion.3, bf16[512,364]{1,0:T(8,128)(2,1)S(1)} %collective-permute-done.23, bf16[512,364]{1,0:T(8,128)(2,1)S(1)} %bitcast.149), kind=kOutput, calls=%fused_computation.40 | convolution fusion | flops 2291580928 | bytes 11509760 | tf_op jit(solution)/shard_map/dot_general | solution.py:11
  169.8 6.8 %collective-permute-done.17 = bf16[512,384]{0,1:T(8,128)(2,1)S(1)} collective-permute-done((bf16[512,384]{0,1:T(8,128)(2,1)}, bf16[512,384]{0,1:T(8,128)(2,1)S(1)}, u32[]{:S(2)}, u32[]{:S(2)}) %collective-permute-start.17) | collective-permute-done | bytes 393248 | tf_op jit(solution)/shard_map/ppermute | solution.py:17
  177.7 7.3 %collective-permute-done.18 = bf16[512,384]{0,1:T(8,128)(2,1)S(1)} collective-permute-done((bf16[512,384]{0,1:T(8,128)(2,1)}, bf16[512,384]{0,1:T(8,128)(2,1)S(1)}, u32[]{:S(2)}, u32[]{:S(2)}) %collective-permute-start.18) | collective-permute-done | bytes 393248 | tf_op jit(solution)/shard_map/ppermute | solution.py:17
  186.2 5.5 %collective-permute-done.19 = bf16[512,384]{0,1:T(8,128)(2,1)S(1)} collective-permute-done((bf16[512,384]{0,1:T(8,128)(2,1)}, bf16[512,384]{0,1:T(8,128)(2,1)S(1)}, u32[]{:S(2)}, u32[]{:S(2)}) %collective-permute-start.19) | collective-permute-done | bytes 393248 | tf_op jit(solution)/shard_map/ppermute | solution.py:17
  192.9 1.1 fusion.28
  194.0 1.1 fusion.26
  195.1 1.1 fusion.24
  196.2 13.1 %fusion = f32[4,384,3072]{2,1,0:T(8,128)} fusion(bf16[1024,3072]{1,0:T(8,128)(2,1)S(1)} %bitcast.136, bf16[8,1024,384]{1,2,0:T(8,128)(2,1)S(1)} %fusion.24, s32[]{:T(128)S(6)} %select_n.114), kind=kOutput, calls=%fused_computation | convolution fusion | flops 9663676416 | bytes 28311556 | tf_op jit(solution)/shard_map/dot_general | solution.py:275
  209.5 1.5 slice_bitcast_fusion
  (137 shorter events, 34.0 us)
Async XLA Ops:
  2.7 2.7 %copy-start.5 = (bf16[1,128,364]{2,1,0:T(8,128)(2,1)}, bf16[1,128,364]{2,1,0:T(8,128)(2,1)S(1)}, u32[]{:S(2)}) copy-start(bf16[1,128,364]{2,1,0:T(8,128)(2,1)S(1)} %copy.30) | copy-start | bytes 279556
  5.2 4.4 %copy-start.12 = (bf16[1,128,3072]{2,1,0:T(8,128)(2,1)S(1)}, bf16[1,128,3072]{2,1,0:T(8,128)(2,1)}, u32[]{:S(2)}) copy-start(bf16[1,128,3072]{2,1,0:T(8,128)(2,1)} %param.11) | copy-start | bytes 2359300
  6.6 15.2 %collective-permute-start = (bf16[194048]{0:T(1024)(128)(2,1)}, bf16[194048]{0:T(1024)(128)(2,1)S(1)}, u32[]{:S(2)}, u32[]{:S(2)}) collective-permute-start(bf16[194048]{0:T(1024)(128)(2,1)} %get-tuple-element.57), channel_id=1, source_target_pairs={{0,1},{1,2},{2,3},{3,0},{4,5},{5,6},{6,7},{7,4},{8,9},{9,10},{10,1... | collective-permute-start | bytes 1164296 | tf_op jit(solution)/shard_map/ppermute | solution.py:115
  9.7 36.7 %collective-permute-start.5 = (bf16[128,3072]{1,0:T(8,128)(2,1)S(1)}, bf16[128,3072]{1,0:T(8,128)(2,1)S(1)}, u32[]{:S(2)}, u32[]{:S(2)}) collective-permute-start(bf16[128,3072]{1,0:T(8,128)(2,1)S(1)} %bitcast.150), channel_id=1, source_target_pairs={{0,12},{4,0},{8,4},{12,8},{1,13},{5,1},{9,5},{13,9},{2,14},{6,2},{... | collective-permute-start | bytes 2359304 | tf_op jit(solution)/shard_map/ppermute | solution.py:115
  10.3 36.1 %collective-permute-start.4 = (bf16[128,3072]{1,0:T(8,128)(2,1)S(1)}, bf16[128,3072]{1,0:T(8,128)(2,1)}, u32[]{:S(2)}, u32[]{:S(2)}) collective-permute-start(bf16[128,3072]{1,0:T(8,128)(2,1)S(1)} %bitcast.151), channel_id=1, source_target_pairs={{0,8},{4,12},{8,0},{12,4},{1,9},{5,13},{9,1},{13,5},{2,10},{6,14},... | collective-permute-start | bytes 2359304 | tf_op jit(solution)/shard_map/ppermute | solution.py:115
  11.1 35.3 %collective-permute-start.3 = (bf16[128,3072]{1,0:T(8,128)(2,1)S(1)}, bf16[128,3072]{1,0:T(8,128)(2,1)}, u32[]{:S(2)}, u32[]{:S(2)}) collective-permute-start(bf16[128,3072]{1,0:T(8,128)(2,1)S(1)} %bitcast.152), channel_id=1, source_target_pairs={{0,4},{4,8},{8,12},{12,0},{1,5},{5,9},{9,13},{13,1},{2,6},{6,10},{... | collective-permute-start | bytes 2359304 | tf_op jit(solution)/shard_map/ppermute | solution.py:115
  11.4 26.3 %collective-permute-start.1 = (bf16[194048]{0:T(1024)(128)(2,1)}, bf16[194048]{0:T(1024)(128)(2,1)}, u32[]{:S(2)}, u32[]{:S(2)}) collective-permute-start(bf16[194048]{0:T(1024)(128)(2,1)} %get-tuple-element.56), channel_id=1, source_target_pairs={{0,2},{1,3},{2,0},{3,1},{4,6},{5,7},{6,4},{7,5},{8,10},{9,11},{10,... | collective-permute-start | bytes 1164296 | tf_op jit(solution)/shard_map/ppermute | solution.py:115
  21.8 1.2 copy-start.15
  21.8 21.6 %collective-permute-start.2 = (bf16[194048]{0:T(1024)(128)(2,1)S(1)}, bf16[194048]{0:T(1024)(128)(2,1)}, u32[]{:S(2)}, u32[]{:S(2)}) collective-permute-start(bf16[194048]{0:T(1024)(128)(2,1)S(1)} %get-tuple-element.55), channel_id=1, source_target_pairs={{0,3},{1,0},{2,1},{3,2},{4,7},{5,4},{6,5},{7,6},{8,11},{9,8},{10,9... | collective-permute-start | bytes 1164296 | tf_op jit(solution)/shard_map/ppermute | solution.py:115
  37.7 19.7 %collective-permute-start.6 = (bf16[1,128,3072]{2,1,0:T(8,128)(2,1)S(1)}, bf16[1,128,3072]{2,1,0:T(8,128)(2,1)}, u32[]{:S(2)}, u32[]{:S(2)}) collective-permute-start(bf16[1,128,3072]{2,1,0:T(8,128)(2,1)S(1)} %copy-done.12), channel_id=1, source_target_pairs={{0,16},{16,0},{1,17},{17,1},{2,18},{18,2},{3,19},{19,3},{4,20},{20... | collective-permute-start | bytes 2359304 | tf_op jit(solution)/shard_map/ppermute | solution.py:17
  46.4 9.5 %copy-start.13 = (bf16[128,3072]{1,0:T(8,128)(2,1)}, bf16[128,3072]{1,0:T(8,128)(2,1)S(1)}, u32[]{:S(2)}) copy-start(bf16[128,3072]{1,0:T(8,128)(2,1)S(1)} %collective-permute-done.5) | copy-start | bytes 2359300
  55.9 13.7 %copy-start.8 = (f32[512,1536]{1,0:T(8,128)}, f32[512,1536]{1,0:T(8,128)S(1)}, u32[]{:S(2)}) copy-start(f32[512,1536]{1,0:T(8,128)S(1)} %fusion.2) | copy-start | bytes 9437188
  57.4 92.5 %collective-permute-start.20 = (bf16[128,3072]{1,0:T(8,128)(2,1)}, bf16[128,3072]{1,0:T(8,128)(2,1)}, u32[]{:S(2)}, u32[]{:S(2)}) collective-permute-start(bf16[128,3072]{1,0:T(8,128)(2,1)} %bitcast.23), channel_id=1, source_target_pairs={{0,4},{4,8},{8,12},{12,0},{1,5},{5,9},{9,13},{13,1},{2,6},{6,10},{... | collective-permute-start | bytes 2359304 | tf_op jit(solution)/shard_map/ppermute | solution.py:115
  57.4 94.9 %collective-permute-start.21 = (bf16[128,3072]{1,0:T(8,128)(2,1)}, bf16[128,3072]{1,0:T(8,128)(2,1)}, u32[]{:S(2)}, u32[]{:S(2)}) collective-permute-start(bf16[128,3072]{1,0:T(8,128)(2,1)} %bitcast.23), channel_id=1, source_target_pairs={{0,8},{4,12},{8,0},{12,4},{1,9},{5,13},{9,1},{13,5},{2,10},{6,14},... | collective-permute-start | bytes 2359304 | tf_op jit(solution)/shard_map/ppermute | solution.py:115
  60.0 28.5 %collective-permute-start.9 = (bf16[512,384]{1,0:T(8,128)(2,1)}, bf16[512,384]{1,0:T(8,128)(2,1)}, u32[]{:S(2)}, u32[]{:S(2)}) collective-permute-start(bf16[512,384]{1,0:T(8,128)(2,1)} %get-tuple-element.40), channel_id=1, source_target_pairs={{0,1},{1,2},{2,3},{3,0},{4,5},{5,6},{6,7},{7,4},{8,9},{9,10},{10,1... | collective-permute-start | bytes 1179656 | tf_op jit(solution)/shard_map/ppermute | solution.py:115
  66.0 29.7 %collective-permute-start.8 = (bf16[512,384]{1,0:T(8,128)(2,1)}, bf16[512,384]{1,0:T(8,128)(2,1)}, u32[]{:S(2)}, u32[]{:S(2)}) collective-permute-start(bf16[512,384]{1,0:T(8,128)(2,1)} %get-tuple-element.41), channel_id=1, source_target_pairs={{0,2},{1,3},{2,0},{3,1},{4,6},{5,7},{6,4},{7,5},{8,10},{9,11},{10,... | collective-permute-start | bytes 1179656 | tf_op jit(solution)/shard_map/ppermute | solution.py:115
  69.4 26.3 %collective-permute-start.7 = (bf16[512,384]{1,0:T(8,128)(2,1)}, bf16[512,384]{1,0:T(8,128)(2,1)}, u32[]{:S(2)}, u32[]{:S(2)}) collective-permute-start(bf16[512,384]{1,0:T(8,128)(2,1)} %get-tuple-element.39), channel_id=1, source_target_pairs={{0,3},{1,0},{2,1},{3,2},{4,7},{5,4},{6,5},{7,6},{8,11},{9,8},{10,9... | collective-permute-start | bytes 1179656 | tf_op jit(solution)/shard_map/ppermute | solution.py:115
  74.6 4.3 %copy-start.14 = (bf16[128,3072]{1,0:T(8,128)(2,1)S(1)}, bf16[128,3072]{1,0:T(8,128)(2,1)}, u32[]{:S(2)}) copy-start(bf16[128,3072]{1,0:T(8,128)(2,1)} %copy-done.13) | copy-start | bytes 2359300
  76.8 5.1 %copy-start.6 = (bf16[1,128,364]{2,1,0:T(8,128)(2,1)S(1)}, bf16[1,128,364]{2,1,0:T(8,128)(2,1)}, u32[]{:S(2)}) copy-start(bf16[1,128,364]{2,1,0:T(8,128)(2,1)} %copy-done.5) | copy-start | bytes 279556
  76.8 5.1 %copy-start.9 = (bf16[128,364]{1,0:T(8,128)(2,1)S(1)}, bf16[128,364]{1,0:T(8,128)(2,1)}, u32[]{:S(2)}) copy-start(bf16[128,364]{1,0:T(8,128)(2,1)} %reshape.139) | copy-start | bytes 279556
  76.8 5.2 %copy-start.10 = (bf16[128,364]{1,0:T(8,128)(2,1)S(1)}, bf16[128,364]{1,0:T(8,128)(2,1)}, u32[]{:S(2)}) copy-start(bf16[128,364]{1,0:T(8,128)(2,1)} %reshape.142) | copy-start | bytes 279556
  76.8 5.2 %copy-start.11 = (bf16[128,364]{1,0:T(8,128)(2,1)S(1)}, bf16[128,364]{1,0:T(8,128)(2,1)}, u32[]{:S(2)}) copy-start(bf16[128,364]{1,0:T(8,128)(2,1)} %reshape.145) | copy-start | bytes 279556
  88.4 9.1 %copy-start = (bf16[3,512,512]{1,2,0:T(8,128)(2,1)S(1)}, bf16[3,512,512]{1,2,0:T(8,128)(2,1)}, u32[]{:S(2)}) copy-start(bf16[3,512,512]{1,2,0:T(8,128)(2,1)} %exponential_convert_fusion) | copy-start | bytes 4718596
  97.4 1.7 copy-start.2
  100.1 1.5 copy-start.1
  102.9 21.4 %collective-permute-start.10 = (bf16[512,384]{0,1:T(8,128)(2,1)S(1)}, bf16[512,384]{0,1:T(8,128)(2,1)}, u32[]{:S(2)}, u32[]{:S(2)}) collective-permute-start(bf16[512,384]{0,1:T(8,128)(2,1)S(1)} %bitcast.140), channel_id=1, source_target_pairs={{0,3},{1,0},{2,1},{3,2},{4,7},{5,4},{6,5},{7,6},{8,11},{9,8},{10,9... | collective-permute-start | bytes 1179656 | tf_op jit(solution)/shard_map/ppermute | solution.py:115
  110.8 37.0 %collective-permute-start.11 = (bf16[512,384]{0,1:T(8,128)(2,1)S(1)}, bf16[512,384]{0,1:T(8,128)(2,1)}, u32[]{:S(2)}, u32[]{:S(2)}) collective-permute-start(bf16[512,384]{0,1:T(8,128)(2,1)S(1)} %bitcast.141), channel_id=1, source_target_pairs={{0,2},{1,3},{2,0},{3,1},{4,6},{5,7},{6,4},{7,5},{8,10},{9,11},{10,... | collective-permute-start | bytes 1179656 | tf_op jit(solution)/shard_map/ppermute | solution.py:115
  113.3 36.0 %collective-permute-start.12 = (bf16[512,384]{0,1:T(8,128)(2,1)S(1)}, bf16[512,384]{0,1:T(8,128)(2,1)}, u32[]{:S(2)}, u32[]{:S(2)}) collective-permute-start(bf16[512,384]{0,1:T(8,128)(2,1)S(1)} %bitcast.142), channel_id=1, source_target_pairs={{0,1},{1,2},{2,3},{3,0},{4,5},{5,6},{6,7},{7,4},{8,9},{9,10},{10,1... | collective-permute-start | bytes 1179656 | tf_op jit(solution)/shard_map/ppermute | solution.py:115
  113.8 4.1 %copy-start.3 = (f32[512,3,128]{0,2,1:T(8,128)S(1)}, f32[512,3,128]{0,2,1:T(8,128)}, u32[]{:S(2)}) copy-start(f32[512,3,128]{0,2,1:T(8,128)} %get-tuple-element.67) | copy-start | bytes 2359300
  114.9 4.1 %copy-start.4 = (f32[512,3,128]{0,2,1:T(8,128)S(1)}, f32[512,3,128]{0,2,1:T(8,128)}, u32[]{:S(2)}) copy-start(f32[512,3,128]{0,2,1:T(8,128)} %get-tuple-element.65) | copy-start | bytes 2359300
  123.5 24.2 %copy-start.7 = (bf16[4,128,364]{2,1,0:T(8,128)(2,1)S(1)}, bf16[4,128,364]{2,1,0:T(8,128)(2,1)}, u32[]{:S(2)}) copy-start(bf16[4,128,364]{2,1,0:T(8,128)(2,1)} %constant_dynamic-slice_fusion) | copy-start | bytes 1118212
  124.3 30.0 %collective-permute-start.22 = (bf16[128,3072]{1,0:T(8,128)(2,1)}, bf16[128,3072]{1,0:T(8,128)(2,1)S(1)}, u32[]{:S(2)}, u32[]{:S(2)}) collective-permute-start(bf16[128,3072]{1,0:T(8,128)(2,1)} %bitcast.23), channel_id=1, source_target_pairs={{0,12},{4,0},{8,4},{12,8},{1,13},{5,1},{9,5},{13,9},{2,14},{6,2},{... | collective-permute-start | bytes 2359304 | tf_op jit(solution)/shard_map/ppermute | solution.py:115
  147.7 12.1 %collective-permute-start.23 = (bf16[512,364]{1,0:T(8,128)(2,1)S(1)}, bf16[512,364]{1,0:T(8,128)(2,1)S(1)}, u32[]{:S(2)}, u32[]{:S(2)}) collective-permute-start(bf16[512,364]{1,0:T(8,128)(2,1)S(1)} %bitcast.148), channel_id=1, source_target_pairs={{0,16},{16,0},{1,17},{17,1},{2,18},{18,2},{3,19},{19,3},{4,20},{20... | collective-permute-start | bytes 1118216 | tf_op jit(solution)/shard_map/ppermute | solution.py:17
  149.3 19.5 %collective-permute-start.16 = (bf16[512,384]{0,1:T(8,128)(2,1)S(1)}, bf16[512,384]{0,1:T(8,128)(2,1)S(1)}, u32[]{:S(2)}, u32[]{:S(2)}) collective-permute-start(bf16[512,384]{0,1:T(8,128)(2,1)S(1)} %bitcast.143), channel_id=1, source_target_pairs={{0,16},{16,0},{1,17},{17,1},{2,18},{18,2},{3,19},{19,3},{4,20},{20... | collective-permute-start | bytes 1179656 | tf_op jit(solution)/shard_map/ppermute | solution.py:17
  149.9 59.4 %collective-permute-start.13 = (bf16[3,128,384]{2,1,0:T(8,128)(2,1)S(1)}, bf16[3,128,384]{2,1,0:T(8,128)(2,1)S(1)}, u32[]{:S(2)}, u32[]{:S(2)}) collective-permute-start(bf16[3,128,384]{2,1,0:T(8,128)(2,1)S(1)} %get-tuple-element.47), channel_id=1, source_target_pairs={{0,3},{1,0},{2,1},{3,2},{4,7},{5,4},{6,5},{7,6},{8,11},{9,8},{10,9... | collective-permute-start | bytes 884744 | tf_op jit(solution)/shard_map/ppermute | solution.py:115
  152.2 57.1 %collective-permute-start.14 = (bf16[3,128,384]{2,1,0:T(8,128)(2,1)S(1)}, bf16[3,128,384]{2,1,0:T(8,128)(2,1)S(1)}, u32[]{:S(2)}, u32[]{:S(2)}) collective-permute-start(bf16[3,128,384]{2,1,0:T(8,128)(2,1)S(1)} %get-tuple-element.46), channel_id=1, source_target_pairs={{0,2},{1,3},{2,0},{3,1},{4,6},{5,7},{6,4},{7,5},{8,10},{9,11},{10,... | collective-permute-start | bytes 884744 | tf_op jit(solution)/shard_map/ppermute | solution.py:115
  154.3 22.3 %collective-permute-start.17 = (bf16[512,384]{0,1:T(8,128)(2,1)}, bf16[512,384]{0,1:T(8,128)(2,1)S(1)}, u32[]{:S(2)}, u32[]{:S(2)}) collective-permute-start(bf16[512,384]{0,1:T(8,128)(2,1)} %collective-permute-done.10), channel_id=1, source_target_pairs={{0,16},{16,0},{1,17},{17,1},{2,18},{18,2},{3,19},{19,3},{4,20},{20... | collective-permute-start | bytes 1179656 | tf_op jit(solution)/shard_map/ppermute | solution.py:17
  159.8 25.3 %collective-permute-start.18 = (bf16[512,384]{0,1:T(8,128)(2,1)}, bf16[512,384]{0,1:T(8,128)(2,1)S(1)}, u32[]{:S(2)}, u32[]{:S(2)}) collective-permute-start(bf16[512,384]{0,1:T(8,128)(2,1)} %collective-permute-done.11), channel_id=1, source_target_pairs={{0,16},{16,0},{1,17},{17,1},{2,18},{18,2},{3,19},{19,3},{4,20},{20... | collective-permute-start | bytes 1179656 | tf_op jit(solution)/shard_map/ppermute | solution.py:17
  168.8 22.9 %collective-permute-start.19 = (bf16[512,384]{0,1:T(8,128)(2,1)}, bf16[512,384]{0,1:T(8,128)(2,1)S(1)}, u32[]{:S(2)}, u32[]{:S(2)}) collective-permute-start(bf16[512,384]{0,1:T(8,128)(2,1)} %collective-permute-done.12), channel_id=1, source_target_pairs={{0,16},{16,0},{1,17},{17,1},{2,18},{18,2},{3,19},{19,3},{4,20},{20... | collective-permute-start | bytes 1179656 | tf_op jit(solution)/shard_map/ppermute | solution.py:17
  169.7 26.4 %slice-start = ((s8[6291456]{0:T(1024)(128)(4,1)}), s8[4194304]{0:T(1024)(128)(4,1)S(1)}, s32[]{:S(2)}) async-start(s8[6291456]{0:T(1024)(128)(4,1)} %bitcast.135), calls=%async_computation | async-start | bytes 8388608
  176.6 32.7 %collective-permute-start.15 = (bf16[3,128,384]{2,1,0:T(8,128)(2,1)S(1)}, bf16[3,128,384]{2,1,0:T(8,128)(2,1)S(1)}, u32[]{:S(2)}, u32[]{:S(2)}) collective-permute-start(bf16[3,128,384]{2,1,0:T(8,128)(2,1)S(1)} %get-tuple-element.45), channel_id=1, source_target_pairs={{0,1},{1,2},{2,3},{3,0},{4,5},{5,6},{6,7},{7,4},{8,9},{9,10},{10,1... | collective-permute-start | bytes 884744 | tf_op jit(solution)/shard_map/ppermute | solution.py:115
  186.2 10.0 %slice-start.1 = ((s8[6291456]{0:T(1024)(128)(4,1)}), s8[2097152]{0:T(1024)(128)(4,1)S(1)}, s32[]{:S(2)}) async-start(s8[6291456]{0:T(1024)(128)(4,1)} %bitcast.135), calls=%async_computation.1 | async-start | bytes 4194304

commit v12 on v10

--- a/solution.py
+++ b/solution.py
@@ -265,9 +265,9 @@
     out_flat = attn_out.reshape(rows, width)
     own_pair = (out_flat, swap_dp(out_flat))
     attn_grad, sent_out = lax.optimization_barrier((attn_grad, out_flat))
-    out_pieces = [own_pair] + [
-        (got, swap_dp(got)) for got in (shifted(sent_out, "col", -s % n) for s in range(1, n))
-    ]
+    gathered = [shifted(sent_out, "col", -s % n) for s in range(1, n)]
+    swapped = swap_dp(jnp.stack(gathered, 0))
+    out_pieces = [own_pair] + [(gathered[s - 1], swapped[s - 1]) for s in range(1, n)]
     out_both = roll_blocks(
         jnp.stack([jnp.concatenate(p, 0) for p in out_pieces], 0), -me
     )
@@ -280,7 +280,7 @@
     sendable = roll_blocks(
         jnp.stack([g.astype(jnp.bfloat16) for g in grad_list], 1), rank - me
     )
-    sendable, _ = lax.optimization_barrier((sendable, [p[0] for p in out_pieces]))
+    sendable, _ = lax.optimization_barrier((sendable, gathered))
     mine = jnp.stack(
         [lax.dynamic_index_in_dim(g, (rank - me) % n, 0, keepdims=False) for g in grad_list], 0
     )

time: 210 us -> 209 us (level)
  local copies, waits for them, and re-layouts: 46.4 us -> 56 us
  other arithmetic: 14.3 us -> 7.96 us
  waiting for transfers between devices: 71.1 us -> 68 us
    unnamed x63 -> x65, local copies, waits for them, and re-layouts: 16.3 us -> 22.6 us
    unnamed x8, other arithmetic: 6.22 us -> 0.64 us
    ppermute x18, waiting for transfers between devices: 55.2 us -> 49.7 us  [shifted(): return lax.ppermute(x, axis, [(j, (j + step) % n) for j in range(n)])]
    ppermute x6 -> x4, waiting for transfers between devices: 15.9 us -> 18.3 us  [swap_dp(): return lax.ppermute(x, 'dp', [(0, 1), (1, 0)])]
    ppermute x6 -> x4, starting transfers between devices: 7.16 us -> 5.06 us  [swap_dp(): return lax.ppermute(x, 'dp', [(0, 1), (1, 0)])]
  transfers between devices with their start and end apart: 24 -> 22, of which waited for: 11 -> 10; matrix products, arithmetic and copies ran while one was open for 35% -> 38% of each run, Pallas kernels for 0% -> 0%
where the time goes in v12:
time: 209 us; the launch traced here: 208 us
  waiting for transfers between devices  68 us (33%)
  local copies, waits for them, and re-layouts  56 us (27%)
  starting transfers between devices  37.4 us (18%)
  matrix products  37 us (18%)
  other arithmetic  7.96 us (4%)
    ppermute x18, waiting for transfers between devices, shifted(): return lax.ppermute(x, axis, [(j, (j + step) % n) for j in range(n)])  49.7 us
    ppermute x18, starting transfers between devices, shifted(): return lax.ppermute(x, axis, [(j, (j + step) % n) for j in range(n)])  32.3 us
    unnamed x65, local copies, waits for them, and re-layouts  22.6 us
    ppermute x4, waiting for transfers between devices, swap_dp(): return lax.ppermute(x, 'dp', [(0, 1), (1, 0)])  18.3 us
    dot_general x1, matrix products, body_heads(): lax.dot_general(out_both, grad_both, (((1,), (0,)), ((), ())), preferred_...  13.1 us
    dot_general x1, matrix products, body_heads(): lax.dot_general(dense_grad, out_weight, (((1,), (1,)), ((), ())), preferr...  9.4 us
    dot_general x1, matrix products, contract_rows(): lax.dot_general(left, right, (((0,), (0,)), ((), ())), preferred_element_...  7.46 us
    slice x6, local copies, waits for them, and re-layouts, unflat(): out.append(vector[..., at:at + size].reshape(vector.shape[:-1] + shape))  5.64 us
  transfers between devices with their start and end apart: 22, of which 10 were waited for; matrix products, arithmetic and copies ran while one was open for 38% of the time, Pallas kernels for 0%

profile of v12, /device:TPU:0, one launch (start us, length us, event | category | flops | bytes accessed | tf_op | source)
XLA Modules:
  0.0 207.7 jit_solution(14366370201632393384)
XLA Ops:
  6.6 3.0 %collective-permute-start = (bf16[194048]{0:T(1024)(128)(2,1)}, bf16[194048]{0:T(1024)(128)(2,1)S(1)}, u32[]{:S(2)}, u32[]{:S(2)}) collective-permute-start(bf16[194048]{0:T(1024)(128)(2,1)} %get-tuple-element.52), channel_id=1, source_target_pairs={{0,1},{1,2},{2,3},{3,0},{4,5},{5,6},{6,7},{7,4},{8,9},{9,10},{10,1... | collective-permute-start | bytes 1164296 | tf_op jit(solution)/shard_map/ppermute | solution.py:115
  11.4 2.6 %collective-permute-start.1 = (bf16[194048]{0:T(1024)(128)(2,1)}, bf16[194048]{0:T(1024)(128)(2,1)}, u32[]{:S(2)}, u32[]{:S(2)}) collective-permute-start(bf16[194048]{0:T(1024)(128)(2,1)} %get-tuple-element.51), channel_id=1, source_target_pairs={{0,2},{1,3},{2,0},{3,1},{4,6},{5,7},{6,4},{7,5},{8,10},{9,11},{10,... | collective-permute-start | bytes 1164296 | tf_op jit(solution)/shard_map/ppermute | solution.py:115
  14.0 7.9 %collective-permute-done = bf16[194048]{0:T(1024)(128)(2,1)S(1)} collective-permute-done((bf16[194048]{0:T(1024)(128)(2,1)}, bf16[194048]{0:T(1024)(128)(2,1)S(1)}, u32[]{:S(2)}, u32[]{:S(2)}) %collective-permute-start) | collective-permute-done | bytes 388128 | tf_op jit(solution)/shard_map/ppermute | solution.py:115
  21.8 1.2 collective-permute-start.2
  26.9 10.8 %collective-permute-done.1 = bf16[194048]{0:T(1024)(128)(2,1)} collective-permute-done((bf16[194048]{0:T(1024)(128)(2,1)}, bf16[194048]{0:T(1024)(128)(2,1)}, u32[]{:S(2)}, u32[]{:S(2)}) %collective-permute-start.1) | collective-permute-done | bytes 388128 | tf_op jit(solution)/shard_map/ppermute | solution.py:115
  37.7 1.5 collective-permute-start.6
  42.1 1.3 collective-permute-done.2
  46.5 9.4 %fusion.2 = f32[512,1536]{1,0:T(8,128)S(1)} fusion(bf16[1536,3072]{1,0:T(8,128)(2,1)} %param.10, bf16[128,3072]{1,0:T(8,128)(2,1)S(1)} %collective-permute-done.5, bf16[128,3072]{1,0:T(8,128)(2,1)} %collective-permute-done.4, bf16[128,3072]{1,0:T(8,128)(2,1)} %collective-permute-done.3, bf16[128,3072]{1,0:T(8,128)(2,1)S(1)} %bitcast.165), kind=kOutput, calls=%fused_computation.2 | convolution fusion | flops 4844421120 | bytes 15728640 | tf_op jit(solution)/shard_map/dot_general | solution.py:222
  55.9 1.4 collective-permute-done.6
  57.4 1.5 collective-permute-start.19
  58.9 1.1 dynamic-slice_convert_fusion.2
  60.0 6.0 %collective-permute-start.9 = (bf16[512,384]{1,0:T(8,128)(2,1)}, bf16[512,384]{1,0:T(8,128)(2,1)}, u32[]{:S(2)}, u32[]{:S(2)}) collective-permute-start(bf16[512,384]{1,0:T(8,128)(2,1)} %get-tuple-element.32), channel_id=1, source_target_pairs={{0,1},{1,2},{2,3},{3,0},{4,5},{5,6},{6,7},{7,4},{8,9},{9,10},{10,1... | collective-permute-start | bytes 1179656 | tf_op jit(solution)/shard_map/ppermute | solution.py:115
  66.0 3.4 %collective-permute-start.8 = (bf16[512,384]{1,0:T(8,128)(2,1)}, bf16[512,384]{1,0:T(8,128)(2,1)}, u32[]{:S(2)}, u32[]{:S(2)}) collective-permute-start(bf16[512,384]{1,0:T(8,128)(2,1)} %get-tuple-element.33), channel_id=1, source_target_pairs={{0,2},{1,3},{2,0},{3,1},{4,6},{5,7},{6,4},{7,5},{8,10},{9,11},{10,... | collective-permute-start | bytes 1179656 | tf_op jit(solution)/shard_map/ppermute | solution.py:115
  72.4 1.6 multiply_reduce_fusion
  74.6 2.1 %constant_dynamic-update-slice_fusion.9 = bf16[1024,3072]{1,0:T(8,128)(2,1)} fusion(bf16[1024,3072]{1,0:T(8,128)(2,1)} %constant_dynamic-update-slice_fusion.10, bf16[128,3072]{1,0:T(8,128)(2,1)} %collective-permute-done.3), kind=kLoop, calls=%fused_computation.97 | loop fusion | bytes 1572864
  76.8 2.1 %constant_dynamic-update-slice_fusion.8 = bf16[1024,3072]{1,0:T(8,128)(2,1)} fusion(bf16[1024,3072]{1,0:T(8,128)(2,1)} %constant_dynamic-update-slice_fusion.9, bf16[128,3072]{1,0:T(8,128)(2,1)} %collective-permute-done.4), kind=kLoop, calls=%fused_computation.96 | loop fusion | bytes 1572864
  79.8 2.1 constant_dynamic-update-slice_fusion.6
  82.9 1.9 copy.37
  84.9 1.9 squeeze.59
  86.8 1.7 exponential_convert_fusion
  88.4 7.2 %collective-permute-done.8 = bf16[512,384]{1,0:T(8,128)(2,1)} collective-permute-done((bf16[512,384]{1,0:T(8,128)(2,1)}, bf16[512,384]{1,0:T(8,128)(2,1)}, u32[]{:S(2)}, u32[]{:S(2)}) %collective-permute-start.8) | collective-permute-done | bytes 393248 | tf_op jit(solution)/shard_map/ppermute | solution.py:115
  95.7 1.7 add_convert_fusion
  97.6 1.6 fusion.37
  100.2 1.5 fusion.36
  101.8 1.3 fusion.35
  103.0 7.9 %collective-permute-start.10 = (bf16[512,384]{0,1:T(8,128)(2,1)S(1)}, bf16[512,384]{0,1:T(8,128)(2,1)S(1)}, u32[]{:S(2)}, u32[]{:S(2)}) collective-permute-start(bf16[512,384]{0,1:T(8,128)(2,1)S(1)} %bitcast.152), channel_id=1, source_target_pairs={{0,3},{1,0},{2,1},{3,2},{4,7},{5,4},{6,5},{7,6},{8,11},{9,8},{10,9... | collective-permute-start | bytes 1179656 | tf_op jit(solution)/shard_map/ppermute | solution.py:115
  110.9 2.5 %collective-permute-start.11 = (bf16[512,384]{0,1:T(8,128)(2,1)S(1)}, bf16[512,384]{0,1:T(8,128)(2,1)S(1)}, u32[]{:S(2)}, u32[]{:S(2)}) collective-permute-start(bf16[512,384]{0,1:T(8,128)(2,1)S(1)} %bitcast.153), channel_id=1, source_target_pairs={{0,2},{1,3},{2,0},{3,1},{4,6},{5,7},{6,4},{7,5},{8,10},{9,11},{10,... | collective-permute-start | bytes 1179656 | tf_op jit(solution)/shard_map/ppermute | solution.py:115
  116.8 2.0 fusion.15
  118.8 1.1 reshape.149
  119.9 2.3 %reshape.148 = f32[4,128,384]{1,0,2:T(4,128)} reshape(f32[512,3,128]{0,2,1:T(8,128)} %get-tuple-element.60) | data formatting | bytes 1572864 | tf_op jit(solution)/shard_map/reshape | solution.py:279
  122.2 1.4 reshape.147
  123.6 2.5 %constant_dynamic-slice_fusion.1 = (f32[1,128,384]{1,0,2:T(1,128)}, f32[1,128,384]{1,0,2:T(1,128)}) fusion(f32[4,128,384]{1,0,2:T(4,128)} %reshape.149, s32[]{:T(128)S(6)} %select_n.111, f32[4,128,384]{1,0,2:T(4,128)} %reshape.148), kind=kLoop, calls=%fused_computation.102 | loop fusion | bytes 786436 | tf_op jit(solution)/shard_map/jit(dynamic_index_in_dim)/dynamic_slice | solution.py:285
  127.0 1.1 copy.64
  128.1 1.1 copy.63
  129.1 1.7 copy.62
  132.0 15.8 %collective-permute-done.11 = bf16[512,384]{0,1:T(8,128)(2,1)S(1)} collective-permute-done((bf16[512,384]{0,1:T(8,128)(2,1)S(1)}, bf16[512,384]{0,1:T(8,128)(2,1)S(1)}, u32[]{:S(2)}, u32[]{:S(2)}) %collective-permute-start.11) | collective-permute-done | bytes 393248 | tf_op jit(solution)/shard_map/ppermute | solution.py:115
  147.8 1.5 collective-permute-start.21
  150.0 2.1 constant_dynamic-update-slice_fusion.5
  152.0 2.1 constant_dynamic-update-slice_fusion.4
  154.3 2.3 %collective-permute-start.15 = (bf16[3,128,384]{2,1,0:T(8,128)(2,1)S(1)}, bf16[3,128,384]{2,1,0:T(8,128)(2,1)S(1)}, u32[]{:S(2)}, u32[]{:S(2)}) collective-permute-start(bf16[3,128,384]{2,1,0:T(8,128)(2,1)S(1)} %get-tuple-element.40), channel_id=1, source_target_pairs={{0,1},{1,2},{2,3},{3,0},{4,5},{5,6},{6,7},{7,4},{8,9},{9,10},{10,1... | collective-permute-start | bytes 884744 | tf_op jit(solution)/shard_map/ppermute | solution.py:115
  157.5 2.3 %collective-permute-done.21 = bf16[512,364]{1,0:T(8,128)(2,1)S(1)} collective-permute-done((bf16[512,364]{1,0:T(8,128)(2,1)S(1)}, bf16[512,364]{1,0:T(8,128)(2,1)S(1)}, u32[]{:S(2)}, u32[]{:S(2)}) %collective-permute-start.21) | collective-permute-done | bytes 372768 | tf_op jit(solution)/shard_map/ppermute | solution.py:17
  159.8 1.5 collective-permute-start.17
  161.3 7.5 %fusion.18 = f32[364,3072]{1,0:T(8,128)} fusion(bf16[1024,3072]{1,0:T(8,128)(2,1)} %constant_dynamic-update-slice_fusion.3, bf16[512,364]{1,0:T(8,128)(2,1)S(1)} %collective-permute-done.21, bf16[512,364]{1,0:T(8,128)(2,1)S(1)} %bitcast.161), kind=kOutput, calls=%fused_computation.41 | convolution fusion | flops 2291580928 | bytes 11509760 | tf_op jit(solution)/shard_map/dot_general | solution.py:11
  169.0 6.6 %collective-permute-done.14 = bf16[3,128,384]{2,1,0:T(8,128)(2,1)S(1)} collective-permute-done((bf16[3,128,384]{2,1,0:T(8,128)(2,1)S(1)}, bf16[3,128,384]{2,1,0:T(8,128)(2,1)S(1)}, u32[]{:S(2)}, u32[]{:S(2)}) %collective-permute-start.14) | collective-permute-done | bytes 294944 | tf_op jit(solution)/shard_map/ppermute | solution.py:115
  175.7 1.5 slice_bitcast_fusion
  177.2 14.5 %collective-permute-done.17 = bf16[3,512,384]{1,2,0:T(8,128)(2,1)S(1)} collective-permute-done((bf16[3,512,384]{1,2,0:T(8,128)(2,1)S(1)}, bf16[3,512,384]{1,2,0:T(8,128)(2,1)S(1)}, u32[]{:S(2)}, u32[]{:S(2)}) %collective-permute-start.17) | collective-permute-done | bytes 1179680 | tf_op jit(solution)/shard_map/ppermute | solution.py:17
  192.5 1.4 slice-done
  194.6 13.1 %fusion = f32[4,384,3072]{2,1,0:T(8,128)} fusion(bf16[1024,3072]{1,0:T(8,128)(2,1)S(1)} %bitcast.145, bf16[8,1024,384]{1,2,0:T(8,128)(2,1)S(1)} %fusion.24, s32[]{:T(128)S(6)} %select_n.114), kind=kOutput, calls=%fused_computation | convolution fusion | flops 9663676416 | bytes 28311556 | tf_op jit(solution)/shard_map/dot_general | solution.py:275
  (137 shorter events, 32.8 us)
Async XLA Ops:
  2.7 2.7 %copy-start.5 = (bf16[1,128,364]{2,1,0:T(8,128)(2,1)}, bf16[1,128,364]{2,1,0:T(8,128)(2,1)S(1)}, u32[]{:S(2)}) copy-start(bf16[1,128,364]{2,1,0:T(8,128)(2,1)S(1)} %copy.30) | copy-start | bytes 279556
  5.2 4.4 %copy-start.12 = (bf16[1,128,3072]{2,1,0:T(8,128)(2,1)S(1)}, bf16[1,128,3072]{2,1,0:T(8,128)(2,1)}, u32[]{:S(2)}) copy-start(bf16[1,128,3072]{2,1,0:T(8,128)(2,1)} %param.11) | copy-start | bytes 2359300
  6.6 15.2 %collective-permute-start = (bf16[194048]{0:T(1024)(128)(2,1)}, bf16[194048]{0:T(1024)(128)(2,1)S(1)}, u32[]{:S(2)}, u32[]{:S(2)}) collective-permute-start(bf16[194048]{0:T(1024)(128)(2,1)} %get-tuple-element.52), channel_id=1, source_target_pairs={{0,1},{1,2},{2,3},{3,0},{4,5},{5,6},{6,7},{7,4},{8,9},{9,10},{10,1... | collective-permute-start | bytes 1164296 | tf_op jit(solution)/shard_map/ppermute | solution.py:115
  9.7 36.7 %collective-permute-start.5 = (bf16[128,3072]{1,0:T(8,128)(2,1)S(1)}, bf16[128,3072]{1,0:T(8,128)(2,1)S(1)}, u32[]{:S(2)}, u32[]{:S(2)}) collective-permute-start(bf16[128,3072]{1,0:T(8,128)(2,1)S(1)} %bitcast.162), channel_id=1, source_target_pairs={{0,12},{4,0},{8,4},{12,8},{1,13},{5,1},{9,5},{13,9},{2,14},{6,2},{... | collective-permute-start | bytes 2359304 | tf_op jit(solution)/shard_map/ppermute | solution.py:115
  10.3 36.1 %collective-permute-start.4 = (bf16[128,3072]{1,0:T(8,128)(2,1)S(1)}, bf16[128,3072]{1,0:T(8,128)(2,1)}, u32[]{:S(2)}, u32[]{:S(2)}) collective-permute-start(bf16[128,3072]{1,0:T(8,128)(2,1)S(1)} %bitcast.163), channel_id=1, source_target_pairs={{0,8},{4,12},{8,0},{12,4},{1,9},{5,13},{9,1},{13,5},{2,10},{6,14},... | collective-permute-start | bytes 2359304 | tf_op jit(solution)/shard_map/ppermute | solution.py:115
  11.1 35.3 %collective-permute-start.3 = (bf16[128,3072]{1,0:T(8,128)(2,1)S(1)}, bf16[128,3072]{1,0:T(8,128)(2,1)}, u32[]{:S(2)}, u32[]{:S(2)}) collective-permute-start(bf16[128,3072]{1,0:T(8,128)(2,1)S(1)} %bitcast.164), channel_id=1, source_target_pairs={{0,4},{4,8},{8,12},{12,0},{1,5},{5,9},{9,13},{13,1},{2,6},{6,10},{... | collective-permute-start | bytes 2359304 | tf_op jit(solution)/shard_map/ppermute | solution.py:115
  11.4 26.3 %collective-permute-start.1 = (bf16[194048]{0:T(1024)(128)(2,1)}, bf16[194048]{0:T(1024)(128)(2,1)}, u32[]{:S(2)}, u32[]{:S(2)}) collective-permute-start(bf16[194048]{0:T(1024)(128)(2,1)} %get-tuple-element.51), channel_id=1, source_target_pairs={{0,2},{1,3},{2,0},{3,1},{4,6},{5,7},{6,4},{7,5},{8,10},{9,11},{10,... | collective-permute-start | bytes 1164296 | tf_op jit(solution)/shard_map/ppermute | solution.py:115
  21.8 1.2 copy-start.16
  21.8 21.6 %collective-permute-start.2 = (bf16[194048]{0:T(1024)(128)(2,1)S(1)}, bf16[194048]{0:T(1024)(128)(2,1)}, u32[]{:S(2)}, u32[]{:S(2)}) collective-permute-start(bf16[194048]{0:T(1024)(128)(2,1)S(1)} %get-tuple-element.50), channel_id=1, source_target_pairs={{0,3},{1,0},{2,1},{3,2},{4,7},{5,4},{6,5},{7,6},{8,11},{9,8},{10,9... | collective-permute-start | bytes 1164296 | tf_op jit(solution)/shard_map/ppermute | solution.py:115
  37.7 19.7 %collective-permute-start.6 = (bf16[1,128,3072]{2,1,0:T(8,128)(2,1)S(1)}, bf16[1,128,3072]{2,1,0:T(8,128)(2,1)}, u32[]{:S(2)}, u32[]{:S(2)}) collective-permute-start(bf16[1,128,3072]{2,1,0:T(8,128)(2,1)S(1)} %copy-done.12), channel_id=1, source_target_pairs={{0,16},{16,0},{1,17},{17,1},{2,18},{18,2},{3,19},{19,3},{4,20},{20... | collective-permute-start | bytes 2359304 | tf_op jit(solution)/shard_map/ppermute | solution.py:17
  46.4 9.5 %copy-start.13 = (bf16[128,3072]{1,0:T(8,128)(2,1)}, bf16[128,3072]{1,0:T(8,128)(2,1)S(1)}, u32[]{:S(2)}) copy-start(bf16[128,3072]{1,0:T(8,128)(2,1)S(1)} %collective-permute-done.5) | copy-start | bytes 2359300
  55.9 13.7 %copy-start.8 = (f32[512,1536]{1,0:T(8,128)}, f32[512,1536]{1,0:T(8,128)S(1)}, u32[]{:S(2)}) copy-start(f32[512,1536]{1,0:T(8,128)S(1)} %fusion.2) | copy-start | bytes 9437188
  57.4 92.5 %collective-permute-start.18 = (bf16[128,3072]{1,0:T(8,128)(2,1)}, bf16[128,3072]{1,0:T(8,128)(2,1)}, u32[]{:S(2)}, u32[]{:S(2)}) collective-permute-start(bf16[128,3072]{1,0:T(8,128)(2,1)} %bitcast.37), channel_id=1, source_target_pairs={{0,4},{4,8},{8,12},{12,0},{1,5},{5,9},{9,13},{13,1},{2,6},{6,10},{... | collective-permute-start | bytes 2359304 | tf_op jit(solution)/shard_map/ppermute | solution.py:115
  57.4 94.7 %collective-permute-start.19 = (bf16[128,3072]{1,0:T(8,128)(2,1)}, bf16[128,3072]{1,0:T(8,128)(2,1)}, u32[]{:S(2)}, u32[]{:S(2)}) collective-permute-start(bf16[128,3072]{1,0:T(8,128)(2,1)} %bitcast.37), channel_id=1, source_target_pairs={{0,8},{4,12},{8,0},{12,4},{1,9},{5,13},{9,1},{13,5},{2,10},{6,14},... | collective-permute-start | bytes 2359304 | tf_op jit(solution)/shard_map/ppermute | solution.py:115
  60.0 28.5 %collective-permute-start.9 = (bf16[512,384]{1,0:T(8,128)(2,1)}, bf16[512,384]{1,0:T(8,128)(2,1)}, u32[]{:S(2)}, u32[]{:S(2)}) collective-permute-start(bf16[512,384]{1,0:T(8,128)(2,1)} %get-tuple-element.32), channel_id=1, source_target_pairs={{0,1},{1,2},{2,3},{3,0},{4,5},{5,6},{6,7},{7,4},{8,9},{9,10},{10,1... | collective-permute-start | bytes 1179656 | tf_op jit(solution)/shard_map/ppermute | solution.py:115
  66.0 29.7 %collective-permute-start.8 = (bf16[512,384]{1,0:T(8,128)(2,1)}, bf16[512,384]{1,0:T(8,128)(2,1)}, u32[]{:S(2)}, u32[]{:S(2)}) collective-permute-start(bf16[512,384]{1,0:T(8,128)(2,1)} %get-tuple-element.33), channel_id=1, source_target_pairs={{0,2},{1,3},{2,0},{3,1},{4,6},{5,7},{6,4},{7,5},{8,10},{9,11},{10,... | collective-permute-start | bytes 1179656 | tf_op jit(solution)/shard_map/ppermute | solution.py:115
  69.4 26.3 %collective-permute-start.7 = (bf16[512,384]{1,0:T(8,128)(2,1)}, bf16[512,384]{1,0:T(8,128)(2,1)}, u32[]{:S(2)}, u32[]{:S(2)}) collective-permute-start(bf16[512,384]{1,0:T(8,128)(2,1)} %get-tuple-element.31), channel_id=1, source_target_pairs={{0,3},{1,0},{2,1},{3,2},{4,7},{5,4},{6,5},{7,6},{8,11},{9,8},{10,9... | collective-permute-start | bytes 1179656 | tf_op jit(solution)/shard_map/ppermute | solution.py:115
  74.6 4.3 %copy-start.14 = (bf16[128,3072]{1,0:T(8,128)(2,1)S(1)}, bf16[128,3072]{1,0:T(8,128)(2,1)}, u32[]{:S(2)}) copy-start(bf16[128,3072]{1,0:T(8,128)(2,1)} %copy-done.13) | copy-start | bytes 2359300
  76.8 5.1 %copy-start.6 = (bf16[1,128,364]{2,1,0:T(8,128)(2,1)S(1)}, bf16[1,128,364]{2,1,0:T(8,128)(2,1)}, u32[]{:S(2)}) copy-start(bf16[1,128,364]{2,1,0:T(8,128)(2,1)} %copy-done.5) | copy-start | bytes 279556
  76.8 5.1 %copy-start.9 = (bf16[128,364]{1,0:T(8,128)(2,1)S(1)}, bf16[128,364]{1,0:T(8,128)(2,1)}, u32[]{:S(2)}) copy-start(bf16[128,364]{1,0:T(8,128)(2,1)} %reshape.139) | copy-start | bytes 279556
  76.8 5.2 %copy-start.10 = (bf16[128,364]{1,0:T(8,128)(2,1)S(1)}, bf16[128,364]{1,0:T(8,128)(2,1)}, u32[]{:S(2)}) copy-start(bf16[128,364]{1,0:T(8,128)(2,1)} %reshape.142) | copy-start | bytes 279556
  76.8 5.2 %copy-start.11 = (bf16[128,364]{1,0:T(8,128)(2,1)S(1)}, bf16[128,364]{1,0:T(8,128)(2,1)}, u32[]{:S(2)}) copy-start(bf16[128,364]{1,0:T(8,128)(2,1)} %reshape.145) | copy-start | bytes 279556
  88.4 9.1 %copy-start = (bf16[3,512,512]{1,2,0:T(8,128)(2,1)S(1)}, bf16[3,512,512]{1,2,0:T(8,128)(2,1)}, u32[]{:S(2)}) copy-start(bf16[3,512,512]{1,2,0:T(8,128)(2,1)} %exponential_convert_fusion) | copy-start | bytes 4718596
  97.4 1.9 copy-start.2
  100.2 1.5 copy-start.1
  103.0 12.6 %copy-start.4 = (bf16[512,3,128]{0,2,1:T(8,128)(2,1)S(1)}, bf16[512,3,128]{0,2,1:T(8,128)(2,1)}, u32[]{:S(2)}) copy-start(bf16[512,3,128]{0,2,1:T(8,128)(2,1)} %get-tuple-element.61) | copy-start | bytes 1179652
  103.0 28.8 %collective-permute-start.10 = (bf16[512,384]{0,1:T(8,128)(2,1)S(1)}, bf16[512,384]{0,1:T(8,128)(2,1)S(1)}, u32[]{:S(2)}, u32[]{:S(2)}) collective-permute-start(bf16[512,384]{0,1:T(8,128)(2,1)S(1)} %bitcast.152), channel_id=1, source_target_pairs={{0,3},{1,0},{2,1},{3,2},{4,7},{5,4},{6,5},{7,6},{8,11},{9,8},{10,9... | collective-permute-start | bytes 1179656 | tf_op jit(solution)/shard_map/ppermute | solution.py:115
  110.9 36.9 %collective-permute-start.11 = (bf16[512,384]{0,1:T(8,128)(2,1)S(1)}, bf16[512,384]{0,1:T(8,128)(2,1)S(1)}, u32[]{:S(2)}, u32[]{:S(2)}) collective-permute-start(bf16[512,384]{0,1:T(8,128)(2,1)S(1)} %bitcast.153), channel_id=1, source_target_pairs={{0,2},{1,3},{2,0},{3,1},{4,6},{5,7},{6,4},{7,5},{8,10},{9,11},{10,... | collective-permute-start | bytes 1179656 | tf_op jit(solution)/shard_map/ppermute | solution.py:115
  113.4 35.9 %collective-permute-start.12 = (bf16[512,384]{0,1:T(8,128)(2,1)S(1)}, bf16[512,384]{0,1:T(8,128)(2,1)S(1)}, u32[]{:S(2)}, u32[]{:S(2)}) collective-permute-start(bf16[512,384]{0,1:T(8,128)(2,1)S(1)} %bitcast.154), channel_id=1, source_target_pairs={{0,1},{1,2},{2,3},{3,0},{4,5},{5,6},{6,7},{7,4},{8,9},{9,10},{10,1... | collective-permute-start | bytes 1179656 | tf_op jit(solution)/shard_map/ppermute | solution.py:115
  114.6 4.2 %copy-start.3 = (f32[512,3,128]{0,2,1:T(8,128)S(1)}, f32[512,3,128]{0,2,1:T(8,128)}, u32[]{:S(2)}) copy-start(f32[512,3,128]{0,2,1:T(8,128)} %get-tuple-element.62) | copy-start | bytes 2359300
  127.0 20.8 %copy-start.7 = (bf16[4,128,364]{2,1,0:T(8,128)(2,1)S(1)}, bf16[4,128,364]{2,1,0:T(8,128)(2,1)}, u32[]{:S(2)}) copy-start(bf16[4,128,364]{2,1,0:T(8,128)(2,1)} %constant_dynamic-slice_fusion) | copy-start | bytes 1118212
  130.9 0.9 copy-start.15
  131.9 22.4 %collective-permute-start.20 = (bf16[128,3072]{1,0:T(8,128)(2,1)}, bf16[128,3072]{1,0:T(8,128)(2,1)S(1)}, u32[]{:S(2)}, u32[]{:S(2)}) collective-permute-start(bf16[128,3072]{1,0:T(8,128)(2,1)} %bitcast.37), channel_id=1, source_target_pairs={{0,12},{4,0},{8,4},{12,8},{1,13},{5,1},{9,5},{13,9},{2,14},{6,2},{... | collective-permute-start | bytes 2359304 | tf_op jit(solution)/shard_map/ppermute | solution.py:115
  147.8 12.1 %collective-permute-start.21 = (bf16[512,364]{1,0:T(8,128)(2,1)S(1)}, bf16[512,364]{1,0:T(8,128)(2,1)S(1)}, u32[]{:S(2)}, u32[]{:S(2)}) collective-permute-start(bf16[512,364]{1,0:T(8,128)(2,1)S(1)} %bitcast.160), channel_id=1, source_target_pairs={{0,16},{16,0},{1,17},{17,1},{2,18},{18,2},{3,19},{19,3},{4,20},{20... | collective-permute-start | bytes 1118216 | tf_op jit(solution)/shard_map/ppermute | solution.py:17
  149.3 19.5 %collective-permute-start.16 = (bf16[512,384]{0,1:T(8,128)(2,1)S(1)}, bf16[512,384]{0,1:T(8,128)(2,1)S(1)}, u32[]{:S(2)}, u32[]{:S(2)}) collective-permute-start(bf16[512,384]{0,1:T(8,128)(2,1)S(1)} %bitcast.155), channel_id=1, source_target_pairs={{0,16},{16,0},{1,17},{17,1},{2,18},{18,2},{3,19},{19,3},{4,20},{20... | collective-permute-start | bytes 1179656 | tf_op jit(solution)/shard_map/ppermute | solution.py:17
  149.9 19.0 %collective-permute-start.13 = (bf16[3,128,384]{2,1,0:T(8,128)(2,1)S(1)}, bf16[3,128,384]{2,1,0:T(8,128)(2,1)S(1)}, u32[]{:S(2)}, u32[]{:S(2)}) collective-permute-start(bf16[3,128,384]{2,1,0:T(8,128)(2,1)S(1)} %get-tuple-element.42), channel_id=1, source_target_pairs={{0,3},{1,0},{2,1},{3,2},{4,7},{5,4},{6,5},{7,6},{8,11},{9,8},{10,9... | collective-permute-start | bytes 884744 | tf_op jit(solution)/shard_map/ppermute | solution.py:115
  152.0 23.5 %collective-permute-start.14 = (bf16[3,128,384]{2,1,0:T(8,128)(2,1)S(1)}, bf16[3,128,384]{2,1,0:T(8,128)(2,1)S(1)}, u32[]{:S(2)}, u32[]{:S(2)}) collective-permute-start(bf16[3,128,384]{2,1,0:T(8,128)(2,1)S(1)} %get-tuple-element.41), channel_id=1, source_target_pairs={{0,2},{1,3},{2,0},{3,1},{4,6},{5,7},{6,4},{7,5},{8,10},{9,11},{10,... | collective-permute-start | bytes 884744 | tf_op jit(solution)/shard_map/ppermute | solution.py:115
  154.3 21.4 %collective-permute-start.15 = (bf16[3,128,384]{2,1,0:T(8,128)(2,1)S(1)}, bf16[3,128,384]{2,1,0:T(8,128)(2,1)S(1)}, u32[]{:S(2)}, u32[]{:S(2)}) collective-permute-start(bf16[3,128,384]{2,1,0:T(8,128)(2,1)S(1)} %get-tuple-element.40), channel_id=1, source_target_pairs={{0,1},{1,2},{2,3},{3,0},{4,5},{5,6},{6,7},{7,4},{8,9},{9,10},{10,1... | collective-permute-start | bytes 884744 | tf_op jit(solution)/shard_map/ppermute | solution.py:115
  159.8 31.9 %collective-permute-start.17 = (bf16[3,512,384]{1,2,0:T(8,128)(2,1)S(1)}, bf16[3,512,384]{1,2,0:T(8,128)(2,1)S(1)}, u32[]{:S(2)}, u32[]{:S(2)}) collective-permute-start(bf16[3,512,384]{1,2,0:T(8,128)(2,1)S(1)} %pad_maximum_fusion), channel_id=1, source_target_pairs={{0,16},{16,0},{1,17},{17,1},{2,18},{18,2},{3,19},{19,3},{4,20},{20... | collective-permute-start | bytes 3538952 | tf_op jit(solution)/shard_map/ppermute | solution.py:17
  191.7 2.2 %slice-start = ((s8[6291456]{0:T(1024)(128)(4,1)}), s8[4194304]{0:T(1024)(128)(4,1)S(1)}, s32[]{:S(2)}) async-start(s8[6291456]{0:T(1024)(128)(4,1)} %bitcast.144), calls=%async_computation | async-start | bytes 8388608
  192.0 2.7 %slice-start.1 = ((s8[6291456]{0:T(1024)(128)(4,1)}), s8[2097152]{0:T(1024)(128)(4,1)S(1)}, s32[]{:S(2)}) async-start(s8[6291456]{0:T(1024)(128)(4,1)} %bitcast.144), calls=%async_computation.1 | async-start | bytes 4194304

commit v13 on v9

--- a/solution.py
+++ b/solution.py
@@ -201,6 +201,22 @@
     return lax.dynamic_slice_in_dim(jnp.concatenate([x, x], 0), shift % n, n, 0)
 
 
+def relayed_blocks(x, axis):
+    n, me = axis_size(axis), lax.axis_index(axis)
+    if n != 4:
+        return [x] + [shifted(x, axis, s) for s in range(1, n)]
+    across = lax.ppermute(x, axis, [(j, (j + 2) % n) for j in range(n)])
+    partner = lax.ppermute(x, axis, [(j, j ^ 1) for j in range(n)])
+    forwarded = lax.ppermute(across, axis, [(j, j ^ 1) for j in range(n)])
+    even = (me % 2) == 0
+    return [
+        x,
+        jnp.where(even, forwarded, partner),
+        across,
+        jnp.where(even, partner, forwarded),
+    ]
+
+
 def body_heads(patches, queries, attn_keys, attn_values, out_weight, output_grad):
     factor = DH ** (-0.5)
     n, me = axis_size("col"), lax.axis_index("col")
@@ -209,7 +225,7 @@
     width = width_all // n
     heads = width // DH
     patch_here = patches[0]
-    grad_blocks = [output_grad[0]] + [shifted(output_grad[0], "row", s) for s in range(1, n)]
+    grad_blocks = relayed_blocks(output_grad[0], "row")
     dense_grad = jnp.concatenate(grad_blocks, 0)
     grad_other = swap_dp(output_grad)
     qkv = jnp.stack([queries[0], attn_keys[0], attn_values[0]], 0)

time: 205 us -> 221 us (1.078)
  waiting for transfers between devices: 70.2 us -> 81.9 us
  other arithmetic: 12.9 us -> 15.9 us
    ppermute x0 -> x3, waiting for transfers between devices: none -> 12.3 us  [the longest x1 12.3 us: relayed_blocks(): across = lax.ppermute(x, axis, [(j, (j + 2) % n) for j in range(n)])]
    ppermute x0 -> x3, starting transfers between devices: none -> 3.01 us  [the longest x1 3 us: relayed_blocks(): across = lax.ppermute(x, axis, [(j, (j + 2) % n) for j in range(n)])]
    unnamed x8 -> x10, other arithmetic: 6.88 us -> 9.14 us
    ppermute x18 -> x15, starting transfers between devices: 33.1 us -> 31.4 us  [shifted(): return lax.ppermute(x, axis, [(j, (j + step) % n) for j in range(n)])]
    unnamed x65 -> x61, local copies, waits for them, and re-layouts: 16.3 us -> 15.2 us
    ppermute x18 -> x15, waiting for transfers between devices: 58.1 us -> 58.7 us  [shifted(): return lax.ppermute(x, axis, [(j, (j + step) % n) for j in range(n)])]
  transfers between devices with their start and end apart: 24 -> 24, of which waited for: 9 -> 8; matrix products, arithmetic and copies ran while one was open for 39% -> 40% of each run, Pallas kernels for 0% -> 0%
where the time goes in v13:
time: 221 us; the launch traced here: 220 us
  waiting for transfers between devices  81.9 us (37%)
  local copies, waits for them, and re-layouts  43.1 us (20%)
  starting transfers between devices  41.6 us (19%)
  matrix products  36.5 us (17%)
  other arithmetic  15.9 us (7%)
    ppermute x15, waiting for transfers between devices, shifted(): return lax.ppermute(x, axis, [(j, (j + step) % n) for j in range(n)])  58.7 us
    ppermute x15, starting transfers between devices, shifted(): return lax.ppermute(x, axis, [(j, (j + step) % n) for j in range(n)])  31.4 us
    unnamed x61, local copies, waits for them, and re-layouts  15.2 us
    dot_general x1, matrix products, body_heads(): lax.dot_general(out_both, grad_both, (((1,), (0,)), ((), ())), preferred_...  13 us
    ppermute x1, waiting for transfers between devices, relayed_blocks(): across = lax.ppermute(x, axis, [(j, (j + 2) % n) for j in range(n)])  12.3 us
    ppermute x6, waiting for transfers between devices, swap_dp(): return lax.ppermute(x, 'dp', [(0, 1), (1, 0)])  10.9 us
    unnamed x10, other arithmetic  9.14 us
    dot_general x1, matrix products, body_heads(): lax.dot_general(dense_grad, out_weight, (((1,), (1,)), ((), ())), preferr...  9 us
  transfers between devices with their start and end apart: 24, of which 8 were waited for; matrix products, arithmetic and copies ran while one was open for 40% of the time, Pallas kernels for 0%

profile of v13, /device:TPU:0, one launch (start us, length us, event | category | flops | bytes accessed | tf_op | source)
XLA Modules:
  0.0 220.3 jit_solution(1047941195877277524)
XLA Ops:
  0.6 3.0 %collective-permute-start.3 = (bf16[128,3072]{1,0:T(8,128)(2,1)}, bf16[128,3072]{1,0:T(8,128)(2,1)}, u32[]{:S(2)}, u32[]{:S(2)}) collective-permute-start(bf16[128,3072]{1,0:T(8,128)(2,1)} %bitcast.145), channel_id=1, source_target_pairs={{0,8},{4,12},{8,0},{12,4},{1,9},{5,13},{9,1},{13,5},{2,10},{6,14},... | collective-permute-start | bytes 2359304 | tf_op jit(solution)/shard_map/ppermute | solution.py:208
  9.2 12.3 %collective-permute-done.3 = bf16[128,3072]{1,0:T(8,128)(2,1)} collective-permute-done((bf16[128,3072]{1,0:T(8,128)(2,1)}, bf16[128,3072]{1,0:T(8,128)(2,1)}, u32[]{:S(2)}, u32[]{:S(2)}) %collective-permute-start.3) | collective-permute-done | bytes 786464 | tf_op jit(solution)/shard_map/ppermute | solution.py:208
  21.5 1.7 pad_maximum_fusion
  23.2 1.8 collective-permute-start
  25.0 2.6 %collective-permute-start.1 = (bf16[194048]{0:T(1024)(128)(2,1)S(1)}, bf16[194048]{0:T(1024)(128)(2,1)}, u32[]{:S(2)}, u32[]{:S(2)}) collective-permute-start(bf16[194048]{0:T(1024)(128)(2,1)S(1)} %get-tuple-element.52), channel_id=1, source_target_pairs={{0,2},{1,3},{2,0},{3,1},{4,6},{5,7},{6,4},{7,5},{8,10},{9,11},{10,... | collective-permute-start | bytes 1164296 | tf_op jit(solution)/shard_map/ppermute | solution.py:115
  27.6 1.3 collective-permute-start.2
  29.0 2.1 constant_dynamic-update-slice_fusion.10
  31.0 6.3 %collective-permute-done = bf16[194048]{0:T(1024)(128)(2,1)S(1)} collective-permute-done((bf16[194048]{0:T(1024)(128)(2,1)}, bf16[194048]{0:T(1024)(128)(2,1)S(1)}, u32[]{:S(2)}, u32[]{:S(2)}) %collective-permute-start) | collective-permute-done | bytes 388128 | tf_op jit(solution)/shard_map/ppermute | solution.py:115
  38.0 1.7 collective-permute-start.6
  42.6 11.2 %collective-permute-done.1 = bf16[194048]{0:T(1024)(128)(2,1)} collective-permute-done((bf16[194048]{0:T(1024)(128)(2,1)S(1)}, bf16[194048]{0:T(1024)(128)(2,1)}, u32[]{:S(2)}, u32[]{:S(2)}) %collective-permute-start.1) | collective-permute-done | bytes 388128 | tf_op jit(solution)/shard_map/ppermute | solution.py:115
  59.7 1.1 constant_dynamic-update-slice_fusion.9
  60.8 2.1 constant_dynamic-update-slice_fusion.8
  63.0 1.1 constant_dynamic-update-slice_fusion.7
  64.1 9.0 %fusion.2 = f32[512,1536]{1,0:T(8,128)S(1)} fusion(bf16[1536,3072]{1,0:T(8,128)(2,1)} %param.10, bf16[128,3072]{1,0:T(8,128)(2,1)S(1)} %get-tuple-element.32, bf16[128,3072]{1,0:T(8,128)(2,1)} %collective-permute-done.3, bf16[128,3072]{1,0:T(8,128)(2,1)S(1)} %get-tuple-element.34, bf16[128,3072]{1,0:T(8,128)(2,1)S(1)} %bitcast.147), kind=kOutput, calls=%fused_computation.2 | convolution fusion | flops 4844421120 | bytes 15728640 | tf_op jit(solution)/shard_map/dot_general | solution.py:238
  73.2 1.6 collective-permute-start.21
  75.8 6.9 %collective-permute-start.9 = (bf16[512,384]{1,0:T(8,128)(2,1)}, bf16[512,384]{1,0:T(8,128)(2,1)}, u32[]{:S(2)}, u32[]{:S(2)}) collective-permute-start(bf16[512,384]{1,0:T(8,128)(2,1)} %get-tuple-element.36), channel_id=1, source_target_pairs={{0,1},{1,2},{2,3},{3,0},{4,5},{5,6},{6,7},{7,4},{8,9},{9,10},{10,1... | collective-permute-start | bytes 1179656 | tf_op jit(solution)/shard_map/ppermute | solution.py:115
  82.8 3.5 %collective-permute-start.8 = (bf16[512,384]{1,0:T(8,128)(2,1)}, bf16[512,384]{1,0:T(8,128)(2,1)}, u32[]{:S(2)}, u32[]{:S(2)}) collective-permute-start(bf16[512,384]{1,0:T(8,128)(2,1)} %get-tuple-element.37), channel_id=1, source_target_pairs={{0,2},{1,3},{2,0},{3,1},{4,6},{5,7},{6,4},{7,5},{8,10},{9,11},{10,... | collective-permute-start | bytes 1179656 | tf_op jit(solution)/shard_map/ppermute | solution.py:115
  89.4 1.8 multiply_reduce_fusion
  91.8 2.1 constant_dynamic-update-slice_fusion.6
  95.9 1.1 squeeze.47
  97.0 1.7 exponential_convert_fusion
  99.6 13.0 %collective-permute-done.8 = bf16[512,384]{1,0:T(8,128)(2,1)} collective-permute-done((bf16[512,384]{1,0:T(8,128)(2,1)}, bf16[512,384]{1,0:T(8,128)(2,1)}, u32[]{:S(2)}, u32[]{:S(2)}) %collective-permute-start.8) | collective-permute-done | bytes 393248 | tf_op jit(solution)/shard_map/ppermute | solution.py:115
  112.6 1.7 add_convert_fusion
  114.4 1.4 fusion.35
  115.8 1.1 multiply_reduce_fusion.1
  116.9 7.7 %collective-permute-start.11 = (bf16[512,384]{0,1:T(8,128)(2,1)}, bf16[512,384]{0,1:T(8,128)(2,1)}, u32[]{:S(2)}, u32[]{:S(2)}) collective-permute-start(bf16[512,384]{0,1:T(8,128)(2,1)} %bitcast.14), channel_id=1, source_target_pairs={{0,3},{1,0},{2,1},{3,2},{4,7},{5,4},{6,5},{7,6},{8,11},{9,8},{10,9... | collective-permute-start | bytes 1179656 | tf_op jit(solution)/shard_map/ppermute | solution.py:115
  124.7 2.6 %collective-permute-start.13 = (bf16[512,384]{0,1:T(8,128)(2,1)}, bf16[512,384]{0,1:T(8,128)(2,1)}, u32[]{:S(2)}, u32[]{:S(2)}) collective-permute-start(bf16[512,384]{0,1:T(8,128)(2,1)} %bitcast.14), channel_id=1, source_target_pairs={{0,2},{1,3},{2,0},{3,1},{4,6},{5,7},{6,4},{7,5},{8,10},{9,11},{10,... | collective-permute-start | bytes 1179656 | tf_op jit(solution)/shard_map/ppermute | solution.py:115
  127.3 1.1 reshape.149
  128.5 1.7 multiply_convert_fusion
  130.8 1.1 reshape.148
  132.6 1.8 constant_dynamic-slice_fusion.2
  137.7 2.1 constant_dynamic-update-slice_fusion.5
  139.7 1.5 collective-permute-start.23
  141.2 2.1 constant_dynamic-update-slice_fusion.4
  143.8 18.1 %collective-permute-done.13 = bf16[512,384]{0,1:T(8,128)(2,1)} collective-permute-done((bf16[512,384]{0,1:T(8,128)(2,1)}, bf16[512,384]{0,1:T(8,128)(2,1)}, u32[]{:S(2)}, u32[]{:S(2)}) %collective-permute-start.13) | collective-permute-done | bytes 393248 | tf_op jit(solution)/shard_map/ppermute | solution.py:115
  162.0 1.5 collective-permute-start.12
  164.0 1.5 collective-permute-start.16
  165.5 2.1 constant_dynamic-update-slice_fusion.3
  167.6 7.5 %fusion.17 = f32[364,3072]{1,0:T(8,128)} fusion(bf16[1024,3072]{1,0:T(8,128)(2,1)} %constant_dynamic-update-slice_fusion.3, bf16[512,364]{1,0:T(8,128)(2,1)S(1)} %collective-permute-done.23, bf16[512,364]{1,0:T(8,128)(2,1)S(1)} %bitcast.144), kind=kOutput, calls=%fused_computation.39 | convolution fusion | flops 2291580928 | bytes 11509760 | tf_op jit(solution)/shard_map/dot_general | solution.py:11
  177.3 5.4 %collective-permute-done.14 = bf16[512,384]{0,1:T(8,128)(2,1)S(1)} collective-permute-done((bf16[512,384]{0,1:T(8,128)(2,1)}, bf16[512,384]{0,1:T(8,128)(2,1)S(1)}, u32[]{:S(2)}, u32[]{:S(2)}) %collective-permute-start.14) | collective-permute-done | bytes 393248 | tf_op jit(solution)/shard_map/ppermute | solution.py:17
  183.7 5.5 %collective-permute-done.16 = bf16[512,384]{0,1:T(8,128)(2,1)S(1)} collective-permute-done((bf16[512,384]{0,1:T(8,128)(2,1)S(1)}, bf16[512,384]{0,1:T(8,128)(2,1)S(1)}, u32[]{:S(2)}, u32[]{:S(2)}) %collective-permute-start.16) | collective-permute-done | bytes 393248 | tf_op jit(solution)/shard_map/ppermute | solution.py:17
  189.3 1.1 fusion.29
  190.4 1.2 fusion.27
  191.7 1.2 fusion.25
  193.5 2.0 collective-permute-start.18
  195.5 13.0 %fusion = f32[4,384,3072]{2,1,0:T(8,128)} fusion(bf16[4,1024,384]{1,2,0:T(8,128)(2,1)S(1)} %constant_dynamic-slice_fusion.1, bf16[1024,3072]{1,0:T(8,128)(2,1)S(1)} %bitcast.137), kind=kOutput, calls=%fused_computation | convolution fusion | flops 9663676416 | bytes 28311552 | tf_op jit(solution)/shard_map/dot_general | solution.py:291
  208.7 10.1 %collective-permute-done.18 = bf16[3,128,384]{2,1,0:T(8,128)(2,1)S(1)} collective-permute-done((bf16[3,128,384]{2,1,0:T(8,128)(2,1)S(1)}, bf16[3,128,384]{2,1,0:T(8,128)(2,1)S(1)}, u32[]{:S(2)}, u32[]{:S(2)}) %collective-permute-start.18) | collective-permute-done | bytes 294944 | tf_op jit(solution)/shard_map/ppermute | solution.py:115
  218.9 1.5 slice_bitcast_fusion
  (138 shorter events, 32.3 us)
Async XLA Ops:
  0.6 20.9 %collective-permute-start.3 = (bf16[128,3072]{1,0:T(8,128)(2,1)}, bf16[128,3072]{1,0:T(8,128)(2,1)}, u32[]{:S(2)}, u32[]{:S(2)}) collective-permute-start(bf16[128,3072]{1,0:T(8,128)(2,1)} %bitcast.145), channel_id=1, source_target_pairs={{0,8},{4,12},{8,0},{12,4},{1,9},{5,13},{9,1},{13,5},{2,10},{6,14},... | collective-permute-start | bytes 2359304 | tf_op jit(solution)/shard_map/ppermute | solution.py:208
  3.6 56.1 %collective-permute-start.5 = (bf16[128,3072]{1,0:T(8,128)(2,1)}, bf16[128,3072]{1,0:T(8,128)(2,1)S(1)}, u32[]{:S(2)}, u32[]{:S(2)}) collective-permute-start(bf16[128,3072]{1,0:T(8,128)(2,1)} %bitcast.146), channel_id=1, source_target_pairs={{0,4},{4,0},{8,12},{12,8},{1,5},{5,1},{9,13},{13,9},{2,6},{6,2},{1... | collective-permute-start | bytes 2359304 | tf_op jit(solution)/shard_map/ppermute | solution.py:209
  4.6 4.1 %copy-start.7 = (bf16[1,128,364]{2,1,0:T(8,128)(2,1)}, bf16[1,128,364]{2,1,0:T(8,128)(2,1)S(1)}, u32[]{:S(2)}) copy-start(bf16[1,128,364]{2,1,0:T(8,128)(2,1)S(1)} %copy.30) | copy-start | bytes 279556
  21.5 38.2 %collective-permute-start.4 = (bf16[128,3072]{1,0:T(8,128)(2,1)}, bf16[128,3072]{1,0:T(8,128)(2,1)S(1)}, u32[]{:S(2)}, u32[]{:S(2)}) collective-permute-start(bf16[128,3072]{1,0:T(8,128)(2,1)} %collective-permute-done.3), channel_id=1, source_target_pairs={{0,4},{4,0},{8,12},{12,8},{1,5},{5,1},{9,13},{13,9},{2,6},{6,2},{1... | collective-permute-start | bytes 2359304 | tf_op jit(solution)/shard_map/ppermute | solution.py:210
  23.2 14.1 %collective-permute-start = (bf16[194048]{0:T(1024)(128)(2,1)}, bf16[194048]{0:T(1024)(128)(2,1)S(1)}, u32[]{:S(2)}, u32[]{:S(2)}) collective-permute-start(bf16[194048]{0:T(1024)(128)(2,1)} %get-tuple-element.53), channel_id=1, source_target_pairs={{0,1},{1,2},{2,3},{3,0},{4,5},{5,6},{6,7},{7,4},{8,9},{9,10},{10,1... | collective-permute-start | bytes 1164296 | tf_op jit(solution)/shard_map/ppermute | solution.py:115
  25.0 28.8 %collective-permute-start.1 = (bf16[194048]{0:T(1024)(128)(2,1)S(1)}, bf16[194048]{0:T(1024)(128)(2,1)}, u32[]{:S(2)}, u32[]{:S(2)}) collective-permute-start(bf16[194048]{0:T(1024)(128)(2,1)S(1)} %get-tuple-element.52), channel_id=1, source_target_pairs={{0,2},{1,3},{2,0},{3,1},{4,6},{5,7},{6,4},{7,5},{8,10},{9,11},{10,... | collective-permute-start | bytes 1164296 | tf_op jit(solution)/shard_map/ppermute | solution.py:115
  27.6 29.1 %collective-permute-start.2 = (bf16[194048]{0:T(1024)(128)(2,1)S(1)}, bf16[194048]{0:T(1024)(128)(2,1)}, u32[]{:S(2)}, u32[]{:S(2)}) collective-permute-start(bf16[194048]{0:T(1024)(128)(2,1)S(1)} %get-tuple-element.51), channel_id=1, source_target_pairs={{0,3},{1,0},{2,1},{3,2},{4,7},{5,4},{6,5},{7,6},{8,11},{9,8},{10,9... | collective-permute-start | bytes 1164296 | tf_op jit(solution)/shard_map/ppermute | solution.py:115
  37.3 0.7 copy-start.15
  38.0 35.1 %collective-permute-start.6 = (bf16[1,128,3072]{2,1,0:T(8,128)(2,1)}, bf16[1,128,3072]{2,1,0:T(8,128)(2,1)}, u32[]{:S(2)}, u32[]{:S(2)}) collective-permute-start(bf16[1,128,3072]{2,1,0:T(8,128)(2,1)} %param.11), channel_id=1, source_target_pairs={{0,16},{16,0},{1,17},{17,1},{2,18},{18,2},{3,19},{19,3},{4,20},{20... | collective-permute-start | bytes 2359304 | tf_op jit(solution)/shard_map/ppermute | solution.py:17
  60.8 3.3 %copy-start.14 = (bf16[1,128,3072]{2,1,0:T(8,128)(2,1)S(1)}, bf16[1,128,3072]{2,1,0:T(8,128)(2,1)}, u32[]{:S(2)}) copy-start(bf16[1,128,3072]{2,1,0:T(8,128)(2,1)} %param.11) | copy-start | bytes 2359300
  73.1 13.4 %copy-start.10 = (f32[512,1536]{1,0:T(8,128)}, f32[512,1536]{1,0:T(8,128)S(1)}, u32[]{:S(2)}) copy-start(f32[512,1536]{1,0:T(8,128)S(1)} %fusion.2) | copy-start | bytes 9437188
  73.1 64.2 %collective-permute-start.20 = (bf16[128,3072]{1,0:T(8,128)(2,1)}, bf16[128,3072]{1,0:T(8,128)(2,1)}, u32[]{:S(2)}, u32[]{:S(2)}) collective-permute-start(bf16[128,3072]{1,0:T(8,128)(2,1)} %bitcast.31), channel_id=1, source_target_pairs={{0,4},{4,8},{8,12},{12,0},{1,5},{5,9},{9,13},{13,1},{2,6},{6,10},{... | collective-permute-start | bytes 2359304 | tf_op jit(solution)/shard_map/ppermute | solution.py:115
  73.2 66.5 %collective-permute-start.21 = (bf16[128,3072]{1,0:T(8,128)(2,1)}, bf16[128,3072]{1,0:T(8,128)(2,1)}, u32[]{:S(2)}, u32[]{:S(2)}) collective-permute-start(bf16[128,3072]{1,0:T(8,128)(2,1)} %bitcast.31), channel_id=1, source_target_pairs={{0,8},{4,12},{8,0},{12,4},{1,9},{5,13},{9,1},{13,5},{2,10},{6,14},... | collective-permute-start | bytes 2359304 | tf_op jit(solution)/shard_map/ppermute | solution.py:115
  75.8 22.9 %collective-permute-start.9 = (bf16[512,384]{1,0:T(8,128)(2,1)}, bf16[512,384]{1,0:T(8,128)(2,1)}, u32[]{:S(2)}, u32[]{:S(2)}) collective-permute-start(bf16[512,384]{1,0:T(8,128)(2,1)} %get-tuple-element.36), channel_id=1, source_target_pairs={{0,1},{1,2},{2,3},{3,0},{4,5},{5,6},{6,7},{7,4},{8,9},{9,10},{10,1... | collective-permute-start | bytes 1179656 | tf_op jit(solution)/shard_map/ppermute | solution.py:115
  82.8 29.8 %collective-permute-start.8 = (bf16[512,384]{1,0:T(8,128)(2,1)}, bf16[512,384]{1,0:T(8,128)(2,1)}, u32[]{:S(2)}, u32[]{:S(2)}) collective-permute-start(bf16[512,384]{1,0:T(8,128)(2,1)} %get-tuple-element.37), channel_id=1, source_target_pairs={{0,2},{1,3},{2,0},{3,1},{4,6},{5,7},{6,4},{7,5},{8,10},{9,11},{10,... | collective-permute-start | bytes 1179656 | tf_op jit(solution)/shard_map/ppermute | solution.py:115
  86.3 26.3 %collective-permute-start.7 = (bf16[512,384]{1,0:T(8,128)(2,1)}, bf16[512,384]{1,0:T(8,128)(2,1)}, u32[]{:S(2)}, u32[]{:S(2)}) collective-permute-start(bf16[512,384]{1,0:T(8,128)(2,1)} %get-tuple-element.35), channel_id=1, source_target_pairs={{0,3},{1,0},{2,1},{3,2},{4,7},{5,4},{6,5},{7,6},{8,11},{9,8},{10,9... | collective-permute-start | bytes 1179656 | tf_op jit(solution)/shard_map/ppermute | solution.py:115
  89.4 2.4 %copy-start.1 = (bf16[512,3,128]{0,2,1:T(8,128)(2,1)}, bf16[512,3,128]{0,2,1:T(8,128)(2,1)S(1)}, u32[]{:S(2)}) copy-start(bf16[512,3,128]{0,2,1:T(8,128)(2,1)S(1)} %squeeze.45) | copy-start | bytes 1179652
  91.1 2.7 %copy-start.8 = (bf16[1,128,364]{2,1,0:T(8,128)(2,1)S(1)}, bf16[1,128,364]{2,1,0:T(8,128)(2,1)}, u32[]{:S(2)}) copy-start(bf16[1,128,364]{2,1,0:T(8,128)(2,1)} %copy-done.7) | copy-start | bytes 279556
  91.2 2.7 %copy-start.11 = (bf16[128,364]{1,0:T(8,128)(2,1)S(1)}, bf16[128,364]{1,0:T(8,128)(2,1)}, u32[]{:S(2)}) copy-start(bf16[128,364]{1,0:T(8,128)(2,1)} %reshape.139) | copy-start | bytes 279556
  91.2 2.8 %copy-start.12 = (bf16[128,364]{1,0:T(8,128)(2,1)S(1)}, bf16[128,364]{1,0:T(8,128)(2,1)}, u32[]{:S(2)}) copy-start(bf16[128,364]{1,0:T(8,128)(2,1)} %reshape.142) | copy-start | bytes 279556
  91.2 2.8 %copy-start.13 = (bf16[128,364]{1,0:T(8,128)(2,1)S(1)}, bf16[128,364]{1,0:T(8,128)(2,1)}, u32[]{:S(2)}) copy-start(bf16[128,364]{1,0:T(8,128)(2,1)} %reshape.145) | copy-start | bytes 279556
  91.7 3.2 %copy-start.6 = (bf16[1,4,128,384]{3,2,0,1:T(8,128)(2,1)S(1)}, bf16[1,4,128,384]{3,2,0,1:T(8,128)(2,1)}, u32[]{:S(2)}) copy-start(bf16[1,4,128,384]{3,2,0,1:T(8,128)(2,1)} %get-tuple-element.44) | copy-start | bytes 1179652
  97.0 18.8 %copy-start.4 = (bf16[512,3,128]{0,2,1:T(8,128)(2,1)}, bf16[512,3,128]{0,2,1:T(8,128)(2,1)S(1)}, u32[]{:S(2)}) copy-start(bf16[512,3,128]{0,2,1:T(8,128)(2,1)S(1)} %squeeze.47) | copy-start | bytes 1179652
  98.7 15.7 %copy-start = (bf16[3,512,512]{1,2,0:T(8,128)(2,1)S(1)}, bf16[3,512,512]{1,2,0:T(8,128)(2,1)}, u32[]{:S(2)}) copy-start(bf16[3,512,512]{1,2,0:T(8,128)(2,1)} %exponential_convert_fusion) | copy-start | bytes 4718596
  98.7 65.3 %collective-permute-start.22 = (bf16[128,3072]{1,0:T(8,128)(2,1)}, bf16[128,3072]{1,0:T(8,128)(2,1)}, u32[]{:S(2)}, u32[]{:S(2)}) collective-permute-start(bf16[128,3072]{1,0:T(8,128)(2,1)} %bitcast.31), channel_id=1, source_target_pairs={{0,12},{4,0},{8,4},{12,8},{1,13},{5,1},{9,5},{13,9},{2,14},{6,2},{... | collective-permute-start | bytes 2359304 | tf_op jit(solution)/shard_map/ppermute | solution.py:115
  116.9 26.4 %collective-permute-start.11 = (bf16[512,384]{0,1:T(8,128)(2,1)}, bf16[512,384]{0,1:T(8,128)(2,1)}, u32[]{:S(2)}, u32[]{:S(2)}) collective-permute-start(bf16[512,384]{0,1:T(8,128)(2,1)} %bitcast.14), channel_id=1, source_target_pairs={{0,3},{1,0},{2,1},{3,2},{4,7},{5,4},{6,5},{7,6},{8,11},{9,8},{10,9... | collective-permute-start | bytes 1179656 | tf_op jit(solution)/shard_map/ppermute | solution.py:115
  124.7 37.3 %collective-permute-start.13 = (bf16[512,384]{0,1:T(8,128)(2,1)}, bf16[512,384]{0,1:T(8,128)(2,1)}, u32[]{:S(2)}, u32[]{:S(2)}) collective-permute-start(bf16[512,384]{0,1:T(8,128)(2,1)} %bitcast.14), channel_id=1, source_target_pairs={{0,2},{1,3},{2,0},{3,1},{4,6},{5,7},{6,4},{7,5},{8,10},{9,11},{10,... | collective-permute-start | bytes 1179656 | tf_op jit(solution)/shard_map/ppermute | solution.py:115
  128.5 1.7 copy-start.3
  130.1 1.8 copy-start.2
  134.4 1.4 copy-start.5
  137.0 2.7 %copy-start.9 = (bf16[4,128,364]{2,1,0:T(8,128)(2,1)S(1)}, bf16[4,128,364]{2,1,0:T(8,128)(2,1)}, u32[]{:S(2)}) copy-start(bf16[4,128,364]{2,1,0:T(8,128)(2,1)} %constant_dynamic-slice_fusion) | copy-start | bytes 1118212
  137.4 26.1 %collective-permute-start.15 = (bf16[512,384]{0,1:T(8,128)(2,1)}, bf16[512,384]{0,1:T(8,128)(2,1)S(1)}, u32[]{:S(2)}, u32[]{:S(2)}) collective-permute-start(bf16[512,384]{0,1:T(8,128)(2,1)} %bitcast.14), channel_id=1, source_target_pairs={{0,1},{1,2},{2,3},{3,0},{4,5},{5,6},{6,7},{7,4},{8,9},{9,10},{10,1... | collective-permute-start | bytes 1179656 | tf_op jit(solution)/shard_map/ppermute | solution.py:115
  139.7 27.9 %collective-permute-start.23 = (bf16[512,364]{1,0:T(8,128)(2,1)S(1)}, bf16[512,364]{1,0:T(8,128)(2,1)S(1)}, u32[]{:S(2)}, u32[]{:S(2)}) collective-permute-start(bf16[512,364]{1,0:T(8,128)(2,1)S(1)} %bitcast.143), channel_id=1, source_target_pairs={{0,16},{16,0},{1,17},{17,1},{2,18},{18,2},{3,19},{19,3},{4,20},{20... | collective-permute-start | bytes 1118216 | tf_op jit(solution)/shard_map/ppermute | solution.py:17
  143.3 31.8 %collective-permute-start.10 = (bf16[512,384]{0,1:T(8,128)(2,1)}, bf16[512,384]{0,1:T(8,128)(2,1)S(1)}, u32[]{:S(2)}, u32[]{:S(2)}) collective-permute-start(bf16[512,384]{0,1:T(8,128)(2,1)} %bitcast.14), channel_id=1, source_target_pairs={{0,16},{16,0},{1,17},{17,1},{2,18},{18,2},{3,19},{19,3},{4,20},{20... | collective-permute-start | bytes 1179656 | tf_op jit(solution)/shard_map/ppermute | solution.py:17
  162.0 14.2 %collective-permute-start.12 = (bf16[512,384]{0,1:T(8,128)(2,1)}, bf16[512,384]{0,1:T(8,128)(2,1)S(1)}, u32[]{:S(2)}, u32[]{:S(2)}) collective-permute-start(bf16[512,384]{0,1:T(8,128)(2,1)} %collective-permute-done.11), channel_id=1, source_target_pairs={{0,16},{16,0},{1,17},{17,1},{2,18},{18,2},{3,19},{19,3},{4,20},{20... | collective-permute-start | bytes 1179656 | tf_op jit(solution)/shard_map/ppermute | solution.py:17
  163.5 19.2 %collective-permute-start.14 = (bf16[512,384]{0,1:T(8,128)(2,1)}, bf16[512,384]{0,1:T(8,128)(2,1)S(1)}, u32[]{:S(2)}, u32[]{:S(2)}) collective-permute-start(bf16[512,384]{0,1:T(8,128)(2,1)} %collective-permute-done.13), channel_id=1, source_target_pairs={{0,16},{16,0},{1,17},{17,1},{2,18},{18,2},{3,19},{19,3},{4,20},{20... | collective-permute-start | bytes 1179656 | tf_op jit(solution)/shard_map/ppermute | solution.py:17
  164.0 25.3 %collective-permute-start.16 = (bf16[512,384]{0,1:T(8,128)(2,1)S(1)}, bf16[512,384]{0,1:T(8,128)(2,1)S(1)}, u32[]{:S(2)}, u32[]{:S(2)}) collective-permute-start(bf16[512,384]{0,1:T(8,128)(2,1)S(1)} %collective-permute-done.15), channel_id=1, source_target_pairs={{0,16},{16,0},{1,17},{17,1},{2,18},{18,2},{3,19},{19,3},{4,20},{20... | collective-permute-start | bytes 1179656 | tf_op jit(solution)/shard_map/ppermute | solution.py:17
  190.4 5.1 %slice-start = ((s8[6291456]{0:T(1024)(128)(4,1)}), s8[4194304]{0:T(1024)(128)(4,1)S(1)}, s32[]{:S(2)}) async-start(s8[6291456]{0:T(1024)(128)(4,1)} %bitcast.136), calls=%async_computation | async-start | bytes 8388608
  193.0 2.5 %slice-start.1 = ((s8[6291456]{0:T(1024)(128)(4,1)}), s8[2097152]{0:T(1024)(128)(4,1)S(1)}, s32[]{:S(2)}) async-start(s8[6291456]{0:T(1024)(128)(4,1)} %bitcast.136), calls=%async_computation.1 | async-start | bytes 4194304
  193.4 15.2 %collective-permute-start.17 = (bf16[3,128,384]{2,1,0:T(8,128)(2,1)S(1)}, bf16[3,128,384]{2,1,0:T(8,128)(2,1)S(1)}, u32[]{:S(2)}, u32[]{:S(2)}) collective-permute-start(bf16[3,128,384]{2,1,0:T(8,128)(2,1)S(1)} %get-tuple-element.43), channel_id=1, source_target_pairs={{0,3},{1,0},{2,1},{3,2},{4,7},{5,4},{6,5},{7,6},{8,11},{9,8},{10,9... | collective-permute-start | bytes 884744 | tf_op jit(solution)/shard_map/ppermute | solution.py:115
  193.5 25.2 %collective-permute-start.18 = (bf16[3,128,384]{2,1,0:T(8,128)(2,1)S(1)}, bf16[3,128,384]{2,1,0:T(8,128)(2,1)S(1)}, u32[]{:S(2)}, u32[]{:S(2)}) collective-permute-start(bf16[3,128,384]{2,1,0:T(8,128)(2,1)S(1)} %get-tuple-element.42), channel_id=1, source_target_pairs={{0,2},{1,3},{2,0},{3,1},{4,6},{5,7},{6,4},{7,5},{8,10},{9,11},{10,... | collective-permute-start | bytes 884744 | tf_op jit(solution)/shard_map/ppermute | solution.py:115
  208.6 10.2 %collective-permute-start.19 = (bf16[3,128,384]{2,1,0:T(8,128)(2,1)S(1)}, bf16[3,128,384]{2,1,0:T(8,128)(2,1)S(1)}, u32[]{:S(2)}, u32[]{:S(2)}) collective-permute-start(bf16[3,128,384]{2,1,0:T(8,128)(2,1)S(1)} %get-tuple-element.41), channel_id=1, source_target_pairs={{0,1},{1,2},{2,3},{3,0},{4,5},{5,6},{6,7},{7,4},{8,9},{9,10},{10,1... | collective-permute-start | bytes 884744 | tf_op jit(solution)/shard_map/ppermute | solution.py:115

commit v14 on v10

--- a/solution.py
+++ b/solution.py
@@ -280,7 +280,6 @@
     sendable = roll_blocks(
         jnp.stack([g.astype(jnp.bfloat16) for g in grad_list], 1), rank - me
     )
-    sendable, _ = lax.optimization_barrier((sendable, [p[0] for p in out_pieces]))
     mine = jnp.stack(
         [lax.dynamic_index_in_dim(g, (rank - me) % n, 0, keepdims=False) for g in grad_list], 0
     )

time: 210 us -> 212 us (level)
  waiting for transfers between devices: 71.1 us -> 79.6 us
  other arithmetic: 14.3 us -> 7.77 us
  matrix products: 36.9 us -> 34.1 us
    ppermute x18, waiting for transfers between devices: 55.2 us -> 68.5 us  [shifted(): return lax.ppermute(x, axis, [(j, (j + step) % n) for j in range(n)])]
    unnamed x8, other arithmetic: 6.22 us -> 0.68 us
    ppermute x6, waiting for transfers between devices: 15.9 us -> 11.1 us  [swap_dp(): return lax.ppermute(x, 'dp', [(0, 1), (1, 0)])]
    dot_general x1, matrix products: 7.47 us -> 4.69 us  [contract_rows(): lax.dot_general(left, right, (((0,), (0,)), ((), ())), preferred_element_...]
    unnamed x63 -> x73, local copies, waits for them, and re-layouts: 16.3 us -> 16.8 us
  transfers between devices with their start and end apart: 24 -> 24, of which waited for: 11 -> 11; matrix products, arithmetic and copies ran while one was open for 35% -> 33% of each run, Pallas kernels for 0% -> 0%
where the time goes in v14:
time: 212 us; the launch traced here: 211 us
  waiting for transfers between devices  79.6 us (38%)
  local copies, waits for them, and re-layouts  48.4 us (23%)
  starting transfers between devices  40.2 us (19%)
  matrix products  34.1 us (16%)
  other arithmetic  7.77 us (4%)
    ppermute x18, waiting for transfers between devices, shifted(): return lax.ppermute(x, axis, [(j, (j + step) % n) for j in range(n)])  68.5 us
    ppermute x18, starting transfers between devices, shifted(): return lax.ppermute(x, axis, [(j, (j + step) % n) for j in range(n)])  32.9 us
    unnamed x73, local copies, waits for them, and re-layouts  16.8 us
    dot_general x1, matrix products, body_heads(): lax.dot_general(out_both, grad_both, (((1,), (0,)), ((), ())), preferred_...  13.1 us
    ppermute x6, waiting for transfers between devices, swap_dp(): return lax.ppermute(x, 'dp', [(0, 1), (1, 0)])  11.1 us
    dot_general x1, matrix products, body_heads(): lax.dot_general(dense_grad, out_weight, (((1,), (1,)), ((), ())), preferr...  9.41 us
    ppermute x6, starting transfers between devices, swap_dp(): return lax.ppermute(x, 'dp', [(0, 1), (1, 0)])  7.23 us
    slice x6, local copies, waits for them, and re-layouts, unflat(): out.append(vector[..., at:at + size].reshape(vector.shape[:-1] + shape))  5.64 us
  transfers between devices with their start and end apart: 24, of which 11 were waited for; matrix products, arithmetic and copies ran while one was open for 33% of the time, Pallas kernels for 0%

profile of v14, /device:TPU:0, one launch (start us, length us, event | category | flops | bytes accessed | tf_op | source)
XLA Modules:
  0.0 211.4 jit_solution(7555257897669715812)
XLA Ops:
  6.6 3.0 %collective-permute-start = (bf16[194048]{0:T(1024)(128)(2,1)}, bf16[194048]{0:T(1024)(128)(2,1)S(1)}, u32[]{:S(2)}, u32[]{:S(2)}) collective-permute-start(bf16[194048]{0:T(1024)(128)(2,1)} %get-tuple-element.47), channel_id=1, source_target_pairs={{0,1},{1,2},{2,3},{3,0},{4,5},{5,6},{6,7},{7,4},{8,9},{9,10},{10,1... | collective-permute-start | bytes 1164296 | tf_op jit(solution)/shard_map/ppermute | solution.py:115
  11.4 2.6 %collective-permute-start.1 = (bf16[194048]{0:T(1024)(128)(2,1)}, bf16[194048]{0:T(1024)(128)(2,1)}, u32[]{:S(2)}, u32[]{:S(2)}) collective-permute-start(bf16[194048]{0:T(1024)(128)(2,1)} %get-tuple-element.46), channel_id=1, source_target_pairs={{0,2},{1,3},{2,0},{3,1},{4,6},{5,7},{6,4},{7,5},{8,10},{9,11},{10,... | collective-permute-start | bytes 1164296 | tf_op jit(solution)/shard_map/ppermute | solution.py:115
  14.0 7.9 %collective-permute-done = bf16[194048]{0:T(1024)(128)(2,1)S(1)} collective-permute-done((bf16[194048]{0:T(1024)(128)(2,1)}, bf16[194048]{0:T(1024)(128)(2,1)S(1)}, u32[]{:S(2)}, u32[]{:S(2)}) %collective-permute-start) | collective-permute-done | bytes 388128 | tf_op jit(solution)/shard_map/ppermute | solution.py:115
  21.8 1.2 collective-permute-start.2
  26.9 10.8 %collective-permute-done.1 = bf16[194048]{0:T(1024)(128)(2,1)} collective-permute-done((bf16[194048]{0:T(1024)(128)(2,1)}, bf16[194048]{0:T(1024)(128)(2,1)}, u32[]{:S(2)}, u32[]{:S(2)}) %collective-permute-start.1) | collective-permute-done | bytes 388128 | tf_op jit(solution)/shard_map/ppermute | solution.py:115
  37.7 1.5 collective-permute-start.6
  42.1 1.3 collective-permute-done.2
  46.5 9.4 %fusion.2 = f32[512,1536]{1,0:T(8,128)S(1)} fusion(bf16[1536,3072]{1,0:T(8,128)(2,1)} %param.10, bf16[128,3072]{1,0:T(8,128)(2,1)S(1)} %collective-permute-done.5, bf16[128,3072]{1,0:T(8,128)(2,1)} %collective-permute-done.4, bf16[128,3072]{1,0:T(8,128)(2,1)} %collective-permute-done.3, bf16[128,3072]{1,0:T(8,128)(2,1)S(1)} %bitcast.153), kind=kOutput, calls=%fused_computation.2 | convolution fusion | flops 4844421120 | bytes 15728640 | tf_op jit(solution)/shard_map/dot_general | solution.py:222
  55.9 1.4 collective-permute-done.6
  57.4 1.5 collective-permute-start.21
  60.0 6.0 %collective-permute-start.9 = (bf16[512,384]{1,0:T(8,128)(2,1)}, bf16[512,384]{1,0:T(8,128)(2,1)}, u32[]{:S(2)}, u32[]{:S(2)}) collective-permute-start(bf16[512,384]{1,0:T(8,128)(2,1)} %get-tuple-element.30), channel_id=1, source_target_pairs={{0,1},{1,2},{2,3},{3,0},{4,5},{5,6},{6,7},{7,4},{8,9},{9,10},{10,1... | collective-permute-start | bytes 1179656 | tf_op jit(solution)/shard_map/ppermute | solution.py:115
  66.0 3.4 %collective-permute-start.8 = (bf16[512,384]{1,0:T(8,128)(2,1)}, bf16[512,384]{1,0:T(8,128)(2,1)}, u32[]{:S(2)}, u32[]{:S(2)}) collective-permute-start(bf16[512,384]{1,0:T(8,128)(2,1)} %get-tuple-element.31), channel_id=1, source_target_pairs={{0,2},{1,3},{2,0},{3,1},{4,6},{5,7},{6,4},{7,5},{8,10},{9,11},{10,... | collective-permute-start | bytes 1179656 | tf_op jit(solution)/shard_map/ppermute | solution.py:115
  72.4 1.6 multiply_reduce_fusion
  74.6 2.1 %constant_dynamic-update-slice_fusion.9 = bf16[1024,3072]{1,0:T(8,128)(2,1)} fusion(bf16[1024,3072]{1,0:T(8,128)(2,1)} %constant_dynamic-update-slice_fusion.10, bf16[128,3072]{1,0:T(8,128)(2,1)} %collective-permute-done.3), kind=kLoop, calls=%fused_computation.93 | loop fusion | bytes 1572864
  76.8 2.1 %constant_dynamic-update-slice_fusion.8 = bf16[1024,3072]{1,0:T(8,128)(2,1)} fusion(bf16[1024,3072]{1,0:T(8,128)(2,1)} %constant_dynamic-update-slice_fusion.9, bf16[128,3072]{1,0:T(8,128)(2,1)} %collective-permute-done.4), kind=kLoop, calls=%fused_computation.92 | loop fusion | bytes 1572864
  79.8 2.1 constant_dynamic-update-slice_fusion.6
  83.0 1.9 copy.37
  84.9 1.9 squeeze.50
  86.8 1.7 exponential_convert_fusion
  89.4 6.3 %collective-permute-done.8 = bf16[512,384]{1,0:T(8,128)(2,1)} collective-permute-done((bf16[512,384]{1,0:T(8,128)(2,1)}, bf16[512,384]{1,0:T(8,128)(2,1)}, u32[]{:S(2)}, u32[]{:S(2)}) %collective-permute-start.8) | collective-permute-done | bytes 393248 | tf_op jit(solution)/shard_map/ppermute | solution.py:115
  95.7 1.7 add_convert_fusion
  97.6 1.7 fusion.37
  100.3 1.4 fusion.36
  101.7 1.3 fusion.35
  102.9 1.1 reshape.149
  104.1 1.1 reshape.148
  108.2 7.9 %collective-permute-start.10 = (bf16[3,128,384]{2,1,0:T(8,128)(2,1)}, bf16[3,128,384]{2,1,0:T(8,128)(2,1)}, u32[]{:S(2)}, u32[]{:S(2)}) collective-permute-start(bf16[3,128,384]{2,1,0:T(8,128)(2,1)} %get-tuple-element.37), channel_id=1, source_target_pairs={{0,3},{1,0},{2,1},{3,2},{4,7},{5,4},{6,5},{7,6},{8,11},{9,8},{10,9... | collective-permute-start | bytes 884744 | tf_op jit(solution)/shard_map/ppermute | solution.py:115
  116.1 2.6 %constant_dynamic-slice_fusion.1 = (f32[1,128,384]{1,0,2:T(1,128)}, f32[1,128,384]{1,0,2:T(1,128)S(1)}) fusion(f32[4,128,384]{1,0,2:T(4,128)} %reshape.149, s32[]{:T(128)S(6)} %select_n.111, f32[4,128,384]{1,0,2:T(4,128)} %reshape.148), kind=kLoop, calls=%fused_computation.98 | loop fusion | bytes 786436 | tf_op jit(solution)/shard_map/jit(dynamic_index_in_dim)/dynamic_slice | solution.py:284
  118.6 1.7 copy.64
  121.2 1.1 reshape.147
  122.3 1.3 constant_dynamic-slice_fusion.3
  123.8 2.6 %collective-permute-start.11 = (bf16[3,128,384]{2,1,0:T(8,128)(2,1)}, bf16[3,128,384]{2,1,0:T(8,128)(2,1)S(1)}, u32[]{:S(2)}, u32[]{:S(2)}) collective-permute-start(bf16[3,128,384]{2,1,0:T(8,128)(2,1)} %get-tuple-element.36), channel_id=1, source_target_pairs={{0,2},{1,3},{2,0},{3,1},{4,6},{5,7},{6,4},{7,5},{8,10},{9,11},{10,... | collective-permute-start | bytes 884744 | tf_op jit(solution)/shard_map/ppermute | solution.py:115
  126.8 1.2 convert_dynamic-update-slice_fusion.2
  128.0 18.5 %collective-permute-done.11 = bf16[3,128,384]{2,1,0:T(8,128)(2,1)S(1)} collective-permute-done((bf16[3,128,384]{2,1,0:T(8,128)(2,1)}, bf16[3,128,384]{2,1,0:T(8,128)(2,1)S(1)}, u32[]{:S(2)}, u32[]{:S(2)}) %collective-permute-start.11) | collective-permute-done | bytes 294944 | tf_op jit(solution)/shard_map/ppermute | solution.py:115
  147.0 1.5 slice_bitcast_fusion
  148.4 1.8 collective-permute-start.18
  150.3 1.2 constant_dynamic-update-slice_fusion.5
  151.5 1.6 collective-permute-start.23
  153.1 1.2 constant_dynamic-update-slice_fusion.4
  154.8 2.6 %collective-permute-done.14 = bf16[512,384]{0,1:T(8,128)(2,1)S(1)} collective-permute-done((bf16[512,384]{0,1:T(8,128)(2,1)S(1)}, bf16[512,384]{0,1:T(8,128)(2,1)S(1)}, u32[]{:S(2)}, u32[]{:S(2)}) %collective-permute-start.14) | collective-permute-done | bytes 393248 | tf_op jit(solution)/shard_map/ppermute | solution.py:115
  157.4 1.5 collective-permute-start.15
  158.9 21.0 %collective-permute-done.16 = bf16[512,384]{0,1:T(8,128)(2,1)S(1)} collective-permute-done((bf16[512,384]{0,1:T(8,128)(2,1)S(1)}, bf16[512,384]{0,1:T(8,128)(2,1)S(1)}, u32[]{:S(2)}, u32[]{:S(2)}) %collective-permute-start.16) | collective-permute-done | bytes 393248 | tf_op jit(solution)/shard_map/ppermute | solution.py:115
  179.9 1.5 collective-permute-start.17
  181.9 1.2 constant_dynamic-update-slice_fusion.3
  183.1 4.7 %fusion.18 = f32[364,3072]{1,0:T(8,128)} fusion(bf16[1024,3072]{1,0:T(8,128)(2,1)S(1)} %constant_dynamic-update-slice_fusion.3, bf16[512,364]{1,0:T(8,128)(2,1)S(1)} %collective-permute-done.23, bf16[512,364]{1,0:T(8,128)(2,1)S(1)} %bitcast.149), kind=kOutput, calls=%fused_computation.40 | convolution fusion | flops 2291580928 | bytes 11509760 | tf_op jit(solution)/shard_map/dot_general | solution.py:11
  188.0 3.9 %collective-permute-done.17 = bf16[512,384]{0,1:T(8,128)(2,1)S(1)} collective-permute-done((bf16[512,384]{0,1:T(8,128)(2,1)S(1)}, bf16[512,384]{0,1:T(8,128)(2,1)S(1)}, u32[]{:S(2)}, u32[]{:S(2)}) %collective-permute-start.17) | collective-permute-done | bytes 393248 | tf_op jit(solution)/shard_map/ppermute | solution.py:17
  192.0 5.8 %collective-permute-done.19 = bf16[512,384]{0,1:T(8,128)(2,1)S(1)} collective-permute-done((bf16[512,384]{0,1:T(8,128)(2,1)S(1)}, bf16[512,384]{0,1:T(8,128)(2,1)S(1)}, u32[]{:S(2)}, u32[]{:S(2)}) %collective-permute-start.19) | collective-permute-done | bytes 393248 | tf_op jit(solution)/shard_map/ppermute | solution.py:17
  198.4 13.1 %fusion = f32[4,384,3072]{2,1,0:T(8,128)} fusion(bf16[1024,3072]{1,0:T(8,128)(2,1)S(1)} %constant_dynamic-update-slice_fusion.3, bf16[8,1024,384]{1,2,0:T(8,128)(2,1)S(1)} %fusion.24, s32[]{:T(128)S(6)} %select_n.114), kind=kOutput, calls=%fused_computation | convolution fusion | flops 9663676416 | bytes 28311556 | tf_op jit(solution)/shard_map/dot_general | solution.py:275
  (147 shorter events, 32.6 us)
Async XLA Ops:
  2.7 2.7 %copy-start.7 = (bf16[1,128,364]{2,1,0:T(8,128)(2,1)}, bf16[1,128,364]{2,1,0:T(8,128)(2,1)S(1)}, u32[]{:S(2)}) copy-start(bf16[1,128,364]{2,1,0:T(8,128)(2,1)S(1)} %copy.30) | copy-start | bytes 279556
  5.2 4.4 %copy-start.14 = (bf16[1,128,3072]{2,1,0:T(8,128)(2,1)S(1)}, bf16[1,128,3072]{2,1,0:T(8,128)(2,1)}, u32[]{:S(2)}) copy-start(bf16[1,128,3072]{2,1,0:T(8,128)(2,1)} %param.11) | copy-start | bytes 2359300
  6.6 15.2 %collective-permute-start = (bf16[194048]{0:T(1024)(128)(2,1)}, bf16[194048]{0:T(1024)(128)(2,1)S(1)}, u32[]{:S(2)}, u32[]{:S(2)}) collective-permute-start(bf16[194048]{0:T(1024)(128)(2,1)} %get-tuple-element.47), channel_id=1, source_target_pairs={{0,1},{1,2},{2,3},{3,0},{4,5},{5,6},{6,7},{7,4},{8,9},{9,10},{10,1... | collective-permute-start | bytes 1164296 | tf_op jit(solution)/shard_map/ppermute | solution.py:115
  9.7 36.7 %collective-permute-start.5 = (bf16[128,3072]{1,0:T(8,128)(2,1)S(1)}, bf16[128,3072]{1,0:T(8,128)(2,1)S(1)}, u32[]{:S(2)}, u32[]{:S(2)}) collective-permute-start(bf16[128,3072]{1,0:T(8,128)(2,1)S(1)} %bitcast.150), channel_id=1, source_target_pairs={{0,12},{4,0},{8,4},{12,8},{1,13},{5,1},{9,5},{13,9},{2,14},{6,2},{... | collective-permute-start | bytes 2359304 | tf_op jit(solution)/shard_map/ppermute | solution.py:115
  10.3 36.1 %collective-permute-start.4 = (bf16[128,3072]{1,0:T(8,128)(2,1)S(1)}, bf16[128,3072]{1,0:T(8,128)(2,1)}, u32[]{:S(2)}, u32[]{:S(2)}) collective-permute-start(bf16[128,3072]{1,0:T(8,128)(2,1)S(1)} %bitcast.151), channel_id=1, source_target_pairs={{0,8},{4,12},{8,0},{12,4},{1,9},{5,13},{9,1},{13,5},{2,10},{6,14},... | collective-permute-start | bytes 2359304 | tf_op jit(solution)/shard_map/ppermute | solution.py:115
  11.1 35.3 %collective-permute-start.3 = (bf16[128,3072]{1,0:T(8,128)(2,1)S(1)}, bf16[128,3072]{1,0:T(8,128)(2,1)}, u32[]{:S(2)}, u32[]{:S(2)}) collective-permute-start(bf16[128,3072]{1,0:T(8,128)(2,1)S(1)} %bitcast.152), channel_id=1, source_target_pairs={{0,4},{4,8},{8,12},{12,0},{1,5},{5,9},{9,13},{13,1},{2,6},{6,10},{... | collective-permute-start | bytes 2359304 | tf_op jit(solution)/shard_map/ppermute | solution.py:115
  11.4 26.3 %collective-permute-start.1 = (bf16[194048]{0:T(1024)(128)(2,1)}, bf16[194048]{0:T(1024)(128)(2,1)}, u32[]{:S(2)}, u32[]{:S(2)}) collective-permute-start(bf16[194048]{0:T(1024)(128)(2,1)} %get-tuple-element.46), channel_id=1, source_target_pairs={{0,2},{1,3},{2,0},{3,1},{4,6},{5,7},{6,4},{7,5},{8,10},{9,11},{10,... | collective-permute-start | bytes 1164296 | tf_op jit(solution)/shard_map/ppermute | solution.py:115
  21.8 1.2 copy-start.19
  21.8 21.6 %collective-permute-start.2 = (bf16[194048]{0:T(1024)(128)(2,1)S(1)}, bf16[194048]{0:T(1024)(128)(2,1)}, u32[]{:S(2)}, u32[]{:S(2)}) collective-permute-start(bf16[194048]{0:T(1024)(128)(2,1)S(1)} %get-tuple-element.45), channel_id=1, source_target_pairs={{0,3},{1,0},{2,1},{3,2},{4,7},{5,4},{6,5},{7,6},{8,11},{9,8},{10,9... | collective-permute-start | bytes 1164296 | tf_op jit(solution)/shard_map/ppermute | solution.py:115
  37.7 19.7 %collective-permute-start.6 = (bf16[1,128,3072]{2,1,0:T(8,128)(2,1)S(1)}, bf16[1,128,3072]{2,1,0:T(8,128)(2,1)}, u32[]{:S(2)}, u32[]{:S(2)}) collective-permute-start(bf16[1,128,3072]{2,1,0:T(8,128)(2,1)S(1)} %copy-done.14), channel_id=1, source_target_pairs={{0,16},{16,0},{1,17},{17,1},{2,18},{18,2},{3,19},{19,3},{4,20},{20... | collective-permute-start | bytes 2359304 | tf_op jit(solution)/shard_map/ppermute | solution.py:17
  46.4 9.5 %copy-start.15 = (bf16[128,3072]{1,0:T(8,128)(2,1)}, bf16[128,3072]{1,0:T(8,128)(2,1)S(1)}, u32[]{:S(2)}) copy-start(bf16[128,3072]{1,0:T(8,128)(2,1)S(1)} %collective-permute-done.5) | copy-start | bytes 2359300
  55.9 13.7 %copy-start.10 = (f32[512,1536]{1,0:T(8,128)}, f32[512,1536]{1,0:T(8,128)S(1)}, u32[]{:S(2)}) copy-start(f32[512,1536]{1,0:T(8,128)S(1)} %fusion.2) | copy-start | bytes 9437188
  57.4 91.1 %collective-permute-start.20 = (bf16[128,3072]{1,0:T(8,128)(2,1)}, bf16[128,3072]{1,0:T(8,128)(2,1)}, u32[]{:S(2)}, u32[]{:S(2)}) collective-permute-start(bf16[128,3072]{1,0:T(8,128)(2,1)} %bitcast.31), channel_id=1, source_target_pairs={{0,4},{4,8},{8,12},{12,0},{1,5},{5,9},{9,13},{13,1},{2,6},{6,10},{... | collective-permute-start | bytes 2359304 | tf_op jit(solution)/shard_map/ppermute | solution.py:115
  57.4 94.1 %collective-permute-start.21 = (bf16[128,3072]{1,0:T(8,128)(2,1)}, bf16[128,3072]{1,0:T(8,128)(2,1)}, u32[]{:S(2)}, u32[]{:S(2)}) collective-permute-start(bf16[128,3072]{1,0:T(8,128)(2,1)} %bitcast.31), channel_id=1, source_target_pairs={{0,8},{4,12},{8,0},{12,4},{1,9},{5,13},{9,1},{13,5},{2,10},{6,14},... | collective-permute-start | bytes 2359304 | tf_op jit(solution)/shard_map/ppermute | solution.py:115
  60.0 28.5 %collective-permute-start.9 = (bf16[512,384]{1,0:T(8,128)(2,1)}, bf16[512,384]{1,0:T(8,128)(2,1)}, u32[]{:S(2)}, u32[]{:S(2)}) collective-permute-start(bf16[512,384]{1,0:T(8,128)(2,1)} %get-tuple-element.30), channel_id=1, source_target_pairs={{0,1},{1,2},{2,3},{3,0},{4,5},{5,6},{6,7},{7,4},{8,9},{9,10},{10,1... | collective-permute-start | bytes 1179656 | tf_op jit(solution)/shard_map/ppermute | solution.py:115
  66.0 29.7 %collective-permute-start.8 = (bf16[512,384]{1,0:T(8,128)(2,1)}, bf16[512,384]{1,0:T(8,128)(2,1)}, u32[]{:S(2)}, u32[]{:S(2)}) collective-permute-start(bf16[512,384]{1,0:T(8,128)(2,1)} %get-tuple-element.31), channel_id=1, source_target_pairs={{0,2},{1,3},{2,0},{3,1},{4,6},{5,7},{6,4},{7,5},{8,10},{9,11},{10,... | collective-permute-start | bytes 1179656 | tf_op jit(solution)/shard_map/ppermute | solution.py:115
  69.4 26.3 %collective-permute-start.7 = (bf16[512,384]{1,0:T(8,128)(2,1)}, bf16[512,384]{1,0:T(8,128)(2,1)}, u32[]{:S(2)}, u32[]{:S(2)}) collective-permute-start(bf16[512,384]{1,0:T(8,128)(2,1)} %get-tuple-element.29), channel_id=1, source_target_pairs={{0,3},{1,0},{2,1},{3,2},{4,7},{5,4},{6,5},{7,6},{8,11},{9,8},{10,9... | collective-permute-start | bytes 1179656 | tf_op jit(solution)/shard_map/ppermute | solution.py:115
  74.6 4.3 %copy-start.16 = (bf16[128,3072]{1,0:T(8,128)(2,1)S(1)}, bf16[128,3072]{1,0:T(8,128)(2,1)}, u32[]{:S(2)}) copy-start(bf16[128,3072]{1,0:T(8,128)(2,1)} %copy-done.15) | copy-start | bytes 2359300
  76.8 5.1 %copy-start.8 = (bf16[1,128,364]{2,1,0:T(8,128)(2,1)S(1)}, bf16[1,128,364]{2,1,0:T(8,128)(2,1)}, u32[]{:S(2)}) copy-start(bf16[1,128,364]{2,1,0:T(8,128)(2,1)} %copy-done.7) | copy-start | bytes 279556
  76.8 5.1 %copy-start.11 = (bf16[128,364]{1,0:T(8,128)(2,1)S(1)}, bf16[128,364]{1,0:T(8,128)(2,1)}, u32[]{:S(2)}) copy-start(bf16[128,364]{1,0:T(8,128)(2,1)} %reshape.139) | copy-start | bytes 279556
  76.8 5.2 %copy-start.12 = (bf16[128,364]{1,0:T(8,128)(2,1)S(1)}, bf16[128,364]{1,0:T(8,128)(2,1)}, u32[]{:S(2)}) copy-start(bf16[128,364]{1,0:T(8,128)(2,1)} %reshape.142) | copy-start | bytes 279556
  76.8 5.2 %copy-start.13 = (bf16[128,364]{1,0:T(8,128)(2,1)S(1)}, bf16[128,364]{1,0:T(8,128)(2,1)}, u32[]{:S(2)}) copy-start(bf16[128,364]{1,0:T(8,128)(2,1)} %reshape.145) | copy-start | bytes 279556
  88.5 9.1 %copy-start = (bf16[3,512,512]{1,2,0:T(8,128)(2,1)S(1)}, bf16[3,512,512]{1,2,0:T(8,128)(2,1)}, u32[]{:S(2)}) copy-start(bf16[3,512,512]{1,2,0:T(8,128)(2,1)} %exponential_convert_fusion) | copy-start | bytes 4718596
  88.5 65.8 %collective-permute-start.22 = (bf16[128,3072]{1,0:T(8,128)(2,1)}, bf16[128,3072]{1,0:T(8,128)(2,1)}, u32[]{:S(2)}, u32[]{:S(2)}) collective-permute-start(bf16[128,3072]{1,0:T(8,128)(2,1)} %bitcast.31), channel_id=1, source_target_pairs={{0,12},{4,0},{8,4},{12,8},{1,13},{5,1},{9,5},{13,9},{2,14},{6,2},{... | collective-permute-start | bytes 2359304 | tf_op jit(solution)/shard_map/ppermute | solution.py:115
  97.4 1.9 copy-start.2
  100.2 1.4 copy-start.1
  101.7 1.3 copy-start.4
  102.9 2.7 %copy-start.6 = (bf16[512,3,128]{0,2,1:T(8,128)(2,1)S(1)}, bf16[512,3,128]{0,2,1:T(8,128)(2,1)}, u32[]{:S(2)}) copy-start(bf16[512,3,128]{0,2,1:T(8,128)(2,1)} %get-tuple-element.54) | copy-start | bytes 1179652
  104.1 1.9 copy-start.5
  106.4 14.8 %copy-start.3 = (f32[512,3,128]{0,2,1:T(8,128)S(1)}, f32[512,3,128]{0,2,1:T(8,128)}, u32[]{:S(2)}) copy-start(f32[512,3,128]{0,2,1:T(8,128)} %get-tuple-element.53) | copy-start | bytes 2359300
  108.2 18.6 %collective-permute-start.10 = (bf16[3,128,384]{2,1,0:T(8,128)(2,1)}, bf16[3,128,384]{2,1,0:T(8,128)(2,1)}, u32[]{:S(2)}, u32[]{:S(2)}) collective-permute-start(bf16[3,128,384]{2,1,0:T(8,128)(2,1)} %get-tuple-element.37), channel_id=1, source_target_pairs={{0,3},{1,0},{2,1},{3,2},{4,7},{5,4},{6,5},{7,6},{8,11},{9,8},{10,9... | collective-permute-start | bytes 884744 | tf_op jit(solution)/shard_map/ppermute | solution.py:115
  116.1 34.2 %slice-start = ((s8[6291456]{0:T(1024)(128)(4,1)}), s8[2097152]{0:T(1024)(128)(4,1)S(1)}, s32[]{:S(2)}) async-start(s8[6291456]{0:T(1024)(128)(4,1)} %bitcast.135), calls=%async_computation | async-start | bytes 4194304
  121.2 5.5 %copy-start.17 = (f32[1,128,384]{2,1,0:T(8,128)S(1)}, f32[1,128,384]{2,1,0:T(8,128)}, u32[]{:S(2)}) copy-start(f32[1,128,384]{2,1,0:T(8,128)} %copy.64) | copy-start | bytes 589828
  122.3 4.3 %copy-start.18 = (f32[1,128,384]{2,1,0:T(8,128)S(1)}, f32[1,128,384]{2,1,0:T(8,128)}, u32[]{:S(2)}) copy-start(f32[1,128,384]{2,1,0:T(8,128)} %copy.63) | copy-start | bytes 589828
  123.8 3.0 %copy-start.20 = (bf16[3,128,384]{2,1,0:T(8,128)(2,1)S(1)}, bf16[3,128,384]{2,1,0:T(8,128)(2,1)}, u32[]{:S(2)}) copy-start(bf16[3,128,384]{2,1,0:T(8,128)(2,1)} %get-tuple-element.35) | copy-start | bytes 884740
  123.8 22.7 %collective-permute-start.11 = (bf16[3,128,384]{2,1,0:T(8,128)(2,1)}, bf16[3,128,384]{2,1,0:T(8,128)(2,1)S(1)}, u32[]{:S(2)}, u32[]{:S(2)}) collective-permute-start(bf16[3,128,384]{2,1,0:T(8,128)(2,1)} %get-tuple-element.36), channel_id=1, source_target_pairs={{0,2},{1,3},{2,0},{3,1},{4,6},{5,7},{6,4},{7,5},{8,10},{9,11},{10,... | collective-permute-start | bytes 884744 | tf_op jit(solution)/shard_map/ppermute | solution.py:115
  126.7 23.6 %slice-start.1 = ((s8[6291456]{0:T(1024)(128)(4,1)}), s8[4194304]{0:T(1024)(128)(4,1)S(1)}, s32[]{:S(2)}) async-start(s8[6291456]{0:T(1024)(128)(4,1)} %bitcast.135), calls=%async_computation.1 | async-start | bytes 8388608
  126.8 19.8 %collective-permute-start.12 = (bf16[3,128,384]{2,1,0:T(8,128)(2,1)S(1)}, bf16[3,128,384]{2,1,0:T(8,128)(2,1)S(1)}, u32[]{:S(2)}, u32[]{:S(2)}) collective-permute-start(bf16[3,128,384]{2,1,0:T(8,128)(2,1)S(1)} %copy-done.20), channel_id=1, source_target_pairs={{0,1},{1,2},{2,3},{3,0},{4,5},{5,6},{6,7},{7,4},{8,9},{9,10},{10,1... | collective-permute-start | bytes 884744 | tf_op jit(solution)/shard_map/ppermute | solution.py:115
  146.5 10.8 %collective-permute-start.14 = (bf16[512,384]{0,1:T(8,128)(2,1)S(1)}, bf16[512,384]{0,1:T(8,128)(2,1)S(1)}, u32[]{:S(2)}, u32[]{:S(2)}) collective-permute-start(bf16[512,384]{0,1:T(8,128)(2,1)S(1)} %bitcast.140), channel_id=1, source_target_pairs={{0,3},{1,0},{2,1},{3,2},{4,7},{5,4},{6,5},{7,6},{8,11},{9,8},{10,9... | collective-permute-start | bytes 1179656 | tf_op jit(solution)/shard_map/ppermute | solution.py:115
  146.6 33.3 %collective-permute-start.16 = (bf16[512,384]{0,1:T(8,128)(2,1)S(1)}, bf16[512,384]{0,1:T(8,128)(2,1)S(1)}, u32[]{:S(2)}, u32[]{:S(2)}) collective-permute-start(bf16[512,384]{0,1:T(8,128)(2,1)S(1)} %bitcast.141), channel_id=1, source_target_pairs={{0,2},{1,3},{2,0},{3,1},{4,6},{5,7},{6,4},{7,5},{8,10},{9,11},{10,... | collective-permute-start | bytes 1179656 | tf_op jit(solution)/shard_map/ppermute | solution.py:115
  147.0 4.5 %copy-start.9 = (bf16[4,128,364]{2,1,0:T(8,128)(2,1)S(1)}, bf16[4,128,364]{2,1,0:T(8,128)(2,1)}, u32[]{:S(2)}) copy-start(bf16[4,128,364]{2,1,0:T(8,128)(2,1)} %constant_dynamic-slice_fusion) | copy-start | bytes 1118212
  148.4 33.0 %collective-permute-start.18 = (bf16[512,384]{0,1:T(8,128)(2,1)S(1)}, bf16[512,384]{0,1:T(8,128)(2,1)S(1)}, u32[]{:S(2)}, u32[]{:S(2)}) collective-permute-start(bf16[512,384]{0,1:T(8,128)(2,1)S(1)} %bitcast.142), channel_id=1, source_target_pairs={{0,1},{1,2},{2,3},{3,0},{4,5},{5,6},{6,7},{7,4},{8,9},{9,10},{10,1... | collective-permute-start | bytes 1179656 | tf_op jit(solution)/shard_map/ppermute | solution.py:115
  151.5 31.6 %collective-permute-start.23 = (bf16[512,364]{1,0:T(8,128)(2,1)S(1)}, bf16[512,364]{1,0:T(8,128)(2,1)S(1)}, u32[]{:S(2)}, u32[]{:S(2)}) collective-permute-start(bf16[512,364]{1,0:T(8,128)(2,1)S(1)} %bitcast.148), channel_id=1, source_target_pairs={{0,16},{16,0},{1,17},{17,1},{2,18},{18,2},{3,19},{19,3},{4,20},{20... | collective-permute-start | bytes 1118216 | tf_op jit(solution)/shard_map/ppermute | solution.py:17
  154.3 33.6 %collective-permute-start.13 = (bf16[512,384]{0,1:T(8,128)(2,1)S(1)}, bf16[512,384]{0,1:T(8,128)(2,1)S(1)}, u32[]{:S(2)}, u32[]{:S(2)}) collective-permute-start(bf16[512,384]{0,1:T(8,128)(2,1)S(1)} %bitcast.143), channel_id=1, source_target_pairs={{0,16},{16,0},{1,17},{17,1},{2,18},{18,2},{3,19},{19,3},{4,20},{20... | collective-permute-start | bytes 1179656 | tf_op jit(solution)/shard_map/ppermute | solution.py:17
  157.4 30.5 %collective-permute-start.15 = (bf16[512,384]{0,1:T(8,128)(2,1)S(1)}, bf16[512,384]{0,1:T(8,128)(2,1)S(1)}, u32[]{:S(2)}, u32[]{:S(2)}) collective-permute-start(bf16[512,384]{0,1:T(8,128)(2,1)S(1)} %collective-permute-done.14), channel_id=1, source_target_pairs={{0,16},{16,0},{1,17},{17,1},{2,18},{18,2},{3,19},{19,3},{4,20},{20... | collective-permute-start | bytes 1179656 | tf_op jit(solution)/shard_map/ppermute | solution.py:17
  179.9 12.1 %collective-permute-start.17 = (bf16[512,384]{0,1:T(8,128)(2,1)S(1)}, bf16[512,384]{0,1:T(8,128)(2,1)S(1)}, u32[]{:S(2)}, u32[]{:S(2)}) collective-permute-start(bf16[512,384]{0,1:T(8,128)(2,1)S(1)} %collective-permute-done.16), channel_id=1, source_target_pairs={{0,16},{16,0},{1,17},{17,1},{2,18},{18,2},{3,19},{19,3},{4,20},{20... | collective-permute-start | bytes 1179656 | tf_op jit(solution)/shard_map/ppermute | solution.py:17
  181.4 16.4 %collective-permute-start.19 = (bf16[512,384]{0,1:T(8,128)(2,1)S(1)}, bf16[512,384]{0,1:T(8,128)(2,1)S(1)}, u32[]{:S(2)}, u32[]{:S(2)}) collective-permute-start(bf16[512,384]{0,1:T(8,128)(2,1)S(1)} %collective-permute-done.18), channel_id=1, source_target_pairs={{0,16},{16,0},{1,17},{17,1},{2,18},{18,2},{3,19},{19,3},{4,20},{20... | collective-permute-start | bytes 1179656 | tf_op jit(solution)/shard_map/ppermute | solution.py:17

commit v15 on v9

--- a/solution.py
+++ b/solution.py
@@ -212,12 +212,12 @@
     grad_blocks = [output_grad[0]] + [shifted(output_grad[0], "row", s) for s in range(1, n)]
     dense_grad = jnp.concatenate(grad_blocks, 0)
     grad_other = swap_dp(output_grad)
-    qkv = jnp.stack([queries[0], attn_keys[0], attn_values[0]], 0)
-    part = lambda g: lax.dynamic_slice_in_dim(qkv, g * width, width, 2)
+    sources = (queries[0], attn_keys[0], attn_values[0])
+    part = lambda g: [lax.dynamic_slice_in_dim(a, g * width, width, 1) for a in sources]
     shapes = [(3, tokens, width), patch_here.shape]
-    pieces = [(part(me), patch_here)]
+    pieces = [(jnp.stack(part(me), 0), patch_here)]
     for s in range(1, n):
-        got = shifted(flat(part((me + s) % n), patch_here), "col", s)
+        got = shifted(flat(*part((me + s) % n), patch_here), "col", s)
         pieces.append(tuple(unflat(got, shapes)))
     grad_partial = lax.dot_general(
         dense_grad, out_weight, (((1,), (1,)), ((), ())), preferred_element_type=jnp.float32

time: 205 us -> 203 us (level)
  other arithmetic: 12.9 us -> 8.74 us
    unnamed x8, other arithmetic: 6.88 us -> 2.83 us
    dynamic_slice x1 -> x2, local copies, waits for them, and re-layouts: 0.13 us -> 2.49 us  [body_heads(): lax.dynamic_slice_in_dim(a, g * width, width, 1)]
    unnamed x65 -> x61, local copies, waits for them, and re-layouts: 16.3 us -> 14.2 us
  transfers between devices with their start and end apart: 24 -> 24, of which waited for: 9 -> 11; matrix products, arithmetic and copies ran while one was open for 39% -> 39% of each run, Pallas kernels for 0% -> 0%
where the time goes in v15:
time: 203 us; the launch traced here: 202 us
  waiting for transfers between devices  72.2 us (36%)
  local copies, waits for them, and re-layouts  43.6 us (21%)
  starting transfers between devices  40.2 us (20%)
  matrix products  35.8 us (18%)
  other arithmetic  8.74 us (4%)
    ppermute x18, waiting for transfers between devices, shifted(): return lax.ppermute(x, axis, [(j, (j + step) % n) for j in range(n)])  58.1 us
    ppermute x18, starting transfers between devices, shifted(): return lax.ppermute(x, axis, [(j, (j + step) % n) for j in range(n)])  33.1 us
    unnamed x61, local copies, waits for them, and re-layouts  14.2 us
    ppermute x6, waiting for transfers between devices, swap_dp(): return lax.ppermute(x, 'dp', [(0, 1), (1, 0)])  14.1 us
    dot_general x1, matrix products, body_heads(): lax.dot_general(out_both, grad_both, (((1,), (0,)), ((), ())), preferred_...  13 us
    dot_general x1, matrix products, body_heads(): lax.dot_general(dense_grad, out_weight, (((1,), (1,)), ((), ())), preferr...  9.23 us
    dot_general x1, matrix products, contract_rows(): lax.dot_general(left, right, (((0,), (0,)), ((), ())), preferred_element_...  7.48 us
    ppermute x6, starting transfers between devices, swap_dp(): return lax.ppermute(x, 'dp', [(0, 1), (1, 0)])  7.08 us
  transfers between devices with their start and end apart: 24, of which 11 were waited for; matrix products, arithmetic and copies ran while one was open for 39% of the time, Pallas kernels for 0%

profile of v15, /device:TPU:0, one launch (start us, length us, event | category | flops | bytes accessed | tf_op | source)
XLA Modules:
  0.0 202.0 jit_solution(1374743404795451836)
XLA Ops:
  2.0 1.2 constant_dynamic-slice_fusion.7
  3.2 1.3 constant_dynamic-slice_fusion.5
  5.9 3.0 %collective-permute-start = (bf16[194048]{0:T(1024)(128)(2,1)S(1)}, bf16[194048]{0:T(1024)(128)(2,1)S(1)}, u32[]{:S(2)}, u32[]{:S(2)}) collective-permute-start(bf16[194048]{0:T(1024)(128)(2,1)S(1)} %get-tuple-element.57), channel_id=1, source_target_pairs={{0,1},{1,2},{2,3},{3,0},{4,5},{5,6},{6,7},{7,4},{8,9},{9,10},{10,1... | collective-permute-start | bytes 1164296 | tf_op jit(solution)/shard_map/ppermute | solution.py:115
  10.6 2.6 %collective-permute-start.1 = (bf16[194048]{0:T(1024)(128)(2,1)}, bf16[194048]{0:T(1024)(128)(2,1)}, u32[]{:S(2)}, u32[]{:S(2)}) collective-permute-start(bf16[194048]{0:T(1024)(128)(2,1)} %get-tuple-element.56), channel_id=1, source_target_pairs={{0,2},{1,3},{2,0},{3,1},{4,6},{5,7},{6,4},{7,5},{8,10},{9,11},{10,... | collective-permute-start | bytes 1164296 | tf_op jit(solution)/shard_map/ppermute | solution.py:115
  13.2 7.7 %collective-permute-done = bf16[194048]{0:T(1024)(128)(2,1)S(1)} collective-permute-done((bf16[194048]{0:T(1024)(128)(2,1)S(1)}, bf16[194048]{0:T(1024)(128)(2,1)S(1)}, u32[]{:S(2)}, u32[]{:S(2)}) %collective-permute-start) | collective-permute-done | bytes 388128 | tf_op jit(solution)/shard_map/ppermute | solution.py:115
  20.9 1.2 collective-permute-start.2
  24.1 12.6 %collective-permute-done.1 = bf16[194048]{0:T(1024)(128)(2,1)} collective-permute-done((bf16[194048]{0:T(1024)(128)(2,1)}, bf16[194048]{0:T(1024)(128)(2,1)}, u32[]{:S(2)}, u32[]{:S(2)}) %collective-permute-start.1) | collective-permute-done | bytes 388128 | tf_op jit(solution)/shard_map/ppermute | solution.py:115
  36.7 1.5 collective-permute-start.6
  41.2 1.2 collective-permute-done.2
  45.7 9.2 %fusion.2 = f32[512,1536]{1,0:T(8,128)S(1)} fusion(bf16[1536,3072]{1,0:T(8,128)(2,1)} %param.10, bf16[128,3072]{1,0:T(8,128)(2,1)S(1)} %collective-permute-done.5, bf16[128,3072]{1,0:T(8,128)(2,1)} %collective-permute-done.4, bf16[128,3072]{1,0:T(8,128)(2,1)} %collective-permute-done.3, bf16[128,3072]{1,0:T(8,128)(2,1)S(1)} %bitcast.154), kind=kOutput, calls=%fused_computation.2 | convolution fusion | flops 4844421120 | bytes 15728640 | tf_op jit(solution)/shard_map/dot_general | solution.py:222
  55.0 1.4 collective-permute-done.6
  56.4 1.5 collective-permute-start.21
  57.9 1.1 dynamic-slice_convert_fusion.2
  59.0 6.0 %collective-permute-start.9 = (bf16[512,384]{1,0:T(8,128)(2,1)}, bf16[512,384]{1,0:T(8,128)(2,1)}, u32[]{:S(2)}, u32[]{:S(2)}) collective-permute-start(bf16[512,384]{1,0:T(8,128)(2,1)} %get-tuple-element.32), channel_id=1, source_target_pairs={{0,1},{1,2},{2,3},{3,0},{4,5},{5,6},{6,7},{7,4},{8,9},{9,10},{10,1... | collective-permute-start | bytes 1179656 | tf_op jit(solution)/shard_map/ppermute | solution.py:115
  65.0 3.4 %collective-permute-start.8 = (bf16[512,384]{1,0:T(8,128)(2,1)}, bf16[512,384]{1,0:T(8,128)(2,1)}, u32[]{:S(2)}, u32[]{:S(2)}) collective-permute-start(bf16[512,384]{1,0:T(8,128)(2,1)} %get-tuple-element.33), channel_id=1, source_target_pairs={{0,2},{1,3},{2,0},{3,1},{4,6},{5,7},{6,4},{7,5},{8,10},{9,11},{10,... | collective-permute-start | bytes 1179656 | tf_op jit(solution)/shard_map/ppermute | solution.py:115
  71.5 1.6 multiply_reduce_fusion
  73.7 2.1 %constant_dynamic-update-slice_fusion.6 = bf16[1024,3072]{1,0:T(8,128)(2,1)} fusion(bf16[1024,3072]{1,0:T(8,128)(2,1)} %constant_dynamic-update-slice_fusion.7, bf16[128,3072]{1,0:T(8,128)(2,1)} %collective-permute-done.3), kind=kLoop, calls=%fused_computation.90 | loop fusion | bytes 1572864
  75.8 2.1 %constant_dynamic-update-slice_fusion.5 = bf16[1024,3072]{1,0:T(8,128)(2,1)} fusion(bf16[1024,3072]{1,0:T(8,128)(2,1)} %constant_dynamic-update-slice_fusion.6, bf16[128,3072]{1,0:T(8,128)(2,1)} %collective-permute-done.4), kind=kLoop, calls=%fused_computation.89 | loop fusion | bytes 1572864
  78.8 2.1 %constant_dynamic-update-slice_fusion.3 = bf16[1024,3072]{1,0:T(8,128)(2,1)} fusion(bf16[1024,3072]{1,0:T(8,128)(2,1)} %constant_dynamic-update-slice_fusion.4, bf16[1,128,3072]{2,1,0:T(8,128)(2,1)} %collective-permute-done.6), kind=kLoop, calls=%fused_computation.87 | loop fusion | bytes 1572864
  81.9 1.9 copy.37
  83.9 1.9 squeeze.53
  85.7 1.7 exponential_convert_fusion
  88.3 6.4 %collective-permute-done.8 = bf16[512,384]{1,0:T(8,128)(2,1)} collective-permute-done((bf16[512,384]{1,0:T(8,128)(2,1)}, bf16[512,384]{1,0:T(8,128)(2,1)}, u32[]{:S(2)}, u32[]{:S(2)}) %collective-permute-start.8) | collective-permute-done | bytes 393248 | tf_op jit(solution)/shard_map/ppermute | solution.py:115
  94.7 1.7 add_convert_fusion
  96.6 1.7 fusion.35
  99.9 1.1 fusion.33
  101.1 7.9 %collective-permute-start.11 = (bf16[512,384]{0,1:T(8,128)(2,1)S(1)}, bf16[512,384]{0,1:T(8,128)(2,1)S(1)}, u32[]{:S(2)}, u32[]{:S(2)}) collective-permute-start(bf16[512,384]{0,1:T(8,128)(2,1)S(1)} %bitcast.141), channel_id=1, source_target_pairs={{0,3},{1,0},{2,1},{3,2},{4,7},{5,4},{6,5},{7,6},{8,11},{9,8},{10,9... | collective-permute-start | bytes 1179656 | tf_op jit(solution)/shard_map/ppermute | solution.py:115
  108.9 2.5 %collective-permute-start.13 = (bf16[512,384]{0,1:T(8,128)(2,1)S(1)}, bf16[512,384]{0,1:T(8,128)(2,1)}, u32[]{:S(2)}, u32[]{:S(2)}) collective-permute-start(bf16[512,384]{0,1:T(8,128)(2,1)S(1)} %bitcast.142), channel_id=1, source_target_pairs={{0,2},{1,3},{2,0},{3,1},{4,6},{5,7},{6,4},{7,5},{8,10},{9,11},{10,... | collective-permute-start | bytes 1179656 | tf_op jit(solution)/shard_map/ppermute | solution.py:115
  111.5 1.1 reshape.197
  112.6 1.1 reshape.196
  114.0 1.4 constant_dynamic-slice_fusion.2
  115.4 1.3 constant_dynamic-slice_fusion.3
  120.0 2.1 %constant_dynamic-update-slice_fusion.2 = bf16[1024,3072]{1,0:T(8,128)(2,1)} fusion(bf16[1024,3072]{1,0:T(8,128)(2,1)} %constant_dynamic-update-slice_fusion.3, bf16[128,3072]{1,0:T(8,128)(2,1)} %collective-permute-done.20), kind=kLoop, calls=%fused_computation.86 | loop fusion | bytes 1572864
  122.0 1.5 collective-permute-start.23
  123.5 2.1 %constant_dynamic-update-slice_fusion.1 = bf16[1024,3072]{1,0:T(8,128)(2,1)} fusion(bf16[1024,3072]{1,0:T(8,128)(2,1)} %constant_dynamic-update-slice_fusion.2, bf16[128,3072]{1,0:T(8,128)(2,1)} %collective-permute-done.21), kind=kLoop, calls=%fused_computation.85 | loop fusion | bytes 1572864
  126.1 19.8 %collective-permute-done.13 = bf16[512,384]{0,1:T(8,128)(2,1)} collective-permute-done((bf16[512,384]{0,1:T(8,128)(2,1)S(1)}, bf16[512,384]{0,1:T(8,128)(2,1)}, u32[]{:S(2)}, u32[]{:S(2)}) %collective-permute-start.13) | collective-permute-done | bytes 393248 | tf_op jit(solution)/shard_map/ppermute | solution.py:115
  145.9 1.5 collective-permute-start.12
  147.9 1.5 collective-permute-start.16
  149.4 2.1 %constant_dynamic-update-slice_fusion = bf16[1024,3072]{1,0:T(8,128)(2,1)} fusion(bf16[1024,3072]{1,0:T(8,128)(2,1)} %constant_dynamic-update-slice_fusion.1, bf16[128,3072]{1,0:T(8,128)(2,1)} %collective-permute-done.22), kind=kLoop, calls=%fused_computation.84 | loop fusion | bytes 1572864 | tf_op jit(solution)/shard_map/concatenate | solution.py:274
  151.5 7.5 %fusion.17 = f32[364,3072]{1,0:T(8,128)} fusion(bf16[1024,3072]{1,0:T(8,128)(2,1)} %constant_dynamic-update-slice_fusion, bf16[512,364]{1,0:T(8,128)(2,1)S(1)} %collective-permute-done.23, bf16[512,364]{1,0:T(8,128)(2,1)S(1)} %bitcast.150), kind=kOutput, calls=%fused_computation.39 | convolution fusion | flops 2291580928 | bytes 11509760 | tf_op jit(solution)/shard_map/dot_general | solution.py:11
  159.2 7.2 %collective-permute-done.14 = bf16[512,384]{0,1:T(8,128)(2,1)S(1)} collective-permute-done((bf16[512,384]{0,1:T(8,128)(2,1)}, bf16[512,384]{0,1:T(8,128)(2,1)S(1)}, u32[]{:S(2)}, u32[]{:S(2)}) %collective-permute-start.14) | collective-permute-done | bytes 393248 | tf_op jit(solution)/shard_map/ppermute | solution.py:17
  166.4 1.1 fusion.24
  167.5 5.5 %collective-permute-done.16 = bf16[512,384]{0,1:T(8,128)(2,1)S(1)} collective-permute-done((bf16[512,384]{0,1:T(8,128)(2,1)S(1)}, bf16[512,384]{0,1:T(8,128)(2,1)S(1)}, u32[]{:S(2)}, u32[]{:S(2)}) %collective-permute-start.16) | collective-permute-done | bytes 393248 | tf_op jit(solution)/shard_map/ppermute | solution.py:17
  173.3 1.3 fusion.25
  175.2 1.9 collective-permute-start.18
  177.1 13.0 %fusion = f32[4,384,3072]{2,1,0:T(8,128)} fusion(bf16[4,1024,384]{1,2,0:T(8,128)(2,1)S(1)} %constant_dynamic-slice_fusion.1, bf16[1024,3072]{1,0:T(8,128)(2,1)S(1)} %bitcast.137), kind=kOutput, calls=%fused_computation | convolution fusion | flops 9663676416 | bytes 28311552 | tf_op jit(solution)/shard_map/dot_general | solution.py:275
  190.4 10.0 %collective-permute-done.18 = bf16[3,128,384]{2,1,0:T(8,128)(2,1)S(1)} collective-permute-done((bf16[3,128,384]{2,1,0:T(8,128)(2,1)S(1)}, bf16[3,128,384]{2,1,0:T(8,128)(2,1)S(1)}, u32[]{:S(2)}, u32[]{:S(2)}) %collective-permute-start.18) | collective-permute-done | bytes 294944 | tf_op jit(solution)/shard_map/ppermute | solution.py:115
  200.5 1.5 slice_bitcast_fusion
  (144 shorter events, 26.7 us)
Async XLA Ops:
  1.7 4.2 %copy-start.6 = (bf16[1,128,364]{2,1,0:T(8,128)(2,1)}, bf16[1,128,364]{2,1,0:T(8,128)(2,1)S(1)}, u32[]{:S(2)}) copy-start(bf16[1,128,364]{2,1,0:T(8,128)(2,1)S(1)} %copy.30) | copy-start | bytes 279556
  2.0 6.9 %copy-start.13 = (bf16[1,128,3072]{2,1,0:T(8,128)(2,1)S(1)}, bf16[1,128,3072]{2,1,0:T(8,128)(2,1)}, u32[]{:S(2)}) copy-start(bf16[1,128,3072]{2,1,0:T(8,128)(2,1)} %param.11) | copy-start | bytes 2359300
  5.9 15.0 %collective-permute-start = (bf16[194048]{0:T(1024)(128)(2,1)S(1)}, bf16[194048]{0:T(1024)(128)(2,1)S(1)}, u32[]{:S(2)}, u32[]{:S(2)}) collective-permute-start(bf16[194048]{0:T(1024)(128)(2,1)S(1)} %get-tuple-element.57), channel_id=1, source_target_pairs={{0,1},{1,2},{2,3},{3,0},{4,5},{5,6},{6,7},{7,4},{8,9},{9,10},{10,1... | collective-permute-start | bytes 1164296 | tf_op jit(solution)/shard_map/ppermute | solution.py:115
  8.9 36.4 %collective-permute-start.5 = (bf16[128,3072]{1,0:T(8,128)(2,1)S(1)}, bf16[128,3072]{1,0:T(8,128)(2,1)S(1)}, u32[]{:S(2)}, u32[]{:S(2)}) collective-permute-start(bf16[128,3072]{1,0:T(8,128)(2,1)S(1)} %bitcast.151), channel_id=1, source_target_pairs={{0,12},{4,0},{8,4},{12,8},{1,13},{5,1},{9,5},{13,9},{2,14},{6,2},{... | collective-permute-start | bytes 2359304 | tf_op jit(solution)/shard_map/ppermute | solution.py:115
  9.5 36.1 %collective-permute-start.4 = (bf16[128,3072]{1,0:T(8,128)(2,1)S(1)}, bf16[128,3072]{1,0:T(8,128)(2,1)}, u32[]{:S(2)}, u32[]{:S(2)}) collective-permute-start(bf16[128,3072]{1,0:T(8,128)(2,1)S(1)} %bitcast.152), channel_id=1, source_target_pairs={{0,8},{4,12},{8,0},{12,4},{1,9},{5,13},{9,1},{13,5},{2,10},{6,14},... | collective-permute-start | bytes 2359304 | tf_op jit(solution)/shard_map/ppermute | solution.py:115
  10.4 35.3 %collective-permute-start.3 = (bf16[128,3072]{1,0:T(8,128)(2,1)S(1)}, bf16[128,3072]{1,0:T(8,128)(2,1)}, u32[]{:S(2)}, u32[]{:S(2)}) collective-permute-start(bf16[128,3072]{1,0:T(8,128)(2,1)S(1)} %bitcast.153), channel_id=1, source_target_pairs={{0,4},{4,8},{8,12},{12,0},{1,5},{5,9},{9,13},{13,1},{2,6},{6,10},{... | collective-permute-start | bytes 2359304 | tf_op jit(solution)/shard_map/ppermute | solution.py:115
  10.6 26.1 %collective-permute-start.1 = (bf16[194048]{0:T(1024)(128)(2,1)}, bf16[194048]{0:T(1024)(128)(2,1)}, u32[]{:S(2)}, u32[]{:S(2)}) collective-permute-start(bf16[194048]{0:T(1024)(128)(2,1)} %get-tuple-element.56), channel_id=1, source_target_pairs={{0,2},{1,3},{2,0},{3,1},{4,6},{5,7},{6,4},{7,5},{8,10},{9,11},{10,... | collective-permute-start | bytes 1164296 | tf_op jit(solution)/shard_map/ppermute | solution.py:115
  20.9 21.5 %collective-permute-start.2 = (bf16[194048]{0:T(1024)(128)(2,1)S(1)}, bf16[194048]{0:T(1024)(128)(2,1)}, u32[]{:S(2)}, u32[]{:S(2)}) collective-permute-start(bf16[194048]{0:T(1024)(128)(2,1)S(1)} %get-tuple-element.55), channel_id=1, source_target_pairs={{0,3},{1,0},{2,1},{3,2},{4,7},{5,4},{6,5},{7,6},{8,11},{9,8},{10,9... | collective-permute-start | bytes 1164296 | tf_op jit(solution)/shard_map/ppermute | solution.py:115
  36.7 19.7 %collective-permute-start.6 = (bf16[1,128,3072]{2,1,0:T(8,128)(2,1)S(1)}, bf16[1,128,3072]{2,1,0:T(8,128)(2,1)}, u32[]{:S(2)}, u32[]{:S(2)}) collective-permute-start(bf16[1,128,3072]{2,1,0:T(8,128)(2,1)S(1)} %copy-done.13), channel_id=1, source_target_pairs={{0,16},{16,0},{1,17},{17,1},{2,18},{18,2},{3,19},{19,3},{4,20},{20... | collective-permute-start | bytes 2359304 | tf_op jit(solution)/shard_map/ppermute | solution.py:17
  45.3 9.7 %copy-start.14 = (bf16[128,3072]{1,0:T(8,128)(2,1)}, bf16[128,3072]{1,0:T(8,128)(2,1)S(1)}, u32[]{:S(2)}) copy-start(bf16[128,3072]{1,0:T(8,128)(2,1)S(1)} %collective-permute-done.5) | copy-start | bytes 2359300
  55.0 13.8 %copy-start.9 = (f32[512,1536]{1,0:T(8,128)}, f32[512,1536]{1,0:T(8,128)S(1)}, u32[]{:S(2)}) copy-start(f32[512,1536]{1,0:T(8,128)S(1)} %fusion.2) | copy-start | bytes 9437188
  56.4 63.3 %collective-permute-start.20 = (bf16[128,3072]{1,0:T(8,128)(2,1)}, bf16[128,3072]{1,0:T(8,128)(2,1)}, u32[]{:S(2)}, u32[]{:S(2)}) collective-permute-start(bf16[128,3072]{1,0:T(8,128)(2,1)} %bitcast.31), channel_id=1, source_target_pairs={{0,4},{4,8},{8,12},{12,0},{1,5},{5,9},{9,13},{13,1},{2,6},{6,10},{... | collective-permute-start | bytes 2359304 | tf_op jit(solution)/shard_map/ppermute | solution.py:115
  56.4 65.6 %collective-permute-start.21 = (bf16[128,3072]{1,0:T(8,128)(2,1)}, bf16[128,3072]{1,0:T(8,128)(2,1)}, u32[]{:S(2)}, u32[]{:S(2)}) collective-permute-start(bf16[128,3072]{1,0:T(8,128)(2,1)} %bitcast.31), channel_id=1, source_target_pairs={{0,8},{4,12},{8,0},{12,4},{1,9},{5,13},{9,1},{13,5},{2,10},{6,14},... | collective-permute-start | bytes 2359304 | tf_op jit(solution)/shard_map/ppermute | solution.py:115
  59.0 28.4 %collective-permute-start.9 = (bf16[512,384]{1,0:T(8,128)(2,1)}, bf16[512,384]{1,0:T(8,128)(2,1)}, u32[]{:S(2)}, u32[]{:S(2)}) collective-permute-start(bf16[512,384]{1,0:T(8,128)(2,1)} %get-tuple-element.32), channel_id=1, source_target_pairs={{0,1},{1,2},{2,3},{3,0},{4,5},{5,6},{6,7},{7,4},{8,9},{9,10},{10,1... | collective-permute-start | bytes 1179656 | tf_op jit(solution)/shard_map/ppermute | solution.py:115
  65.0 29.7 %collective-permute-start.8 = (bf16[512,384]{1,0:T(8,128)(2,1)}, bf16[512,384]{1,0:T(8,128)(2,1)}, u32[]{:S(2)}, u32[]{:S(2)}) collective-permute-start(bf16[512,384]{1,0:T(8,128)(2,1)} %get-tuple-element.33), channel_id=1, source_target_pairs={{0,2},{1,3},{2,0},{3,1},{4,6},{5,7},{6,4},{7,5},{8,10},{9,11},{10,... | collective-permute-start | bytes 1179656 | tf_op jit(solution)/shard_map/ppermute | solution.py:115
  68.4 26.3 %collective-permute-start.7 = (bf16[512,384]{1,0:T(8,128)(2,1)}, bf16[512,384]{1,0:T(8,128)(2,1)}, u32[]{:S(2)}, u32[]{:S(2)}) collective-permute-start(bf16[512,384]{1,0:T(8,128)(2,1)} %get-tuple-element.31), channel_id=1, source_target_pairs={{0,3},{1,0},{2,1},{3,2},{4,7},{5,4},{6,5},{7,6},{8,11},{9,8},{10,9... | collective-permute-start | bytes 1179656 | tf_op jit(solution)/shard_map/ppermute | solution.py:115
  73.1 4.8 %copy-start.15 = (bf16[128,3072]{1,0:T(8,128)(2,1)S(1)}, bf16[128,3072]{1,0:T(8,128)(2,1)}, u32[]{:S(2)}) copy-start(bf16[128,3072]{1,0:T(8,128)(2,1)} %copy-done.14) | copy-start | bytes 2359300
  73.7 7.2 %copy-start.7 = (bf16[1,128,364]{2,1,0:T(8,128)(2,1)S(1)}, bf16[1,128,364]{2,1,0:T(8,128)(2,1)}, u32[]{:S(2)}) copy-start(bf16[1,128,364]{2,1,0:T(8,128)(2,1)} %copy-done.6) | copy-start | bytes 279556
  73.7 7.2 %copy-start.10 = (bf16[128,364]{1,0:T(8,128)(2,1)S(1)}, bf16[128,364]{1,0:T(8,128)(2,1)}, u32[]{:S(2)}) copy-start(bf16[128,364]{1,0:T(8,128)(2,1)} %reshape.183) | copy-start | bytes 279556
  73.7 7.2 %copy-start.11 = (bf16[128,364]{1,0:T(8,128)(2,1)S(1)}, bf16[128,364]{1,0:T(8,128)(2,1)}, u32[]{:S(2)}) copy-start(bf16[128,364]{1,0:T(8,128)(2,1)} %reshape.188) | copy-start | bytes 279556
  73.7 7.3 %copy-start.12 = (bf16[128,364]{1,0:T(8,128)(2,1)S(1)}, bf16[128,364]{1,0:T(8,128)(2,1)}, u32[]{:S(2)}) copy-start(bf16[128,364]{1,0:T(8,128)(2,1)} %reshape.193) | copy-start | bytes 279556
  87.4 9.2 %copy-start = (bf16[3,512,512]{1,2,0:T(8,128)(2,1)S(1)}, bf16[3,512,512]{1,2,0:T(8,128)(2,1)}, u32[]{:S(2)}) copy-start(bf16[3,512,512]{1,2,0:T(8,128)(2,1)} %exponential_convert_fusion) | copy-start | bytes 4718596
  87.4 10.8 %copy-start.2 = (bf16[512,3,128]{0,2,1:T(8,128)(2,1)S(1)}, bf16[512,3,128]{0,2,1:T(8,128)(2,1)}, u32[]{:S(2)}) copy-start(bf16[512,3,128]{0,2,1:T(8,128)(2,1)} %squeeze.53) | copy-start | bytes 1179652
  87.4 60.5 %collective-permute-start.22 = (bf16[128,3072]{1,0:T(8,128)(2,1)}, bf16[128,3072]{1,0:T(8,128)(2,1)}, u32[]{:S(2)}, u32[]{:S(2)}) collective-permute-start(bf16[128,3072]{1,0:T(8,128)(2,1)} %bitcast.31), channel_id=1, source_target_pairs={{0,12},{4,0},{8,4},{12,8},{1,13},{5,1},{9,5},{13,9},{2,14},{6,2},{... | collective-permute-start | bytes 2359304 | tf_op jit(solution)/shard_map/ppermute | solution.py:115
  98.6 1.3 copy-start.1
  99.3 12.2 %copy-start.3 = (f32[512,3,128]{0,2,1:T(8,128)S(1)}, f32[512,3,128]{0,2,1:T(8,128)}, u32[]{:S(2)}) copy-start(f32[512,3,128]{0,2,1:T(8,128)} %get-tuple-element.67) | copy-start | bytes 2359300
  101.1 24.5 %collective-permute-start.11 = (bf16[512,384]{0,1:T(8,128)(2,1)S(1)}, bf16[512,384]{0,1:T(8,128)(2,1)S(1)}, u32[]{:S(2)}, u32[]{:S(2)}) collective-permute-start(bf16[512,384]{0,1:T(8,128)(2,1)S(1)} %bitcast.141), channel_id=1, source_target_pairs={{0,3},{1,0},{2,1},{3,2},{4,7},{5,4},{6,5},{7,6},{8,11},{9,8},{10,9... | collective-permute-start | bytes 1179656 | tf_op jit(solution)/shard_map/ppermute | solution.py:115
  108.9 37.0 %collective-permute-start.13 = (bf16[512,384]{0,1:T(8,128)(2,1)S(1)}, bf16[512,384]{0,1:T(8,128)(2,1)}, u32[]{:S(2)}, u32[]{:S(2)}) collective-permute-start(bf16[512,384]{0,1:T(8,128)(2,1)S(1)} %bitcast.142), channel_id=1, source_target_pairs={{0,2},{1,3},{2,0},{3,1},{4,6},{5,7},{6,4},{7,5},{8,10},{9,11},{10,... | collective-permute-start | bytes 1179656 | tf_op jit(solution)/shard_map/ppermute | solution.py:115
  112.6 4.7 %copy-start.5 = (bf16[512,3,128]{0,2,1:T(8,128)(2,1)S(1)}, bf16[512,3,128]{0,2,1:T(8,128)(2,1)}, u32[]{:S(2)}) copy-start(bf16[512,3,128]{0,2,1:T(8,128)(2,1)} %get-tuple-element.62) | copy-start | bytes 1179652
  114.0 4.1 %copy-start.4 = (bf16[512,3,128]{0,2,1:T(8,128)(2,1)S(1)}, bf16[512,3,128]{0,2,1:T(8,128)(2,1)}, u32[]{:S(2)}) copy-start(bf16[512,3,128]{0,2,1:T(8,128)(2,1)} %get-tuple-element.66) | copy-start | bytes 1179652
  119.3 2.7 %copy-start.8 = (bf16[4,128,364]{2,1,0:T(8,128)(2,1)S(1)}, bf16[4,128,364]{2,1,0:T(8,128)(2,1)}, u32[]{:S(2)}) copy-start(bf16[4,128,364]{2,1,0:T(8,128)(2,1)} %constant_dynamic-slice_fusion) | copy-start | bytes 1118212
  119.7 27.7 %collective-permute-start.15 = (bf16[512,384]{0,1:T(8,128)(2,1)S(1)}, bf16[512,384]{0,1:T(8,128)(2,1)S(1)}, u32[]{:S(2)}, u32[]{:S(2)}) collective-permute-start(bf16[512,384]{0,1:T(8,128)(2,1)S(1)} %bitcast.143), channel_id=1, source_target_pairs={{0,1},{1,2},{2,3},{3,0},{4,5},{5,6},{6,7},{7,4},{8,9},{9,10},{10,1... | collective-permute-start | bytes 1179656 | tf_op jit(solution)/shard_map/ppermute | solution.py:115
  122.0 29.5 %collective-permute-start.23 = (bf16[512,364]{1,0:T(8,128)(2,1)S(1)}, bf16[512,364]{1,0:T(8,128)(2,1)S(1)}, u32[]{:S(2)}, u32[]{:S(2)}) collective-permute-start(bf16[512,364]{1,0:T(8,128)(2,1)S(1)} %bitcast.149), channel_id=1, source_target_pairs={{0,16},{16,0},{1,17},{17,1},{2,18},{18,2},{3,19},{19,3},{4,20},{20... | collective-permute-start | bytes 1118216 | tf_op jit(solution)/shard_map/ppermute | solution.py:17
  125.6 33.4 %collective-permute-start.10 = (bf16[512,384]{0,1:T(8,128)(2,1)S(1)}, bf16[512,384]{0,1:T(8,128)(2,1)S(1)}, u32[]{:S(2)}, u32[]{:S(2)}) collective-permute-start(bf16[512,384]{0,1:T(8,128)(2,1)S(1)} %bitcast.144), channel_id=1, source_target_pairs={{0,16},{16,0},{1,17},{17,1},{2,18},{18,2},{3,19},{19,3},{4,20},{20... | collective-permute-start | bytes 1179656 | tf_op jit(solution)/shard_map/ppermute | solution.py:17
  145.9 13.2 %collective-permute-start.12 = (bf16[512,384]{0,1:T(8,128)(2,1)S(1)}, bf16[512,384]{0,1:T(8,128)(2,1)S(1)}, u32[]{:S(2)}, u32[]{:S(2)}) collective-permute-start(bf16[512,384]{0,1:T(8,128)(2,1)S(1)} %collective-permute-done.11), channel_id=1, source_target_pairs={{0,16},{16,0},{1,17},{17,1},{2,18},{18,2},{3,19},{19,3},{4,20},{20... | collective-permute-start | bytes 1179656 | tf_op jit(solution)/shard_map/ppermute | solution.py:17
  147.4 19.0 %collective-permute-start.14 = (bf16[512,384]{0,1:T(8,128)(2,1)}, bf16[512,384]{0,1:T(8,128)(2,1)S(1)}, u32[]{:S(2)}, u32[]{:S(2)}) collective-permute-start(bf16[512,384]{0,1:T(8,128)(2,1)} %collective-permute-done.13), channel_id=1, source_target_pairs={{0,16},{16,0},{1,17},{17,1},{2,18},{18,2},{3,19},{19,3},{4,20},{20... | collective-permute-start | bytes 1179656 | tf_op jit(solution)/shard_map/ppermute | solution.py:17
  147.9 25.1 %collective-permute-start.16 = (bf16[512,384]{0,1:T(8,128)(2,1)S(1)}, bf16[512,384]{0,1:T(8,128)(2,1)S(1)}, u32[]{:S(2)}, u32[]{:S(2)}) collective-permute-start(bf16[512,384]{0,1:T(8,128)(2,1)S(1)} %collective-permute-done.15), channel_id=1, source_target_pairs={{0,16},{16,0},{1,17},{17,1},{2,18},{18,2},{3,19},{19,3},{4,20},{20... | collective-permute-start | bytes 1179656 | tf_op jit(solution)/shard_map/ppermute | solution.py:17
  173.2 3.9 %slice-start = ((s8[6291456]{0:T(1024)(128)(4,1)}), s8[4194304]{0:T(1024)(128)(4,1)S(1)}, s32[]{:S(2)}) async-start(s8[6291456]{0:T(1024)(128)(4,1)} %bitcast.136), calls=%async_computation | async-start | bytes 8388608
  174.7 2.4 %slice-start.1 = ((s8[6291456]{0:T(1024)(128)(4,1)}), s8[2097152]{0:T(1024)(128)(4,1)S(1)}, s32[]{:S(2)}) async-start(s8[6291456]{0:T(1024)(128)(4,1)} %bitcast.136), calls=%async_computation.1 | async-start | bytes 4194304
  175.1 15.2 %collective-permute-start.17 = (bf16[3,128,384]{2,1,0:T(8,128)(2,1)S(1)}, bf16[3,128,384]{2,1,0:T(8,128)(2,1)S(1)}, u32[]{:S(2)}, u32[]{:S(2)}) collective-permute-start(bf16[3,128,384]{2,1,0:T(8,128)(2,1)S(1)} %get-tuple-element.39), channel_id=1, source_target_pairs={{0,3},{1,0},{2,1},{3,2},{4,7},{5,4},{6,5},{7,6},{8,11},{9,8},{10,9... | collective-permute-start | bytes 884744 | tf_op jit(solution)/shard_map/ppermute | solution.py:115
  175.2 25.2 %collective-permute-start.18 = (bf16[3,128,384]{2,1,0:T(8,128)(2,1)S(1)}, bf16[3,128,384]{2,1,0:T(8,128)(2,1)S(1)}, u32[]{:S(2)}, u32[]{:S(2)}) collective-permute-start(bf16[3,128,384]{2,1,0:T(8,128)(2,1)S(1)} %get-tuple-element.38), channel_id=1, source_target_pairs={{0,2},{1,3},{2,0},{3,1},{4,6},{5,7},{6,4},{7,5},{8,10},{9,11},{10,... | collective-permute-start | bytes 884744 | tf_op jit(solution)/shard_map/ppermute | solution.py:115
  190.1 10.3 %collective-permute-start.19 = (bf16[3,128,384]{2,1,0:T(8,128)(2,1)S(1)}, bf16[3,128,384]{2,1,0:T(8,128)(2,1)S(1)}, u32[]{:S(2)}, u32[]{:S(2)}) collective-permute-start(bf16[3,128,384]{2,1,0:T(8,128)(2,1)S(1)} %get-tuple-element.37), channel_id=1, source_target_pairs={{0,1},{1,2},{2,3},{3,0},{4,5},{5,6},{6,7},{7,4},{8,9},{9,10},{10,1... | collective-permute-start | bytes 884744 | tf_op jit(solution)/shard_map/ppermute | solution.py:115

commit v16 on v15

--- a/solution.py
+++ b/solution.py
@@ -215,14 +215,12 @@
     sources = (queries[0], attn_keys[0], attn_values[0])
     part = lambda g: [lax.dynamic_slice_in_dim(a, g * width, width, 1) for a in sources]
     shapes = [(3, tokens, width), patch_here.shape]
-    pieces = [(jnp.stack(part(me), 0), patch_here)]
-    for s in range(1, n):
-        got = shifted(flat(*part((me + s) % n), patch_here), "col", s)
-        pieces.append(tuple(unflat(got, shapes)))
+    packets = [shifted(flat(*part((me + s) % n), patch_here), "col", s) for s in range(1, n)]
     grad_partial = lax.dot_general(
         dense_grad, out_weight, (((1,), (1,)), ((), ())), preferred_element_type=jnp.float32
     )
-    pieces, grad_partial = lax.optimization_barrier((pieces, grad_partial))
+    packets, grad_partial = lax.optimization_barrier((packets, grad_partial))
+    pieces = [(jnp.stack(part(me), 0), patch_here)] + [tuple(unflat(p, shapes)) for p in packets]
     order = me - rank
     qkv_h = roll_blocks(jnp.stack([p[0] for p in pieces], 0), order)
     every_patch = roll_blocks(jnp.stack([p[1] for p in pieces], 0), order).reshape(n * tokens, -1)

time: 203 us -> 203 us (level)
  local copies, waits for them, and re-layouts: 43.6 us -> 66.5 us
  waiting for transfers between devices: 72.2 us -> 58.5 us
  starting transfers between devices: 40.2 us -> 28.9 us
  other arithmetic: 8.74 us -> 11.4 us
    ppermute x18, waiting for transfers between devices: 58.1 us -> 44.8 us  [shifted(): return lax.ppermute(x, axis, [(j, (j + step) % n) for j in range(n)])]
    unnamed x61 -> x55, local copies, waits for them, and re-layouts: 14.2 us -> 27.4 us
    ppermute x18, starting transfers between devices: 33.1 us -> 22.9 us  [shifted(): return lax.ppermute(x, axis, [(j, (j + step) % n) for j in range(n)])]
    another operation x0 -> x6, local copies, waits for them, and re-layouts: none -> 5.76 us  [the longest x3 5.34 us: body_heads(): jnp.stack([p[1] for p in pieces], 0)]
    reshape x6 -> x0, local copies, waits for them, and re-layouts: 3.1 us -> none  [unflat(): out.append(vector[..., at:at + size].reshape(vector.shape[:-1] + shape))]
    reshape x9, local copies, waits for them, and re-layouts: 0.48 us -> 2.91 us  [flat(): return jnp.concatenate([a.reshape(-1) for a in arrays])]
    concatenate x2, local copies, waits for them, and re-layouts: 0.07 us -> 2.31 us  [roll_blocks(): return lax.dynamic_slice_in_dim(jnp.concatenate([x, x], 0), shift % n, n, 0)]
    unnamed x8 -> x10, other arithmetic: 2.83 us -> 4.31 us
  transfers between devices with their start and end apart: 24 -> 24, of which waited for: 11 -> 6; matrix products, arithmetic and copies ran while one was open for 39% -> 54% of each run, Pallas kernels for 0% -> 0%
where the time goes in v16:
time: 203 us; the launch traced here: 202 us
  local copies, waits for them, and re-layouts  66.5 us (33%)
  waiting for transfers between devices  58.5 us (29%)
  matrix products  35.6 us (18%)
  starting transfers between devices  28.9 us (14%)
  other arithmetic  11.4 us (6%)
    ppermute x18, waiting for transfers between devices, shifted(): return lax.ppermute(x, axis, [(j, (j + step) % n) for j in range(n)])  44.8 us
    unnamed x55, local copies, waits for them, and re-layouts  27.4 us
    ppermute x18, starting transfers between devices, shifted(): return lax.ppermute(x, axis, [(j, (j + step) % n) for j in range(n)])  22.9 us
    ppermute x6, waiting for transfers between devices, swap_dp(): return lax.ppermute(x, 'dp', [(0, 1), (1, 0)])  13.8 us
    dot_general x1, matrix products, body_heads(): lax.dot_general(out_both, grad_both, (((1,), (0,)), ((), ())), preferred_...  13 us
    dot_general x1, matrix products, body_heads(): lax.dot_general(dense_grad, out_weight, (((1,), (1,)), ((), ())), preferr...  9 us
    dot_general x1, matrix products, contract_rows(): lax.dot_general(left, right, (((0,), (0,)), ((), ())), preferred_element_...  7.48 us
    ppermute x6, starting transfers between devices, swap_dp(): return lax.ppermute(x, 'dp', [(0, 1), (1, 0)])  6.07 us
  transfers between devices with their start and end apart: 24, of which 6 were waited for; matrix products, arithmetic and copies ran while one was open for 54% of the time, Pallas kernels for 0%

profile of v16, /device:TPU:0, one launch (start us, length us, event | category | flops | bytes accessed | tf_op | source)
XLA Modules:
  0.0 202.2 jit_solution(4300314137888745233)
XLA Ops:
  0.6 2.4 %collective-permute-start.5 = (bf16[128,3072]{1,0:T(8,128)(2,1)}, bf16[128,3072]{1,0:T(8,128)(2,1)S(1)}, u32[]{:S(2)}, u32[]{:S(2)}) collective-permute-start(bf16[128,3072]{1,0:T(8,128)(2,1)} %bitcast.130), channel_id=1, source_target_pairs={{0,12},{4,0},{8,4},{12,8},{1,13},{5,1},{9,5},{13,9},{2,14},{6,2},{... | collective-permute-start | bytes 2359304 | tf_op jit(solution)/shard_map/ppermute | solution.py:115
  3.9 1.5 collective-permute-start.6
  7.3 2.0 constant_dynamic-slice_fusion.14
  9.4 1.8 constant_dynamic-slice_fusion.16
  12.4 1.6 reshape.161
  14.0 2.0 pad_maximum_fusion
  16.0 1.6 collective-permute-start
  21.2 2.6 %collective-permute-start.1 = (bf16[194048]{0:T(1024)(128)(2,1)}, bf16[194048]{0:T(1024)(128)(2,1)S(1)}, u32[]{:S(2)}, u32[]{:S(2)}) collective-permute-start(bf16[194048]{0:T(1024)(128)(2,1)} %get-tuple-element.46), channel_id=1, source_target_pairs={{0,2},{1,3},{2,0},{3,1},{4,6},{5,7},{6,4},{7,5},{8,10},{9,11},{10,... | collective-permute-start | bytes 1164296 | tf_op jit(solution)/shard_map/ppermute | solution.py:115
  23.8 15.1 %collective-permute-done.4 = bf16[128,3072]{1,0:T(8,128)(2,1)S(1)} collective-permute-done((bf16[128,3072]{1,0:T(8,128)(2,1)}, bf16[128,3072]{1,0:T(8,128)(2,1)S(1)}, u32[]{:S(2)}, u32[]{:S(2)}) %collective-permute-start.4) | collective-permute-done | bytes 786464 | tf_op jit(solution)/shard_map/ppermute | solution.py:115
  38.9 3.7 %collective-permute-start.2 = (bf16[194048]{0:T(1024)(128)(2,1)}, bf16[194048]{0:T(1024)(128)(2,1)S(1)}, u32[]{:S(2)}, u32[]{:S(2)}) collective-permute-start(bf16[194048]{0:T(1024)(128)(2,1)} %get-tuple-element.45), channel_id=1, source_target_pairs={{0,3},{1,0},{2,1},{3,2},{4,7},{5,4},{6,5},{7,6},{8,11},{9,8},{10,9... | collective-permute-start | bytes 1164296 | tf_op jit(solution)/shard_map/ppermute | solution.py:115
  42.6 9.0 %fusion.2 = f32[512,1536]{1,0:T(8,128)S(1)} fusion(bf16[1536,3072]{1,0:T(8,128)(2,1)} %param.10, bf16[128,3072]{1,0:T(8,128)(2,1)S(1)} %collective-permute-done.5, bf16[128,3072]{1,0:T(8,128)(2,1)S(1)} %collective-permute-done.4, bf16[128,3072]{1,0:T(8,128)(2,1)} %collective-permute-done.3, bf16[128,3072]{1,0:T(8,128)(2,1)S(1)} %bitcast.133), kind=kOutput, calls=%fused_computation.2 | convolution fusion | flops 4844421120 | bytes 15728640 | tf_op jit(solution)/shard_map/dot_general | solution.py:219
  51.8 1.5 collective-permute-start.21
  56.3 3.1 %collective-permute-start.9 = (bf16[512,384]{1,0:T(8,128)(2,1)}, bf16[512,384]{1,0:T(8,128)(2,1)}, u32[]{:S(2)}, u32[]{:S(2)}) collective-permute-start(bf16[512,384]{1,0:T(8,128)(2,1)} %get-tuple-element.22), channel_id=1, source_target_pairs={{0,1},{1,2},{2,3},{3,0},{4,5},{5,6},{6,7},{7,4},{8,9},{9,10},{10,1... | collective-permute-start | bytes 1179656 | tf_op jit(solution)/shard_map/ppermute | solution.py:115
  59.4 1.6 collective-permute-start.8
  67.5 1.4 dynamic-slice_bitcast_fusion
  71.4 1.6 multiply_reduce_fusion
  73.6 2.1 %constant_dynamic-update-slice_fusion.12 = bf16[1024,3072]{1,0:T(8,128)(2,1)} fusion(bf16[1024,3072]{1,0:T(8,128)(2,1)} %constant_dynamic-update-slice_fusion.13, bf16[128,3072]{1,0:T(8,128)(2,1)} %collective-permute-done.3), kind=kLoop, calls=%fused_computation.82 | loop fusion | bytes 1572864
  77.5 2.1 %constant_dynamic-update-slice_fusion.9 = bf16[1024,3072]{1,0:T(8,128)(2,1)} fusion(bf16[1024,3072]{1,0:T(8,128)(2,1)} %constant_dynamic-update-slice_fusion.10, bf16[1,128,3072]{2,1,0:T(8,128)(2,1)} %collective-permute-done.6), kind=kLoop, calls=%fused_computation.79 | loop fusion | bytes 1572864
  79.6 1.8 stack_reshape.21
  81.3 1.8 stack_reshape.22
  83.1 1.8 stack_reshape.23
  84.9 1.5 constant_dynamic-update-slice_fusion.20
  86.4 1.5 constant_dynamic-update-slice_fusion.19
  88.0 1.5 constant_dynamic-update-slice_fusion.18
  89.5 1.5 constant_dynamic-update-slice_fusion.17
  91.1 1.5 constant_dynamic-update-slice_fusion.16
  92.6 1.5 constant_dynamic-update-slice_fusion.15
  94.2 1.5 constant_dynamic-update-slice_fusion.14
  95.7 1.8 constant_dynamic-slice_fusion
  97.5 1.9 copy.36
  99.4 1.9 squeeze.49
  101.3 1.7 exponential_convert_fusion
  103.9 1.7 add_convert_fusion
  105.8 1.7 fusion.37
  110.3 1.8 collective-permute-start.11
  115.3 1.4 constant_dynamic-slice_fusion.2
  116.7 1.3 constant_dynamic-slice_fusion.3
  121.5 2.1 %constant_dynamic-update-slice_fusion.8 = bf16[1024,3072]{1,0:T(8,128)(2,1)} fusion(bf16[1024,3072]{1,0:T(8,128)(2,1)} %constant_dynamic-update-slice_fusion.9, bf16[128,3072]{1,0:T(8,128)(2,1)} %collective-permute-done.20), kind=kLoop, calls=%fused_computation.78 | loop fusion | bytes 1572864
  124.5 2.1 %constant_dynamic-update-slice_fusion.7 = bf16[1024,3072]{1,0:T(8,128)(2,1)} fusion(bf16[1024,3072]{1,0:T(8,128)(2,1)} %constant_dynamic-update-slice_fusion.8, bf16[128,3072]{1,0:T(8,128)(2,1)} %collective-permute-done.21), kind=kLoop, calls=%fused_computation.77 | loop fusion | bytes 1572864
  127.7 19.6 %collective-permute-done.13 = bf16[512,384]{0,1:T(8,128)(2,1)} collective-permute-done((bf16[512,384]{0,1:T(8,128)(2,1)S(1)}, bf16[512,384]{0,1:T(8,128)(2,1)}, u32[]{:S(2)}, u32[]{:S(2)}) %collective-permute-start.13) | collective-permute-done | bytes 393248 | tf_op jit(solution)/shard_map/ppermute | solution.py:115
  147.8 1.5 collective-permute-start.14
  149.8 2.1 %constant_dynamic-update-slice_fusion.6 = bf16[1024,3072]{1,0:T(8,128)(2,1)} fusion(bf16[1024,3072]{1,0:T(8,128)(2,1)} %constant_dynamic-update-slice_fusion.7, bf16[128,3072]{1,0:T(8,128)(2,1)} %collective-permute-done.22), kind=kLoop, calls=%fused_computation.76 | loop fusion | bytes 1572864 | tf_op jit(solution)/shard_map/concatenate | solution.py:272
  151.9 7.5 %fusion.17 = f32[364,3072]{1,0:T(8,128)} fusion(bf16[1024,3072]{1,0:T(8,128)(2,1)} %constant_dynamic-update-slice_fusion.6, bf16[512,364]{1,0:T(8,128)(2,1)S(1)} %collective-permute-done.23, bf16[512,364]{1,0:T(8,128)(2,1)S(1)} %bitcast.129), kind=kOutput, calls=%fused_computation.39 | convolution fusion | flops 2291580928 | bytes 11509760 | tf_op jit(solution)/shard_map/dot_general | solution.py:11
  159.6 8.2 %collective-permute-done.14 = bf16[512,384]{0,1:T(8,128)(2,1)S(1)} collective-permute-done((bf16[512,384]{0,1:T(8,128)(2,1)}, bf16[512,384]{0,1:T(8,128)(2,1)S(1)}, u32[]{:S(2)}, u32[]{:S(2)}) %collective-permute-start.14) | collective-permute-done | bytes 393248 | tf_op jit(solution)/shard_map/ppermute | solution.py:17
  168.9 5.6 %collective-permute-done.16 = bf16[512,384]{0,1:T(8,128)(2,1)S(1)} collective-permute-done((bf16[512,384]{0,1:T(8,128)(2,1)S(1)}, bf16[512,384]{0,1:T(8,128)(2,1)S(1)}, u32[]{:S(2)}, u32[]{:S(2)}) %collective-permute-start.16) | collective-permute-done | bytes 393248 | tf_op jit(solution)/shard_map/ppermute | solution.py:17
  177.9 13.0 %fusion = f32[4,384,3072]{2,1,0:T(8,128)} fusion(bf16[4,1024,384]{1,2,0:T(8,128)(2,1)S(1)} %constant_dynamic-slice_fusion.1, bf16[1024,3072]{1,0:T(8,128)(2,1)S(1)} %bitcast.118), kind=kOutput, calls=%fused_computation | convolution fusion | flops 9663676416 | bytes 28311552 | tf_op jit(solution)/shard_map/dot_general | solution.py:273
  191.8 8.8 %collective-permute-done.18 = bf16[3,128,384]{2,1,0:T(8,128)(2,1)S(1)} collective-permute-done((bf16[3,128,384]{2,1,0:T(8,128)(2,1)S(1)}, bf16[3,128,384]{2,1,0:T(8,128)(2,1)S(1)}, u32[]{:S(2)}, u32[]{:S(2)}) %collective-permute-start.18) | collective-permute-done | bytes 294944 | tf_op jit(solution)/shard_map/ppermute | solution.py:115
  200.7 1.5 slice_bitcast_fusion
  (139 shorter events, 41.3 us)
Async XLA Ops:
  0.6 20.6 %collective-permute-start.5 = (bf16[128,3072]{1,0:T(8,128)(2,1)}, bf16[128,3072]{1,0:T(8,128)(2,1)S(1)}, u32[]{:S(2)}, u32[]{:S(2)}) collective-permute-start(bf16[128,3072]{1,0:T(8,128)(2,1)} %bitcast.130), channel_id=1, source_target_pairs={{0,12},{4,0},{8,4},{12,8},{1,13},{5,1},{9,5},{13,9},{2,14},{6,2},{... | collective-permute-start | bytes 2359304 | tf_op jit(solution)/shard_map/ppermute | solution.py:115
  3.1 35.8 %collective-permute-start.4 = (bf16[128,3072]{1,0:T(8,128)(2,1)}, bf16[128,3072]{1,0:T(8,128)(2,1)S(1)}, u32[]{:S(2)}, u32[]{:S(2)}) collective-permute-start(bf16[128,3072]{1,0:T(8,128)(2,1)} %bitcast.131), channel_id=1, source_target_pairs={{0,8},{4,12},{8,0},{12,4},{1,9},{5,13},{9,1},{13,5},{2,10},{6,14},... | collective-permute-start | bytes 2359304 | tf_op jit(solution)/shard_map/ppermute | solution.py:115
  3.7 38.9 %collective-permute-start.3 = (bf16[128,3072]{1,0:T(8,128)(2,1)}, bf16[128,3072]{1,0:T(8,128)(2,1)}, u32[]{:S(2)}, u32[]{:S(2)}) collective-permute-start(bf16[128,3072]{1,0:T(8,128)(2,1)} %bitcast.132), channel_id=1, source_target_pairs={{0,4},{4,8},{8,12},{12,0},{1,5},{5,9},{9,13},{13,1},{2,6},{6,10},{... | collective-permute-start | bytes 2359304 | tf_op jit(solution)/shard_map/ppermute | solution.py:115
  3.9 47.8 %collective-permute-start.6 = (bf16[1,128,3072]{2,1,0:T(8,128)(2,1)}, bf16[1,128,3072]{2,1,0:T(8,128)(2,1)}, u32[]{:S(2)}, u32[]{:S(2)}) collective-permute-start(bf16[1,128,3072]{2,1,0:T(8,128)(2,1)} %param.11), channel_id=1, source_target_pairs={{0,16},{16,0},{1,17},{17,1},{2,18},{18,2},{3,19},{19,3},{4,20},{20... | collective-permute-start | bytes 2359304 | tf_op jit(solution)/shard_map/ppermute | solution.py:17
  6.4 11.9 %copy-start.6 = (bf16[1,128,364]{2,1,0:T(8,128)(2,1)}, bf16[1,128,364]{2,1,0:T(8,128)(2,1)S(1)}, u32[]{:S(2)}) copy-start(bf16[1,128,364]{2,1,0:T(8,128)(2,1)S(1)} %copy.30) | copy-start | bytes 279556
  9.3 9.7 %copy-start.9 = (bf16[1,128,3072]{2,1,0:T(8,128)(2,1)S(1)}, bf16[1,128,3072]{2,1,0:T(8,128)(2,1)}, u32[]{:S(2)}) copy-start(bf16[1,128,3072]{2,1,0:T(8,128)(2,1)} %param.11) | copy-start | bytes 2359300
  16.0 35.7 %collective-permute-start = (bf16[194048]{0:T(1024)(128)(2,1)}, bf16[194048]{0:T(1024)(128)(2,1)S(1)}, u32[]{:S(2)}, u32[]{:S(2)}) collective-permute-start(bf16[194048]{0:T(1024)(128)(2,1)} %get-tuple-element.47), channel_id=1, source_target_pairs={{0,1},{1,2},{2,3},{3,0},{4,5},{5,6},{6,7},{7,4},{8,9},{9,10},{10,1... | collective-permute-start | bytes 1164296 | tf_op jit(solution)/shard_map/ppermute | solution.py:115
  21.2 30.4 %copy-start.10 = (bf16[128,3072]{1,0:T(8,128)(2,1)}, bf16[128,3072]{1,0:T(8,128)(2,1)S(1)}, u32[]{:S(2)}) copy-start(bf16[128,3072]{1,0:T(8,128)(2,1)S(1)} %collective-permute-done.5) | copy-start | bytes 2359300
  21.2 30.5 %collective-permute-start.1 = (bf16[194048]{0:T(1024)(128)(2,1)}, bf16[194048]{0:T(1024)(128)(2,1)S(1)}, u32[]{:S(2)}, u32[]{:S(2)}) collective-permute-start(bf16[194048]{0:T(1024)(128)(2,1)} %get-tuple-element.46), channel_id=1, source_target_pairs={{0,2},{1,3},{2,0},{3,1},{4,6},{5,7},{6,4},{7,5},{8,10},{9,11},{10,... | collective-permute-start | bytes 1164296 | tf_op jit(solution)/shard_map/ppermute | solution.py:115
  38.9 12.7 %copy-start.12 = (bf16[128,3072]{1,0:T(8,128)(2,1)}, bf16[128,3072]{1,0:T(8,128)(2,1)S(1)}, u32[]{:S(2)}) copy-start(bf16[128,3072]{1,0:T(8,128)(2,1)S(1)} %collective-permute-done.4) | copy-start | bytes 2359300
  38.9 12.8 %collective-permute-start.2 = (bf16[194048]{0:T(1024)(128)(2,1)}, bf16[194048]{0:T(1024)(128)(2,1)S(1)}, u32[]{:S(2)}, u32[]{:S(2)}) collective-permute-start(bf16[194048]{0:T(1024)(128)(2,1)} %get-tuple-element.45), channel_id=1, source_target_pairs={{0,3},{1,0},{2,1},{3,2},{4,7},{5,4},{6,5},{7,6},{8,11},{9,8},{10,9... | collective-permute-start | bytes 1164296 | tf_op jit(solution)/shard_map/ppermute | solution.py:115
  51.6 9.4 %copy-start.8 = (f32[512,1536]{1,0:T(8,128)}, f32[512,1536]{1,0:T(8,128)S(1)}, u32[]{:S(2)}) copy-start(f32[512,1536]{1,0:T(8,128)S(1)} %fusion.2) | copy-start | bytes 9437188
  51.7 69.3 %collective-permute-start.20 = (bf16[128,3072]{1,0:T(8,128)(2,1)}, bf16[128,3072]{1,0:T(8,128)(2,1)}, u32[]{:S(2)}, u32[]{:S(2)}) collective-permute-start(bf16[128,3072]{1,0:T(8,128)(2,1)} %bitcast.27), channel_id=1, source_target_pairs={{0,4},{4,8},{8,12},{12,0},{1,5},{5,9},{9,13},{13,1},{2,6},{6,10},{... | collective-permute-start | bytes 2359304 | tf_op jit(solution)/shard_map/ppermute | solution.py:115
  51.8 71.8 %collective-permute-start.21 = (bf16[128,3072]{1,0:T(8,128)(2,1)}, bf16[128,3072]{1,0:T(8,128)(2,1)}, u32[]{:S(2)}, u32[]{:S(2)}) collective-permute-start(bf16[128,3072]{1,0:T(8,128)(2,1)} %bitcast.27), channel_id=1, source_target_pairs={{0,8},{4,12},{8,0},{12,4},{1,9},{5,13},{9,1},{13,5},{2,10},{6,14},... | collective-permute-start | bytes 2359304 | tf_op jit(solution)/shard_map/ppermute | solution.py:115
  56.3 46.8 %collective-permute-start.9 = (bf16[512,384]{1,0:T(8,128)(2,1)}, bf16[512,384]{1,0:T(8,128)(2,1)}, u32[]{:S(2)}, u32[]{:S(2)}) collective-permute-start(bf16[512,384]{1,0:T(8,128)(2,1)} %get-tuple-element.22), channel_id=1, source_target_pairs={{0,1},{1,2},{2,3},{3,0},{4,5},{5,6},{6,7},{7,4},{8,9},{9,10},{10,1... | collective-permute-start | bytes 1179656 | tf_op jit(solution)/shard_map/ppermute | solution.py:115
  59.4 44.5 %collective-permute-start.8 = (bf16[512,384]{1,0:T(8,128)(2,1)}, bf16[512,384]{1,0:T(8,128)(2,1)}, u32[]{:S(2)}, u32[]{:S(2)}) collective-permute-start(bf16[512,384]{1,0:T(8,128)(2,1)} %get-tuple-element.23), channel_id=1, source_target_pairs={{0,2},{1,3},{2,0},{3,1},{4,6},{5,7},{6,4},{7,5},{8,10},{9,11},{10,... | collective-permute-start | bytes 1179656 | tf_op jit(solution)/shard_map/ppermute | solution.py:115
  61.1 42.8 %collective-permute-start.7 = (bf16[512,384]{1,0:T(8,128)(2,1)}, bf16[512,384]{1,0:T(8,128)(2,1)}, u32[]{:S(2)}, u32[]{:S(2)}) collective-permute-start(bf16[512,384]{1,0:T(8,128)(2,1)} %get-tuple-element.21), channel_id=1, source_target_pairs={{0,3},{1,0},{2,1},{3,2},{4,7},{5,4},{6,5},{7,6},{8,11},{9,8},{10,9... | collective-permute-start | bytes 1179656 | tf_op jit(solution)/shard_map/ppermute | solution.py:115
  73.0 2.6 %copy-start.13 = (bf16[128,3072]{1,0:T(8,128)(2,1)S(1)}, bf16[128,3072]{1,0:T(8,128)(2,1)}, u32[]{:S(2)}) copy-start(bf16[128,3072]{1,0:T(8,128)(2,1)} %copy-done.12) | copy-start | bytes 2359300
  73.0 3.6 %copy-start.11 = (bf16[128,3072]{1,0:T(8,128)(2,1)S(1)}, bf16[128,3072]{1,0:T(8,128)(2,1)}, u32[]{:S(2)}) copy-start(bf16[128,3072]{1,0:T(8,128)(2,1)} %copy-done.10) | copy-start | bytes 2359300
  103.1 2.7 %copy-start = (bf16[3,512,512]{1,2,0:T(8,128)(2,1)S(1)}, bf16[3,512,512]{1,2,0:T(8,128)(2,1)}, u32[]{:S(2)}) copy-start(bf16[3,512,512]{1,2,0:T(8,128)(2,1)} %exponential_convert_fusion) | copy-start | bytes 4718596
  103.1 4.4 %copy-start.2 = (bf16[512,3,128]{0,2,1:T(8,128)(2,1)S(1)}, bf16[512,3,128]{0,2,1:T(8,128)(2,1)}, u32[]{:S(2)}) copy-start(bf16[512,3,128]{0,2,1:T(8,128)(2,1)} %squeeze.49) | copy-start | bytes 1179652
  103.1 46.2 %collective-permute-start.22 = (bf16[128,3072]{1,0:T(8,128)(2,1)}, bf16[128,3072]{1,0:T(8,128)(2,1)}, u32[]{:S(2)}, u32[]{:S(2)}) collective-permute-start(bf16[128,3072]{1,0:T(8,128)(2,1)} %bitcast.27), channel_id=1, source_target_pairs={{0,12},{4,0},{8,4},{12,8},{1,13},{5,1},{9,5},{13,9},{2,14},{6,2},{... | collective-permute-start | bytes 2359304 | tf_op jit(solution)/shard_map/ppermute | solution.py:115
  107.8 1.3 copy-start.1
  108.5 4.3 %copy-start.3 = (f32[512,3,128]{0,2,1:T(8,128)S(1)}, f32[512,3,128]{0,2,1:T(8,128)}, u32[]{:S(2)}) copy-start(f32[512,3,128]{0,2,1:T(8,128)} %get-tuple-element.57) | copy-start | bytes 2359300
  110.3 16.3 %collective-permute-start.11 = (bf16[512,384]{0,1:T(8,128)(2,1)S(1)}, bf16[512,384]{0,1:T(8,128)(2,1)S(1)}, u32[]{:S(2)}, u32[]{:S(2)}) collective-permute-start(bf16[512,384]{0,1:T(8,128)(2,1)S(1)} %bitcast.122), channel_id=1, source_target_pairs={{0,3},{1,0},{2,1},{3,2},{4,7},{5,4},{6,5},{7,6},{8,11},{9,8},{10,9... | collective-permute-start | bytes 1179656 | tf_op jit(solution)/shard_map/ppermute | solution.py:115
  112.0 35.2 %collective-permute-start.13 = (bf16[512,384]{0,1:T(8,128)(2,1)S(1)}, bf16[512,384]{0,1:T(8,128)(2,1)}, u32[]{:S(2)}, u32[]{:S(2)}) collective-permute-start(bf16[512,384]{0,1:T(8,128)(2,1)S(1)} %bitcast.123), channel_id=1, source_target_pairs={{0,2},{1,3},{2,0},{3,1},{4,6},{5,7},{6,4},{7,5},{8,10},{9,11},{10,... | collective-permute-start | bytes 1179656 | tf_op jit(solution)/shard_map/ppermute | solution.py:115
  113.9 4.7 %copy-start.5 = (bf16[512,3,128]{0,2,1:T(8,128)(2,1)S(1)}, bf16[512,3,128]{0,2,1:T(8,128)(2,1)}, u32[]{:S(2)}) copy-start(bf16[512,3,128]{0,2,1:T(8,128)(2,1)} %get-tuple-element.52) | copy-start | bytes 1179652
  115.3 4.1 %copy-start.4 = (bf16[512,3,128]{0,2,1:T(8,128)(2,1)S(1)}, bf16[512,3,128]{0,2,1:T(8,128)(2,1)}, u32[]{:S(2)}) copy-start(bf16[512,3,128]{0,2,1:T(8,128)(2,1)} %get-tuple-element.56) | copy-start | bytes 1179652
  120.6 3.0 %copy-start.7 = (bf16[4,128,364]{2,1,0:T(8,128)(2,1)S(1)}, bf16[4,128,364]{2,1,0:T(8,128)(2,1)}, u32[]{:S(2)}) copy-start(bf16[4,128,364]{2,1,0:T(8,128)(2,1)} %constant_dynamic-slice_fusion) | copy-start | bytes 1118212
  121.0 26.8 %collective-permute-start.15 = (bf16[512,384]{0,1:T(8,128)(2,1)S(1)}, bf16[512,384]{0,1:T(8,128)(2,1)S(1)}, u32[]{:S(2)}, u32[]{:S(2)}) collective-permute-start(bf16[512,384]{0,1:T(8,128)(2,1)S(1)} %bitcast.124), channel_id=1, source_target_pairs={{0,1},{1,2},{2,3},{3,0},{4,5},{5,6},{6,7},{7,4},{8,9},{9,10},{10,1... | collective-permute-start | bytes 1179656 | tf_op jit(solution)/shard_map/ppermute | solution.py:115
  123.6 28.3 %collective-permute-start.23 = (bf16[512,364]{1,0:T(8,128)(2,1)S(1)}, bf16[512,364]{1,0:T(8,128)(2,1)S(1)}, u32[]{:S(2)}, u32[]{:S(2)}) collective-permute-start(bf16[512,364]{1,0:T(8,128)(2,1)S(1)} %bitcast.128), channel_id=1, source_target_pairs={{0,16},{16,0},{1,17},{17,1},{2,18},{18,2},{3,19},{19,3},{4,20},{20... | collective-permute-start | bytes 1118216 | tf_op jit(solution)/shard_map/ppermute | solution.py:17
  126.6 32.8 %collective-permute-start.10 = (bf16[512,384]{0,1:T(8,128)(2,1)S(1)}, bf16[512,384]{0,1:T(8,128)(2,1)S(1)}, u32[]{:S(2)}, u32[]{:S(2)}) collective-permute-start(bf16[512,384]{0,1:T(8,128)(2,1)S(1)} %bitcast.125), channel_id=1, source_target_pairs={{0,16},{16,0},{1,17},{17,1},{2,18},{18,2},{3,19},{19,3},{4,20},{20... | collective-permute-start | bytes 1179656 | tf_op jit(solution)/shard_map/ppermute | solution.py:17
  147.3 12.2 %collective-permute-start.12 = (bf16[512,384]{0,1:T(8,128)(2,1)S(1)}, bf16[512,384]{0,1:T(8,128)(2,1)S(1)}, u32[]{:S(2)}, u32[]{:S(2)}) collective-permute-start(bf16[512,384]{0,1:T(8,128)(2,1)S(1)} %collective-permute-done.11), channel_id=1, source_target_pairs={{0,16},{16,0},{1,17},{17,1},{2,18},{18,2},{3,19},{19,3},{4,20},{20... | collective-permute-start | bytes 1179656 | tf_op jit(solution)/shard_map/ppermute | solution.py:17
  147.8 20.0 %collective-permute-start.14 = (bf16[512,384]{0,1:T(8,128)(2,1)}, bf16[512,384]{0,1:T(8,128)(2,1)S(1)}, u32[]{:S(2)}, u32[]{:S(2)}) collective-permute-start(bf16[512,384]{0,1:T(8,128)(2,1)} %collective-permute-done.13), channel_id=1, source_target_pairs={{0,16},{16,0},{1,17},{17,1},{2,18},{18,2},{3,19},{19,3},{4,20},{20... | collective-permute-start | bytes 1179656 | tf_op jit(solution)/shard_map/ppermute | solution.py:17
  149.3 25.1 %collective-permute-start.16 = (bf16[512,384]{0,1:T(8,128)(2,1)S(1)}, bf16[512,384]{0,1:T(8,128)(2,1)S(1)}, u32[]{:S(2)}, u32[]{:S(2)}) collective-permute-start(bf16[512,384]{0,1:T(8,128)(2,1)S(1)} %collective-permute-done.15), channel_id=1, source_target_pairs={{0,16},{16,0},{1,17},{17,1},{2,18},{18,2},{3,19},{19,3},{4,20},{20... | collective-permute-start | bytes 1179656 | tf_op jit(solution)/shard_map/ppermute | solution.py:17
  174.7 2.3 %slice-start = ((s8[6291456]{0:T(1024)(128)(4,1)}), s8[4194304]{0:T(1024)(128)(4,1)S(1)}, s32[]{:S(2)}) async-start(s8[6291456]{0:T(1024)(128)(4,1)} %bitcast.117), calls=%async_computation | async-start | bytes 8388608
  176.1 1.8 slice-start.1
  176.6 15.2 %collective-permute-start.17 = (bf16[3,128,384]{2,1,0:T(8,128)(2,1)S(1)}, bf16[3,128,384]{2,1,0:T(8,128)(2,1)S(1)}, u32[]{:S(2)}, u32[]{:S(2)}) collective-permute-start(bf16[3,128,384]{2,1,0:T(8,128)(2,1)S(1)} %get-tuple-element.29), channel_id=1, source_target_pairs={{0,3},{1,0},{2,1},{3,2},{4,7},{5,4},{6,5},{7,6},{8,11},{9,8},{10,9... | collective-permute-start | bytes 884744 | tf_op jit(solution)/shard_map/ppermute | solution.py:115
  176.6 23.9 %collective-permute-start.18 = (bf16[3,128,384]{2,1,0:T(8,128)(2,1)S(1)}, bf16[3,128,384]{2,1,0:T(8,128)(2,1)S(1)}, u32[]{:S(2)}, u32[]{:S(2)}) collective-permute-start(bf16[3,128,384]{2,1,0:T(8,128)(2,1)S(1)} %get-tuple-element.28), channel_id=1, source_target_pairs={{0,2},{1,3},{2,0},{3,1},{4,6},{5,7},{6,4},{7,5},{8,10},{9,11},{10,... | collective-permute-start | bytes 884744 | tf_op jit(solution)/shard_map/ppermute | solution.py:115
  191.0 9.7 %collective-permute-start.19 = (bf16[3,128,384]{2,1,0:T(8,128)(2,1)S(1)}, bf16[3,128,384]{2,1,0:T(8,128)(2,1)S(1)}, u32[]{:S(2)}, u32[]{:S(2)}) collective-permute-start(bf16[3,128,384]{2,1,0:T(8,128)(2,1)S(1)} %get-tuple-element.27), channel_id=1, source_target_pairs={{0,1},{1,2},{2,3},{3,0},{4,5},{5,6},{6,7},{7,4},{8,9},{9,10},{10,1... | collective-permute-start | bytes 884744 | tf_op jit(solution)/shard_map/ppermute | solution.py:115

commit v17 on v15

--- a/solution.py
+++ b/solution.py
@@ -272,15 +272,15 @@
         jnp.stack([jnp.concatenate(p, 0) for p in out_pieces], 0), -me
     )
     grad_both = jnp.concatenate([dense_grad] + other_blocks, 0)
-    out_weight_grad = lax.dot_general(
-        out_both, grad_both, (((1,), (0,)), ((), ())), preferred_element_type=jnp.float32
-    ).reshape(width_all, -1)
     embed_weight_grad = contract_rows(jnp.concatenate([every_patch, other_patch], 0), grad_both)
     grad_list = [g.reshape(n, tokens, width) for g in (query_grad, key_grad, value_grad)]
     sendable = roll_blocks(
         jnp.stack([g.astype(jnp.bfloat16) for g in grad_list], 1), rank - me
     )
     sendable, out_both = lax.optimization_barrier((sendable, out_both))
+    out_weight_grad = lax.dot_general(
+        out_both, grad_both, (((1,), (0,)), ((), ())), preferred_element_type=jnp.float32
+    ).reshape(width_all, -1)
     mine = jnp.stack(
         [lax.dynamic_index_in_dim(g, (rank - me) % n, 0, keepdims=False) for g in grad_list], 0
     )

time: 203 us -> 203 us (level)
  no operation moved by 1% of the time
where the time goes in v17:
time: 203 us; the launch traced here: 202 us
  waiting for transfers between devices  72.2 us (36%)
  local copies, waits for them, and re-layouts  43.6 us (21%)
  starting transfers between devices  40.1 us (20%)
  matrix products  35.8 us (18%)
  other arithmetic  8.74 us (4%)
    ppermute x18, waiting for transfers between devices, shifted(): return lax.ppermute(x, axis, [(j, (j + step) % n) for j in range(n)])  58.1 us
    ppermute x18, starting transfers between devices, shifted(): return lax.ppermute(x, axis, [(j, (j + step) % n) for j in range(n)])  33.1 us
    unnamed x61, local copies, waits for them, and re-layouts  14.2 us
    ppermute x6, waiting for transfers between devices, swap_dp(): return lax.ppermute(x, 'dp', [(0, 1), (1, 0)])  14.1 us
    dot_general x1, matrix products, body_heads(): lax.dot_general(out_both, grad_both, (((1,), (0,)), ((), ())), preferred_...  13 us
    dot_general x1, matrix products, body_heads(): lax.dot_general(dense_grad, out_weight, (((1,), (1,)), ((), ())), preferr...  9.23 us
    dot_general x1, matrix products, contract_rows(): lax.dot_general(left, right, (((0,), (0,)), ((), ())), preferred_element_...  7.48 us
    ppermute x6, starting transfers between devices, swap_dp(): return lax.ppermute(x, 'dp', [(0, 1), (1, 0)])  7.08 us
  transfers between devices with their start and end apart: 24, of which 11 were waited for; matrix products, arithmetic and copies ran while one was open for 39% of the time, Pallas kernels for 0%

profile of v17, /device:TPU:0, one launch (start us, length us, event | category | flops | bytes accessed | tf_op | source)
XLA Modules:
  0.0 202.0 jit_solution(18390887335590088263)
XLA Ops:
  2.0 1.2 constant_dynamic-slice_fusion.7
  3.2 1.3 constant_dynamic-slice_fusion.5
  5.9 3.0 %collective-permute-start = (bf16[194048]{0:T(1024)(128)(2,1)S(1)}, bf16[194048]{0:T(1024)(128)(2,1)S(1)}, u32[]{:S(2)}, u32[]{:S(2)}) collective-permute-start(bf16[194048]{0:T(1024)(128)(2,1)S(1)} %get-tuple-element.59), channel_id=1, source_target_pairs={{0,1},{1,2},{2,3},{3,0},{4,5},{5,6},{6,7},{7,4},{8,9},{9,10},{10,1... | collective-permute-start | bytes 1164296 | tf_op jit(solution)/shard_map/ppermute | solution.py:115
  10.6 2.6 %collective-permute-start.1 = (bf16[194048]{0:T(1024)(128)(2,1)}, bf16[194048]{0:T(1024)(128)(2,1)}, u32[]{:S(2)}, u32[]{:S(2)}) collective-permute-start(bf16[194048]{0:T(1024)(128)(2,1)} %get-tuple-element.58), channel_id=1, source_target_pairs={{0,2},{1,3},{2,0},{3,1},{4,6},{5,7},{6,4},{7,5},{8,10},{9,11},{10,... | collective-permute-start | bytes 1164296 | tf_op jit(solution)/shard_map/ppermute | solution.py:115
  13.2 7.7 %collective-permute-done = bf16[194048]{0:T(1024)(128)(2,1)S(1)} collective-permute-done((bf16[194048]{0:T(1024)(128)(2,1)S(1)}, bf16[194048]{0:T(1024)(128)(2,1)S(1)}, u32[]{:S(2)}, u32[]{:S(2)}) %collective-permute-start) | collective-permute-done | bytes 388128 | tf_op jit(solution)/shard_map/ppermute | solution.py:115
  20.9 1.2 collective-permute-start.2
  24.1 12.6 %collective-permute-done.1 = bf16[194048]{0:T(1024)(128)(2,1)} collective-permute-done((bf16[194048]{0:T(1024)(128)(2,1)}, bf16[194048]{0:T(1024)(128)(2,1)}, u32[]{:S(2)}, u32[]{:S(2)}) %collective-permute-start.1) | collective-permute-done | bytes 388128 | tf_op jit(solution)/shard_map/ppermute | solution.py:115
  36.7 1.5 collective-permute-start.6
  41.2 1.2 collective-permute-done.2
  45.7 9.2 %fusion.2 = f32[512,1536]{1,0:T(8,128)S(1)} fusion(bf16[1536,3072]{1,0:T(8,128)(2,1)} %param.10, bf16[128,3072]{1,0:T(8,128)(2,1)S(1)} %collective-permute-done.5, bf16[128,3072]{1,0:T(8,128)(2,1)} %collective-permute-done.4, bf16[128,3072]{1,0:T(8,128)(2,1)} %collective-permute-done.3, bf16[128,3072]{1,0:T(8,128)(2,1)S(1)} %bitcast.154), kind=kOutput, calls=%fused_computation.2 | convolution fusion | flops 4844421120 | bytes 15728640 | tf_op jit(solution)/shard_map/dot_general | solution.py:222
  55.0 1.4 collective-permute-done.6
  56.4 1.5 collective-permute-start.21
  57.9 1.1 dynamic-slice_convert_fusion.2
  59.0 6.0 %collective-permute-start.9 = (bf16[512,384]{1,0:T(8,128)(2,1)}, bf16[512,384]{1,0:T(8,128)(2,1)}, u32[]{:S(2)}, u32[]{:S(2)}) collective-permute-start(bf16[512,384]{1,0:T(8,128)(2,1)} %get-tuple-element.34), channel_id=1, source_target_pairs={{0,1},{1,2},{2,3},{3,0},{4,5},{5,6},{6,7},{7,4},{8,9},{9,10},{10,1... | collective-permute-start | bytes 1179656 | tf_op jit(solution)/shard_map/ppermute | solution.py:115
  65.0 3.4 %collective-permute-start.8 = (bf16[512,384]{1,0:T(8,128)(2,1)}, bf16[512,384]{1,0:T(8,128)(2,1)}, u32[]{:S(2)}, u32[]{:S(2)}) collective-permute-start(bf16[512,384]{1,0:T(8,128)(2,1)} %get-tuple-element.35), channel_id=1, source_target_pairs={{0,2},{1,3},{2,0},{3,1},{4,6},{5,7},{6,4},{7,5},{8,10},{9,11},{10,... | collective-permute-start | bytes 1179656 | tf_op jit(solution)/shard_map/ppermute | solution.py:115
  71.5 1.6 multiply_reduce_fusion
  73.7 2.1 %constant_dynamic-update-slice_fusion.6 = bf16[1024,3072]{1,0:T(8,128)(2,1)} fusion(bf16[1024,3072]{1,0:T(8,128)(2,1)} %constant_dynamic-update-slice_fusion.7, bf16[128,3072]{1,0:T(8,128)(2,1)} %collective-permute-done.3), kind=kLoop, calls=%fused_computation.90 | loop fusion | bytes 1572864
  75.8 2.1 %constant_dynamic-update-slice_fusion.5 = bf16[1024,3072]{1,0:T(8,128)(2,1)} fusion(bf16[1024,3072]{1,0:T(8,128)(2,1)} %constant_dynamic-update-slice_fusion.6, bf16[128,3072]{1,0:T(8,128)(2,1)} %collective-permute-done.4), kind=kLoop, calls=%fused_computation.89 | loop fusion | bytes 1572864
  78.8 2.1 %constant_dynamic-update-slice_fusion.3 = bf16[1024,3072]{1,0:T(8,128)(2,1)} fusion(bf16[1024,3072]{1,0:T(8,128)(2,1)} %constant_dynamic-update-slice_fusion.4, bf16[1,128,3072]{2,1,0:T(8,128)(2,1)} %collective-permute-done.6), kind=kLoop, calls=%fused_computation.87 | loop fusion | bytes 1572864
  81.9 1.9 copy.37
  83.9 1.9 squeeze.53
  85.7 1.7 exponential_convert_fusion
  88.3 6.4 %collective-permute-done.8 = bf16[512,384]{1,0:T(8,128)(2,1)} collective-permute-done((bf16[512,384]{1,0:T(8,128)(2,1)}, bf16[512,384]{1,0:T(8,128)(2,1)}, u32[]{:S(2)}, u32[]{:S(2)}) %collective-permute-start.8) | collective-permute-done | bytes 393248 | tf_op jit(solution)/shard_map/ppermute | solution.py:115
  94.7 1.7 add_convert_fusion
  96.6 1.7 fusion.35
  99.9 1.1 fusion.33
  101.1 7.9 %collective-permute-start.11 = (bf16[512,384]{0,1:T(8,128)(2,1)S(1)}, bf16[512,384]{0,1:T(8,128)(2,1)S(1)}, u32[]{:S(2)}, u32[]{:S(2)}) collective-permute-start(bf16[512,384]{0,1:T(8,128)(2,1)S(1)} %bitcast.141), channel_id=1, source_target_pairs={{0,3},{1,0},{2,1},{3,2},{4,7},{5,4},{6,5},{7,6},{8,11},{9,8},{10,9... | collective-permute-start | bytes 1179656 | tf_op jit(solution)/shard_map/ppermute | solution.py:115
  108.9 2.5 %collective-permute-start.13 = (bf16[512,384]{0,1:T(8,128)(2,1)S(1)}, bf16[512,384]{0,1:T(8,128)(2,1)}, u32[]{:S(2)}, u32[]{:S(2)}) collective-permute-start(bf16[512,384]{0,1:T(8,128)(2,1)S(1)} %bitcast.142), channel_id=1, source_target_pairs={{0,2},{1,3},{2,0},{3,1},{4,6},{5,7},{6,4},{7,5},{8,10},{9,11},{10,... | collective-permute-start | bytes 1179656 | tf_op jit(solution)/shard_map/ppermute | solution.py:115
  111.5 1.1 reshape.197
  112.6 1.1 reshape.196
  114.0 1.4 constant_dynamic-slice_fusion.2
  115.4 1.3 constant_dynamic-slice_fusion.3
  120.0 2.1 %constant_dynamic-update-slice_fusion.2 = bf16[1024,3072]{1,0:T(8,128)(2,1)} fusion(bf16[1024,3072]{1,0:T(8,128)(2,1)} %constant_dynamic-update-slice_fusion.3, bf16[128,3072]{1,0:T(8,128)(2,1)} %collective-permute-done.20), kind=kLoop, calls=%fused_computation.86 | loop fusion | bytes 1572864
  122.0 1.5 collective-permute-start.23
  123.5 2.1 %constant_dynamic-update-slice_fusion.1 = bf16[1024,3072]{1,0:T(8,128)(2,1)} fusion(bf16[1024,3072]{1,0:T(8,128)(2,1)} %constant_dynamic-update-slice_fusion.2, bf16[128,3072]{1,0:T(8,128)(2,1)} %collective-permute-done.21), kind=kLoop, calls=%fused_computation.85 | loop fusion | bytes 1572864
  126.1 19.8 %collective-permute-done.13 = bf16[512,384]{0,1:T(8,128)(2,1)} collective-permute-done((bf16[512,384]{0,1:T(8,128)(2,1)S(1)}, bf16[512,384]{0,1:T(8,128)(2,1)}, u32[]{:S(2)}, u32[]{:S(2)}) %collective-permute-start.13) | collective-permute-done | bytes 393248 | tf_op jit(solution)/shard_map/ppermute | solution.py:115
  145.9 1.5 collective-permute-start.12
  147.9 1.5 collective-permute-start.16
  149.4 2.1 %constant_dynamic-update-slice_fusion = bf16[1024,3072]{1,0:T(8,128)(2,1)} fusion(bf16[1024,3072]{1,0:T(8,128)(2,1)} %constant_dynamic-update-slice_fusion.1, bf16[128,3072]{1,0:T(8,128)(2,1)} %collective-permute-done.22), kind=kLoop, calls=%fused_computation.84 | loop fusion | bytes 1572864 | tf_op jit(solution)/shard_map/concatenate | solution.py:274
  151.5 7.5 %fusion.17 = f32[364,3072]{1,0:T(8,128)} fusion(bf16[1024,3072]{1,0:T(8,128)(2,1)} %constant_dynamic-update-slice_fusion, bf16[512,364]{1,0:T(8,128)(2,1)S(1)} %collective-permute-done.23, bf16[512,364]{1,0:T(8,128)(2,1)S(1)} %bitcast.150), kind=kOutput, calls=%fused_computation.39 | convolution fusion | flops 2291580928 | bytes 11509760 | tf_op jit(solution)/shard_map/dot_general | solution.py:11
  159.2 7.2 %collective-permute-done.14 = bf16[512,384]{0,1:T(8,128)(2,1)S(1)} collective-permute-done((bf16[512,384]{0,1:T(8,128)(2,1)}, bf16[512,384]{0,1:T(8,128)(2,1)S(1)}, u32[]{:S(2)}, u32[]{:S(2)}) %collective-permute-start.14) | collective-permute-done | bytes 393248 | tf_op jit(solution)/shard_map/ppermute | solution.py:17
  166.4 1.1 fusion.24
  167.5 5.5 %collective-permute-done.16 = bf16[512,384]{0,1:T(8,128)(2,1)S(1)} collective-permute-done((bf16[512,384]{0,1:T(8,128)(2,1)S(1)}, bf16[512,384]{0,1:T(8,128)(2,1)S(1)}, u32[]{:S(2)}, u32[]{:S(2)}) %collective-permute-start.16) | collective-permute-done | bytes 393248 | tf_op jit(solution)/shard_map/ppermute | solution.py:17
  173.3 1.3 fusion.25
  175.2 1.9 collective-permute-start.18
  177.2 13.0 %fusion = f32[4,384,3072]{2,1,0:T(8,128)} fusion(bf16[4,1024,384]{1,2,0:T(8,128)(2,1)S(1)} %constant_dynamic-slice_fusion.1, bf16[1024,3072]{1,0:T(8,128)(2,1)S(1)} %bitcast.137), kind=kOutput, calls=%fused_computation | convolution fusion | flops 9663676416 | bytes 28311552 | tf_op jit(solution)/shard_map/dot_general | solution.py:281
  190.3 10.0 %collective-permute-done.18 = bf16[3,128,384]{2,1,0:T(8,128)(2,1)S(1)} collective-permute-done((bf16[3,128,384]{2,1,0:T(8,128)(2,1)S(1)}, bf16[3,128,384]{2,1,0:T(8,128)(2,1)S(1)}, u32[]{:S(2)}, u32[]{:S(2)}) %collective-permute-start.18) | collective-permute-done | bytes 294944 | tf_op jit(solution)/shard_map/ppermute | solution.py:115
  200.5 1.5 slice_bitcast_fusion
  (144 shorter events, 26.6 us)
Async XLA Ops:
  1.7 4.2 %copy-start.6 = (bf16[1,128,364]{2,1,0:T(8,128)(2,1)}, bf16[1,128,364]{2,1,0:T(8,128)(2,1)S(1)}, u32[]{:S(2)}) copy-start(bf16[1,128,364]{2,1,0:T(8,128)(2,1)S(1)} %copy.30) | copy-start | bytes 279556
  2.0 6.9 %copy-start.13 = (bf16[1,128,3072]{2,1,0:T(8,128)(2,1)S(1)}, bf16[1,128,3072]{2,1,0:T(8,128)(2,1)}, u32[]{:S(2)}) copy-start(bf16[1,128,3072]{2,1,0:T(8,128)(2,1)} %param.11) | copy-start | bytes 2359300
  5.9 15.0 %collective-permute-start = (bf16[194048]{0:T(1024)(128)(2,1)S(1)}, bf16[194048]{0:T(1024)(128)(2,1)S(1)}, u32[]{:S(2)}, u32[]{:S(2)}) collective-permute-start(bf16[194048]{0:T(1024)(128)(2,1)S(1)} %get-tuple-element.59), channel_id=1, source_target_pairs={{0,1},{1,2},{2,3},{3,0},{4,5},{5,6},{6,7},{7,4},{8,9},{9,10},{10,1... | collective-permute-start | bytes 1164296 | tf_op jit(solution)/shard_map/ppermute | solution.py:115
  8.9 36.4 %collective-permute-start.5 = (bf16[128,3072]{1,0:T(8,128)(2,1)S(1)}, bf16[128,3072]{1,0:T(8,128)(2,1)S(1)}, u32[]{:S(2)}, u32[]{:S(2)}) collective-permute-start(bf16[128,3072]{1,0:T(8,128)(2,1)S(1)} %bitcast.151), channel_id=1, source_target_pairs={{0,12},{4,0},{8,4},{12,8},{1,13},{5,1},{9,5},{13,9},{2,14},{6,2},{... | collective-permute-start | bytes 2359304 | tf_op jit(solution)/shard_map/ppermute | solution.py:115
  9.5 36.1 %collective-permute-start.4 = (bf16[128,3072]{1,0:T(8,128)(2,1)S(1)}, bf16[128,3072]{1,0:T(8,128)(2,1)}, u32[]{:S(2)}, u32[]{:S(2)}) collective-permute-start(bf16[128,3072]{1,0:T(8,128)(2,1)S(1)} %bitcast.152), channel_id=1, source_target_pairs={{0,8},{4,12},{8,0},{12,4},{1,9},{5,13},{9,1},{13,5},{2,10},{6,14},... | collective-permute-start | bytes 2359304 | tf_op jit(solution)/shard_map/ppermute | solution.py:115
  10.4 35.3 %collective-permute-start.3 = (bf16[128,3072]{1,0:T(8,128)(2,1)S(1)}, bf16[128,3072]{1,0:T(8,128)(2,1)}, u32[]{:S(2)}, u32[]{:S(2)}) collective-permute-start(bf16[128,3072]{1,0:T(8,128)(2,1)S(1)} %bitcast.153), channel_id=1, source_target_pairs={{0,4},{4,8},{8,12},{12,0},{1,5},{5,9},{9,13},{13,1},{2,6},{6,10},{... | collective-permute-start | bytes 2359304 | tf_op jit(solution)/shard_map/ppermute | solution.py:115
  10.6 26.1 %collective-permute-start.1 = (bf16[194048]{0:T(1024)(128)(2,1)}, bf16[194048]{0:T(1024)(128)(2,1)}, u32[]{:S(2)}, u32[]{:S(2)}) collective-permute-start(bf16[194048]{0:T(1024)(128)(2,1)} %get-tuple-element.58), channel_id=1, source_target_pairs={{0,2},{1,3},{2,0},{3,1},{4,6},{5,7},{6,4},{7,5},{8,10},{9,11},{10,... | collective-permute-start | bytes 1164296 | tf_op jit(solution)/shard_map/ppermute | solution.py:115
  20.9 21.5 %collective-permute-start.2 = (bf16[194048]{0:T(1024)(128)(2,1)S(1)}, bf16[194048]{0:T(1024)(128)(2,1)}, u32[]{:S(2)}, u32[]{:S(2)}) collective-permute-start(bf16[194048]{0:T(1024)(128)(2,1)S(1)} %get-tuple-element.57), channel_id=1, source_target_pairs={{0,3},{1,0},{2,1},{3,2},{4,7},{5,4},{6,5},{7,6},{8,11},{9,8},{10,9... | collective-permute-start | bytes 1164296 | tf_op jit(solution)/shard_map/ppermute | solution.py:115
  36.7 19.7 %collective-permute-start.6 = (bf16[1,128,3072]{2,1,0:T(8,128)(2,1)S(1)}, bf16[1,128,3072]{2,1,0:T(8,128)(2,1)}, u32[]{:S(2)}, u32[]{:S(2)}) collective-permute-start(bf16[1,128,3072]{2,1,0:T(8,128)(2,1)S(1)} %copy-done.13), channel_id=1, source_target_pairs={{0,16},{16,0},{1,17},{17,1},{2,18},{18,2},{3,19},{19,3},{4,20},{20... | collective-permute-start | bytes 2359304 | tf_op jit(solution)/shard_map/ppermute | solution.py:17
  45.3 9.7 %copy-start.14 = (bf16[128,3072]{1,0:T(8,128)(2,1)}, bf16[128,3072]{1,0:T(8,128)(2,1)S(1)}, u32[]{:S(2)}) copy-start(bf16[128,3072]{1,0:T(8,128)(2,1)S(1)} %collective-permute-done.5) | copy-start | bytes 2359300
  55.0 13.8 %copy-start.9 = (f32[512,1536]{1,0:T(8,128)}, f32[512,1536]{1,0:T(8,128)S(1)}, u32[]{:S(2)}) copy-start(f32[512,1536]{1,0:T(8,128)S(1)} %fusion.2) | copy-start | bytes 9437188
  56.4 63.3 %collective-permute-start.20 = (bf16[128,3072]{1,0:T(8,128)(2,1)}, bf16[128,3072]{1,0:T(8,128)(2,1)}, u32[]{:S(2)}, u32[]{:S(2)}) collective-permute-start(bf16[128,3072]{1,0:T(8,128)(2,1)} %bitcast.31), channel_id=1, source_target_pairs={{0,4},{4,8},{8,12},{12,0},{1,5},{5,9},{9,13},{13,1},{2,6},{6,10},{... | collective-permute-start | bytes 2359304 | tf_op jit(solution)/shard_map/ppermute | solution.py:115
  56.4 65.6 %collective-permute-start.21 = (bf16[128,3072]{1,0:T(8,128)(2,1)}, bf16[128,3072]{1,0:T(8,128)(2,1)}, u32[]{:S(2)}, u32[]{:S(2)}) collective-permute-start(bf16[128,3072]{1,0:T(8,128)(2,1)} %bitcast.31), channel_id=1, source_target_pairs={{0,8},{4,12},{8,0},{12,4},{1,9},{5,13},{9,1},{13,5},{2,10},{6,14},... | collective-permute-start | bytes 2359304 | tf_op jit(solution)/shard_map/ppermute | solution.py:115
  59.0 28.4 %collective-permute-start.9 = (bf16[512,384]{1,0:T(8,128)(2,1)}, bf16[512,384]{1,0:T(8,128)(2,1)}, u32[]{:S(2)}, u32[]{:S(2)}) collective-permute-start(bf16[512,384]{1,0:T(8,128)(2,1)} %get-tuple-element.34), channel_id=1, source_target_pairs={{0,1},{1,2},{2,3},{3,0},{4,5},{5,6},{6,7},{7,4},{8,9},{9,10},{10,1... | collective-permute-start | bytes 1179656 | tf_op jit(solution)/shard_map/ppermute | solution.py:115
  65.0 29.7 %collective-permute-start.8 = (bf16[512,384]{1,0:T(8,128)(2,1)}, bf16[512,384]{1,0:T(8,128)(2,1)}, u32[]{:S(2)}, u32[]{:S(2)}) collective-permute-start(bf16[512,384]{1,0:T(8,128)(2,1)} %get-tuple-element.35), channel_id=1, source_target_pairs={{0,2},{1,3},{2,0},{3,1},{4,6},{5,7},{6,4},{7,5},{8,10},{9,11},{10,... | collective-permute-start | bytes 1179656 | tf_op jit(solution)/shard_map/ppermute | solution.py:115
  68.4 26.3 %collective-permute-start.7 = (bf16[512,384]{1,0:T(8,128)(2,1)}, bf16[512,384]{1,0:T(8,128)(2,1)}, u32[]{:S(2)}, u32[]{:S(2)}) collective-permute-start(bf16[512,384]{1,0:T(8,128)(2,1)} %get-tuple-element.33), channel_id=1, source_target_pairs={{0,3},{1,0},{2,1},{3,2},{4,7},{5,4},{6,5},{7,6},{8,11},{9,8},{10,9... | collective-permute-start | bytes 1179656 | tf_op jit(solution)/shard_map/ppermute | solution.py:115
  73.1 4.8 %copy-start.15 = (bf16[128,3072]{1,0:T(8,128)(2,1)S(1)}, bf16[128,3072]{1,0:T(8,128)(2,1)}, u32[]{:S(2)}) copy-start(bf16[128,3072]{1,0:T(8,128)(2,1)} %copy-done.14) | copy-start | bytes 2359300
  73.7 7.2 %copy-start.7 = (bf16[1,128,364]{2,1,0:T(8,128)(2,1)S(1)}, bf16[1,128,364]{2,1,0:T(8,128)(2,1)}, u32[]{:S(2)}) copy-start(bf16[1,128,364]{2,1,0:T(8,128)(2,1)} %copy-done.6) | copy-start | bytes 279556
  73.7 7.2 %copy-start.10 = (bf16[128,364]{1,0:T(8,128)(2,1)S(1)}, bf16[128,364]{1,0:T(8,128)(2,1)}, u32[]{:S(2)}) copy-start(bf16[128,364]{1,0:T(8,128)(2,1)} %reshape.183) | copy-start | bytes 279556
  73.7 7.2 %copy-start.11 = (bf16[128,364]{1,0:T(8,128)(2,1)S(1)}, bf16[128,364]{1,0:T(8,128)(2,1)}, u32[]{:S(2)}) copy-start(bf16[128,364]{1,0:T(8,128)(2,1)} %reshape.188) | copy-start | bytes 279556
  73.7 7.3 %copy-start.12 = (bf16[128,364]{1,0:T(8,128)(2,1)S(1)}, bf16[128,364]{1,0:T(8,128)(2,1)}, u32[]{:S(2)}) copy-start(bf16[128,364]{1,0:T(8,128)(2,1)} %reshape.193) | copy-start | bytes 279556
  87.4 9.2 %copy-start = (bf16[3,512,512]{1,2,0:T(8,128)(2,1)S(1)}, bf16[3,512,512]{1,2,0:T(8,128)(2,1)}, u32[]{:S(2)}) copy-start(bf16[3,512,512]{1,2,0:T(8,128)(2,1)} %exponential_convert_fusion) | copy-start | bytes 4718596
  87.4 10.8 %copy-start.2 = (bf16[512,3,128]{0,2,1:T(8,128)(2,1)S(1)}, bf16[512,3,128]{0,2,1:T(8,128)(2,1)}, u32[]{:S(2)}) copy-start(bf16[512,3,128]{0,2,1:T(8,128)(2,1)} %squeeze.53) | copy-start | bytes 1179652
  87.4 60.5 %collective-permute-start.22 = (bf16[128,3072]{1,0:T(8,128)(2,1)}, bf16[128,3072]{1,0:T(8,128)(2,1)}, u32[]{:S(2)}, u32[]{:S(2)}) collective-permute-start(bf16[128,3072]{1,0:T(8,128)(2,1)} %bitcast.31), channel_id=1, source_target_pairs={{0,12},{4,0},{8,4},{12,8},{1,13},{5,1},{9,5},{13,9},{2,14},{6,2},{... | collective-permute-start | bytes 2359304 | tf_op jit(solution)/shard_map/ppermute | solution.py:115
  98.6 1.3 copy-start.1
  99.3 12.2 %copy-start.3 = (f32[512,3,128]{0,2,1:T(8,128)S(1)}, f32[512,3,128]{0,2,1:T(8,128)}, u32[]{:S(2)}) copy-start(f32[512,3,128]{0,2,1:T(8,128)} %get-tuple-element.69) | copy-start | bytes 2359300
  101.1 24.5 %collective-permute-start.11 = (bf16[512,384]{0,1:T(8,128)(2,1)S(1)}, bf16[512,384]{0,1:T(8,128)(2,1)S(1)}, u32[]{:S(2)}, u32[]{:S(2)}) collective-permute-start(bf16[512,384]{0,1:T(8,128)(2,1)S(1)} %bitcast.141), channel_id=1, source_target_pairs={{0,3},{1,0},{2,1},{3,2},{4,7},{5,4},{6,5},{7,6},{8,11},{9,8},{10,9... | collective-permute-start | bytes 1179656 | tf_op jit(solution)/shard_map/ppermute | solution.py:115
  108.9 37.0 %collective-permute-start.13 = (bf16[512,384]{0,1:T(8,128)(2,1)S(1)}, bf16[512,384]{0,1:T(8,128)(2,1)}, u32[]{:S(2)}, u32[]{:S(2)}) collective-permute-start(bf16[512,384]{0,1:T(8,128)(2,1)S(1)} %bitcast.142), channel_id=1, source_target_pairs={{0,2},{1,3},{2,0},{3,1},{4,6},{5,7},{6,4},{7,5},{8,10},{9,11},{10,... | collective-permute-start | bytes 1179656 | tf_op jit(solution)/shard_map/ppermute | solution.py:115
  112.6 4.7 %copy-start.5 = (bf16[512,3,128]{0,2,1:T(8,128)(2,1)S(1)}, bf16[512,3,128]{0,2,1:T(8,128)(2,1)}, u32[]{:S(2)}) copy-start(bf16[512,3,128]{0,2,1:T(8,128)(2,1)} %get-tuple-element.64) | copy-start | bytes 1179652
  114.0 4.1 %copy-start.4 = (bf16[512,3,128]{0,2,1:T(8,128)(2,1)S(1)}, bf16[512,3,128]{0,2,1:T(8,128)(2,1)}, u32[]{:S(2)}) copy-start(bf16[512,3,128]{0,2,1:T(8,128)(2,1)} %get-tuple-element.68) | copy-start | bytes 1179652
  119.3 2.7 %copy-start.8 = (bf16[4,128,364]{2,1,0:T(8,128)(2,1)S(1)}, bf16[4,128,364]{2,1,0:T(8,128)(2,1)}, u32[]{:S(2)}) copy-start(bf16[4,128,364]{2,1,0:T(8,128)(2,1)} %constant_dynamic-slice_fusion) | copy-start | bytes 1118212
  119.7 27.7 %collective-permute-start.15 = (bf16[512,384]{0,1:T(8,128)(2,1)S(1)}, bf16[512,384]{0,1:T(8,128)(2,1)S(1)}, u32[]{:S(2)}, u32[]{:S(2)}) collective-permute-start(bf16[512,384]{0,1:T(8,128)(2,1)S(1)} %bitcast.143), channel_id=1, source_target_pairs={{0,1},{1,2},{2,3},{3,0},{4,5},{5,6},{6,7},{7,4},{8,9},{9,10},{10,1... | collective-permute-start | bytes 1179656 | tf_op jit(solution)/shard_map/ppermute | solution.py:115
  122.0 29.5 %collective-permute-start.23 = (bf16[512,364]{1,0:T(8,128)(2,1)S(1)}, bf16[512,364]{1,0:T(8,128)(2,1)S(1)}, u32[]{:S(2)}, u32[]{:S(2)}) collective-permute-start(bf16[512,364]{1,0:T(8,128)(2,1)S(1)} %bitcast.149), channel_id=1, source_target_pairs={{0,16},{16,0},{1,17},{17,1},{2,18},{18,2},{3,19},{19,3},{4,20},{20... | collective-permute-start | bytes 1118216 | tf_op jit(solution)/shard_map/ppermute | solution.py:17
  125.6 33.4 %collective-permute-start.10 = (bf16[512,384]{0,1:T(8,128)(2,1)S(1)}, bf16[512,384]{0,1:T(8,128)(2,1)S(1)}, u32[]{:S(2)}, u32[]{:S(2)}) collective-permute-start(bf16[512,384]{0,1:T(8,128)(2,1)S(1)} %bitcast.144), channel_id=1, source_target_pairs={{0,16},{16,0},{1,17},{17,1},{2,18},{18,2},{3,19},{19,3},{4,20},{20... | collective-permute-start | bytes 1179656 | tf_op jit(solution)/shard_map/ppermute | solution.py:17
  145.9 13.2 %collective-permute-start.12 = (bf16[512,384]{0,1:T(8,128)(2,1)S(1)}, bf16[512,384]{0,1:T(8,128)(2,1)S(1)}, u32[]{:S(2)}, u32[]{:S(2)}) collective-permute-start(bf16[512,384]{0,1:T(8,128)(2,1)S(1)} %collective-permute-done.11), channel_id=1, source_target_pairs={{0,16},{16,0},{1,17},{17,1},{2,18},{18,2},{3,19},{19,3},{4,20},{20... | collective-permute-start | bytes 1179656 | tf_op jit(solution)/shard_map/ppermute | solution.py:17
  147.4 19.0 %collective-permute-start.14 = (bf16[512,384]{0,1:T(8,128)(2,1)}, bf16[512,384]{0,1:T(8,128)(2,1)S(1)}, u32[]{:S(2)}, u32[]{:S(2)}) collective-permute-start(bf16[512,384]{0,1:T(8,128)(2,1)} %collective-permute-done.13), channel_id=1, source_target_pairs={{0,16},{16,0},{1,17},{17,1},{2,18},{18,2},{3,19},{19,3},{4,20},{20... | collective-permute-start | bytes 1179656 | tf_op jit(solution)/shard_map/ppermute | solution.py:17
  147.9 25.1 %collective-permute-start.16 = (bf16[512,384]{0,1:T(8,128)(2,1)S(1)}, bf16[512,384]{0,1:T(8,128)(2,1)S(1)}, u32[]{:S(2)}, u32[]{:S(2)}) collective-permute-start(bf16[512,384]{0,1:T(8,128)(2,1)S(1)} %collective-permute-done.15), channel_id=1, source_target_pairs={{0,16},{16,0},{1,17},{17,1},{2,18},{18,2},{3,19},{19,3},{4,20},{20... | collective-permute-start | bytes 1179656 | tf_op jit(solution)/shard_map/ppermute | solution.py:17
  173.2 4.0 %slice-start = ((s8[6291456]{0:T(1024)(128)(4,1)}), s8[4194304]{0:T(1024)(128)(4,1)S(1)}, s32[]{:S(2)}) async-start(s8[6291456]{0:T(1024)(128)(4,1)} %bitcast.136), calls=%async_computation | async-start | bytes 8388608
  174.7 2.5 %slice-start.1 = ((s8[6291456]{0:T(1024)(128)(4,1)}), s8[2097152]{0:T(1024)(128)(4,1)S(1)}, s32[]{:S(2)}) async-start(s8[6291456]{0:T(1024)(128)(4,1)} %bitcast.136), calls=%async_computation.1 | async-start | bytes 4194304
  175.1 15.1 %collective-permute-start.17 = (bf16[3,128,384]{2,1,0:T(8,128)(2,1)S(1)}, bf16[3,128,384]{2,1,0:T(8,128)(2,1)S(1)}, u32[]{:S(2)}, u32[]{:S(2)}) collective-permute-start(bf16[3,128,384]{2,1,0:T(8,128)(2,1)S(1)} %get-tuple-element.41), channel_id=1, source_target_pairs={{0,3},{1,0},{2,1},{3,2},{4,7},{5,4},{6,5},{7,6},{8,11},{9,8},{10,9... | collective-permute-start | bytes 884744 | tf_op jit(solution)/shard_map/ppermute | solution.py:115
  175.2 25.2 %collective-permute-start.18 = (bf16[3,128,384]{2,1,0:T(8,128)(2,1)S(1)}, bf16[3,128,384]{2,1,0:T(8,128)(2,1)S(1)}, u32[]{:S(2)}, u32[]{:S(2)}) collective-permute-start(bf16[3,128,384]{2,1,0:T(8,128)(2,1)S(1)} %get-tuple-element.40), channel_id=1, source_target_pairs={{0,2},{1,3},{2,0},{3,1},{4,6},{5,7},{6,4},{7,5},{8,10},{9,11},{10,... | collective-permute-start | bytes 884744 | tf_op jit(solution)/shard_map/ppermute | solution.py:115
  177.1 23.3 %collective-permute-start.19 = (bf16[3,128,384]{2,1,0:T(8,128)(2,1)S(1)}, bf16[3,128,384]{2,1,0:T(8,128)(2,1)S(1)}, u32[]{:S(2)}, u32[]{:S(2)}) collective-permute-start(bf16[3,128,384]{2,1,0:T(8,128)(2,1)S(1)} %get-tuple-element.39), channel_id=1, source_target_pairs={{0,1},{1,2},{2,3},{3,0},{4,5},{5,6},{6,7},{7,4},{8,9},{9,10},{10,1... | collective-permute-start | bytes 884744 | tf_op jit(solution)/shard_map/ppermute | solution.py:115

commit v18 on v17

--- a/solution.py
+++ b/solution.py
@@ -277,7 +277,8 @@
     sendable = roll_blocks(
         jnp.stack([g.astype(jnp.bfloat16) for g in grad_list], 1), rank - me
     )
-    sendable, out_both = lax.optimization_barrier((sendable, out_both))
+    sendable, _ = lax.optimization_barrier((sendable, [p[0] for p in out_pieces]))
+    out_both, sendable = lax.optimization_barrier((out_both, sendable))
     out_weight_grad = lax.dot_general(
         out_both, grad_both, (((1,), (0,)), ((), ())), preferred_element_type=jnp.float32
     ).reshape(width_all, -1)

time: 203 us -> 206 us (1.015)
  starting transfers between devices: 40.1 us -> 58.3 us
  waiting for transfers between devices: 72.2 us -> 59.3 us
  other arithmetic: 8.74 us -> 6.61 us
    ppermute x18, starting transfers between devices: 33.1 us -> 50.2 us  [shifted(): return lax.ppermute(x, axis, [(j, (j + step) % n) for j in range(n)])]
    ppermute x18, waiting for transfers between devices: 58.1 us -> 44.5 us  [shifted(): return lax.ppermute(x, axis, [(j, (j + step) % n) for j in range(n)])]
    unnamed x8, other arithmetic: 2.83 us -> 0.69 us
    unnamed x61 -> x59, local copies, waits for them, and re-layouts: 14.2 us -> 14.2 us
  transfers between devices with their start and end apart: 24 -> 24, of which waited for: 11 -> 12; matrix products, arithmetic and copies ran while one was open for 39% -> 38% of each run, Pallas kernels for 0% -> 0%
where the time goes in v18:
time: 206 us; the launch traced here: 205 us
  waiting for transfers between devices  59.3 us (29%)
  starting transfers between devices  58.3 us (28%)
  local copies, waits for them, and re-layouts  43.7 us (21%)
  matrix products  36 us (17%)
  other arithmetic  6.61 us (3%)
    ppermute x18, starting transfers between devices, shifted(): return lax.ppermute(x, axis, [(j, (j + step) % n) for j in range(n)])  50.2 us
    ppermute x18, waiting for transfers between devices, shifted(): return lax.ppermute(x, axis, [(j, (j + step) % n) for j in range(n)])  44.5 us
    ppermute x6, waiting for transfers between devices, swap_dp(): return lax.ppermute(x, 'dp', [(0, 1), (1, 0)])  14.8 us
    unnamed x59, local copies, waits for them, and re-layouts  14.2 us
    dot_general x1, matrix products, body_heads(): lax.dot_general(out_both, grad_both, (((1,), (0,)), ((), ())), preferred_...  13 us
    dot_general x1, matrix products, body_heads(): lax.dot_general(dense_grad, out_weight, (((1,), (1,)), ((), ())), preferr...  9.23 us
    ppermute x6, starting transfers between devices, swap_dp(): return lax.ppermute(x, 'dp', [(0, 1), (1, 0)])  8.1 us
    dot_general x1, matrix products, contract_rows(): lax.dot_general(left, right, (((0,), (0,)), ((), ())), preferred_element_...  7.73 us
  transfers between devices with their start and end apart: 24, of which 12 were waited for; matrix products, arithmetic and copies ran while one was open for 38% of the time, Pallas kernels for 0%

profile of v18, /device:TPU:0, one launch (start us, length us, event | category | flops | bytes accessed | tf_op | source)
XLA Modules:
  0.0 205.4 jit_solution(12099134447756512260)
XLA Ops:
  2.0 1.2 constant_dynamic-slice_fusion.7
  3.2 1.3 constant_dynamic-slice_fusion.5
  5.9 3.0 %collective-permute-start = (bf16[194048]{0:T(1024)(128)(2,1)S(1)}, bf16[194048]{0:T(1024)(128)(2,1)S(1)}, u32[]{:S(2)}, u32[]{:S(2)}) collective-permute-start(bf16[194048]{0:T(1024)(128)(2,1)S(1)} %get-tuple-element.61), channel_id=1, source_target_pairs={{0,1},{1,2},{2,3},{3,0},{4,5},{5,6},{6,7},{7,4},{8,9},{9,10},{10,1... | collective-permute-start | bytes 1164296 | tf_op jit(solution)/shard_map/ppermute | solution.py:115
  10.6 2.6 %collective-permute-start.1 = (bf16[194048]{0:T(1024)(128)(2,1)}, bf16[194048]{0:T(1024)(128)(2,1)}, u32[]{:S(2)}, u32[]{:S(2)}) collective-permute-start(bf16[194048]{0:T(1024)(128)(2,1)} %get-tuple-element.60), channel_id=1, source_target_pairs={{0,2},{1,3},{2,0},{3,1},{4,6},{5,7},{6,4},{7,5},{8,10},{9,11},{10,... | collective-permute-start | bytes 1164296 | tf_op jit(solution)/shard_map/ppermute | solution.py:115
  13.2 7.7 %collective-permute-done = bf16[194048]{0:T(1024)(128)(2,1)S(1)} collective-permute-done((bf16[194048]{0:T(1024)(128)(2,1)S(1)}, bf16[194048]{0:T(1024)(128)(2,1)S(1)}, u32[]{:S(2)}, u32[]{:S(2)}) %collective-permute-start) | collective-permute-done | bytes 388128 | tf_op jit(solution)/shard_map/ppermute | solution.py:115
  20.9 1.2 collective-permute-start.2
  24.1 12.6 %collective-permute-done.1 = bf16[194048]{0:T(1024)(128)(2,1)} collective-permute-done((bf16[194048]{0:T(1024)(128)(2,1)}, bf16[194048]{0:T(1024)(128)(2,1)}, u32[]{:S(2)}, u32[]{:S(2)}) %collective-permute-start.1) | collective-permute-done | bytes 388128 | tf_op jit(solution)/shard_map/ppermute | solution.py:115
  36.7 1.5 collective-permute-start.6
  41.2 1.2 collective-permute-done.2
  45.7 9.2 %fusion.2 = f32[512,1536]{1,0:T(8,128)S(1)} fusion(bf16[1536,3072]{1,0:T(8,128)(2,1)} %param.10, bf16[128,3072]{1,0:T(8,128)(2,1)S(1)} %collective-permute-done.5, bf16[128,3072]{1,0:T(8,128)(2,1)} %collective-permute-done.4, bf16[128,3072]{1,0:T(8,128)(2,1)} %collective-permute-done.3, bf16[128,3072]{1,0:T(8,128)(2,1)S(1)} %bitcast.152), kind=kOutput, calls=%fused_computation.2 | convolution fusion | flops 4844421120 | bytes 15728640 | tf_op jit(solution)/shard_map/dot_general | solution.py:222
  55.0 1.4 collective-permute-done.6
  56.4 1.5 collective-permute-start.21
  57.9 1.1 dynamic-slice_convert_fusion.2
  59.0 6.0 %collective-permute-start.9 = (bf16[512,384]{1,0:T(8,128)(2,1)}, bf16[512,384]{1,0:T(8,128)(2,1)}, u32[]{:S(2)}, u32[]{:S(2)}) collective-permute-start(bf16[512,384]{1,0:T(8,128)(2,1)} %get-tuple-element.36), channel_id=1, source_target_pairs={{0,1},{1,2},{2,3},{3,0},{4,5},{5,6},{6,7},{7,4},{8,9},{9,10},{10,1... | collective-permute-start | bytes 1179656 | tf_op jit(solution)/shard_map/ppermute | solution.py:115
  65.0 3.4 %collective-permute-start.8 = (bf16[512,384]{1,0:T(8,128)(2,1)}, bf16[512,384]{1,0:T(8,128)(2,1)}, u32[]{:S(2)}, u32[]{:S(2)}) collective-permute-start(bf16[512,384]{1,0:T(8,128)(2,1)} %get-tuple-element.37), channel_id=1, source_target_pairs={{0,2},{1,3},{2,0},{3,1},{4,6},{5,7},{6,4},{7,5},{8,10},{9,11},{10,... | collective-permute-start | bytes 1179656 | tf_op jit(solution)/shard_map/ppermute | solution.py:115
  71.5 1.6 multiply_reduce_fusion
  73.7 2.1 %constant_dynamic-update-slice_fusion.6 = bf16[1024,3072]{1,0:T(8,128)(2,1)} fusion(bf16[1024,3072]{1,0:T(8,128)(2,1)} %constant_dynamic-update-slice_fusion.7, bf16[128,3072]{1,0:T(8,128)(2,1)} %collective-permute-done.3), kind=kLoop, calls=%fused_computation.90 | loop fusion | bytes 1572864
  75.8 2.1 %constant_dynamic-update-slice_fusion.5 = bf16[1024,3072]{1,0:T(8,128)(2,1)} fusion(bf16[1024,3072]{1,0:T(8,128)(2,1)} %constant_dynamic-update-slice_fusion.6, bf16[128,3072]{1,0:T(8,128)(2,1)} %collective-permute-done.4), kind=kLoop, calls=%fused_computation.89 | loop fusion | bytes 1572864
  78.8 2.1 %constant_dynamic-update-slice_fusion.3 = bf16[1024,3072]{1,0:T(8,128)(2,1)} fusion(bf16[1024,3072]{1,0:T(8,128)(2,1)} %constant_dynamic-update-slice_fusion.4, bf16[1,128,3072]{2,1,0:T(8,128)(2,1)} %collective-permute-done.6), kind=kLoop, calls=%fused_computation.87 | loop fusion | bytes 1572864
  81.9 1.9 copy.37
  83.9 1.9 squeeze.53
  85.8 1.7 exponential_convert_fusion
  88.3 6.4 %collective-permute-done.8 = bf16[512,384]{1,0:T(8,128)(2,1)} collective-permute-done((bf16[512,384]{1,0:T(8,128)(2,1)}, bf16[512,384]{1,0:T(8,128)(2,1)}, u32[]{:S(2)}, u32[]{:S(2)}) %collective-permute-start.8) | collective-permute-done | bytes 393248 | tf_op jit(solution)/shard_map/ppermute | solution.py:115
  94.7 1.5 collective-permute-start.23
  96.2 1.7 add_convert_fusion
  98.1 1.6 fusion.35
  101.5 1.1 fusion.33
  102.6 1.1 reshape.197
  103.7 1.1 reshape.196
  105.1 1.4 constant_dynamic-slice_fusion.2
  106.5 1.3 constant_dynamic-slice_fusion.3
  108.4 7.9 %collective-permute-start.11 = (bf16[512,384]{0,1:T(8,128)(2,1)S(1)}, bf16[512,384]{0,1:T(8,128)(2,1)S(1)}, u32[]{:S(2)}, u32[]{:S(2)}) collective-permute-start(bf16[512,384]{0,1:T(8,128)(2,1)S(1)} %bitcast.141), channel_id=1, source_target_pairs={{0,3},{1,0},{2,1},{3,2},{4,7},{5,4},{6,5},{7,6},{8,11},{9,8},{10,9... | collective-permute-start | bytes 1179656 | tf_op jit(solution)/shard_map/ppermute | solution.py:115
  118.7 1.1 collective-permute-start.13
  119.8 2.1 %constant_dynamic-update-slice_fusion.2 = bf16[1024,3072]{1,0:T(8,128)(2,1)} fusion(bf16[1024,3072]{1,0:T(8,128)(2,1)} %constant_dynamic-update-slice_fusion.3, bf16[128,3072]{1,0:T(8,128)(2,1)} %collective-permute-done.20), kind=kLoop, calls=%fused_computation.86 | loop fusion | bytes 1572864
  121.8 1.5 collective-permute-start.10
  123.4 2.1 %constant_dynamic-update-slice_fusion.1 = bf16[1024,3072]{1,0:T(8,128)(2,1)} fusion(bf16[1024,3072]{1,0:T(8,128)(2,1)} %constant_dynamic-update-slice_fusion.2, bf16[128,3072]{1,0:T(8,128)(2,1)} %collective-permute-done.21), kind=kLoop, calls=%fused_computation.85 | loop fusion | bytes 1572864
  125.9 18.8 %collective-permute-start.15 = (bf16[512,384]{0,1:T(8,128)(2,1)S(1)}, bf16[512,384]{0,1:T(8,128)(2,1)S(1)}, u32[]{:S(2)}, u32[]{:S(2)}) collective-permute-start(bf16[512,384]{0,1:T(8,128)(2,1)S(1)} %bitcast.144), channel_id=1, source_target_pairs={{0,1},{1,2},{2,3},{3,0},{4,5},{5,6},{6,7},{7,4},{8,9},{9,10},{10,1... | collective-permute-start | bytes 1179656 | tf_op jit(solution)/shard_map/ppermute | solution.py:115
  144.7 7.0 %collective-permute-done.13 = bf16[512,384]{0,1:T(8,128)(2,1)S(1)} collective-permute-done((bf16[512,384]{0,1:T(8,128)(2,1)S(1)}, bf16[512,384]{0,1:T(8,128)(2,1)S(1)}, u32[]{:S(2)}, u32[]{:S(2)}) %collective-permute-start.13) | collective-permute-done | bytes 393248 | tf_op jit(solution)/shard_map/ppermute | solution.py:115
  151.7 1.5 collective-permute-start.12
  153.7 2.1 %constant_dynamic-update-slice_fusion = bf16[1024,3072]{1,0:T(8,128)(2,1)} fusion(bf16[1024,3072]{1,0:T(8,128)(2,1)} %constant_dynamic-update-slice_fusion.1, bf16[128,3072]{1,0:T(8,128)(2,1)} %collective-permute-done.22), kind=kLoop, calls=%fused_computation.84 | loop fusion | bytes 1572864 | tf_op jit(solution)/shard_map/concatenate | solution.py:274
  155.7 7.7 %fusion.17 = f32[364,3072]{1,0:T(8,128)} fusion(bf16[1024,3072]{1,0:T(8,128)(2,1)} %constant_dynamic-update-slice_fusion, bf16[512,364]{1,0:T(8,128)(2,1)} %collective-permute-done.23, bf16[512,364]{1,0:T(8,128)(2,1)} %bitcast.38), kind=kOutput, calls=%fused_computation.39 | convolution fusion | flops 2291580928 | bytes 11509760 | tf_op jit(solution)/shard_map/dot_general | solution.py:11
  163.5 1.5 collective-permute-start.16
  165.2 6.9 %collective-permute-done.14 = bf16[512,384]{0,1:T(8,128)(2,1)S(1)} collective-permute-done((bf16[512,384]{0,1:T(8,128)(2,1)S(1)}, bf16[512,384]{0,1:T(8,128)(2,1)S(1)}, u32[]{:S(2)}, u32[]{:S(2)}) %collective-permute-start.14) | collective-permute-done | bytes 393248 | tf_op jit(solution)/shard_map/ppermute | solution.py:17
  172.2 6.5 %collective-permute-done.16 = bf16[512,384]{0,1:T(8,128)(2,1)S(1)} collective-permute-done((bf16[512,384]{0,1:T(8,128)(2,1)S(1)}, bf16[512,384]{0,1:T(8,128)(2,1)S(1)}, u32[]{:S(2)}, u32[]{:S(2)}) %collective-permute-start.16) | collective-permute-done | bytes 393248 | tf_op jit(solution)/shard_map/ppermute | solution.py:17
  179.9 1.9 collective-permute-start.19
  181.9 13.0 %fusion = f32[4,384,3072]{2,1,0:T(8,128)} fusion(bf16[4,1024,384]{1,2,0:T(8,128)(2,1)S(1)} %constant_dynamic-slice_fusion.1, bf16[1024,3072]{1,0:T(8,128)(2,1)S(1)} %bitcast.137), kind=kOutput, calls=%fused_computation | convolution fusion | flops 9663676416 | bytes 28311552 | tf_op jit(solution)/shard_map/dot_general | solution.py:282
  195.0 8.7 %collective-permute-done.18 = bf16[3,128,384]{2,1,0:T(8,128)(2,1)S(1)} collective-permute-done((bf16[3,128,384]{2,1,0:T(8,128)(2,1)S(1)}, bf16[3,128,384]{2,1,0:T(8,128)(2,1)S(1)}, u32[]{:S(2)}, u32[]{:S(2)}) %collective-permute-start.18) | collective-permute-done | bytes 294944 | tf_op jit(solution)/shard_map/ppermute | solution.py:115
  203.9 1.5 slice_bitcast_fusion
  (142 shorter events, 26.5 us)
Async XLA Ops:
  1.7 4.2 %copy-start.6 = (bf16[1,128,364]{2,1,0:T(8,128)(2,1)}, bf16[1,128,364]{2,1,0:T(8,128)(2,1)S(1)}, u32[]{:S(2)}) copy-start(bf16[1,128,364]{2,1,0:T(8,128)(2,1)S(1)} %copy.30) | copy-start | bytes 279556
  2.0 6.9 %copy-start.12 = (bf16[1,128,3072]{2,1,0:T(8,128)(2,1)S(1)}, bf16[1,128,3072]{2,1,0:T(8,128)(2,1)}, u32[]{:S(2)}) copy-start(bf16[1,128,3072]{2,1,0:T(8,128)(2,1)} %param.11) | copy-start | bytes 2359300
  5.9 15.0 %collective-permute-start = (bf16[194048]{0:T(1024)(128)(2,1)S(1)}, bf16[194048]{0:T(1024)(128)(2,1)S(1)}, u32[]{:S(2)}, u32[]{:S(2)}) collective-permute-start(bf16[194048]{0:T(1024)(128)(2,1)S(1)} %get-tuple-element.61), channel_id=1, source_target_pairs={{0,1},{1,2},{2,3},{3,0},{4,5},{5,6},{6,7},{7,4},{8,9},{9,10},{10,1... | collective-permute-start | bytes 1164296 | tf_op jit(solution)/shard_map/ppermute | solution.py:115
  8.9 36.4 %collective-permute-start.5 = (bf16[128,3072]{1,0:T(8,128)(2,1)S(1)}, bf16[128,3072]{1,0:T(8,128)(2,1)S(1)}, u32[]{:S(2)}, u32[]{:S(2)}) collective-permute-start(bf16[128,3072]{1,0:T(8,128)(2,1)S(1)} %bitcast.149), channel_id=1, source_target_pairs={{0,12},{4,0},{8,4},{12,8},{1,13},{5,1},{9,5},{13,9},{2,14},{6,2},{... | collective-permute-start | bytes 2359304 | tf_op jit(solution)/shard_map/ppermute | solution.py:115
  9.5 36.1 %collective-permute-start.4 = (bf16[128,3072]{1,0:T(8,128)(2,1)S(1)}, bf16[128,3072]{1,0:T(8,128)(2,1)}, u32[]{:S(2)}, u32[]{:S(2)}) collective-permute-start(bf16[128,3072]{1,0:T(8,128)(2,1)S(1)} %bitcast.150), channel_id=1, source_target_pairs={{0,8},{4,12},{8,0},{12,4},{1,9},{5,13},{9,1},{13,5},{2,10},{6,14},... | collective-permute-start | bytes 2359304 | tf_op jit(solution)/shard_map/ppermute | solution.py:115
  10.4 35.3 %collective-permute-start.3 = (bf16[128,3072]{1,0:T(8,128)(2,1)S(1)}, bf16[128,3072]{1,0:T(8,128)(2,1)}, u32[]{:S(2)}, u32[]{:S(2)}) collective-permute-start(bf16[128,3072]{1,0:T(8,128)(2,1)S(1)} %bitcast.151), channel_id=1, source_target_pairs={{0,4},{4,8},{8,12},{12,0},{1,5},{5,9},{9,13},{13,1},{2,6},{6,10},{... | collective-permute-start | bytes 2359304 | tf_op jit(solution)/shard_map/ppermute | solution.py:115
  10.6 26.1 %collective-permute-start.1 = (bf16[194048]{0:T(1024)(128)(2,1)}, bf16[194048]{0:T(1024)(128)(2,1)}, u32[]{:S(2)}, u32[]{:S(2)}) collective-permute-start(bf16[194048]{0:T(1024)(128)(2,1)} %get-tuple-element.60), channel_id=1, source_target_pairs={{0,2},{1,3},{2,0},{3,1},{4,6},{5,7},{6,4},{7,5},{8,10},{9,11},{10,... | collective-permute-start | bytes 1164296 | tf_op jit(solution)/shard_map/ppermute | solution.py:115
  20.9 21.5 %collective-permute-start.2 = (bf16[194048]{0:T(1024)(128)(2,1)S(1)}, bf16[194048]{0:T(1024)(128)(2,1)}, u32[]{:S(2)}, u32[]{:S(2)}) collective-permute-start(bf16[194048]{0:T(1024)(128)(2,1)S(1)} %get-tuple-element.59), channel_id=1, source_target_pairs={{0,3},{1,0},{2,1},{3,2},{4,7},{5,4},{6,5},{7,6},{8,11},{9,8},{10,9... | collective-permute-start | bytes 1164296 | tf_op jit(solution)/shard_map/ppermute | solution.py:115
  36.7 19.7 %collective-permute-start.6 = (bf16[1,128,3072]{2,1,0:T(8,128)(2,1)S(1)}, bf16[1,128,3072]{2,1,0:T(8,128)(2,1)}, u32[]{:S(2)}, u32[]{:S(2)}) collective-permute-start(bf16[1,128,3072]{2,1,0:T(8,128)(2,1)S(1)} %copy-done.12), channel_id=1, source_target_pairs={{0,16},{16,0},{1,17},{17,1},{2,18},{18,2},{3,19},{19,3},{4,20},{20... | collective-permute-start | bytes 2359304 | tf_op jit(solution)/shard_map/ppermute | solution.py:17
  45.3 9.6 %copy-start.13 = (bf16[128,3072]{1,0:T(8,128)(2,1)}, bf16[128,3072]{1,0:T(8,128)(2,1)S(1)}, u32[]{:S(2)}) copy-start(bf16[128,3072]{1,0:T(8,128)(2,1)S(1)} %collective-permute-done.5) | copy-start | bytes 2359300
  55.0 13.8 %copy-start.8 = (f32[512,1536]{1,0:T(8,128)}, f32[512,1536]{1,0:T(8,128)S(1)}, u32[]{:S(2)}) copy-start(f32[512,1536]{1,0:T(8,128)S(1)} %fusion.2) | copy-start | bytes 9437188
  56.4 62.3 %collective-permute-start.20 = (bf16[128,3072]{1,0:T(8,128)(2,1)}, bf16[128,3072]{1,0:T(8,128)(2,1)}, u32[]{:S(2)}, u32[]{:S(2)}) collective-permute-start(bf16[128,3072]{1,0:T(8,128)(2,1)} %bitcast.31), channel_id=1, source_target_pairs={{0,4},{4,8},{8,12},{12,0},{1,5},{5,9},{9,13},{13,1},{2,6},{6,10},{... | collective-permute-start | bytes 2359304 | tf_op jit(solution)/shard_map/ppermute | solution.py:115
  56.4 65.4 %collective-permute-start.21 = (bf16[128,3072]{1,0:T(8,128)(2,1)}, bf16[128,3072]{1,0:T(8,128)(2,1)}, u32[]{:S(2)}, u32[]{:S(2)}) collective-permute-start(bf16[128,3072]{1,0:T(8,128)(2,1)} %bitcast.31), channel_id=1, source_target_pairs={{0,8},{4,12},{8,0},{12,4},{1,9},{5,13},{9,1},{13,5},{2,10},{6,14},... | collective-permute-start | bytes 2359304 | tf_op jit(solution)/shard_map/ppermute | solution.py:115
  59.0 28.4 %collective-permute-start.9 = (bf16[512,384]{1,0:T(8,128)(2,1)}, bf16[512,384]{1,0:T(8,128)(2,1)}, u32[]{:S(2)}, u32[]{:S(2)}) collective-permute-start(bf16[512,384]{1,0:T(8,128)(2,1)} %get-tuple-element.36), channel_id=1, source_target_pairs={{0,1},{1,2},{2,3},{3,0},{4,5},{5,6},{6,7},{7,4},{8,9},{9,10},{10,1... | collective-permute-start | bytes 1179656 | tf_op jit(solution)/shard_map/ppermute | solution.py:115
  65.0 29.7 %collective-permute-start.8 = (bf16[512,384]{1,0:T(8,128)(2,1)}, bf16[512,384]{1,0:T(8,128)(2,1)}, u32[]{:S(2)}, u32[]{:S(2)}) collective-permute-start(bf16[512,384]{1,0:T(8,128)(2,1)} %get-tuple-element.37), channel_id=1, source_target_pairs={{0,2},{1,3},{2,0},{3,1},{4,6},{5,7},{6,4},{7,5},{8,10},{9,11},{10,... | collective-permute-start | bytes 1179656 | tf_op jit(solution)/shard_map/ppermute | solution.py:115
  68.4 27.8 %collective-permute-start.7 = (bf16[512,384]{1,0:T(8,128)(2,1)}, bf16[512,384]{1,0:T(8,128)(2,1)}, u32[]{:S(2)}, u32[]{:S(2)}) collective-permute-start(bf16[512,384]{1,0:T(8,128)(2,1)} %get-tuple-element.35), channel_id=1, source_target_pairs={{0,3},{1,0},{2,1},{3,2},{4,7},{5,4},{6,5},{7,6},{8,11},{9,8},{10,9... | collective-permute-start | bytes 1179656 | tf_op jit(solution)/shard_map/ppermute | solution.py:115
  73.1 4.8 %copy-start.14 = (bf16[128,3072]{1,0:T(8,128)(2,1)S(1)}, bf16[128,3072]{1,0:T(8,128)(2,1)}, u32[]{:S(2)}) copy-start(bf16[128,3072]{1,0:T(8,128)(2,1)} %copy-done.13) | copy-start | bytes 2359300
  73.7 7.2 %copy-start.7 = (bf16[1,128,364]{2,1,0:T(8,128)(2,1)S(1)}, bf16[1,128,364]{2,1,0:T(8,128)(2,1)}, u32[]{:S(2)}) copy-start(bf16[1,128,364]{2,1,0:T(8,128)(2,1)} %copy-done.6) | copy-start | bytes 279556
  73.7 7.2 %copy-start.9 = (bf16[128,364]{1,0:T(8,128)(2,1)S(1)}, bf16[128,364]{1,0:T(8,128)(2,1)}, u32[]{:S(2)}) copy-start(bf16[128,364]{1,0:T(8,128)(2,1)} %reshape.183) | copy-start | bytes 279556
  73.7 7.2 %copy-start.10 = (bf16[128,364]{1,0:T(8,128)(2,1)S(1)}, bf16[128,364]{1,0:T(8,128)(2,1)}, u32[]{:S(2)}) copy-start(bf16[128,364]{1,0:T(8,128)(2,1)} %reshape.188) | copy-start | bytes 279556
  73.7 7.3 %copy-start.11 = (bf16[128,364]{1,0:T(8,128)(2,1)S(1)}, bf16[128,364]{1,0:T(8,128)(2,1)}, u32[]{:S(2)}) copy-start(bf16[128,364]{1,0:T(8,128)(2,1)} %reshape.193) | copy-start | bytes 279556
  87.4 10.7 %copy-start = (bf16[3,512,512]{1,2,0:T(8,128)(2,1)S(1)}, bf16[3,512,512]{1,2,0:T(8,128)(2,1)}, u32[]{:S(2)}) copy-start(bf16[3,512,512]{1,2,0:T(8,128)(2,1)} %exponential_convert_fusion) | copy-start | bytes 4718596
  87.4 65.7 %collective-permute-start.22 = (bf16[128,3072]{1,0:T(8,128)(2,1)}, bf16[128,3072]{1,0:T(8,128)(2,1)}, u32[]{:S(2)}, u32[]{:S(2)}) collective-permute-start(bf16[128,3072]{1,0:T(8,128)(2,1)} %bitcast.31), channel_id=1, source_target_pairs={{0,12},{4,0},{8,4},{12,8},{1,13},{5,1},{9,5},{13,9},{2,14},{6,2},{... | collective-permute-start | bytes 2359304 | tf_op jit(solution)/shard_map/ppermute | solution.py:115
  94.7 5.0 %copy-start.2 = (bf16[512,3,128]{0,2,1:T(8,128)(2,1)S(1)}, bf16[512,3,128]{0,2,1:T(8,128)(2,1)}, u32[]{:S(2)}) copy-start(bf16[512,3,128]{0,2,1:T(8,128)(2,1)} %squeeze.53) | copy-start | bytes 1179652
  94.7 61.0 %collective-permute-start.23 = (bf16[512,364]{1,0:T(8,128)(2,1)}, bf16[512,364]{1,0:T(8,128)(2,1)}, u32[]{:S(2)}, u32[]{:S(2)}) collective-permute-start(bf16[512,364]{1,0:T(8,128)(2,1)} %bitcast.38), channel_id=1, source_target_pairs={{0,16},{16,0},{1,17},{17,1},{2,18},{18,2},{3,19},{19,3},{4,20},{20... | collective-permute-start | bytes 1118216 | tf_op jit(solution)/shard_map/ppermute | solution.py:17
  100.1 1.3 copy-start.1
  100.8 1.8 copy-start.3
  103.7 12.6 %copy-start.5 = (bf16[512,3,128]{0,2,1:T(8,128)(2,1)S(1)}, bf16[512,3,128]{0,2,1:T(8,128)(2,1)}, u32[]{:S(2)}) copy-start(bf16[512,3,128]{0,2,1:T(8,128)(2,1)} %get-tuple-element.66) | copy-start | bytes 1179652
  105.1 12.0 %copy-start.4 = (bf16[512,3,128]{0,2,1:T(8,128)(2,1)S(1)}, bf16[512,3,128]{0,2,1:T(8,128)(2,1)}, u32[]{:S(2)}) copy-start(bf16[512,3,128]{0,2,1:T(8,128)(2,1)} %get-tuple-element.70) | copy-start | bytes 1179652
  108.4 17.5 %collective-permute-start.11 = (bf16[512,384]{0,1:T(8,128)(2,1)S(1)}, bf16[512,384]{0,1:T(8,128)(2,1)S(1)}, u32[]{:S(2)}, u32[]{:S(2)}) collective-permute-start(bf16[512,384]{0,1:T(8,128)(2,1)S(1)} %bitcast.141), channel_id=1, source_target_pairs={{0,3},{1,0},{2,1},{3,2},{4,7},{5,4},{6,5},{7,6},{8,11},{9,8},{10,9... | collective-permute-start | bytes 1179656 | tf_op jit(solution)/shard_map/ppermute | solution.py:115
  118.7 33.0 %collective-permute-start.13 = (bf16[512,384]{0,1:T(8,128)(2,1)S(1)}, bf16[512,384]{0,1:T(8,128)(2,1)S(1)}, u32[]{:S(2)}, u32[]{:S(2)}) collective-permute-start(bf16[512,384]{0,1:T(8,128)(2,1)S(1)} %bitcast.142), channel_id=1, source_target_pairs={{0,2},{1,3},{2,0},{3,1},{4,6},{5,7},{6,4},{7,5},{8,10},{9,11},{10,... | collective-permute-start | bytes 1179656 | tf_op jit(solution)/shard_map/ppermute | solution.py:115
  121.8 43.2 %collective-permute-start.10 = (bf16[512,384]{0,1:T(8,128)(2,1)S(1)}, bf16[512,384]{0,1:T(8,128)(2,1)S(1)}, u32[]{:S(2)}, u32[]{:S(2)}) collective-permute-start(bf16[512,384]{0,1:T(8,128)(2,1)S(1)} %bitcast.143), channel_id=1, source_target_pairs={{0,16},{16,0},{1,17},{17,1},{2,18},{18,2},{3,19},{19,3},{4,20},{20... | collective-permute-start | bytes 1179656 | tf_op jit(solution)/shard_map/ppermute | solution.py:17
  125.9 37.6 %collective-permute-start.15 = (bf16[512,384]{0,1:T(8,128)(2,1)S(1)}, bf16[512,384]{0,1:T(8,128)(2,1)S(1)}, u32[]{:S(2)}, u32[]{:S(2)}) collective-permute-start(bf16[512,384]{0,1:T(8,128)(2,1)S(1)} %bitcast.144), channel_id=1, source_target_pairs={{0,1},{1,2},{2,3},{3,0},{4,5},{5,6},{6,7},{7,4},{8,9},{9,10},{10,1... | collective-permute-start | bytes 1179656 | tf_op jit(solution)/shard_map/ppermute | solution.py:115
  151.7 13.5 %collective-permute-start.12 = (bf16[512,384]{0,1:T(8,128)(2,1)S(1)}, bf16[512,384]{0,1:T(8,128)(2,1)S(1)}, u32[]{:S(2)}, u32[]{:S(2)}) collective-permute-start(bf16[512,384]{0,1:T(8,128)(2,1)S(1)} %collective-permute-done.11), channel_id=1, source_target_pairs={{0,16},{16,0},{1,17},{17,1},{2,18},{18,2},{3,19},{19,3},{4,20},{20... | collective-permute-start | bytes 1179656 | tf_op jit(solution)/shard_map/ppermute | solution.py:17
  153.2 19.0 %collective-permute-start.14 = (bf16[512,384]{0,1:T(8,128)(2,1)S(1)}, bf16[512,384]{0,1:T(8,128)(2,1)S(1)}, u32[]{:S(2)}, u32[]{:S(2)}) collective-permute-start(bf16[512,384]{0,1:T(8,128)(2,1)S(1)} %collective-permute-done.13), channel_id=1, source_target_pairs={{0,16},{16,0},{1,17},{17,1},{2,18},{18,2},{3,19},{19,3},{4,20},{20... | collective-permute-start | bytes 1179656 | tf_op jit(solution)/shard_map/ppermute | solution.py:17
  163.5 15.3 %collective-permute-start.16 = (bf16[512,384]{0,1:T(8,128)(2,1)S(1)}, bf16[512,384]{0,1:T(8,128)(2,1)S(1)}, u32[]{:S(2)}, u32[]{:S(2)}) collective-permute-start(bf16[512,384]{0,1:T(8,128)(2,1)S(1)} %collective-permute-done.15), channel_id=1, source_target_pairs={{0,16},{16,0},{1,17},{17,1},{2,18},{18,2},{3,19},{19,3},{4,20},{20... | collective-permute-start | bytes 1179656 | tf_op jit(solution)/shard_map/ppermute | solution.py:17
  179.0 2.9 %slice-start = ((s8[6291456]{0:T(1024)(128)(4,1)}), s8[4194304]{0:T(1024)(128)(4,1)S(1)}, s32[]{:S(2)}) async-start(s8[6291456]{0:T(1024)(128)(4,1)} %bitcast.136), calls=%async_computation | async-start | bytes 8388608
  179.3 2.6 %slice-start.1 = ((s8[6291456]{0:T(1024)(128)(4,1)}), s8[2097152]{0:T(1024)(128)(4,1)S(1)}, s32[]{:S(2)}) async-start(s8[6291456]{0:T(1024)(128)(4,1)} %bitcast.136), calls=%async_computation.1 | async-start | bytes 4194304
  179.7 15.2 %collective-permute-start.17 = (bf16[3,128,384]{2,1,0:T(8,128)(2,1)S(1)}, bf16[3,128,384]{2,1,0:T(8,128)(2,1)S(1)}, u32[]{:S(2)}, u32[]{:S(2)}) collective-permute-start(bf16[3,128,384]{2,1,0:T(8,128)(2,1)S(1)} %get-tuple-element.43), channel_id=1, source_target_pairs={{0,3},{1,0},{2,1},{3,2},{4,7},{5,4},{6,5},{7,6},{8,11},{9,8},{10,9... | collective-permute-start | bytes 884744 | tf_op jit(solution)/shard_map/ppermute | solution.py:115
  179.8 24.0 %collective-permute-start.18 = (bf16[3,128,384]{2,1,0:T(8,128)(2,1)S(1)}, bf16[3,128,384]{2,1,0:T(8,128)(2,1)S(1)}, u32[]{:S(2)}, u32[]{:S(2)}) collective-permute-start(bf16[3,128,384]{2,1,0:T(8,128)(2,1)S(1)} %get-tuple-element.42), channel_id=1, source_target_pairs={{0,2},{1,3},{2,0},{3,1},{4,6},{5,7},{6,4},{7,5},{8,10},{9,11},{10,... | collective-permute-start | bytes 884744 | tf_op jit(solution)/shard_map/ppermute | solution.py:115
  179.9 23.9 %collective-permute-start.19 = (bf16[3,128,384]{2,1,0:T(8,128)(2,1)S(1)}, bf16[3,128,384]{2,1,0:T(8,128)(2,1)S(1)}, u32[]{:S(2)}, u32[]{:S(2)}) collective-permute-start(bf16[3,128,384]{2,1,0:T(8,128)(2,1)S(1)} %get-tuple-element.41), channel_id=1, source_target_pairs={{0,1},{1,2},{2,3},{3,0},{4,5},{5,6},{6,7},{7,4},{8,9},{9,10},{10,1... | collective-permute-start | bytes 884744 | tf_op jit(solution)/shard_map/ppermute | solution.py:115

commit v19 on v18

--- a/solution.py
+++ b/solution.py
@@ -277,7 +277,8 @@
     sendable = roll_blocks(
         jnp.stack([g.astype(jnp.bfloat16) for g in grad_list], 1), rank - me
     )
-    sendable, _ = lax.optimization_barrier((sendable, [p[0] for p in out_pieces]))
+    early = [p[0] for p in out_pieces] + [out_pieces[k][1] for k in range(n) if k != n // 2]
+    sendable, _ = lax.optimization_barrier((sendable, early))
     out_both, sendable = lax.optimization_barrier((out_both, sendable))
     out_weight_grad = lax.dot_general(
         out_both, grad_both, (((1,), (0,)), ((), ())), preferred_element_type=jnp.float32

time: 206 us -> 204 us (level)
  starting transfers between devices: 58.3 us -> 40.1 us
  waiting for transfers between devices: 59.3 us -> 73.4 us
  other arithmetic: 6.61 us -> 8.75 us
    ppermute x18, starting transfers between devices: 50.2 us -> 33.1 us  [shifted(): return lax.ppermute(x, axis, [(j, (j + step) % n) for j in range(n)])]
    ppermute x18, waiting for transfers between devices: 44.5 us -> 58.1 us  [shifted(): return lax.ppermute(x, axis, [(j, (j + step) % n) for j in range(n)])]
    unnamed x8, other arithmetic: 0.69 us -> 2.84 us
    unnamed x59 -> x61, local copies, waits for them, and re-layouts: 14.2 us -> 14.2 us
  transfers between devices with their start and end apart: 24 -> 24, of which waited for: 12 -> 10; matrix products, arithmetic and copies ran while one was open for 38% -> 39% of each run, Pallas kernels for 0% -> 0%
where the time goes in v19:
time: 204 us; the launch traced here: 203 us
  waiting for transfers between devices  73.4 us (36%)
  local copies, waits for them, and re-layouts  43.6 us (21%)
  starting transfers between devices  40.1 us (20%)
  matrix products  35.8 us (18%)
  other arithmetic  8.75 us (4%)
    ppermute x18, waiting for transfers between devices, shifted(): return lax.ppermute(x, axis, [(j, (j + step) % n) for j in range(n)])  58.1 us
    ppermute x18, starting transfers between devices, shifted(): return lax.ppermute(x, axis, [(j, (j + step) % n) for j in range(n)])  33.1 us
    ppermute x6, waiting for transfers between devices, swap_dp(): return lax.ppermute(x, 'dp', [(0, 1), (1, 0)])  15.3 us
    unnamed x61, local copies, waits for them, and re-layouts  14.2 us
    dot_general x1, matrix products, body_heads(): lax.dot_general(out_both, grad_both, (((1,), (0,)), ((), ())), preferred_...  13 us
    dot_general x1, matrix products, body_heads(): lax.dot_general(dense_grad, out_weight, (((1,), (1,)), ((), ())), preferr...  9.23 us
    dot_general x1, matrix products, contract_rows(): lax.dot_general(left, right, (((0,), (0,)), ((), ())), preferred_element_...  7.48 us
    ppermute x6, starting transfers between devices, swap_dp(): return lax.ppermute(x, 'dp', [(0, 1), (1, 0)])  7.08 us
  transfers between devices with their start and end apart: 24, of which 10 were waited for; matrix products, arithmetic and copies ran while one was open for 39% of the time, Pallas kernels for 0%

profile of v19, /device:TPU:0, one launch (start us, length us, event | category | flops | bytes accessed | tf_op | source)
XLA Modules:
  0.0 203.2 jit_solution(8105530923200405898)
XLA Ops:
  0.7 1.0 copy.30
  2.0 1.2 constant_dynamic-slice_fusion.7
  3.2 1.3 constant_dynamic-slice_fusion.5
  5.9 3.0 %collective-permute-start = (bf16[194048]{0:T(1024)(128)(2,1)S(1)}, bf16[194048]{0:T(1024)(128)(2,1)S(1)}, u32[]{:S(2)}, u32[]{:S(2)}) collective-permute-start(bf16[194048]{0:T(1024)(128)(2,1)S(1)} %get-tuple-element.61), channel_id=1, source_target_pairs={{0,1},{1,2},{2,3},{3,0},{4,5},{5,6},{6,7},{7,4},{8,9},{9,10},{10,1... | collective-permute-start | bytes 1164296 | tf_op jit(solution)/shard_map/ppermute | solution.py:115
  10.6 2.6 %collective-permute-start.1 = (bf16[194048]{0:T(1024)(128)(2,1)}, bf16[194048]{0:T(1024)(128)(2,1)}, u32[]{:S(2)}, u32[]{:S(2)}) collective-permute-start(bf16[194048]{0:T(1024)(128)(2,1)} %get-tuple-element.60), channel_id=1, source_target_pairs={{0,2},{1,3},{2,0},{3,1},{4,6},{5,7},{6,4},{7,5},{8,10},{9,11},{10,... | collective-permute-start | bytes 1164296 | tf_op jit(solution)/shard_map/ppermute | solution.py:115
  13.2 7.7 %collective-permute-done = bf16[194048]{0:T(1024)(128)(2,1)S(1)} collective-permute-done((bf16[194048]{0:T(1024)(128)(2,1)S(1)}, bf16[194048]{0:T(1024)(128)(2,1)S(1)}, u32[]{:S(2)}, u32[]{:S(2)}) %collective-permute-start) | collective-permute-done | bytes 388128 | tf_op jit(solution)/shard_map/ppermute | solution.py:115
  20.9 1.2 collective-permute-start.2
  24.1 12.6 %collective-permute-done.1 = bf16[194048]{0:T(1024)(128)(2,1)} collective-permute-done((bf16[194048]{0:T(1024)(128)(2,1)}, bf16[194048]{0:T(1024)(128)(2,1)}, u32[]{:S(2)}, u32[]{:S(2)}) %collective-permute-start.1) | collective-permute-done | bytes 388128 | tf_op jit(solution)/shard_map/ppermute | solution.py:115
  36.7 1.5 collective-permute-start.6
  41.2 1.2 collective-permute-done.2
  45.7 9.2 %fusion.2 = f32[512,1536]{1,0:T(8,128)S(1)} fusion(bf16[1536,3072]{1,0:T(8,128)(2,1)} %param.10, bf16[128,3072]{1,0:T(8,128)(2,1)S(1)} %collective-permute-done.5, bf16[128,3072]{1,0:T(8,128)(2,1)} %collective-permute-done.4, bf16[128,3072]{1,0:T(8,128)(2,1)} %collective-permute-done.3, bf16[128,3072]{1,0:T(8,128)(2,1)S(1)} %bitcast.154), kind=kOutput, calls=%fused_computation.2 | convolution fusion | flops 4844421120 | bytes 15728640 | tf_op jit(solution)/shard_map/dot_general | solution.py:222
  55.0 1.4 collective-permute-done.6
  56.4 1.5 collective-permute-start.21
  57.9 1.1 dynamic-slice_convert_fusion.2
  59.0 6.0 %collective-permute-start.9 = (bf16[512,384]{1,0:T(8,128)(2,1)}, bf16[512,384]{1,0:T(8,128)(2,1)}, u32[]{:S(2)}, u32[]{:S(2)}) collective-permute-start(bf16[512,384]{1,0:T(8,128)(2,1)} %get-tuple-element.36), channel_id=1, source_target_pairs={{0,1},{1,2},{2,3},{3,0},{4,5},{5,6},{6,7},{7,4},{8,9},{9,10},{10,1... | collective-permute-start | bytes 1179656 | tf_op jit(solution)/shard_map/ppermute | solution.py:115
  65.0 3.4 %collective-permute-start.8 = (bf16[512,384]{1,0:T(8,128)(2,1)}, bf16[512,384]{1,0:T(8,128)(2,1)}, u32[]{:S(2)}, u32[]{:S(2)}) collective-permute-start(bf16[512,384]{1,0:T(8,128)(2,1)} %get-tuple-element.37), channel_id=1, source_target_pairs={{0,2},{1,3},{2,0},{3,1},{4,6},{5,7},{6,4},{7,5},{8,10},{9,11},{10,... | collective-permute-start | bytes 1179656 | tf_op jit(solution)/shard_map/ppermute | solution.py:115
  71.5 1.6 multiply_reduce_fusion
  73.7 2.1 %constant_dynamic-update-slice_fusion.6 = bf16[1024,3072]{1,0:T(8,128)(2,1)} fusion(bf16[1024,3072]{1,0:T(8,128)(2,1)} %constant_dynamic-update-slice_fusion.7, bf16[128,3072]{1,0:T(8,128)(2,1)} %collective-permute-done.3), kind=kLoop, calls=%fused_computation.90 | loop fusion | bytes 1572864
  75.8 2.1 %constant_dynamic-update-slice_fusion.5 = bf16[1024,3072]{1,0:T(8,128)(2,1)} fusion(bf16[1024,3072]{1,0:T(8,128)(2,1)} %constant_dynamic-update-slice_fusion.6, bf16[128,3072]{1,0:T(8,128)(2,1)} %collective-permute-done.4), kind=kLoop, calls=%fused_computation.89 | loop fusion | bytes 1572864
  78.8 2.1 %constant_dynamic-update-slice_fusion.3 = bf16[1024,3072]{1,0:T(8,128)(2,1)} fusion(bf16[1024,3072]{1,0:T(8,128)(2,1)} %constant_dynamic-update-slice_fusion.4, bf16[1,128,3072]{2,1,0:T(8,128)(2,1)} %collective-permute-done.6), kind=kLoop, calls=%fused_computation.87 | loop fusion | bytes 1572864
  81.9 1.9 copy.37
  83.9 1.9 squeeze.53
  85.7 1.7 exponential_convert_fusion
  88.3 6.4 %collective-permute-done.8 = bf16[512,384]{1,0:T(8,128)(2,1)} collective-permute-done((bf16[512,384]{1,0:T(8,128)(2,1)}, bf16[512,384]{1,0:T(8,128)(2,1)}, u32[]{:S(2)}, u32[]{:S(2)}) %collective-permute-start.8) | collective-permute-done | bytes 393248 | tf_op jit(solution)/shard_map/ppermute | solution.py:115
  94.7 1.7 add_convert_fusion
  96.6 1.7 fusion.35
  99.9 1.1 fusion.33
  101.1 7.9 %collective-permute-start.11 = (bf16[512,384]{0,1:T(8,128)(2,1)S(1)}, bf16[512,384]{0,1:T(8,128)(2,1)S(1)}, u32[]{:S(2)}, u32[]{:S(2)}) collective-permute-start(bf16[512,384]{0,1:T(8,128)(2,1)S(1)} %bitcast.141), channel_id=1, source_target_pairs={{0,3},{1,0},{2,1},{3,2},{4,7},{5,4},{6,5},{7,6},{8,11},{9,8},{10,9... | collective-permute-start | bytes 1179656 | tf_op jit(solution)/shard_map/ppermute | solution.py:115
  108.9 2.5 %collective-permute-start.13 = (bf16[512,384]{0,1:T(8,128)(2,1)S(1)}, bf16[512,384]{0,1:T(8,128)(2,1)}, u32[]{:S(2)}, u32[]{:S(2)}) collective-permute-start(bf16[512,384]{0,1:T(8,128)(2,1)S(1)} %bitcast.142), channel_id=1, source_target_pairs={{0,2},{1,3},{2,0},{3,1},{4,6},{5,7},{6,4},{7,5},{8,10},{9,11},{10,... | collective-permute-start | bytes 1179656 | tf_op jit(solution)/shard_map/ppermute | solution.py:115
  111.5 1.1 reshape.197
  112.6 1.1 reshape.196
  114.0 1.4 constant_dynamic-slice_fusion.2
  115.4 1.3 constant_dynamic-slice_fusion.3
  120.0 2.1 %constant_dynamic-update-slice_fusion.2 = bf16[1024,3072]{1,0:T(8,128)(2,1)} fusion(bf16[1024,3072]{1,0:T(8,128)(2,1)} %constant_dynamic-update-slice_fusion.3, bf16[128,3072]{1,0:T(8,128)(2,1)} %collective-permute-done.20), kind=kLoop, calls=%fused_computation.86 | loop fusion | bytes 1572864
  122.0 1.5 collective-permute-start.23
  123.5 2.1 %constant_dynamic-update-slice_fusion.1 = bf16[1024,3072]{1,0:T(8,128)(2,1)} fusion(bf16[1024,3072]{1,0:T(8,128)(2,1)} %constant_dynamic-update-slice_fusion.2, bf16[128,3072]{1,0:T(8,128)(2,1)} %collective-permute-done.21), kind=kLoop, calls=%fused_computation.85 | loop fusion | bytes 1572864
  126.1 19.8 %collective-permute-done.13 = bf16[512,384]{0,1:T(8,128)(2,1)} collective-permute-done((bf16[512,384]{0,1:T(8,128)(2,1)S(1)}, bf16[512,384]{0,1:T(8,128)(2,1)}, u32[]{:S(2)}, u32[]{:S(2)}) %collective-permute-start.13) | collective-permute-done | bytes 393248 | tf_op jit(solution)/shard_map/ppermute | solution.py:115
  145.9 1.5 collective-permute-start.12
  147.9 1.5 collective-permute-start.16
  149.4 2.1 %constant_dynamic-update-slice_fusion = bf16[1024,3072]{1,0:T(8,128)(2,1)} fusion(bf16[1024,3072]{1,0:T(8,128)(2,1)} %constant_dynamic-update-slice_fusion.1, bf16[128,3072]{1,0:T(8,128)(2,1)} %collective-permute-done.22), kind=kLoop, calls=%fused_computation.84 | loop fusion | bytes 1572864 | tf_op jit(solution)/shard_map/concatenate | solution.py:274
  151.5 7.5 %fusion.17 = f32[364,3072]{1,0:T(8,128)} fusion(bf16[1024,3072]{1,0:T(8,128)(2,1)} %constant_dynamic-update-slice_fusion, bf16[512,364]{1,0:T(8,128)(2,1)S(1)} %collective-permute-done.23, bf16[512,364]{1,0:T(8,128)(2,1)S(1)} %bitcast.150), kind=kOutput, calls=%fused_computation.39 | convolution fusion | flops 2291580928 | bytes 11509760 | tf_op jit(solution)/shard_map/dot_general | solution.py:11
  159.1 13.9 %collective-permute-done.16 = bf16[512,384]{0,1:T(8,128)(2,1)S(1)} collective-permute-done((bf16[512,384]{0,1:T(8,128)(2,1)S(1)}, bf16[512,384]{0,1:T(8,128)(2,1)S(1)}, u32[]{:S(2)}, u32[]{:S(2)}) %collective-permute-start.16) | collective-permute-done | bytes 393248 | tf_op jit(solution)/shard_map/ppermute | solution.py:17
  173.1 1.1 fusion.24
  174.5 1.3 fusion.25
  176.4 1.9 collective-permute-start.18
  178.4 13.0 %fusion = f32[4,384,3072]{2,1,0:T(8,128)} fusion(bf16[4,1024,384]{1,2,0:T(8,128)(2,1)S(1)} %constant_dynamic-slice_fusion.1, bf16[1024,3072]{1,0:T(8,128)(2,1)S(1)} %bitcast.137), kind=kOutput, calls=%fused_computation | convolution fusion | flops 9663676416 | bytes 28311552 | tf_op jit(solution)/shard_map/dot_general | solution.py:283
  191.6 10.0 %collective-permute-done.18 = bf16[3,128,384]{2,1,0:T(8,128)(2,1)S(1)} collective-permute-done((bf16[3,128,384]{2,1,0:T(8,128)(2,1)S(1)}, bf16[3,128,384]{2,1,0:T(8,128)(2,1)S(1)}, u32[]{:S(2)}, u32[]{:S(2)}) %collective-permute-start.18) | collective-permute-done | bytes 294944 | tf_op jit(solution)/shard_map/ppermute | solution.py:115
  201.7 1.5 slice_bitcast_fusion
  (144 shorter events, 25.6 us)
Async XLA Ops:
  1.7 4.2 %copy-start.6 = (bf16[1,128,364]{2,1,0:T(8,128)(2,1)}, bf16[1,128,364]{2,1,0:T(8,128)(2,1)S(1)}, u32[]{:S(2)}) copy-start(bf16[1,128,364]{2,1,0:T(8,128)(2,1)S(1)} %copy.30) | copy-start | bytes 279556
  2.0 6.9 %copy-start.13 = (bf16[1,128,3072]{2,1,0:T(8,128)(2,1)S(1)}, bf16[1,128,3072]{2,1,0:T(8,128)(2,1)}, u32[]{:S(2)}) copy-start(bf16[1,128,3072]{2,1,0:T(8,128)(2,1)} %param.11) | copy-start | bytes 2359300
  5.9 15.0 %collective-permute-start = (bf16[194048]{0:T(1024)(128)(2,1)S(1)}, bf16[194048]{0:T(1024)(128)(2,1)S(1)}, u32[]{:S(2)}, u32[]{:S(2)}) collective-permute-start(bf16[194048]{0:T(1024)(128)(2,1)S(1)} %get-tuple-element.61), channel_id=1, source_target_pairs={{0,1},{1,2},{2,3},{3,0},{4,5},{5,6},{6,7},{7,4},{8,9},{9,10},{10,1... | collective-permute-start | bytes 1164296 | tf_op jit(solution)/shard_map/ppermute | solution.py:115
  8.9 36.4 %collective-permute-start.5 = (bf16[128,3072]{1,0:T(8,128)(2,1)S(1)}, bf16[128,3072]{1,0:T(8,128)(2,1)S(1)}, u32[]{:S(2)}, u32[]{:S(2)}) collective-permute-start(bf16[128,3072]{1,0:T(8,128)(2,1)S(1)} %bitcast.151), channel_id=1, source_target_pairs={{0,12},{4,0},{8,4},{12,8},{1,13},{5,1},{9,5},{13,9},{2,14},{6,2},{... | collective-permute-start | bytes 2359304 | tf_op jit(solution)/shard_map/ppermute | solution.py:115
  9.5 36.1 %collective-permute-start.4 = (bf16[128,3072]{1,0:T(8,128)(2,1)S(1)}, bf16[128,3072]{1,0:T(8,128)(2,1)}, u32[]{:S(2)}, u32[]{:S(2)}) collective-permute-start(bf16[128,3072]{1,0:T(8,128)(2,1)S(1)} %bitcast.152), channel_id=1, source_target_pairs={{0,8},{4,12},{8,0},{12,4},{1,9},{5,13},{9,1},{13,5},{2,10},{6,14},... | collective-permute-start | bytes 2359304 | tf_op jit(solution)/shard_map/ppermute | solution.py:115
  10.4 35.3 %collective-permute-start.3 = (bf16[128,3072]{1,0:T(8,128)(2,1)S(1)}, bf16[128,3072]{1,0:T(8,128)(2,1)}, u32[]{:S(2)}, u32[]{:S(2)}) collective-permute-start(bf16[128,3072]{1,0:T(8,128)(2,1)S(1)} %bitcast.153), channel_id=1, source_target_pairs={{0,4},{4,8},{8,12},{12,0},{1,5},{5,9},{9,13},{13,1},{2,6},{6,10},{... | collective-permute-start | bytes 2359304 | tf_op jit(solution)/shard_map/ppermute | solution.py:115
  10.6 26.1 %collective-permute-start.1 = (bf16[194048]{0:T(1024)(128)(2,1)}, bf16[194048]{0:T(1024)(128)(2,1)}, u32[]{:S(2)}, u32[]{:S(2)}) collective-permute-start(bf16[194048]{0:T(1024)(128)(2,1)} %get-tuple-element.60), channel_id=1, source_target_pairs={{0,2},{1,3},{2,0},{3,1},{4,6},{5,7},{6,4},{7,5},{8,10},{9,11},{10,... | collective-permute-start | bytes 1164296 | tf_op jit(solution)/shard_map/ppermute | solution.py:115
  20.9 21.5 %collective-permute-start.2 = (bf16[194048]{0:T(1024)(128)(2,1)S(1)}, bf16[194048]{0:T(1024)(128)(2,1)}, u32[]{:S(2)}, u32[]{:S(2)}) collective-permute-start(bf16[194048]{0:T(1024)(128)(2,1)S(1)} %get-tuple-element.59), channel_id=1, source_target_pairs={{0,3},{1,0},{2,1},{3,2},{4,7},{5,4},{6,5},{7,6},{8,11},{9,8},{10,9... | collective-permute-start | bytes 1164296 | tf_op jit(solution)/shard_map/ppermute | solution.py:115
  36.7 19.7 %collective-permute-start.6 = (bf16[1,128,3072]{2,1,0:T(8,128)(2,1)S(1)}, bf16[1,128,3072]{2,1,0:T(8,128)(2,1)}, u32[]{:S(2)}, u32[]{:S(2)}) collective-permute-start(bf16[1,128,3072]{2,1,0:T(8,128)(2,1)S(1)} %copy-done.13), channel_id=1, source_target_pairs={{0,16},{16,0},{1,17},{17,1},{2,18},{18,2},{3,19},{19,3},{4,20},{20... | collective-permute-start | bytes 2359304 | tf_op jit(solution)/shard_map/ppermute | solution.py:17
  45.3 9.7 %copy-start.14 = (bf16[128,3072]{1,0:T(8,128)(2,1)}, bf16[128,3072]{1,0:T(8,128)(2,1)S(1)}, u32[]{:S(2)}) copy-start(bf16[128,3072]{1,0:T(8,128)(2,1)S(1)} %collective-permute-done.5) | copy-start | bytes 2359300
  55.0 13.8 %copy-start.9 = (f32[512,1536]{1,0:T(8,128)}, f32[512,1536]{1,0:T(8,128)S(1)}, u32[]{:S(2)}) copy-start(f32[512,1536]{1,0:T(8,128)S(1)} %fusion.2) | copy-start | bytes 9437188
  56.4 63.3 %collective-permute-start.20 = (bf16[128,3072]{1,0:T(8,128)(2,1)}, bf16[128,3072]{1,0:T(8,128)(2,1)}, u32[]{:S(2)}, u32[]{:S(2)}) collective-permute-start(bf16[128,3072]{1,0:T(8,128)(2,1)} %bitcast.31), channel_id=1, source_target_pairs={{0,4},{4,8},{8,12},{12,0},{1,5},{5,9},{9,13},{13,1},{2,6},{6,10},{... | collective-permute-start | bytes 2359304 | tf_op jit(solution)/shard_map/ppermute | solution.py:115
  56.4 65.6 %collective-permute-start.21 = (bf16[128,3072]{1,0:T(8,128)(2,1)}, bf16[128,3072]{1,0:T(8,128)(2,1)}, u32[]{:S(2)}, u32[]{:S(2)}) collective-permute-start(bf16[128,3072]{1,0:T(8,128)(2,1)} %bitcast.31), channel_id=1, source_target_pairs={{0,8},{4,12},{8,0},{12,4},{1,9},{5,13},{9,1},{13,5},{2,10},{6,14},... | collective-permute-start | bytes 2359304 | tf_op jit(solution)/shard_map/ppermute | solution.py:115
  59.0 28.4 %collective-permute-start.9 = (bf16[512,384]{1,0:T(8,128)(2,1)}, bf16[512,384]{1,0:T(8,128)(2,1)}, u32[]{:S(2)}, u32[]{:S(2)}) collective-permute-start(bf16[512,384]{1,0:T(8,128)(2,1)} %get-tuple-element.36), channel_id=1, source_target_pairs={{0,1},{1,2},{2,3},{3,0},{4,5},{5,6},{6,7},{7,4},{8,9},{9,10},{10,1... | collective-permute-start | bytes 1179656 | tf_op jit(solution)/shard_map/ppermute | solution.py:115
  65.0 29.7 %collective-permute-start.8 = (bf16[512,384]{1,0:T(8,128)(2,1)}, bf16[512,384]{1,0:T(8,128)(2,1)}, u32[]{:S(2)}, u32[]{:S(2)}) collective-permute-start(bf16[512,384]{1,0:T(8,128)(2,1)} %get-tuple-element.37), channel_id=1, source_target_pairs={{0,2},{1,3},{2,0},{3,1},{4,6},{5,7},{6,4},{7,5},{8,10},{9,11},{10,... | collective-permute-start | bytes 1179656 | tf_op jit(solution)/shard_map/ppermute | solution.py:115
  68.4 26.3 %collective-permute-start.7 = (bf16[512,384]{1,0:T(8,128)(2,1)}, bf16[512,384]{1,0:T(8,128)(2,1)}, u32[]{:S(2)}, u32[]{:S(2)}) collective-permute-start(bf16[512,384]{1,0:T(8,128)(2,1)} %get-tuple-element.35), channel_id=1, source_target_pairs={{0,3},{1,0},{2,1},{3,2},{4,7},{5,4},{6,5},{7,6},{8,11},{9,8},{10,9... | collective-permute-start | bytes 1179656 | tf_op jit(solution)/shard_map/ppermute | solution.py:115
  73.1 4.8 %copy-start.15 = (bf16[128,3072]{1,0:T(8,128)(2,1)S(1)}, bf16[128,3072]{1,0:T(8,128)(2,1)}, u32[]{:S(2)}) copy-start(bf16[128,3072]{1,0:T(8,128)(2,1)} %copy-done.14) | copy-start | bytes 2359300
  73.7 7.2 %copy-start.7 = (bf16[1,128,364]{2,1,0:T(8,128)(2,1)S(1)}, bf16[1,128,364]{2,1,0:T(8,128)(2,1)}, u32[]{:S(2)}) copy-start(bf16[1,128,364]{2,1,0:T(8,128)(2,1)} %copy-done.6) | copy-start | bytes 279556
  73.7 7.2 %copy-start.10 = (bf16[128,364]{1,0:T(8,128)(2,1)S(1)}, bf16[128,364]{1,0:T(8,128)(2,1)}, u32[]{:S(2)}) copy-start(bf16[128,364]{1,0:T(8,128)(2,1)} %reshape.183) | copy-start | bytes 279556
  73.7 7.2 %copy-start.11 = (bf16[128,364]{1,0:T(8,128)(2,1)S(1)}, bf16[128,364]{1,0:T(8,128)(2,1)}, u32[]{:S(2)}) copy-start(bf16[128,364]{1,0:T(8,128)(2,1)} %reshape.188) | copy-start | bytes 279556
  73.7 7.3 %copy-start.12 = (bf16[128,364]{1,0:T(8,128)(2,1)S(1)}, bf16[128,364]{1,0:T(8,128)(2,1)}, u32[]{:S(2)}) copy-start(bf16[128,364]{1,0:T(8,128)(2,1)} %reshape.193) | copy-start | bytes 279556
  87.4 9.2 %copy-start = (bf16[3,512,512]{1,2,0:T(8,128)(2,1)S(1)}, bf16[3,512,512]{1,2,0:T(8,128)(2,1)}, u32[]{:S(2)}) copy-start(bf16[3,512,512]{1,2,0:T(8,128)(2,1)} %exponential_convert_fusion) | copy-start | bytes 4718596
  87.4 10.8 %copy-start.2 = (bf16[512,3,128]{0,2,1:T(8,128)(2,1)S(1)}, bf16[512,3,128]{0,2,1:T(8,128)(2,1)}, u32[]{:S(2)}) copy-start(bf16[512,3,128]{0,2,1:T(8,128)(2,1)} %squeeze.53) | copy-start | bytes 1179652
  87.4 60.5 %collective-permute-start.22 = (bf16[128,3072]{1,0:T(8,128)(2,1)}, bf16[128,3072]{1,0:T(8,128)(2,1)}, u32[]{:S(2)}, u32[]{:S(2)}) collective-permute-start(bf16[128,3072]{1,0:T(8,128)(2,1)} %bitcast.31), channel_id=1, source_target_pairs={{0,12},{4,0},{8,4},{12,8},{1,13},{5,1},{9,5},{13,9},{2,14},{6,2},{... | collective-permute-start | bytes 2359304 | tf_op jit(solution)/shard_map/ppermute | solution.py:115
  98.6 1.3 copy-start.1
  99.3 12.2 %copy-start.3 = (f32[512,3,128]{0,2,1:T(8,128)S(1)}, f32[512,3,128]{0,2,1:T(8,128)}, u32[]{:S(2)}) copy-start(f32[512,3,128]{0,2,1:T(8,128)} %get-tuple-element.71) | copy-start | bytes 2359300
  101.1 24.5 %collective-permute-start.11 = (bf16[512,384]{0,1:T(8,128)(2,1)S(1)}, bf16[512,384]{0,1:T(8,128)(2,1)S(1)}, u32[]{:S(2)}, u32[]{:S(2)}) collective-permute-start(bf16[512,384]{0,1:T(8,128)(2,1)S(1)} %bitcast.141), channel_id=1, source_target_pairs={{0,3},{1,0},{2,1},{3,2},{4,7},{5,4},{6,5},{7,6},{8,11},{9,8},{10,9... | collective-permute-start | bytes 1179656 | tf_op jit(solution)/shard_map/ppermute | solution.py:115
  108.9 37.0 %collective-permute-start.13 = (bf16[512,384]{0,1:T(8,128)(2,1)S(1)}, bf16[512,384]{0,1:T(8,128)(2,1)}, u32[]{:S(2)}, u32[]{:S(2)}) collective-permute-start(bf16[512,384]{0,1:T(8,128)(2,1)S(1)} %bitcast.142), channel_id=1, source_target_pairs={{0,2},{1,3},{2,0},{3,1},{4,6},{5,7},{6,4},{7,5},{8,10},{9,11},{10,... | collective-permute-start | bytes 1179656 | tf_op jit(solution)/shard_map/ppermute | solution.py:115
  112.6 4.7 %copy-start.5 = (bf16[512,3,128]{0,2,1:T(8,128)(2,1)S(1)}, bf16[512,3,128]{0,2,1:T(8,128)(2,1)}, u32[]{:S(2)}) copy-start(bf16[512,3,128]{0,2,1:T(8,128)(2,1)} %get-tuple-element.66) | copy-start | bytes 1179652
  114.0 4.1 %copy-start.4 = (bf16[512,3,128]{0,2,1:T(8,128)(2,1)S(1)}, bf16[512,3,128]{0,2,1:T(8,128)(2,1)}, u32[]{:S(2)}) copy-start(bf16[512,3,128]{0,2,1:T(8,128)(2,1)} %get-tuple-element.70) | copy-start | bytes 1179652
  119.3 2.7 %copy-start.8 = (bf16[4,128,364]{2,1,0:T(8,128)(2,1)S(1)}, bf16[4,128,364]{2,1,0:T(8,128)(2,1)}, u32[]{:S(2)}) copy-start(bf16[4,128,364]{2,1,0:T(8,128)(2,1)} %constant_dynamic-slice_fusion) | copy-start | bytes 1118212
  119.7 27.7 %collective-permute-start.15 = (bf16[512,384]{0,1:T(8,128)(2,1)S(1)}, bf16[512,384]{0,1:T(8,128)(2,1)S(1)}, u32[]{:S(2)}, u32[]{:S(2)}) collective-permute-start(bf16[512,384]{0,1:T(8,128)(2,1)S(1)} %bitcast.143), channel_id=1, source_target_pairs={{0,1},{1,2},{2,3},{3,0},{4,5},{5,6},{6,7},{7,4},{8,9},{9,10},{10,1... | collective-permute-start | bytes 1179656 | tf_op jit(solution)/shard_map/ppermute | solution.py:115
  122.0 29.5 %collective-permute-start.23 = (bf16[512,364]{1,0:T(8,128)(2,1)S(1)}, bf16[512,364]{1,0:T(8,128)(2,1)S(1)}, u32[]{:S(2)}, u32[]{:S(2)}) collective-permute-start(bf16[512,364]{1,0:T(8,128)(2,1)S(1)} %bitcast.149), channel_id=1, source_target_pairs={{0,16},{16,0},{1,17},{17,1},{2,18},{18,2},{3,19},{19,3},{4,20},{20... | collective-permute-start | bytes 1118216 | tf_op jit(solution)/shard_map/ppermute | solution.py:17
  125.6 33.4 %collective-permute-start.10 = (bf16[512,384]{0,1:T(8,128)(2,1)S(1)}, bf16[512,384]{0,1:T(8,128)(2,1)S(1)}, u32[]{:S(2)}, u32[]{:S(2)}) collective-permute-start(bf16[512,384]{0,1:T(8,128)(2,1)S(1)} %bitcast.144), channel_id=1, source_target_pairs={{0,16},{16,0},{1,17},{17,1},{2,18},{18,2},{3,19},{19,3},{4,20},{20... | collective-permute-start | bytes 1179656 | tf_op jit(solution)/shard_map/ppermute | solution.py:17
  145.9 13.2 %collective-permute-start.12 = (bf16[512,384]{0,1:T(8,128)(2,1)S(1)}, bf16[512,384]{0,1:T(8,128)(2,1)S(1)}, u32[]{:S(2)}, u32[]{:S(2)}) collective-permute-start(bf16[512,384]{0,1:T(8,128)(2,1)S(1)} %collective-permute-done.11), channel_id=1, source_target_pairs={{0,16},{16,0},{1,17},{17,1},{2,18},{18,2},{3,19},{19,3},{4,20},{20... | collective-permute-start | bytes 1179656 | tf_op jit(solution)/shard_map/ppermute | solution.py:17
  147.4 25.7 %collective-permute-start.14 = (bf16[512,384]{0,1:T(8,128)(2,1)}, bf16[512,384]{0,1:T(8,128)(2,1)S(1)}, u32[]{:S(2)}, u32[]{:S(2)}) collective-permute-start(bf16[512,384]{0,1:T(8,128)(2,1)} %collective-permute-done.13), channel_id=1, source_target_pairs={{0,16},{16,0},{1,17},{17,1},{2,18},{18,2},{3,19},{19,3},{4,20},{20... | collective-permute-start | bytes 1179656 | tf_op jit(solution)/shard_map/ppermute | solution.py:17
  147.9 25.1 %collective-permute-start.16 = (bf16[512,384]{0,1:T(8,128)(2,1)S(1)}, bf16[512,384]{0,1:T(8,128)(2,1)S(1)}, u32[]{:S(2)}, u32[]{:S(2)}) collective-permute-start(bf16[512,384]{0,1:T(8,128)(2,1)S(1)} %collective-permute-done.15), channel_id=1, source_target_pairs={{0,16},{16,0},{1,17},{17,1},{2,18},{18,2},{3,19},{19,3},{4,20},{20... | collective-permute-start | bytes 1179656 | tf_op jit(solution)/shard_map/ppermute | solution.py:17
  174.4 4.0 %slice-start = ((s8[6291456]{0:T(1024)(128)(4,1)}), s8[4194304]{0:T(1024)(128)(4,1)S(1)}, s32[]{:S(2)}) async-start(s8[6291456]{0:T(1024)(128)(4,1)} %bitcast.136), calls=%async_computation | async-start | bytes 8388608
  175.9 2.5 %slice-start.1 = ((s8[6291456]{0:T(1024)(128)(4,1)}), s8[2097152]{0:T(1024)(128)(4,1)S(1)}, s32[]{:S(2)}) async-start(s8[6291456]{0:T(1024)(128)(4,1)} %bitcast.136), calls=%async_computation.1 | async-start | bytes 4194304
  176.4 15.1 %collective-permute-start.17 = (bf16[3,128,384]{2,1,0:T(8,128)(2,1)S(1)}, bf16[3,128,384]{2,1,0:T(8,128)(2,1)S(1)}, u32[]{:S(2)}, u32[]{:S(2)}) collective-permute-start(bf16[3,128,384]{2,1,0:T(8,128)(2,1)S(1)} %get-tuple-element.43), channel_id=1, source_target_pairs={{0,3},{1,0},{2,1},{3,2},{4,7},{5,4},{6,5},{7,6},{8,11},{9,8},{10,9... | collective-permute-start | bytes 884744 | tf_op jit(solution)/shard_map/ppermute | solution.py:115
  176.4 25.2 %collective-permute-start.18 = (bf16[3,128,384]{2,1,0:T(8,128)(2,1)S(1)}, bf16[3,128,384]{2,1,0:T(8,128)(2,1)S(1)}, u32[]{:S(2)}, u32[]{:S(2)}) collective-permute-start(bf16[3,128,384]{2,1,0:T(8,128)(2,1)S(1)} %get-tuple-element.42), channel_id=1, source_target_pairs={{0,2},{1,3},{2,0},{3,1},{4,6},{5,7},{6,4},{7,5},{8,10},{9,11},{10,... | collective-permute-start | bytes 884744 | tf_op jit(solution)/shard_map/ppermute | solution.py:115
  178.3 23.3 %collective-permute-start.19 = (bf16[3,128,384]{2,1,0:T(8,128)(2,1)S(1)}, bf16[3,128,384]{2,1,0:T(8,128)(2,1)S(1)}, u32[]{:S(2)}, u32[]{:S(2)}) collective-permute-start(bf16[3,128,384]{2,1,0:T(8,128)(2,1)S(1)} %get-tuple-element.41), channel_id=1, source_target_pairs={{0,1},{1,2},{2,3},{3,0},{4,5},{5,6},{6,7},{7,4},{8,9},{9,10},{10,1... | collective-permute-start | bytes 884744 | tf_op jit(solution)/shard_map/ppermute | solution.py:115
